TPU v7x, 32 devices: a whole 2x2x4 slice. The times are simulated.
32 devices in a mesh: dp: 4 (over z), ctx: 8 (over y, x, core).
Axes of the slice: x: 2, y: 2, z: 4, core: 2. Of those that a mesh axis runs over, the one named last changes fastest.
Arguments:
- queries: bfloat16 [4, 1024, 1792], P('dp', 'ctx'), may hold values from -40 to 40
- keys: bfloat16 [4, 1024, 256], P('dp', 'ctx'), may hold values from -8 to 8
- values: bfloat16 [4, 1024, 256], P('dp', 'ctx'), may hold values from -6 to 6
- spikes: int32 [4, 1024, 2], P('dp', 'ctx'), may hold values from 0 to 3
- window_lengths: int32 [2], replicated, may hold values from 128 to 256, as said below
- gain: float32 [1792], replicated, may hold values from 0.1 to 1.9
- cotangent: bfloat16 [4, 1024, 1792], P('dp', 'ctx'), may hold values from -6 to 6
Outputs:
- mixed: bfloat16 [4, 1024, 1792], P('dp', 'ctx')
- d_queries: bfloat16 [4, 1024, 1792], P('dp', 'ctx')
- keys_gradient: bfloat16 [4, 1024, 256], P('dp', 'ctx')
- values_gradient: bfloat16 [4, 1024, 256], P('dp', 'ctx')
- d_gain: float32 [1792], replicated
Inputs may be any that keep to these rules, and one draw needn't show every extreme that they name: `window_lengths`: in every draw one key-value head has a look-back of exactly 256.
All inputs are finite; a program needn't handle non-finite values.
Results may differ from a plain program's by a relative error of at most 0.012.
The roundings to bfloat16 on the way count: a program that leaves them out, or rounds other values in their place, can miss the bound.
Values may be sent and summed in bfloat16 or wider, within the bound.
No kernel may reach another device: no remote copies, remote signals or barrier semaphores. Data moves between devices by JAX's collectives and lax.ppermute only.
A program may use at most 64 MiB of HBM per device.

v0:
```python
import math

import jax
import jax.numpy as jnp
from jax import lax
from jax.sharding import PartitionSpec as P

QUERY_HEADS = 14
KEY_VALUE_HEADS = 2
HEAD_SIZE = 128
WINDOW_REACH = 256


epsilon = 1e-05


def carried_in(part, axis, combine, identity, reverse):
    count = lax.axis_size(axis)
    place = lax.axis_index(axis)
    ahead = count - 1 - place if reverse else place
    gathered = lax.all_gather(part, axis)
    state = jnp.zeros_like(part) + jnp.asarray(identity, part.dtype)

    def one(step, state):
        source = count - 1 - step if reverse else step
        return combine(state, lax.dynamic_index_in_dim(gathered, source, 0, False))

    return lax.fori_loop(0, ahead, one, state)


def shifted(block, axis, distance):
    devices = range(lax.axis_size(axis))
    route = [(i - distance, i) for i in devices if i - distance in devices]
    return lax.ppermute(block, axis, route)


def combine_sum(earlier, later):
    return earlier + later


def per_device(queries, keys, values, spikes, window_lengths, gain, cotangent):
    batch_inputs = queries.shape[0]
    token_rows = queries.shape[1]
    group_size = QUERY_HEADS // KEY_VALUE_HEADS
    reach = (WINDOW_REACH + token_rows - 2) // token_rows
    padding_rows = reach * token_rows
    window_rows = (reach + 1) * token_rows
    scale = HEAD_SIZE ** (-0.5)
    key_value_width = KEY_VALUE_HEADS * HEAD_SIZE
    query_heads = queries.reshape(batch_inputs, token_rows, KEY_VALUE_HEADS, group_size, HEAD_SIZE)
    key_heads = keys.reshape(batch_inputs, token_rows, KEY_VALUE_HEADS, HEAD_SIZE)
    value_heads = values.reshape(batch_inputs, token_rows, KEY_VALUE_HEADS, HEAD_SIZE)
    token_counts = spikes.astype(jnp.float32)[..., None]
    spiked = (value_heads.astype(jnp.float32) * token_counts).astype(jnp.bfloat16)
    local_state = jnp.einsum(
        "nrgd,nrge->ngde", key_heads, spiked, preferred_element_type=jnp.float32
    )
    prior = carried_in(local_state, "ctx", combine_sum, jnp.zeros_like(local_state), False)
    prior_half = prior.astype(jnp.bfloat16)
    earlier = []
    for distance in range(reach, 0, -1):
        earlier.append(shifted((keys, values), "ctx", distance))
    key_window = jnp.concatenate([piece[0] for piece in earlier] + [keys], axis=1).reshape(
        batch_inputs, window_rows, KEY_VALUE_HEADS, HEAD_SIZE
    )
    value_window = jnp.concatenate([piece[1] for piece in earlier] + [values], axis=1).reshape(
        batch_inputs, window_rows, KEY_VALUE_HEADS, HEAD_SIZE
    )
    row_idx = jnp.arange(token_rows)
    causal = (row_idx[:, None] >= row_idx[None, :]).astype(jnp.float32)
    key_idx = jnp.arange(window_rows)
    distance_back = row_idx[:, None] + padding_rows - key_idx[None, :]
    key_pos = lax.axis_index("ctx") * token_rows + key_idx - padding_rows
    visible = (
        (distance_back[None] >= 0)
        & (distance_back[None] < window_lengths[:, None, None])
        & (key_pos >= 0)[None, None, :]
    )
    lin_half = (
        jnp.einsum("nrghd,nsgd->nghrs", query_heads, key_heads, preferred_element_type=jnp.float32)
        * causal
    ).astype(jnp.bfloat16)
    linear = jnp.einsum("nghrs,nsge->nrghe", lin_half, spiked, preferred_element_type=jnp.float32)
    linear = linear + jnp.einsum(
        "nrghd,ngde->nrghe", query_heads, prior_half, preferred_element_type=jnp.float32
    )
    root = jnp.sqrt(jnp.mean(linear * linear, axis=-1, keepdims=True) + epsilon)
    normed = linear / root
    head_gains = gain.reshape(KEY_VALUE_HEADS, group_size, HEAD_SIZE)
    scores = (
        jnp.einsum("nrghd,nmgd->nghrm", query_heads, key_window, preferred_element_type=jnp.float32)
        * scale
    )
    scores = jnp.where(visible[None, :, None], scores, -1e30)
    top = jnp.max(scores, axis=-1, keepdims=True)
    expo = jnp.exp(scores - top)
    probs = expo / jnp.sum(expo, axis=-1, keepdims=True)
    probs_half = probs.astype(jnp.bfloat16)
    window_out = jnp.einsum(
        "nghrm,nmgd->nrghd", probs_half, value_window, preferred_element_type=jnp.float32
    )
    mixed = (
        (head_gains * normed + window_out)
        .astype(jnp.bfloat16)
        .reshape(batch_inputs, token_rows, QUERY_HEADS * HEAD_SIZE)
    )
    head_gradients = cotangent.reshape(
        batch_inputs, token_rows, KEY_VALUE_HEADS, group_size, HEAD_SIZE
    )
    grad_wide = head_gradients.astype(jnp.float32)
    total_tokens = batch_inputs * lax.axis_size("dp") * token_rows * lax.axis_size("ctx")
    gain_local = jnp.sum(grad_wide * normed, axis=(0, 1)).reshape(
        QUERY_HEADS * HEAD_SIZE
    ) / math.sqrt(total_tokens)
    d_gain = lax.psum(gain_local, ("dp", "ctx"))
    scaled = grad_wide * head_gains
    d_linear = (
        (scaled - normed * jnp.mean(scaled * normed, axis=-1, keepdims=True)) / root
    ).astype(jnp.bfloat16)
    suffix_local = jnp.einsum(
        "nrghd,nrghe->ngde", query_heads, d_linear, preferred_element_type=jnp.float32
    )
    later = carried_in(suffix_local, "ctx", combine_sum, jnp.zeros_like(suffix_local), True)
    later_half = later.astype(jnp.bfloat16)
    back_half = (
        jnp.einsum("nrghe,nsge->nghrs", d_linear, spiked, preferred_element_type=jnp.float32)
        * causal
    ).astype(jnp.bfloat16)
    lin_dq = jnp.einsum(
        "nrghe,ngde->nrghd", d_linear, prior_half, preferred_element_type=jnp.float32
    )
    lin_dq = lin_dq + jnp.einsum(
        "nghrs,nsgd->nrghd", back_half, key_heads, preferred_element_type=jnp.float32
    )
    linear_key_gradient = jnp.einsum(
        "nghrs,nrghd->nsgd", back_half, query_heads, preferred_element_type=jnp.float32
    )
    linear_key_gradient = linear_key_gradient + jnp.einsum(
        "nsge,ngde->nsgd", spiked, later_half, preferred_element_type=jnp.float32
    )
    d_spiked = jnp.einsum(
        "nghrs,nrghe->nsge", lin_half, d_linear, preferred_element_type=jnp.float32
    )
    d_spiked = d_spiked + jnp.einsum(
        "nsgd,ngde->nsge", key_heads, later_half, preferred_element_type=jnp.float32
    )
    linear_value_gradient = d_spiked * token_counts
    grad_probs = jnp.einsum(
        "nrghd,nmgd->nghrm", head_gradients, value_window, preferred_element_type=jnp.float32
    )
    delta = jnp.transpose(jnp.sum(grad_wide * window_out, axis=-1), (0, 2, 3, 1))
    grad_scores = (probs * (grad_probs - delta[..., None]) * scale).astype(jnp.bfloat16)
    window_dq = jnp.einsum(
        "nghrm,nmgd->nrghd", grad_scores, key_window, preferred_element_type=jnp.float32
    )
    key_grad_window = jnp.einsum(
        "nghrm,nrghd->nmgd", grad_scores, query_heads, preferred_element_type=jnp.float32
    ).reshape(batch_inputs, window_rows, key_value_width)
    value_grad_window = jnp.einsum(
        "nghrm,nrghd->nmgd", probs_half, head_gradients, preferred_element_type=jnp.float32
    ).reshape(batch_inputs, window_rows, key_value_width)
    received_k = jnp.zeros((batch_inputs, token_rows, key_value_width), jnp.float32)
    received_v = jnp.zeros((batch_inputs, token_rows, key_value_width), jnp.float32)
    for distance in range(1, reach + 1):
        start_row = (reach - distance) * token_rows
        sent_k = key_grad_window[:, start_row : start_row + token_rows]
        sent_v = value_grad_window[:, start_row : start_row + token_rows]
        got_k, got_v = shifted((sent_k, sent_v), "ctx", -distance)
        received_k = received_k + got_k
        received_v = received_v + got_v
    own_k = key_grad_window[:, padding_rows:]
    own_v = value_grad_window[:, padding_rows:]
    d_queries = (
        (lin_dq + window_dq)
        .astype(jnp.bfloat16)
        .reshape(batch_inputs, token_rows, QUERY_HEADS * HEAD_SIZE)
    )
    keys_gradient = (
        linear_key_gradient.reshape(batch_inputs, token_rows, key_value_width) + own_k + received_k
    ).astype(jnp.bfloat16)
    values_gradient = (
        linear_value_gradient.reshape(batch_inputs, token_rows, key_value_width)
        + own_v
        + received_v
    ).astype(jnp.bfloat16)
    return (mixed, d_queries, keys_gradient, values_gradient, d_gain)


def solution(mesh):
    placed = (
        P("dp", "ctx", None),
        P("dp", "ctx", None),
        P("dp", "ctx", None),
        P("dp", "ctx", None),
        P(),
        P(),
        P("dp", "ctx", None),
    )
    return jax.shard_map(
        per_device,
        mesh=mesh,
        in_specs=placed,
        out_specs=(
            P("dp", "ctx", None),
            P("dp", "ctx", None),
            P("dp", "ctx", None),
            P("dp", "ctx", None),
            P(),
        ),
        check_vma=False,
    )
```

profile of v0, /device:TPU:0, one launch (start us, length us, event | category | flops | bytes accessed | tf_op | source)
XLA Modules:
  0.0 137.0 jit_solution(10712127279275393058)
XLA Ops:
  7.2 1.0 copy.113
  8.2 4.8 %collective-permute-start.2 = (bf16[1,128,256]{1,2,0:T(8,128)(2,1)S(1)}, bf16[1,128,256]{1,2,0:T(8,128)(2,1)S(1)}, u32[]{:S(2)}, u32[]{:S(2)}) collective-permute-start(bf16[1,128,256]{1,2,0:T(8,128)(2,1)S(1)} %copy.113), channel_id=1, source_target_pairs={{0,2},{1,3},{2,4},{3,5},{4,6},{5,7},{8,10},{9,11},{10,12},{11,13},... | collective-permute-start | bytes 196616 | tf_op jit(solution)/shard_map/ppermute | solution.py:34
  13.1 1.5 %collective-permute-start.3 = (bf16[1,128,256]{1,2,0:T(8,128)(2,1)S(1)}, bf16[1,128,256]{1,2,0:T(8,128)(2,1)S(1)}, u32[]{:S(2)}, u32[]{:S(2)}) collective-permute-start(bf16[1,128,256]{1,2,0:T(8,128)(2,1)S(1)} %copy.113), channel_id=1, source_target_pairs={{0,1},{1,2},{2,3},{3,4},{4,5},{5,6},{6,7},{8,9},{9,10},{10,11},{11... | collective-permute-start | bytes 196616 | tf_op jit(solution)/shard_map/ppermute | solution.py:34
  14.5 3.9 %collective-permute-start = (bf16[1,128,256]{2,1,0:T(8,128)(2,1)}, bf16[1,128,256]{2,1,0:T(8,128)(2,1)S(1)}, u32[]{:S(2)}, u32[]{:S(2)}) collective-permute-start(bf16[1,128,256]{2,1,0:T(8,128)(2,1)} %param.13), channel_id=1, source_target_pairs={{0,2},{1,3},{2,4},{3,5},{4,6},{5,7},{8,10},{9,11},{10,12},{11,13},... | collective-permute-start | bytes 196616 | tf_op jit(solution)/shard_map/ppermute | solution.py:34
  18.4 3.2 %collective-permute-start.1 = (bf16[1,128,256]{2,1,0:T(8,128)(2,1)}, bf16[1,128,256]{2,1,0:T(8,128)(2,1)S(1)}, u32[]{:S(2)}, u32[]{:S(2)}) collective-permute-start(bf16[1,128,256]{2,1,0:T(8,128)(2,1)} %param.13), channel_id=1, source_target_pairs={{0,1},{1,2},{2,3},{3,4},{4,5},{5,6},{6,7},{8,9},{9,10},{10,11},{11... | collective-permute-start | bytes 196616 | tf_op jit(solution)/shard_map/ppermute | solution.py:34
  21.6 0.9 reshape.302
  22.6 0.9 reshape.284
  23.4 0.7 convert_bitcast_fusion
  24.5 0.8 copy.108
  25.4 1.3 copy.101
  26.9 1.5 %and_and_fusion = pred[2,128,384]{1,2,0:T(8,128)(4,1)} fusion(s32[128,384]{0,1:T(8,128)S(1)} %iota_subtract_fusion, s32[2]{0:T(128)} %param.15, pred[384]{0:T(512)(128)(4,1)S(1)} %add_compare_fusion, pred[128,384]{0,1:T(8,128)(4,1)S(1)} %broadcast_compare_fusion), kind=kLoop, calls=%fused_computation.54 | loop fusion | flops 294912 | bytes 344456 | tf_op jit(solution)/shard_map/and | solution.py:75
  28.3 1.1 fusion.23
  29.5 1.1 copy.119
  30.6 1.0 copy.124
  31.6 0.8 copy.112
  32.5 1.6 %fusion.5 = (f32[2,7,128]{2,1,0:T(8,128)S(1)}, f32[2,384,128,7]{2,1,3,0:T(8,128)S(1)}) fusion(pred[2,128,384]{1,2,0:T(8,128)(4,1)} %and_and_fusion, bf16[384,2,128,1]{0,2,3,1:T(8,128)(2,1)S(1)} %bitcast.263, bf16[128,2,7,128]{0,3,2,1:T(8,128)(2,1)S(1)} %bitcast.255), kind=kOutput, calls=%fused_computation.10 | convolution fusion | flops 178223360 | bytes 3513344 | tf_op jit(solution)/shard_map/nrghd,nmgd->nghrm/dot_general | solution.py:91
  34.7 0.9 fusion.7
  35.6 0.7 fusion.47
  36.4 1.7 %copy.195 = f32[1,128,256]{2,1,0:T(8,128)} copy(f32[1,128,256]{1,2,0:T(8,128)} %get-tuple-element.146) | data formatting | bytes 262144
  38.0 1.3 collective-permute-start.6
  39.3 1.7 %copy.196 = f32[1,128,256]{2,1,0:T(8,128)} copy(f32[1,128,256]{1,2,0:T(8,128)} %get-tuple-element.147) | data formatting | bytes 262144
  41.0 1.3 collective-permute-start.7
  42.3 0.8 copy.194
  43.0 7.1 %all-gather.5.cloned.1.call-done = f32[16,128,128]{2,1,0:T(8,128)} async-done(((f32[2,128,128]{2,1,0:T(8,128)}), f32[16,128,128]{2,1,0:T(8,128)}) %all-gather.5.cloned.1.call-update) | async-done | bytes 1048592 | tf_op jit(solution)/shard_map/all_gather | solution.py:21
  50.5 1.4 %multiply_reduce_fusion.3 = (f32[128,2,7]{0,2,1:T(8,128)S(1)}, f32[1,128,2,7,128]{1,4,3,2,0:T(8,128)S(1)}) fusion(f32[1,128,2,7,128]{1,4,3,2,0:T(8,128)S(1)} %convolution_bitcast_fusion.3, bf16[2,7,128,128]{2,3,1,0:T(8,128)(2,1)} %fusion.23, bf16[128,2,128]{2,0,1:T(8,128)(2,1)} %copy-done.4), kind=kOutput, calls=%fused_computation.48 | convolution fusion | flops 59406592 | bytes 2366464 | tf_op jit(solution)/shard_map/nghrs,nsge->nrghe/dot_general | solution.py:83
  52.0 2.7 %multiply_reduce_fusion = (f32[2,7,128]{2,1,0:T(8,128)}, f32[128,2,7]{0,2,1:T(8,128)S(1)}, f32[128,2,7]{0,2,1:T(8,128)}, bf16[1,128,2,7,128]{1,4,3,2,0:T(8,128)(2,1)}) fusion(f32[1,128,2,7,128]{1,4,3,2,0:T(8,128)S(1)} %bitcast.260, f32[1,128,2,7,128]{1,4,3,2,0:T(8,128)S(1)} %get-tuple-element.152, f32[128,2,7]{0,2,1:T(8,128)S(1)} %add_sqrt_fusion, ...), kind=kOutput, calls=%fused_computation.43 | convolution fusion | flops 182119168 | bytes 5391360 | tf_op jit(solution)/shard_map/nghrm,nmgd->nrghd/dot_general | solution.py:99
  55.3 0.8 copy.130
  56.2 2.9 %fusion.6 = bf16[2,7,128,384]{2,3,1,0:T(8,128)(2,1)S(1)} fusion(bf16[384,2,128,1]{0,2,3,1:T(8,128)(2,1)S(1)} %bitcast.276, bf16[128,2,7,128]{0,3,2,1:T(8,128)(2,1)S(1)} %bitcast.270, f32[2,7,128]{2,1,0:T(8,128)S(1)} %bitcast.277, f32[2,7,128]{2,1,0:T(8,128)S(1)} %copy-done.27, f32[2,7,128]{2,1,0:T(8,128)S(1)} %get-tuple-element.153, ...), kind=kOutput, calls=%fused_computation.11 | convolution fusion | flops 181665792 | bytes 4903936 | tf_op jit(solution)/shard_map/nrghd,nmgd->nghrm/dot_general | solution.py:148
  59.7 0.7 fusion.48
  60.3 1.7 %copy.192 = f32[1,128,256]{2,1,0:T(8,128)} copy(f32[1,128,256]{1,2,0:T(8,128)} %get-tuple-element.149) | data formatting | bytes 262144
  62.0 1.3 collective-permute-start.4
  63.3 0.8 copy.193
  64.0 1.3 collective-permute-start.5
  65.3 0.7 copy.191
  66.9 1.2 fusion.20
  68.1 2.0 %copy.146 = bf16[1,128,1792]{2,1,0:T(8,128)(2,1)} copy(bf16[1,128,1792]{1,2,0:T(8,128)(2,1)} %bitcast.262) | data formatting | bytes 917504
  70.1 2.0 %copy.145 = bf16[1,128,1792]{2,1,0:T(8,128)(2,1)} copy(bf16[1,128,1792]{1,2,0:T(8,128)(2,1)} %bitcast.271) | data formatting | bytes 917504
  72.2 46.7 %psum.7 = f32[1792]{0:T(1024)} all-reduce(f32[1792]{0:T(1024)S(1)} %div.45), channel_id=1, replica_groups=mesh['dp'=4,'ctx'=8] {'dp','ctx'}, use_global_device_ids=true, to_apply=%region_10.11 | all-reduce | flops 1792 | bytes 14336 | tf_op jit(solution)/shard_map/psum | solution.py:115
  119.5 6.8 %while.23 = (s32[]{:T(128)}, f32[1,2,128,128]{3,2,1,0:T(8,128)S(1)}, s32[]{:T(128)}, f32[8,1,2,128,128]{4,3,2,1,0:T(8,128)}, s32[]{:T(128)}, /*index=5*/s32[]{:T(128)}, s32[]{:T(128)}, s32[]{:T(128)}) while((s32[]{:T(128)}, f32[1,2,128,128]{3,2,1,0:T(8,128)S(1)}, s32[]{:T(128)}, f32[8,1,2,128,128]{4,3,2,1,0:T(8,128)}, s32[]{:T(128)}, ...), condition=%wide.region_8.9_spmd, body=%wide.region_7.8_spmd.sunk | while | flops 32774 | bytes 393351 | solution.py:28
  119.5 0.9 bitcast_add_fusion.5
  120.5 0.9 bitcast_add_fusion.5
  121.5 0.9 bitcast_add_fusion.5
  122.4 0.9 bitcast_add_fusion.5
  123.4 0.9 bitcast_add_fusion.5
  124.3 0.9 bitcast_add_fusion.5
  125.3 0.9 bitcast_add_fusion.5
  126.9 1.6 %add_convert_fusion.1 = bf16[1,128,256]{2,1,0:T(8,128)(2,1)} fusion(f32[1,128,256]{2,1,0:T(8,128)} %collective-permute-done.6, f32[1,128,256]{2,1,0:T(8,128)} %collective-permute-done.7, f32[1,128,256]{2,1,0:T(8,128)S(1)} %copy.142, f32[1,128,256]{2,1,0:T(8,128)S(1)} %copy-done.16), kind=kLoop, calls=%fused_computation.60 | loop fusion | flops 131072 | bytes 589824 | tf_op jit(solution)/shard_map/convert_element_type | solution.py:185
  128.6 1.6 %add_convert_fusion.2 = bf16[1,128,256]{2,1,0:T(8,128)(2,1)} fusion(f32[1,128,256]{2,1,0:T(8,128)} %collective-permute-done.4, f32[1,128,256]{2,1,0:T(8,128)} %collective-permute-done.5, f32[1,128,256]{2,1,0:T(8,128)S(1)} %copy.134, f32[1,128,256]{2,1,0:T(8,128)S(1)} %copy-done.17), kind=kLoop, calls=%fused_computation.61 | loop fusion | flops 131072 | bytes 589824 | tf_op jit(solution)/shard_map/convert_element_type | solution.py:180
  (107 shorter events, 5.0 us)
Async XLA Ops:
  7.2 22.3 %copy-start.3 = (bf16[1,128,1792]{2,1,0:T(8,128)(2,1)S(1)}, bf16[1,128,1792]{2,1,0:T(8,128)(2,1)}, u32[]{:S(2)}) copy-start(bf16[1,128,1792]{2,1,0:T(8,128)(2,1)} %param.17) | copy-start | bytes 1376260
  7.2 43.0 %all-gather.5.cloned.1.call-start = ((), (), s32[]{:S(2)}) async-start(), calls=%async_computation | async-start | bytes 1179648 | tf_op jit(solution)/shard_map/all_gather | solution.py:21
  8.2 24.2 %collective-permute-start.2 = (bf16[1,128,256]{1,2,0:T(8,128)(2,1)S(1)}, bf16[1,128,256]{1,2,0:T(8,128)(2,1)S(1)}, u32[]{:S(2)}, u32[]{:S(2)}) collective-permute-start(bf16[1,128,256]{1,2,0:T(8,128)(2,1)S(1)} %copy.113), channel_id=1, source_target_pairs={{0,2},{1,3},{2,4},{3,5},{4,6},{5,7},{8,10},{9,11},{10,12},{11,13},... | collective-permute-start | bytes 196616 | tf_op jit(solution)/shard_map/ppermute | solution.py:34
  13.1 19.4 %collective-permute-start.3 = (bf16[1,128,256]{1,2,0:T(8,128)(2,1)S(1)}, bf16[1,128,256]{1,2,0:T(8,128)(2,1)S(1)}, u32[]{:S(2)}, u32[]{:S(2)}) collective-permute-start(bf16[1,128,256]{1,2,0:T(8,128)(2,1)S(1)} %copy.113), channel_id=1, source_target_pairs={{0,1},{1,2},{2,3},{3,4},{4,5},{5,6},{6,7},{8,9},{9,10},{10,11},{11... | collective-permute-start | bytes 196616 | tf_op jit(solution)/shard_map/ppermute | solution.py:34
  14.5 17.0 %collective-permute-start = (bf16[1,128,256]{2,1,0:T(8,128)(2,1)}, bf16[1,128,256]{2,1,0:T(8,128)(2,1)S(1)}, u32[]{:S(2)}, u32[]{:S(2)}) collective-permute-start(bf16[1,128,256]{2,1,0:T(8,128)(2,1)} %param.13), channel_id=1, source_target_pairs={{0,2},{1,3},{2,4},{3,5},{4,6},{5,7},{8,10},{9,11},{10,12},{11,13},... | collective-permute-start | bytes 196616 | tf_op jit(solution)/shard_map/ppermute | solution.py:34
  18.4 13.2 %collective-permute-start.1 = (bf16[1,128,256]{2,1,0:T(8,128)(2,1)}, bf16[1,128,256]{2,1,0:T(8,128)(2,1)S(1)}, u32[]{:S(2)}, u32[]{:S(2)}) collective-permute-start(bf16[1,128,256]{2,1,0:T(8,128)(2,1)} %param.13), channel_id=1, source_target_pairs={{0,1},{1,2},{2,3},{3,4},{4,5},{5,6},{6,7},{8,9},{9,10},{10,11},{11... | collective-permute-start | bytes 196616 | tf_op jit(solution)/shard_map/ppermute | solution.py:34
  23.4 8.1 %copy-start.7 = (bf16[128,2,128]{2,1,0:T(2,128)(2,1)}, bf16[128,2,128]{2,1,0:T(2,128)(2,1)S(1)}, u32[]{:S(2)}) copy-start(bf16[128,2,128]{2,1,0:T(2,128)(2,1)S(1)} %reshape.284) | copy-start | bytes 196612
  24.1 1.2 copy-start.23
  24.2 1.2 copy-start.4
  24.5 7.1 %copy-start.28 = (f32[1792]{0:T(1024)S(1)}, f32[1792]{0:T(1024)}, u32[]{:S(2)}) copy-start(f32[1792]{0:T(1024)} %param.16) | copy-start | bytes 21508
  24.5 7.1 %copy-start.20 = (bf16[1,128,256]{2,1,0:T(8,128)(2,1)S(1)}, bf16[1,128,256]{2,1,0:T(8,128)(2,1)}, u32[]{:S(2)}) copy-start(bf16[1,128,256]{2,1,0:T(8,128)(2,1)} %param.13) | copy-start | bytes 196612
  25.3 94.2 %all-gather.7.cloned.1.call-start = ((), (), s32[]{:S(2)}) async-start(), calls=%async_computation.1 | async-start | bytes 1179648 | tf_op jit(solution)/shard_map/all_gather | solution.py:21
  26.9 5.6 %copy-start.12 = (bf16[128,2,128,1]{0,2,3,1:T(8,128)(2,1)}, bf16[128,2,128,1]{0,2,3,1:T(8,128)(2,1)S(1)}, u32[]{:S(2)}) copy-start(bf16[128,2,128,1]{0,2,3,1:T(8,128)(2,1)S(1)} %copy.163) | copy-start | bytes 196612
  28.3 4.2 %copy-start.14 = (f32[128,128]{0,1:T(8,128)}, f32[128,128]{0,1:T(8,128)S(1)}, u32[]{:S(2)}) copy-start(f32[128,128]{0,1:T(8,128)S(1)} %fusion.38) | copy-start | bytes 196612
  31.6 2.5 %copy-start.9 = (pred[2,128,384]{1,2,0:T(8,128)(4,1)S(1)}, pred[2,128,384]{1,2,0:T(8,128)(4,1)}, u32[]{:S(2)}) copy-start(pred[2,128,384]{1,2,0:T(8,128)(4,1)} %and_and_fusion) | copy-start | bytes 294916
  32.5 2.2 %copy-start.18 = (bf16[1,128,1792]{1,2,0:T(8,128)(2,1)S(1)}, bf16[1,128,1792]{1,2,0:T(8,128)(2,1)}, u32[]{:S(2)}) copy-start(bf16[1,128,1792]{1,2,0:T(8,128)(2,1)} %copy.124) | copy-start | bytes 1376260
  34.1 17.9 %copy-start = (f32[2,384,128,7]{2,1,3,0:T(8,128)}, f32[2,384,128,7]{2,1,3,0:T(8,128)S(1)}, u32[]{:S(2)}) copy-start(f32[2,384,128,7]{2,1,3,0:T(8,128)S(1)} %get-tuple-element.154) | copy-start | bytes 8257540
  34.7 0.9 copy-start.25
  38.0 88.9 %collective-permute-start.6 = (f32[1,128,256]{2,1,0:T(8,128)}, f32[1,128,256]{2,1,0:T(8,128)}, u32[]{:S(2)}, u32[]{:S(2)}) collective-permute-start(f32[1,128,256]{2,1,0:T(8,128)} %copy.195), channel_id=1, source_target_pairs={{1,0},{2,1},{3,2},{4,3},{5,4},{6,5},{7,6},{9,8},{10,9},{11,10},{12... | collective-permute-start | bytes 393224 | tf_op jit(solution)/shard_map/ppermute | solution.py:34
  41.0 85.9 %collective-permute-start.7 = (f32[1,128,256]{2,1,0:T(8,128)}, f32[1,128,256]{2,1,0:T(8,128)}, u32[]{:S(2)}, u32[]{:S(2)}) collective-permute-start(f32[1,128,256]{2,1,0:T(8,128)} %copy.196), channel_id=1, source_target_pairs={{2,0},{3,1},{4,2},{5,3},{6,4},{7,5},{10,8},{11,9},{12,10},{13,11},... | collective-permute-start | bytes 393224 | tf_op jit(solution)/shard_map/ppermute | solution.py:34
  50.2 1.8 %copy-start.2 = (f32[1,128,1792]{1,2,0:T(8,128)S(1)}, f32[1,128,1792]{1,2,0:T(8,128)}, u32[]{:S(2)}) copy-start(f32[1,128,1792]{1,2,0:T(8,128)} %copy.119) | copy-start | bytes 2752516
  50.2 1.8 %copy-start.10 = (pred[2,128,384]{1,2,0:T(8,128)(4,1)S(1)}, pred[2,128,384]{1,2,0:T(8,128)(4,1)}, u32[]{:S(2)}) copy-start(pred[2,128,384]{1,2,0:T(8,128)(4,1)} %and_and_fusion) | copy-start | bytes 294916
  50.2 1.8 %copy-start.21 = (bf16[1,384,256]{1,2,0:T(8,128)(2,1)S(1)}, bf16[1,384,256]{1,2,0:T(8,128)(2,1)}, u32[]{:S(2)}) copy-start(bf16[1,384,256]{1,2,0:T(8,128)(2,1)} %copy.112) | copy-start | bytes 589828
  50.2 1.8 %copy-start.26 = (f32[2,7,128]{2,1,0:T(8,128)S(1)}, f32[2,7,128]{2,1,0:T(8,128)}, u32[]{:S(2)}) copy-start(f32[2,7,128]{2,1,0:T(8,128)} %copy-done.25) | copy-start | bytes 21508
  54.7 1.4 %copy-start.11 = (pred[2,128,384]{1,2,0:T(8,128)(4,1)S(1)}, pred[2,128,384]{1,2,0:T(8,128)(4,1)}, u32[]{:S(2)}) copy-start(pred[2,128,384]{1,2,0:T(8,128)(4,1)} %and_and_fusion) | copy-start | bytes 294916
  54.7 1.4 %copy-start.19 = (bf16[1,128,1792]{1,2,0:T(8,128)(2,1)S(1)}, bf16[1,128,1792]{1,2,0:T(8,128)(2,1)}, u32[]{:S(2)}) copy-start(bf16[1,128,1792]{1,2,0:T(8,128)(2,1)} %copy.124) | copy-start | bytes 1376260
  54.7 1.4 %copy-start.22 = (bf16[1,384,256]{1,2,0:T(8,128)(2,1)S(1)}, bf16[1,384,256]{1,2,0:T(8,128)(2,1)}, u32[]{:S(2)}) copy-start(bf16[1,384,256]{1,2,0:T(8,128)(2,1)} %copy.112) | copy-start | bytes 589828
  54.7 1.4 %copy-start.27 = (f32[2,7,128]{2,1,0:T(8,128)S(1)}, f32[2,7,128]{2,1,0:T(8,128)}, u32[]{:S(2)}) copy-start(f32[2,7,128]{2,1,0:T(8,128)} %copy-done.25) | copy-start | bytes 21508
  54.7 1.5 %copy-start.30 = (f32[128,2,7]{0,2,1:T(8,128)S(1)}, f32[128,2,7]{0,2,1:T(8,128)}, u32[]{:S(2)}) copy-start(f32[128,2,7]{0,2,1:T(8,128)} %get-tuple-element.127) | copy-start | bytes 21508
  59.1 7.0 %copy-start.5 = (bf16[128,2,128]{2,0,1:T(8,128)(2,1)S(1)}, bf16[128,2,128]{2,0,1:T(8,128)(2,1)}, u32[]{:S(2)}) copy-start(bf16[128,2,128]{2,0,1:T(8,128)(2,1)} %copy-done.4) | copy-start | bytes 196612
  59.1 7.0 %copy-start.15 = (f32[128,128]{0,1:T(8,128)S(1)}, f32[128,128]{0,1:T(8,128)}, u32[]{:S(2)}) copy-start(f32[128,128]{0,1:T(8,128)} %copy-done.14) | copy-start | bytes 196612
  59.1 7.3 %copy-start.13 = (bf16[128,2,128,1]{0,2,3,1:T(8,128)(2,1)S(1)}, bf16[128,2,128,1]{0,2,3,1:T(8,128)(2,1)}, u32[]{:S(2)}) copy-start(bf16[128,2,128,1]{0,2,3,1:T(8,128)(2,1)} %copy-done.12) | copy-start | bytes 196612
  62.0 66.6 %collective-permute-start.4 = (f32[1,128,256]{2,1,0:T(8,128)}, f32[1,128,256]{2,1,0:T(8,128)}, u32[]{:S(2)}, u32[]{:S(2)}) collective-permute-start(f32[1,128,256]{2,1,0:T(8,128)} %copy.192), channel_id=1, source_target_pairs={{1,0},{2,1},{3,2},{4,3},{5,4},{6,5},{7,6},{9,8},{10,9},{11,10},{12... | collective-permute-start | bytes 393224 | tf_op jit(solution)/shard_map/ppermute | solution.py:34
  64.0 64.5 %collective-permute-start.5 = (f32[1,128,256]{2,1,0:T(8,128)}, f32[1,128,256]{2,1,0:T(8,128)}, u32[]{:S(2)}, u32[]{:S(2)}) collective-permute-start(f32[1,128,256]{2,1,0:T(8,128)} %copy.193), channel_id=1, source_target_pairs={{2,0},{3,1},{4,2},{5,3},{6,4},{7,5},{10,8},{11,9},{12,10},{13,11},... | collective-permute-start | bytes 393224 | tf_op jit(solution)/shard_map/ppermute | solution.py:34
  66.9 5.3 %copy-start.29 = (f32[2,7,128]{2,1,0:T(8,128)S(1)}, f32[2,7,128]{2,1,0:T(8,128)}, u32[]{:S(2)}) copy-start(f32[2,7,128]{2,1,0:T(8,128)} %get-tuple-element.125) | copy-start | bytes 21508
  66.9 51.9 %copy-start.1 = (bf16[2,7,128,128]{2,3,1,0:T(8,128)(2,1)S(1)}, bf16[2,7,128,128]{2,3,1,0:T(8,128)(2,1)}, u32[]{:S(2)}) copy-start(bf16[2,7,128,128]{2,3,1,0:T(8,128)(2,1)} %fusion.23) | copy-start | bytes 1376260
  70.1 56.1 %copy-start.8 = (bf16[128,2,128]{2,1,0:T(2,128)(2,1)S(1)}, bf16[128,2,128]{2,1,0:T(2,128)(2,1)}, u32[]{:S(2)}) copy-start(bf16[128,2,128]{2,1,0:T(2,128)(2,1)} %copy-done.7) | copy-start | bytes 196612
  70.1 56.1 %copy-start.24 = (f32[128,2]{0,1:T(2,128)S(1)}, f32[128,2]{0,1:T(2,128)}, u32[]{:S(2)}) copy-start(f32[128,2]{0,1:T(2,128)} %copy-done.23) | copy-start | bytes 3076
  72.2 54.4 %copy-start.6 = (bf16[128,2,128]{2,0,1:T(8,128)(2,1)S(1)}, bf16[128,2,128]{2,0,1:T(8,128)(2,1)}, u32[]{:S(2)}) copy-start(bf16[128,2,128]{2,0,1:T(8,128)(2,1)} %copy-done.4) | copy-start | bytes 196612
  118.8 8.1 %copy-start.16 = (f32[1,128,256]{2,1,0:T(8,128)S(1)}, f32[1,128,256]{2,1,0:T(8,128)}, u32[]{:S(2)}) copy-start(f32[1,128,256]{2,1,0:T(8,128)} %copy.194) | copy-start | bytes 393220
  119.1 9.4 %copy-start.17 = (f32[1,128,256]{2,1,0:T(8,128)S(1)}, f32[1,128,256]{2,1,0:T(8,128)}, u32[]{:S(2)}) copy-start(f32[1,128,256]{2,1,0:T(8,128)} %copy.191) | copy-start | bytes 393220
Sparse Core Ops, SparseCore 0:
  25.4 24.7 all-gather.4
  56.2 32.5 all-gather.6
where the time goes:
time: 138 us; the launch traced here: 137 us
  blocking collectives  46.7 us (34%)
  local copies, waits for them, and re-layouts  21.6 us (16%)
  starting transfers between devices  18.6 us (13%)
  matrix products  14.9 us (11%)
  between operations  14.7 us (11%)
  other arithmetic  13.1 us (9%)
  waiting for transfers between devices  7.19 us (5%)
    psum x1, blocking collectives, per_device(): d_gain = lax.psum(gain_local, ('dp', 'ctx'))  46.7 us
    ppermute x8, starting transfers between devices, shifted(): return lax.ppermute(block, axis, route)  18.5 us
    unnamed x73, local copies, waits for them, and re-layouts  14.6 us
    all_gather x2, waiting for transfers between devices, carried_in(): gathered = lax.all_gather(part, axis)  7.14 us
    add x7, other arithmetic, combine_sum(): return earlier + later  6.56 us
    dot_general x1, matrix products, per_device(): jnp.einsum('nrghd,nmgd->nghrm', head_gradients, value_window, preferred_e...  2.9 us
  transfers between devices with their start and end apart: 10, of which 1 were waited for; matrix products, arithmetic and copies ran while one was open for 34% of the time, Pallas kernels for 0%

commit v1 on v0

--- a/solution.py
+++ b/solution.py
@@ -14,28 +14,42 @@
 epsilon = 1e-05
 
 
-def carried_in(part, axis, combine, identity, reverse):
+def exclusive_scan(part, axis, reverse):
     count = lax.axis_size(axis)
-    place = lax.axis_index(axis)
-    ahead = count - 1 - place if reverse else place
-    gathered = lax.all_gather(part, axis)
-    state = jnp.zeros_like(part) + jnp.asarray(identity, part.dtype)
-
-    def one(step, state):
-        source = count - 1 - step if reverse else step
-        return combine(state, lax.dynamic_index_in_dim(gathered, source, 0, False))
-
-    return lax.fori_loop(0, ahead, one, state)
+    running = part
+    total = None
+    distance = 1
+    while distance < count:
+        if reverse:
+            route = [(i + distance, i) for i in range(count - distance)]
+        else:
+            route = [(i, i + distance) for i in range(count - distance)]
+        got = lax.ppermute(running, axis, route)
+        total = got if total is None else total + got
+        if distance * 2 < count:
+            running = running + got
+        distance *= 2
+    if total is None:
+        total = jnp.zeros_like(part)
+    return total
+
+
+def all_sum(part, axes):
+    count = 1
+    for axis in axes:
+        count *= lax.axis_size(axis)
+    step = 1
+    while step < count:
+        route = [(i, i ^ step) for i in range(count)]
+        part = part + lax.ppermute(part, axes, route)
+        step *= 2
+    return part
 
 
 def shifted(block, axis, distance):
     devices = range(lax.axis_size(axis))
     route = [(i - distance, i) for i in devices if i - distance in devices]
     return lax.ppermute(block, axis, route)
-
-
-def combine_sum(earlier, later):
-    return earlier + later
 
 
 def per_device(queries, keys, values, spikes, window_lengths, gain, cotangent):
@@ -55,15 +69,17 @@
     local_state = jnp.einsum(
         "nrgd,nrge->ngde", key_heads, spiked, preferred_element_type=jnp.float32
     )
-    prior = carried_in(local_state, "ctx", combine_sum, jnp.zeros_like(local_state), False)
+    prior = exclusive_scan(local_state, "ctx", False)
     prior_half = prior.astype(jnp.bfloat16)
+    packed = jnp.concatenate([keys, values], axis=2)
     earlier = []
     for distance in range(reach, 0, -1):
-        earlier.append(shifted((keys, values), "ctx", distance))
-    key_window = jnp.concatenate([piece[0] for piece in earlier] + [keys], axis=1).reshape(
+        earlier.append(shifted(packed, "ctx", distance))
+    window_packed = jnp.concatenate(earlier + [packed], axis=1)
+    key_window = window_packed[:, :, :key_value_width].reshape(
         batch_inputs, window_rows, KEY_VALUE_HEADS, HEAD_SIZE
     )
-    value_window = jnp.concatenate([piece[1] for piece in earlier] + [values], axis=1).reshape(
+    value_window = window_packed[:, :, key_value_width:].reshape(
         batch_inputs, window_rows, KEY_VALUE_HEADS, HEAD_SIZE
     )
     row_idx = jnp.arange(token_rows)
@@ -109,10 +125,8 @@
     )
     grad_wide = head_gradients.astype(jnp.float32)
     total_tokens = batch_inputs * lax.axis_size("dp") * token_rows * lax.axis_size("ctx")
-    gain_local = jnp.sum(grad_wide * normed, axis=(0, 1)).reshape(
-        QUERY_HEADS * HEAD_SIZE
-    ) / math.sqrt(total_tokens)
-    d_gain = lax.psum(gain_local, ("dp", "ctx"))
+    gain_local = jnp.sum(grad_wide * normed, axis=(0, 1)).reshape(QUERY_HEADS * HEAD_SIZE)
+    d_gain = all_sum(gain_local, ("dp", "ctx")) * (total_tokens ** (-0.5))
     scaled = grad_wide * head_gains
     d_linear = (
         (scaled - normed * jnp.mean(scaled * normed, axis=-1, keepdims=True)) / root
@@ -120,7 +134,7 @@
     suffix_local = jnp.einsum(
         "nrghd,nrghe->ngde", query_heads, d_linear, preferred_element_type=jnp.float32
     )
-    later = carried_in(suffix_local, "ctx", combine_sum, jnp.zeros_like(suffix_local), True)
+    later = exclusive_scan(suffix_local, "ctx", True)
     later_half = later.astype(jnp.bfloat16)
     back_half = (
         jnp.einsum("nrghe,nsge->nghrs", d_linear, spiked, preferred_element_type=jnp.float32)
@@ -163,11 +177,16 @@
     received_v = jnp.zeros((batch_inputs, token_rows, key_value_width), jnp.float32)
     for distance in range(1, reach + 1):
         start_row = (reach - distance) * token_rows
-        sent_k = key_grad_window[:, start_row : start_row + token_rows]
-        sent_v = value_grad_window[:, start_row : start_row + token_rows]
-        got_k, got_v = shifted((sent_k, sent_v), "ctx", -distance)
-        received_k = received_k + got_k
-        received_v = received_v + got_v
+        sent = jnp.concatenate(
+            [
+                key_grad_window[:, start_row : start_row + token_rows],
+                value_grad_window[:, start_row : start_row + token_rows],
+            ],
+            axis=2,
+        )
+        got = shifted(sent, "ctx", -distance)
+        received_k = received_k + got[:, :, :key_value_width]
+        received_v = received_v + got[:, :, key_value_width:]
     own_k = key_grad_window[:, padding_rows:]
     own_v = value_grad_window[:, padding_rows:]
     d_queries = (

time: 138 us -> 92.5 us (0.67)
  blocking collectives: 46.7 us -> 0 us
  starting transfers between devices: 18.6 us -> 32 us
  between operations: 14.7 us -> 1.32 us
  waiting for transfers between devices: 7.19 us -> 12.4 us
  local copies, waits for them, and re-layouts: 21.6 us -> 17.3 us
  matrix products: 14.9 us -> 17.1 us
  other arithmetic: 13.1 us -> 11.4 us
    psum x1 -> x0, blocking collectives: 46.7 us -> none  [per_device(): d_gain = lax.psum(gain_local, ('dp', 'ctx'))]
    ppermute x0 -> x11, starting transfers between devices: none -> 23.2 us  [the longest x6 16 us: exclusive_scan(): got = lax.ppermute(running, axis, route)]
    ppermute x0 -> x11, waiting for transfers between devices: none -> 12.4 us  [the longest x6 8.79 us: exclusive_scan(): got = lax.ppermute(running, axis, route)]
    ppermute x8 -> x4, starting transfers between devices: 18.5 us -> 8.88 us  [shifted(): return lax.ppermute(block, axis, route)]
    all_gather x2 -> x0, waiting for transfers between devices: 7.14 us -> none  [carried_in(): gathered = lax.all_gather(part, axis)]
    add x7 -> x8, other arithmetic: 6.56 us -> 2.54 us  [the longest x4 2.53 us: exclusive_scan(): running = running + got]
    concatenate x2 -> x4, other arithmetic: 0.04 us -> 3.35 us  [the longest x2 3.28 us: per_device(): jnp.concatenate([key_grad_window[:, start_row:start_row + token_rows], va...]
    unnamed x73 -> x66, local copies, waits for them, and re-layouts: 14.6 us -> 11.5 us
  transfers between devices with their start and end apart: 10 -> 15, of which waited for: 1 -> 4; matrix products, arithmetic and copies ran while one was open for 34% -> 32% of each run, Pallas kernels for 0% -> 0%
where the time goes in v1:
time: 92.5 us; the launch traced here: 91.6 us
  starting transfers between devices  32 us (35%)
  local copies, waits for them, and re-layouts  17.3 us (19%)
  matrix products  17.1 us (18%)
  waiting for transfers between devices  12.4 us (13%)
  other arithmetic  11.4 us (12%)
  between operations  1.32 us (1%)
    ppermute x6, starting transfers between devices, exclusive_scan(): got = lax.ppermute(running, axis, route)  16 us
    unnamed x66, local copies, waits for them, and re-layouts  11.5 us
    ppermute x4, starting transfers between devices, shifted(): return lax.ppermute(block, axis, route)  8.88 us
    ppermute x6, waiting for transfers between devices, exclusive_scan(): got = lax.ppermute(running, axis, route)  8.79 us
    ppermute x5, starting transfers between devices, all_sum(): part = part + lax.ppermute(part, axes, route)  7.11 us
    ppermute x5, waiting for transfers between devices, all_sum(): part = part + lax.ppermute(part, axes, route)  3.62 us
    concatenate x2, other arithmetic, per_device(): jnp.concatenate([key_grad_window[:, start_row:start_row + token_rows], va...  3.28 us
    dot_general x1, matrix products, per_device(): jnp.einsum('nghrm,nmgd->nrghd', probs_half, value_window, preferred_eleme...  2.64 us
  transfers between devices with their start and end apart: 15, of which 4 were waited for; matrix products, arithmetic and copies ran while one was open for 32% of the time, Pallas kernels for 0%

profile of v1, /device:TPU:0, one launch (start us, length us, event | category | flops | bytes accessed | tf_op | source)
XLA Modules:
  0.0 91.6 jit_solution(8071763392450787605)
XLA Ops:
  0.7 1.0 %copy.62 = bf16[1,128,256]{1,2,0:T(8,128)(2,1)S(1)} copy(bf16[1,128,256]{2,1,0:T(8,128)(2,1)} %param.8) | data formatting | bytes 131072 | tf_op args[1]
  1.7 1.0 %copy.63 = bf16[1,128,256]{1,2,0:T(8,128)(2,1)S(1)} copy(bf16[1,128,256]{2,1,0:T(8,128)(2,1)} %param.9) | data formatting | bytes 131072 | tf_op args[2]
  2.7 4.8 %collective-permute-start.3 = (bf16[1,128,512]{1,2,0:T(8,128)(2,1)S(1)}, bf16[1,128,512]{1,2,0:T(8,128)(2,1)S(1)}, u32[]{:S(2)}, u32[]{:S(2)}) collective-permute-start(bf16[1,128,512]{1,2,0:T(8,128)(2,1)S(1)} %pad_maximum_fusion.2), channel_id=1, source_target_pairs={{0,2},{1,3},{2,4},{3,5},{4,6},{5,7},{8,10},{9,11},{10,12},{11,13},... | collective-permute-start | bytes 393224 | tf_op jit(solution)/shard_map/ppermute | solution.py:52
  7.5 1.5 %collective-permute-start.4 = (bf16[1,128,512]{1,2,0:T(8,128)(2,1)S(1)}, bf16[1,128,512]{1,2,0:T(8,128)(2,1)S(1)}, u32[]{:S(2)}, u32[]{:S(2)}) collective-permute-start(bf16[1,128,512]{1,2,0:T(8,128)(2,1)S(1)} %pad_maximum_fusion.2), channel_id=1, source_target_pairs={{0,1},{1,2},{2,3},{3,4},{4,5},{5,6},{6,7},{8,9},{9,10},{10,11},{11... | collective-permute-start | bytes 393224 | tf_op jit(solution)/shard_map/ppermute | solution.py:52
  9.0 0.9 reshape.301
  9.9 0.9 reshape.282
  10.8 0.7 convert_bitcast_fusion
  11.8 4.0 %collective-permute-start = (f32[1,2,128,128]{2,3,1,0:T(8,128)S(1)}, f32[1,2,128,128]{2,3,1,0:T(8,128)S(1)}, u32[]{:S(2)}, u32[]{:S(2)}) collective-permute-start(f32[1,2,128,128]{2,3,1,0:T(8,128)S(1)} %convolution_bitcast_fusion.10), channel_id=1, source_target_pairs={{0,1},{1,2},{2,3},{3,4},{4,5},{5,6},{6,7},{8,9},{9,10},{10,11},{11... | collective-permute-start | bytes 393224 | tf_op jit(solution)/shard_map/ppermute | solution.py:27
  15.9 2.2 %copy.67 = f32[1,128,1792]{1,2,0:T(8,128)} copy(bf16[1,128,1792]{2,1,0:T(8,128)(2,1)} %param.13) | data formatting | bytes 1376256 | tf_op jit(solution)/shard_map/convert_element_type | solution.py:126
  18.1 1.0 %copy.73 = bf16[1,128,1792]{1,2,0:T(8,128)(2,1)} copy(bf16[1,128,1792]{2,1,0:T(8,128)(2,1)S(1)} %copy-done.5) | data formatting | bytes 917504 | tf_op args[6]
  20.0 1.3 %convolution_bitcast_fusion.4 = f32[1,128,2,7,128]{1,4,3,2,0:T(8,128)} fusion(bf16[2,7,128,128]{2,3,1,0:T(8,128)(2,1)S(1)} %fusion.23, bf16[128,2,128]{2,0,1:T(8,128)(2,1)S(1)} %fusion.35), kind=kOutput, calls=%fused_computation.19 | convolution fusion | flops 58720256 | bytes 1441792 | tf_op jit(solution)/shard_map/nghrs,nsge->nrghe/dot_general | solution.py:99
  21.3 4.0 %collective-permute-start.1 = (f32[1,2,128,128]{2,3,1,0:T(8,128)S(1)}, f32[1,2,128,128]{2,3,1,0:T(8,128)}, u32[]{:S(2)}, u32[]{:S(2)}) collective-permute-start(f32[1,2,128,128]{2,3,1,0:T(8,128)S(1)} %add.126), channel_id=1, source_target_pairs={{0,2},{1,3},{2,4},{3,5},{4,6},{5,7},{8,10},{9,11},{10,12},{11,13},... | collective-permute-start | bytes 393224 | tf_op jit(solution)/shard_map/ppermute | solution.py:27
  25.4 0.7 fusion.47
  27.4 0.9 fusion.7
  28.3 1.6 %add.128 = f32[1,2,128,128]{2,3,1,0:T(8,128)} add(f32[1,2,128,128]{2,3,1,0:T(8,128)S(1)} %add.126, f32[1,2,128,128]{2,3,1,0:T(8,128)} %collective-permute-done.1) | non-fusion elementwise | flops 32768 | bytes 393216 | tf_op jit(solution)/shard_map/add | solution.py:30
  29.9 4.2 %collective-permute-start.2 = (f32[1,2,128,128]{2,3,1,0:T(8,128)}, f32[1,2,128,128]{2,3,1,0:T(8,128)}, u32[]{:S(2)}, u32[]{:S(2)}) collective-permute-start(f32[1,2,128,128]{2,3,1,0:T(8,128)} %add.128), channel_id=1, source_target_pairs={{0,4},{1,5},{2,6},{3,7},{8,12},{9,13},{10,14},{11,15},{16,20},{17,... | collective-permute-start | bytes 393224 | tf_op jit(solution)/shard_map/ppermute | solution.py:27
  34.1 0.8 fusion.45
  34.8 1.7 %copy.140 = f32[1,128,256]{2,1,0:T(8,128)} copy(f32[1,128,256]{1,2,0:T(8,128)} %get-tuple-element.23) | data formatting | bytes 262144
  36.5 1.7 %copy.142 = f32[1,128,256]{2,1,0:T(8,128)} copy(f32[1,128,256]{1,2,0:T(8,128)} %get-tuple-element.22) | data formatting | bytes 262144
  38.1 1.6 %copy.143 = f32[1,128,256]{2,1,0:T(8,128)} copy(f32[1,128,256]{1,2,0:T(8,128)} %get-tuple-element.21) | data formatting | bytes 262144
  39.8 1.1 %fusion.36 = bf16[2,128,128,1]{1,2,3,0:T(8,128)(2,1)S(1)} fusion(f32[1,2,128,128]{2,3,1,0:T(8,128)} %collective-permute-done.2, f32[1,2,128,128]{2,3,1,0:T(8,128)} %copy-done.14, f32[1,2,128,128]{2,3,1,0:T(8,128)} %collective-permute-done.1), kind=kLoop, calls=%fused_computation.69 | loop fusion | flops 98304 | bytes 458752 | tf_op jit(solution)/shard_map/reshape.26
  40.9 1.5 %multiply_reduce_fusion.3 = (f32[128,2,7]{0,2,1:T(8,128)S(1)}, f32[1,128,2,7,128]{1,4,3,2,0:T(8,128)S(1)}) fusion(f32[1,128,2,7,128]{1,4,3,2,0:T(8,128)} %convolution_bitcast_fusion.4, bf16[2,128,128,1]{1,2,3,0:T(8,128)(2,1)S(1)} %fusion.36, bf16[128,2,7,128]{0,3,2,1:T(8,128)(2,1)S(1)} %bitcast.242), kind=kOutput, calls=%fused_computation.46 | convolution fusion | flops 59406592 | bytes 2366464 | tf_op jit(solution)/shard_map/nrghd,ngde->nrghe/dot_general | solution.py:100
  42.5 2.6 %multiply_reduce_fusion = (f32[2,7,128]{2,1,0:T(8,128)}, f32[128,2,7]{0,2,1:T(8,128)S(1)}, f32[128,2,7]{0,2,1:T(8,128)S(1)}, bf16[1,128,2,7,128]{1,4,3,2,0:T(8,128)(2,1)}) fusion(f32[1,128,2,7,128]{1,4,3,2,0:T(8,128)S(1)} %bitcast.246, f32[1,128,2,7,128]{1,4,3,2,0:T(8,128)S(1)} %get-tuple-element.30, f32[128,2,7]{0,2,1:T(8,128)S(1)} %add_sqrt_fusion, ...), kind=kOutput, calls=%fused_computation.41 | convolution fusion | flops 182119168 | bytes 5391360 | tf_op jit(solution)/shard_map/nghrm,nmgd->nrghd/dot_general | solution.py:115
  45.5 1.0 %convolution_bitcast_fusion.8 = f32[1,2,128,128]{2,3,1,0:T(8,128)} fusion(bf16[128,2,7,128]{0,3,2,1:T(8,128)(2,1)S(1)} %bitcast.243, bf16[1,128,2,7,128]{1,4,3,2,0:T(8,128)(2,1)S(1)} %divide_convert_fusion), kind=kOutput, calls=%fused_computation.34 | convolution fusion | flops 58720256 | bytes 1048576 | tf_op jit(solution)/shard_map/nrghd,nrghe->ngde/dot_general | solution.py:134
  46.7 1.0 %convolution_bitcast_fusion.7 = f32[2,128,128]{2,1,0:T(8,128)} fusion(bf16[2,7,128,128]{2,3,1,0:T(8,128)(2,1)S(1)} %copy-done.3, bf16[1,128,2,7,128]{1,4,3,2,0:T(8,128)(2,1)S(1)} %divide_convert_fusion), kind=kOutput, calls=%fused_computation.33 | convolution fusion | flops 58720256 | bytes 1048576 | tf_op jit(solution)/shard_map/nghrs,nrghe->nsge/dot_general | solution.py:155
  47.7 1.2 %fusion.6 = bf16[2,7,128,384]{2,3,1,0:T(8,128)(2,1)S(1)} fusion(bf16[384,2,128,1]{0,2,3,1:T(8,128)(2,1)S(1)} %bitcast.260, bf16[128,2,7,128]{0,3,2,1:T(8,128)(2,1)S(1)} %bitcast.257, f32[2,7,128]{2,1,0:T(8,128)S(1)} %bitcast.261, f32[2,7,128]{2,1,0:T(8,128)S(1)} %copy-done.23, f32[2,7,128]{2,1,0:T(8,128)S(1)} %get-tuple-element.31, ...), kind=kOutput, calls=%fused_computation.9 | convolution fusion | flops 181665792 | bytes 4903936 | tf_op jit(solution)/shard_map/nrghd,nmgd->nghrm/dot_general | solution.py:162
  48.9 1.3 %fusion.48 = f32[2,384,128,1]{1,2,3,0:T(8,128)} fusion(bf16[2,7,128,384]{2,3,1,0:T(8,128)(2,1)S(1)} %fusion.6, bf16[128,2,7,128]{0,3,2,1:T(8,128)(2,1)S(1)} %bitcast.244), kind=kOutput, calls=%fused_computation.86 | convolution fusion | flops 176160768 | bytes 2228224 | tf_op jit(solution)/shard_map/nghrm,nrghd->nmgd/dot_general | solution.py:170
  50.8 0.9 %convolution_bitcast_fusion.9 = f32[2,128,128]{2,1,0:T(8,128)} fusion(bf16[2,7,128,128]{2,3,1,0:T(8,128)(2,1)S(1)} %fusion.24, bf16[128,2,7,128]{0,3,2,1:T(8,128)(2,1)S(1)} %bitcast.245), kind=kOutput, calls=%fused_computation.35 | convolution fusion | flops 58720256 | bytes 1048576 | tf_op jit(solution)/shard_map/nghrs,nrghd->nsgd/dot_general | solution.py:149
  51.7 1.1 %convolution_bitcast_fusion = f32[1,128,2,7,128]{1,4,3,2,0:T(8,128)S(1)} fusion(bf16[128,2,128,1]{0,2,3,1:T(8,128)(2,1)} %copy-done.11, bf16[2,7,128,128]{2,3,1,0:T(8,128)(2,1)S(1)} %fusion.24), kind=kOutput, calls=%fused_computation.15 | convolution fusion | flops 58720256 | bytes 1441792 | tf_op jit(solution)/shard_map/nghrs,nsgd->nrghd/dot_general | solution.py:146
  52.8 1.3 %collective-permute-start.5 = (f32[1,2,128,128]{2,3,1,0:T(8,128)}, f32[1,2,128,128]{2,3,1,0:T(8,128)S(1)}, u32[]{:S(2)}, u32[]{:S(2)}) collective-permute-start(f32[1,2,128,128]{2,3,1,0:T(8,128)} %convolution_bitcast_fusion.8), channel_id=1, source_target_pairs={{1,0},{2,1},{3,2},{4,3},{5,4},{6,5},{7,6},{9,8},{10,9},{11,10},{12... | collective-permute-start | bytes 393224 | tf_op jit(solution)/shard_map/ppermute | solution.py:27
  54.2 2.8 %collective-permute-start.11 = (f32[1792]{0:T(1024)S(1)}, f32[1792]{0:T(1024)S(1)}, u32[]{:S(2)}, u32[]{:S(2)}) collective-permute-start(f32[1792]{0:T(1024)S(1)} %add.156), channel_id=1, source_target_pairs={{0,2},{1,3},{2,0},{3,1},{4,6},{5,7},{6,4},{7,5},{8,10},{9,11},{10,... | collective-permute-start | bytes 21512 | tf_op jit(solution)/shard_map/ppermute | solution.py:44
  57.1 3.0 %collective-permute-done.11 = f32[1792]{0:T(1024)S(1)} collective-permute-done((f32[1792]{0:T(1024)S(1)}, f32[1792]{0:T(1024)S(1)}, u32[]{:S(2)}, u32[]{:S(2)}) %collective-permute-start.11) | collective-permute-done | bytes 7200 | tf_op jit(solution)/shard_map/ppermute | solution.py:44
  60.1 1.6 %pad_maximum_fusion = f32[1,128,512]{2,1,0:T(8,128)} fusion(f32[1,128,256]{2,1,0:T(8,128)} %copy.140, f32[1,128,256]{2,1,0:T(8,128)S(1)} %copy.139), kind=kLoop, calls=%fused_computation.54 | loop fusion | flops 65536 | bytes 524288 | tf_op jit(solution)/shard_map/concatenate | solution.py:180
  61.7 1.3 %collective-permute-start.8 = (f32[1,128,512]{2,1,0:T(8,128)}, f32[1,128,512]{2,1,0:T(8,128)}, u32[]{:S(2)}, u32[]{:S(2)}) collective-permute-start(f32[1,128,512]{2,1,0:T(8,128)} %pad_maximum_fusion), channel_id=1, source_target_pairs={{1,0},{2,1},{3,2},{4,3},{5,4},{6,5},{7,6},{9,8},{10,9},{11,10},{12... | collective-permute-start | bytes 786440 | tf_op jit(solution)/shard_map/ppermute | solution.py:52
  63.8 1.6 %collective-permute-start.13 = (f32[1792]{0:T(1024)S(1)}, f32[1792]{0:T(1024)S(1)}, u32[]{:S(2)}, u32[]{:S(2)}) collective-permute-start(f32[1792]{0:T(1024)S(1)} %add.158), channel_id=1, source_target_pairs={{0,8},{1,9},{2,10},{3,11},{4,12},{5,13},{6,14},{7,15},{8,0},{9,1},... | collective-permute-start | bytes 21512 | tf_op jit(solution)/shard_map/ppermute | solution.py:44
  65.3 1.6 %pad_maximum_fusion.1 = f32[1,128,512]{2,1,0:T(8,128)} fusion(f32[1,128,256]{2,1,0:T(8,128)} %copy.142, f32[1,128,256]{2,1,0:T(8,128)S(1)} %copy.141), kind=kLoop, calls=%fused_computation.55 | loop fusion | flops 65536 | bytes 524288 | tf_op jit(solution)/shard_map/concatenate | solution.py:180
  67.0 1.3 %collective-permute-start.9 = (f32[1,128,512]{2,1,0:T(8,128)}, f32[1,128,512]{2,1,0:T(8,128)}, u32[]{:S(2)}, u32[]{:S(2)}) collective-permute-start(f32[1,128,512]{2,1,0:T(8,128)} %pad_maximum_fusion.1), channel_id=1, source_target_pairs={{2,0},{3,1},{4,2},{5,3},{6,4},{7,5},{10,8},{11,9},{12,10},{13,11},... | collective-permute-start | bytes 786440 | tf_op jit(solution)/shard_map/ppermute | solution.py:52
  68.3 2.7 %collective-permute-start.14 = (f32[1792]{0:T(1024)S(1)}, f32[1792]{0:T(1024)S(1)}, u32[]{:S(2)}, u32[]{:S(2)}) collective-permute-start(f32[1792]{0:T(1024)S(1)} %add.159), channel_id=1, source_target_pairs={{0,16},{1,17},{2,18},{3,19},{4,20},{5,21},{6,22},{7,23},{8,24},{9,... | collective-permute-start | bytes 21512 | tf_op jit(solution)/shard_map/ppermute | solution.py:44
  70.9 0.9 %add.140 = f32[1,2,128,128]{2,3,1,0:T(8,128)S(1)} add(f32[1,2,128,128]{2,3,1,0:T(8,128)} %convolution_bitcast_fusion.8, f32[1,2,128,128]{2,3,1,0:T(8,128)S(1)} %collective-permute-done.5) | non-fusion elementwise | flops 32768 | bytes 393216 | tf_op jit(solution)/shard_map/add | solution.py:30
  71.9 1.3 %collective-permute-start.6 = (f32[1,2,128,128]{2,3,1,0:T(8,128)S(1)}, f32[1,2,128,128]{2,3,1,0:T(8,128)S(1)}, u32[]{:S(2)}, u32[]{:S(2)}) collective-permute-start(f32[1,2,128,128]{2,3,1,0:T(8,128)S(1)} %add.140), channel_id=1, source_target_pairs={{2,0},{3,1},{4,2},{5,3},{6,4},{7,5},{10,8},{11,9},{12,10},{13,11},... | collective-permute-start | bytes 393224 | tf_op jit(solution)/shard_map/ppermute | solution.py:27
  73.6 1.0 %copy.93 = bf16[1,128,1792]{2,1,0:T(8,128)(2,1)} copy(bf16[1,128,1792]{1,2,0:T(8,128)(2,1)S(1)} %bitcast.248) | data formatting | bytes 917504
  74.6 2.0 %copy.92 = bf16[1,128,1792]{2,1,0:T(8,128)(2,1)} copy(bf16[1,128,1792]{1,2,0:T(8,128)(2,1)} %bitcast.255) | data formatting | bytes 917504
  76.6 3.8 %collective-permute-done.6 = f32[1,2,128,128]{2,3,1,0:T(8,128)S(1)} collective-permute-done((f32[1,2,128,128]{2,3,1,0:T(8,128)S(1)}, f32[1,2,128,128]{2,3,1,0:T(8,128)S(1)}, u32[]{:S(2)}, u32[]{:S(2)}) %collective-permute-start.6) | collective-permute-done | bytes 131104 | tf_op jit(solution)/shard_map/ppermute | solution.py:27
  80.4 1.3 %collective-permute-start.7 = (f32[1,2,128,128]{2,3,1,0:T(8,128)S(1)}, f32[1,2,128,128]{2,3,1,0:T(8,128)S(1)}, u32[]{:S(2)}, u32[]{:S(2)}) collective-permute-start(f32[1,2,128,128]{2,3,1,0:T(8,128)S(1)} %add.142), channel_id=1, source_target_pairs={{4,0},{5,1},{6,2},{7,3},{12,8},{13,9},{14,10},{15,11},{20,16},{21,... | collective-permute-start | bytes 393224 | tf_op jit(solution)/shard_map/ppermute | solution.py:27
  82.3 5.0 %collective-permute-done.7 = f32[1,2,128,128]{2,3,1,0:T(8,128)S(1)} collective-permute-done((f32[1,2,128,128]{2,3,1,0:T(8,128)S(1)}, f32[1,2,128,128]{2,3,1,0:T(8,128)S(1)}, u32[]{:S(2)}, u32[]{:S(2)}) %collective-permute-start.7) | collective-permute-done | bytes 131104 | tf_op jit(solution)/shard_map/ppermute | solution.py:27
  87.4 1.1 %convolution_add_fusion.1 = f32[2,128,128]{2,1,0:T(8,128)S(1)} fusion(f32[2,128,128]{2,1,0:T(8,128)} %convolution_bitcast_fusion.9, bf16[2,128,128]{1,2,0:T(8,128)(2,1)S(1)} %fusion.37, bf16[128,2,128]{2,0,1:T(8,128)(2,1)S(1)} %fusion.35), kind=kOutput, calls=%fused_computation.38 | convolution fusion | flops 8421376 | bytes 393216 | tf_op jit(solution)/shard_map/nsge,ngde->nsgd/dot_general | solution.py:152
  88.6 1.1 %fusion.26 = f32[1,128,2,128]{1,3,2,0:T(8,128)S(1)} fusion(f32[2,128,128]{2,1,0:T(8,128)} %convolution_bitcast_fusion.7, bf16[2,128,128]{1,2,0:T(8,128)(2,1)S(1)} %fusion.37, f32[128,2]{0,1:T(2,128)S(1)} %copy-done.21, bf16[128,2,128]{2,1,0:T(2,128)(2,1)S(1)} %reshape.282), kind=kOutput, calls=%fused_computation.40 | convolution fusion | flops 8454144 | bytes 394240 | tf_op jit(solution)/shard_map/nsgd,ngde->nsge/dot_general | solution.py:158
  89.8 1.8 %fusion.32 = (bf16[1,128,256]{2,1,0:T(8,128)(2,1)}, bf16[1,128,256]{2,1,0:T(8,128)(2,1)}) fusion(f32[1,128,512]{2,1,0:T(8,128)} %collective-permute-done.9, f32[1,128,512]{2,1,0:T(8,128)} %collective-permute-done.8, f32[1,128,256]{2,1,0:T(8,128)S(1)} %copy.91, f32[1,128,256]{2,1,0:T(8,128)S(1)} %copy-done.15, f32[1,128,256]{2,1,0:T(8,128)S(1)} %copy.82, ...), kind=kLoop, calls=%fused_computation.59 | loop fusion | flops 262144 | bytes 1179648 | tf_op jit(solution)/shard_map/convert_element_type | solution.py:204
  (105 shorter events, 5.9 us)
Async XLA Ops:
  0.6 17.4 %copy-start.5 = (bf16[1,128,1792]{2,1,0:T(8,128)(2,1)S(1)}, bf16[1,128,1792]{2,1,0:T(8,128)(2,1)}, u32[]{:S(2)}) copy-start(bf16[1,128,1792]{2,1,0:T(8,128)(2,1)} %param.13) | copy-start | bytes 1376260
  0.6 18.4 %copy-start.16 = (bf16[1,128,1792]{2,1,0:T(8,128)(2,1)S(1)}, bf16[1,128,1792]{2,1,0:T(8,128)(2,1)}, u32[]{:S(2)}) copy-start(bf16[1,128,1792]{2,1,0:T(8,128)(2,1)} %param.7) | copy-start | bytes 1376260
  0.7 18.8 %copy-start.24 = (f32[1792]{0:T(1024)S(1)}, f32[1792]{0:T(1024)}, u32[]{:S(2)}) copy-start(f32[1792]{0:T(1024)} %param.12) | copy-start | bytes 21508
  2.7 17.1 %copy-start.26 = (s32[2]{0:T(128)S(1)}, s32[2]{0:T(128)}, u32[]{:S(2)}) copy-start(s32[2]{0:T(128)} %param.11) | copy-start | bytes 28
  2.7 22.7 %collective-permute-start.3 = (bf16[1,128,512]{1,2,0:T(8,128)(2,1)S(1)}, bf16[1,128,512]{1,2,0:T(8,128)(2,1)S(1)}, u32[]{:S(2)}, u32[]{:S(2)}) collective-permute-start(bf16[1,128,512]{1,2,0:T(8,128)(2,1)S(1)} %pad_maximum_fusion.2), channel_id=1, source_target_pairs={{0,2},{1,3},{2,4},{3,5},{4,6},{5,7},{8,10},{9,11},{10,12},{11,13},... | collective-permute-start | bytes 393224 | tf_op jit(solution)/shard_map/ppermute | solution.py:52
  7.5 17.8 %collective-permute-start.4 = (bf16[1,128,512]{1,2,0:T(8,128)(2,1)S(1)}, bf16[1,128,512]{1,2,0:T(8,128)(2,1)S(1)}, u32[]{:S(2)}, u32[]{:S(2)}) collective-permute-start(bf16[1,128,512]{1,2,0:T(8,128)(2,1)S(1)} %pad_maximum_fusion.2), channel_id=1, source_target_pairs={{0,1},{1,2},{2,3},{3,4},{4,5},{5,6},{6,7},{8,9},{9,10},{10,11},{11... | collective-permute-start | bytes 393224 | tf_op jit(solution)/shard_map/ppermute | solution.py:52
  11.5 4.3 %copy-start.20 = (f32[128,2]{0,1:T(2,128)}, f32[128,2]{0,1:T(2,128)S(1)}, u32[]{:S(2)}) copy-start(f32[128,2]{0,1:T(2,128)S(1)} %convert_bitcast_fusion) | copy-start | bytes 3076
  11.8 9.5 %collective-permute-start = (f32[1,2,128,128]{2,3,1,0:T(8,128)S(1)}, f32[1,2,128,128]{2,3,1,0:T(8,128)S(1)}, u32[]{:S(2)}, u32[]{:S(2)}) collective-permute-start(f32[1,2,128,128]{2,3,1,0:T(8,128)S(1)} %convolution_bitcast_fusion.10), channel_id=1, source_target_pairs={{0,1},{1,2},{2,3},{3,4},{4,5},{5,6},{6,7},{8,9},{9,10},{10,11},{11... | collective-permute-start | bytes 393224 | tf_op jit(solution)/shard_map/ppermute | solution.py:27
  15.8 5.5 %copy-start.12 = (f32[128,128]{0,1:T(8,128)}, f32[128,128]{0,1:T(8,128)S(1)}, u32[]{:S(2)}) copy-start(f32[128,128]{0,1:T(8,128)S(1)} %fusion.40) | copy-start | bytes 196612
  19.4 5.9 %copy-start.11 = (bf16[128,2,128,1]{0,2,3,1:T(8,128)(2,1)}, bf16[128,2,128,1]{0,2,3,1:T(8,128)(2,1)S(1)}, u32[]{:S(2)}) copy-start(bf16[128,2,128,1]{0,2,3,1:T(8,128)(2,1)S(1)} %copy.110) | copy-start | bytes 196612
  19.8 6.3 %copy-start.2 = (bf16[2,7,128,128]{2,3,1,0:T(8,128)(2,1)}, bf16[2,7,128,128]{2,3,1,0:T(8,128)(2,1)S(1)}, u32[]{:S(2)}) copy-start(bf16[2,7,128,128]{2,3,1,0:T(8,128)(2,1)S(1)} %fusion.23) | copy-start | bytes 1376260
  20.0 7.4 %copy-start.7 = (pred[2,128,384]{1,2,0:T(8,128)(4,1)}, pred[2,128,384]{1,2,0:T(8,128)(4,1)S(1)}, u32[]{:S(2)}) copy-start(pred[2,128,384]{1,2,0:T(8,128)(4,1)S(1)} %and_and_fusion) | copy-start | bytes 294916
  21.3 4.9 %copy-start.14 = (f32[1,2,128,128]{2,3,1,0:T(8,128)}, f32[1,2,128,128]{2,3,1,0:T(8,128)S(1)}, u32[]{:S(2)}) copy-start(f32[1,2,128,128]{2,3,1,0:T(8,128)S(1)} %collective-permute-done) | copy-start | bytes 393220
  21.3 7.0 %collective-permute-start.1 = (f32[1,2,128,128]{2,3,1,0:T(8,128)S(1)}, f32[1,2,128,128]{2,3,1,0:T(8,128)}, u32[]{:S(2)}, u32[]{:S(2)}) collective-permute-start(f32[1,2,128,128]{2,3,1,0:T(8,128)S(1)} %add.126), channel_id=1, source_target_pairs={{0,2},{1,3},{2,4},{3,5},{4,6},{5,7},{8,10},{9,11},{10,12},{11,13},... | collective-permute-start | bytes 393224 | tf_op jit(solution)/shard_map/ppermute | solution.py:27
  26.1 1.2 %copy-start.17 = (bf16[1,128,1792]{1,2,0:T(8,128)(2,1)S(1)}, bf16[1,128,1792]{1,2,0:T(8,128)(2,1)}, u32[]{:S(2)}) copy-start(bf16[1,128,1792]{1,2,0:T(8,128)(2,1)} %copy.73) | copy-start | bytes 1376260
  26.8 15.7 %copy-start = (f32[2,384,128,7]{2,1,3,0:T(8,128)}, f32[2,384,128,7]{2,1,3,0:T(8,128)S(1)}, u32[]{:S(2)}) copy-start(f32[2,384,128,7]{2,1,3,0:T(8,128)S(1)} %get-tuple-element.32) | copy-start | bytes 8257540
  27.4 0.9 %copy-start.22 = (f32[2,7,128]{2,1,0:T(8,128)}, f32[2,7,128]{2,1,0:T(8,128)S(1)}, u32[]{:S(2)}) copy-start(f32[2,7,128]{2,1,0:T(8,128)S(1)} %fusion.4) | copy-start | bytes 21508
  29.9 9.9 %collective-permute-start.2 = (f32[1,2,128,128]{2,3,1,0:T(8,128)}, f32[1,2,128,128]{2,3,1,0:T(8,128)}, u32[]{:S(2)}, u32[]{:S(2)}) collective-permute-start(f32[1,2,128,128]{2,3,1,0:T(8,128)} %add.128), channel_id=1, source_target_pairs={{0,4},{1,5},{2,6},{3,7},{8,12},{9,13},{10,14},{11,15},{16,20},{17,... | collective-permute-start | bytes 393224 | tf_op jit(solution)/shard_map/ppermute | solution.py:27
  39.8 2.7 %copy-start.4 = (f32[1,128,1792]{1,2,0:T(8,128)S(1)}, f32[1,128,1792]{1,2,0:T(8,128)}, u32[]{:S(2)}) copy-start(f32[1,128,1792]{1,2,0:T(8,128)} %copy.67) | copy-start | bytes 2752516
  39.8 2.7 %copy-start.8 = (pred[2,128,384]{1,2,0:T(8,128)(4,1)S(1)}, pred[2,128,384]{1,2,0:T(8,128)(4,1)}, u32[]{:S(2)}) copy-start(pred[2,128,384]{1,2,0:T(8,128)(4,1)} %copy-done.7) | copy-start | bytes 294916
  39.8 2.7 %copy-start.19 = (bf16[1,384,256]{1,2,0:T(8,128)(2,1)S(1)}, bf16[1,384,256]{1,2,0:T(8,128)(2,1)}, u32[]{:S(2)}) copy-start(bf16[1,384,256]{1,2,0:T(8,128)(2,1)} %get-tuple-element.28) | copy-start | bytes 589828
  39.8 2.7 %copy-start.23 = (f32[2,7,128]{2,1,0:T(8,128)S(1)}, f32[2,7,128]{2,1,0:T(8,128)}, u32[]{:S(2)}) copy-start(f32[2,7,128]{2,1,0:T(8,128)} %copy-done.22) | copy-start | bytes 21508
  40.9 1.5 %copy-start.9 = (bf16[2,128,128,1]{1,2,3,0:T(8,128)(2,1)}, bf16[2,128,128,1]{1,2,3,0:T(8,128)(2,1)S(1)}, u32[]{:S(2)}) copy-start(bf16[2,128,128,1]{1,2,3,0:T(8,128)(2,1)S(1)} %fusion.36) | copy-start | bytes 196612
  45.2 1.3 %copy-start.13 = (f32[128,128]{0,1:T(8,128)S(1)}, f32[128,128]{0,1:T(8,128)}, u32[]{:S(2)}) copy-start(f32[128,128]{0,1:T(8,128)} %copy-done.12) | copy-start | bytes 196612
  45.2 1.6 %copy-start.3 = (bf16[2,7,128,128]{2,3,1,0:T(8,128)(2,1)S(1)}, bf16[2,7,128,128]{2,3,1,0:T(8,128)(2,1)}, u32[]{:S(2)}) copy-start(bf16[2,7,128,128]{2,3,1,0:T(8,128)(2,1)} %copy-done.2) | copy-start | bytes 1376260
  45.2 2.5 %copy-start.1 = (f32[2,384,128,7]{2,1,3,0:T(8,128)S(1)}, f32[2,384,128,7]{2,1,3,0:T(8,128)}, u32[]{:S(2)}) copy-start(f32[2,384,128,7]{2,1,3,0:T(8,128)} %copy-done) | copy-start | bytes 8257540
  45.2 2.5 %copy-start.18 = (bf16[1,128,1792]{1,2,0:T(8,128)(2,1)S(1)}, bf16[1,128,1792]{1,2,0:T(8,128)(2,1)}, u32[]{:S(2)}) copy-start(bf16[1,128,1792]{1,2,0:T(8,128)(2,1)} %copy.73) | copy-start | bytes 1376260
  48.9 1.8 %copy-start.25 = (f32[2,7,128]{2,1,0:T(8,128)S(1)}, f32[2,7,128]{2,1,0:T(8,128)}, u32[]{:S(2)}) copy-start(f32[2,7,128]{2,1,0:T(8,128)} %get-tuple-element.15) | copy-start | bytes 21508
  50.7 22.5 %copy-start.10 = (bf16[2,128,128,1]{1,2,3,0:T(8,128)(2,1)S(1)}, bf16[2,128,128,1]{1,2,3,0:T(8,128)(2,1)}, u32[]{:S(2)}) copy-start(bf16[2,128,128,1]{1,2,3,0:T(8,128)(2,1)} %copy-done.9) | copy-start | bytes 196612
  50.7 6.3 %copy-start.6 = (f32[2,384,128,1]{1,2,3,0:T(8,128)S(1)}, f32[2,384,128,1]{1,2,3,0:T(8,128)}, u32[]{:S(2)}) copy-start(f32[2,384,128,1]{1,2,3,0:T(8,128)} %fusion.48) | copy-start | bytes 1179652
  50.7 3.4 %collective-permute-start.10 = (f32[1792]{0:T(1024)S(1)}, f32[1792]{0:T(1024)S(1)}, u32[]{:S(2)}, u32[]{:S(2)}) collective-permute-start(f32[1792]{0:T(1024)S(1)} %reshape.300), channel_id=1, source_target_pairs={{0,1},{1,0},{2,3},{3,2},{4,5},{5,4},{6,7},{7,6},{8,9},{9,8},{10,11... | collective-permute-start | bytes 21512 | tf_op jit(solution)/shard_map/ppermute | solution.py:44
  52.8 18.1 %collective-permute-start.5 = (f32[1,2,128,128]{2,3,1,0:T(8,128)}, f32[1,2,128,128]{2,3,1,0:T(8,128)S(1)}, u32[]{:S(2)}, u32[]{:S(2)}) collective-permute-start(f32[1,2,128,128]{2,3,1,0:T(8,128)} %convolution_bitcast_fusion.8), channel_id=1, source_target_pairs={{1,0},{2,1},{3,2},{4,3},{5,4},{6,5},{7,6},{9,8},{10,9},{11,10},{12... | collective-permute-start | bytes 393224 | tf_op jit(solution)/shard_map/ppermute | solution.py:27
  54.2 5.9 %collective-permute-start.11 = (f32[1792]{0:T(1024)S(1)}, f32[1792]{0:T(1024)S(1)}, u32[]{:S(2)}, u32[]{:S(2)}) collective-permute-start(f32[1792]{0:T(1024)S(1)} %add.156), channel_id=1, source_target_pairs={{0,2},{1,3},{2,0},{3,1},{4,6},{5,7},{6,4},{7,5},{8,10},{9,11},{10,... | collective-permute-start | bytes 21512 | tf_op jit(solution)/shard_map/ppermute | solution.py:44
  60.1 3.7 %collective-permute-start.12 = (f32[1792]{0:T(1024)S(1)}, f32[1792]{0:T(1024)S(1)}, u32[]{:S(2)}, u32[]{:S(2)}) collective-permute-start(f32[1792]{0:T(1024)S(1)} %add.157), channel_id=1, source_target_pairs={{0,4},{1,5},{2,6},{3,7},{4,0},{5,1},{6,2},{7,3},{8,12},{9,13},{10,... | collective-permute-start | bytes 21512 | tf_op jit(solution)/shard_map/ppermute | solution.py:44
  61.7 28.0 %collective-permute-start.8 = (f32[1,128,512]{2,1,0:T(8,128)}, f32[1,128,512]{2,1,0:T(8,128)}, u32[]{:S(2)}, u32[]{:S(2)}) collective-permute-start(f32[1,128,512]{2,1,0:T(8,128)} %pad_maximum_fusion), channel_id=1, source_target_pairs={{1,0},{2,1},{3,2},{4,3},{5,4},{6,5},{7,6},{9,8},{10,9},{11,10},{12... | collective-permute-start | bytes 786440 | tf_op jit(solution)/shard_map/ppermute | solution.py:52
  63.8 4.5 %collective-permute-start.13 = (f32[1792]{0:T(1024)S(1)}, f32[1792]{0:T(1024)S(1)}, u32[]{:S(2)}, u32[]{:S(2)}) collective-permute-start(f32[1792]{0:T(1024)S(1)} %add.158), channel_id=1, source_target_pairs={{0,8},{1,9},{2,10},{3,11},{4,12},{5,13},{6,14},{7,15},{8,0},{9,1},... | collective-permute-start | bytes 21512 | tf_op jit(solution)/shard_map/ppermute | solution.py:44
  67.0 22.8 %collective-permute-start.9 = (f32[1,128,512]{2,1,0:T(8,128)}, f32[1,128,512]{2,1,0:T(8,128)}, u32[]{:S(2)}, u32[]{:S(2)}) collective-permute-start(f32[1,128,512]{2,1,0:T(8,128)} %pad_maximum_fusion.1), channel_id=1, source_target_pairs={{2,0},{3,1},{4,2},{5,3},{6,4},{7,5},{10,8},{11,9},{12,10},{13,11},... | collective-permute-start | bytes 786440 | tf_op jit(solution)/shard_map/ppermute | solution.py:52
  68.3 13.4 %collective-permute-start.14 = (f32[1792]{0:T(1024)S(1)}, f32[1792]{0:T(1024)S(1)}, u32[]{:S(2)}, u32[]{:S(2)}) collective-permute-start(f32[1792]{0:T(1024)S(1)} %add.159), channel_id=1, source_target_pairs={{0,16},{1,17},{2,18},{3,19},{4,20},{5,21},{6,22},{7,23},{8,24},{9,... | collective-permute-start | bytes 21512 | tf_op jit(solution)/shard_map/ppermute | solution.py:44
  71.9 16.7 %copy-start.21 = (f32[128,2]{0,1:T(2,128)S(1)}, f32[128,2]{0,1:T(2,128)}, u32[]{:S(2)}) copy-start(f32[128,2]{0,1:T(2,128)} %copy-done.20) | copy-start | bytes 3076
  71.9 8.5 %collective-permute-start.6 = (f32[1,2,128,128]{2,3,1,0:T(8,128)S(1)}, f32[1,2,128,128]{2,3,1,0:T(8,128)S(1)}, u32[]{:S(2)}, u32[]{:S(2)}) collective-permute-start(f32[1,2,128,128]{2,3,1,0:T(8,128)S(1)} %add.140), channel_id=1, source_target_pairs={{2,0},{3,1},{4,2},{5,3},{6,4},{7,5},{10,8},{11,9},{12,10},{13,11},... | collective-permute-start | bytes 393224 | tf_op jit(solution)/shard_map/ppermute | solution.py:27
  73.5 16.3 %copy-start.15 = (f32[1,128,256]{2,1,0:T(8,128)S(1)}, f32[1,128,256]{2,1,0:T(8,128)}, u32[]{:S(2)}) copy-start(f32[1,128,256]{2,1,0:T(8,128)} %copy.143) | copy-start | bytes 393220
  80.4 6.9 %collective-permute-start.7 = (f32[1,2,128,128]{2,3,1,0:T(8,128)S(1)}, f32[1,2,128,128]{2,3,1,0:T(8,128)S(1)}, u32[]{:S(2)}, u32[]{:S(2)}) collective-permute-start(f32[1,2,128,128]{2,3,1,0:T(8,128)S(1)} %add.142), channel_id=1, source_target_pairs={{4,0},{5,1},{6,2},{7,3},{12,8},{13,9},{14,10},{15,11},{20,16},{21,... | collective-permute-start | bytes 393224 | tf_op jit(solution)/shard_map/ppermute | solution.py:27

commit v2 on v1

--- a/solution.py
+++ b/solution.py
@@ -14,24 +14,12 @@
 epsilon = 1e-05
 
 
-def exclusive_scan(part, axis, reverse):
+def gathered_before(gathered, axis, reverse):
     count = lax.axis_size(axis)
-    running = part
-    total = None
-    distance = 1
-    while distance < count:
-        if reverse:
-            route = [(i + distance, i) for i in range(count - distance)]
-        else:
-            route = [(i, i + distance) for i in range(count - distance)]
-        got = lax.ppermute(running, axis, route)
-        total = got if total is None else total + got
-        if distance * 2 < count:
-            running = running + got
-        distance *= 2
-    if total is None:
-        total = jnp.zeros_like(part)
-    return total
+    place = lax.axis_index(axis)
+    slots = jnp.arange(count).reshape((count,) + (1,) * (gathered.ndim - 1))
+    chosen = slots > place if reverse else slots < place
+    return jnp.sum(jnp.where(chosen, gathered, 0.0), axis=0)
 
 
 def all_sum(part, axes):
@@ -69,7 +57,7 @@
     local_state = jnp.einsum(
         "nrgd,nrge->ngde", key_heads, spiked, preferred_element_type=jnp.float32
     )
-    prior = exclusive_scan(local_state, "ctx", False)
+    prior = gathered_before(lax.all_gather(local_state, "ctx"), "ctx", False)
     prior_half = prior.astype(jnp.bfloat16)
     packed = jnp.concatenate([keys, values], axis=2)
     earlier = []
@@ -126,7 +114,6 @@
     grad_wide = head_gradients.astype(jnp.float32)
     total_tokens = batch_inputs * lax.axis_size("dp") * token_rows * lax.axis_size("ctx")
     gain_local = jnp.sum(grad_wide * normed, axis=(0, 1)).reshape(QUERY_HEADS * HEAD_SIZE)
-    d_gain = all_sum(gain_local, ("dp", "ctx")) * (total_tokens ** (-0.5))
     scaled = grad_wide * head_gains
     d_linear = (
         (scaled - normed * jnp.mean(scaled * normed, axis=-1, keepdims=True)) / root
@@ -134,7 +121,21 @@
     suffix_local = jnp.einsum(
         "nrghd,nrghe->ngde", query_heads, d_linear, preferred_element_type=jnp.float32
     )
-    later = exclusive_scan(suffix_local, "ctx", True)
+    state_rows = KEY_VALUE_HEADS * HEAD_SIZE
+    gain_rows = QUERY_HEADS * HEAD_SIZE // HEAD_SIZE
+    pad_rows = (-(state_rows + gain_rows)) % 8
+    riding = jnp.concatenate(
+        [
+            suffix_local.reshape(state_rows, HEAD_SIZE),
+            gain_local.reshape(gain_rows, HEAD_SIZE),
+            jnp.zeros((pad_rows, HEAD_SIZE), jnp.float32),
+        ],
+        axis=0,
+    )
+    riding_all = lax.all_gather(riding, "ctx")
+    later = gathered_before(riding_all[:, :state_rows], "ctx", True).reshape(suffix_local.shape)
+    gain_ctx = jnp.sum(riding_all[:, state_rows : state_rows + gain_rows], axis=0)
+    d_gain = all_sum(gain_ctx.reshape(QUERY_HEADS * HEAD_SIZE), ("dp",)) * (total_tokens ** (-0.5))
     later_half = later.astype(jnp.bfloat16)
     back_half = (
         jnp.einsum("nrghe,nsge->nghrs", d_linear, spiked, preferred_element_type=jnp.float32)

time: 92.5 us -> 104 us (1.12)
  starting transfers between devices: 32 us -> 13 us
  waiting for transfers between devices: 12.4 us -> 29.1 us
  between operations: 1.32 us -> 14.7 us
  matrix products: 17.1 us -> 13.1 us
  local copies, waits for them, and re-layouts: 17.3 us -> 21.1 us
    all_gather x0 -> x2, waiting for transfers between devices: none -> 28.6 us  [the longest x1 20.1 us: per_device(): riding_all = lax.all_gather(riding, 'ctx')]
    ppermute x6 -> x0, starting transfers between devices: 16 us -> none  [exclusive_scan(): got = lax.ppermute(running, axis, route)]
    ppermute x6 -> x0, waiting for transfers between devices: 8.79 us -> none  [exclusive_scan(): got = lax.ppermute(running, axis, route)]
    reduce_sum x0 -> x3, other arithmetic: none -> 3.71 us  [the longest x2 2.86 us: gathered_before(): return jnp.sum(jnp.where(chosen, gathered, 0.0), axis=0)]
    ppermute x5 -> x2, starting transfers between devices: 7.11 us -> 3.89 us  [all_sum(): part = part + lax.ppermute(part, axes, route)]
    ppermute x5 -> x2, waiting for transfers between devices: 3.62 us -> 0.5 us  [all_sum(): part = part + lax.ppermute(part, axes, route)]
    all_gather x0 -> x1, local copies, waits for them, and re-layouts: none -> 2.56 us  [per_device(): prior = gathered_before(lax.all_gather(local_state, 'ctx'), 'ctx', False)]
    add x4 -> x0, other arithmetic: 2.53 us -> none  [exclusive_scan(): running = running + got]
  transfers between devices with their start and end apart: 15 -> 8, of which waited for: 4 -> 4; matrix products, arithmetic and copies ran while one was open for 32% -> 33% of each run, Pallas kernels for 0% -> 0%
where the time goes in v2:
time: 104 us; the launch traced here: 103 us
  waiting for transfers between devices  29.1 us (28%)
  local copies, waits for them, and re-layouts  21.1 us (20%)
  between operations  14.7 us (14%)
  matrix products  13.1 us (13%)
  starting transfers between devices  13 us (12%)
  other arithmetic  12.1 us (12%)
    all_gather x1, waiting for transfers between devices, per_device(): riding_all = lax.all_gather(riding, 'ctx')  20.1 us
    unnamed x78, local copies, waits for them, and re-layouts  12.4 us
    ppermute x4, starting transfers between devices, shifted(): return lax.ppermute(block, axis, route)  9.01 us
    all_gather x1, waiting for transfers between devices, per_device(): prior = gathered_before(lax.all_gather(local_state, 'ctx'), 'ctx', False)  8.52 us
    ppermute x2, starting transfers between devices, all_sum(): part = part + lax.ppermute(part, axes, route)  3.89 us
    dot_general x1, matrix products, per_device(): jnp.einsum('nrghd,nmgd->nghrm', head_gradients, value_window, preferred_e...  2.91 us
    reduce_sum x2, other arithmetic, gathered_before(): return jnp.sum(jnp.where(chosen, gathered, 0.0), axis=0)  2.86 us
    dot_general x1, matrix products, per_device(): jnp.einsum('nghrm,nmgd->nrghd', probs_half, value_window, preferred_eleme...  2.66 us
  transfers between devices with their start and end apart: 8, of which 4 were waited for; matrix products, arithmetic and copies ran while one was open for 33% of the time, Pallas kernels for 0%

profile of v2, /device:TPU:0, one launch (start us, length us, event | category | flops | bytes accessed | tf_op | source)
XLA Modules:
  0.0 103.2 jit_solution(14219551550352300206)
XLA Ops:
  7.2 1.0 copy.106
  8.2 1.0 copy.107
  9.2 4.8 %collective-permute-start = (bf16[1,128,512]{1,2,0:T(8,128)(2,1)S(1)}, bf16[1,128,512]{1,2,0:T(8,128)(2,1)S(1)}, u32[]{:S(2)}, u32[]{:S(2)}) collective-permute-start(bf16[1,128,512]{1,2,0:T(8,128)(2,1)S(1)} %pad_maximum_fusion.2), channel_id=1, source_target_pairs={{0,2},{1,3},{2,4},{3,5},{4,6},{5,7},{8,10},{9,11},{10,12},{11,13},... | collective-permute-start | bytes 393224 | tf_op jit(solution)/shard_map/ppermute | solution.py:40
  14.1 1.5 %collective-permute-start.1 = (bf16[1,128,512]{1,2,0:T(8,128)(2,1)S(1)}, bf16[1,128,512]{1,2,0:T(8,128)(2,1)S(1)}, u32[]{:S(2)}, u32[]{:S(2)}) collective-permute-start(bf16[1,128,512]{1,2,0:T(8,128)(2,1)S(1)} %pad_maximum_fusion.2), channel_id=1, source_target_pairs={{0,1},{1,2},{2,3},{3,4},{4,5},{5,6},{6,7},{8,9},{9,10},{10,11},{11... | collective-permute-start | bytes 393224 | tf_op jit(solution)/shard_map/ppermute | solution.py:40
  15.5 0.9 reshape.329
  16.5 0.9 reshape.311
  17.3 0.7 convert_bitcast_fusion
  18.3 0.8 copy.103
  19.3 1.3 %copy.96 = bf16[1,128,1792]{1,2,0:T(8,128)(2,1)S(1)} copy(bf16[1,128,1792]{2,1,0:T(8,128)(2,1)} %param.7) | data formatting | bytes 917504 | tf_op args[0]
  20.7 1.1 %fusion.23 = bf16[2,7,128,128]{2,3,1,0:T(8,128)(2,1)} fusion(bf16[128,2,128,1]{0,2,3,1:T(8,128)(2,1)S(1)} %copy.154, bf16[128,2,7,128]{0,3,2,1:T(8,128)(2,1)S(1)} %bitcast.241, f32[128,128]{0,1:T(8,128)S(1)} %fusion.42), kind=kOutput, calls=%fused_computation.31 | convolution fusion | flops 59179008 | bytes 1048576 | tf_op jit(solution)/shard_map/nrghd,nsgd->nghrs/dot_general | solution.py:84
  21.9 0.8 and_and_fusion
  22.7 0.5 iota_compare_fusion.2
  23.2 1.2 %copy.111 = f32[1,128,1792]{1,2,0:T(8,128)} copy(bf16[1,128,1792]{2,1,0:T(8,128)(2,1)S(1)} %copy-done.4) | data formatting | bytes 1376256 | tf_op jit(solution)/shard_map/convert_element_type | solution.py:114
  24.4 1.0 copy.117
  25.4 0.7 pad.6.clone
  26.0 0.6 iota_compare_fusion.1
  26.7 0.7 fusion.51
  27.4 1.6 %fusion.5 = (f32[2,7,128]{2,1,0:T(8,128)S(1)}, f32[2,384,128,7]{2,1,3,0:T(8,128)S(1)}) fusion(pred[2,128,384]{1,2,0:T(8,128)(4,1)} %and_and_fusion, bf16[384,2,128,1]{0,2,3,1:T(8,128)(2,1)S(1)} %bitcast.250, bf16[128,2,7,128]{0,3,2,1:T(8,128)(2,1)S(1)} %bitcast.242), kind=kOutput, calls=%fused_computation.8 | convolution fusion | flops 178223360 | bytes 3513344 | tf_op jit(solution)/shard_map/nrghd,nmgd->nghrm/dot_general | solution.py:95
  29.0 0.6 fusion.4
  29.6 0.9 fusion.7
  30.5 0.8 fusion.49
  31.3 1.6 %copy.184 = f32[1,128,256]{2,1,0:T(8,128)} copy(f32[1,128,256]{1,2,0:T(8,128)} %get-tuple-element.28) | data formatting | bytes 262144
  32.9 1.6 %copy.186 = f32[1,128,256]{2,1,0:T(8,128)} copy(f32[1,128,256]{1,2,0:T(8,128)} %get-tuple-element.27) | data formatting | bytes 262144
  34.6 1.7 %copy.187 = f32[1,128,256]{2,1,0:T(8,128)} copy(f32[1,128,256]{1,2,0:T(8,128)} %get-tuple-element.26) | data formatting | bytes 262144
  36.2 8.5 %all-gather.5.cloned.1.call-done = f32[16,128,128]{2,1,0:T(8,128)} async-done(((f32[2,128,128]{2,1,0:T(8,128)}), f32[16,128,128]{2,1,0:T(8,128)}) %all-gather.5.cloned.1.call-update) | async-done | bytes 1048592 | tf_op jit(solution)/shard_map/all_gather | solution.py:60
  44.7 2.6 %copy.104 = f32[8,1,2,128,128]{3,4,2,0,1:T(8,128)} copy(f32[8,1,2,128,128]{4,3,2,0,1:T(8,128)} %bitcast.255) | data formatting | bytes 2097152 | tf_op jit(solution)/shard_map/all_gather | solution.py:60
  47.3 1.5 %select_reduce_fusion = bf16[2,128,128]{1,2,0:T(8,128)(2,1)S(1)} fusion(f32[8,1,2,128,128]{3,4,2,0,1:T(8,128)} %copy.104, pred[8]{0:T(512)(128)(4,1)} %iota_compare_fusion.2), kind=kLoop, calls=%fused_computation.42 | loop fusion | flops 491520 | bytes 1114120 | tf_op jit(solution)/shard_map/reduce_sum | solution.py:22
  48.8 0.6 copy-done.8
  49.7 0.3 multiply_reduce_fusion.3
  50.1 2.7 %multiply_reduce_fusion = (f32[2,7,128]{2,1,0:T(8,128)}, f32[128,2,7]{0,2,1:T(8,128)S(1)}, f32[128,2,7]{0,2,1:T(8,128)}, bf16[1,128,2,7,128]{1,4,3,2,0:T(8,128)(2,1)}) fusion(f32[1,128,2,7,128]{1,4,3,2,0:T(8,128)S(1)} %bitcast.247, f32[1,128,2,7,128]{1,4,3,2,0:T(8,128)S(1)} %get-tuple-element.35, f32[128,2,7]{0,2,1:T(8,128)S(1)} %add_sqrt_fusion, ...), kind=kOutput, calls=%fused_computation.43 | convolution fusion | flops 182119168 | bytes 5391360 | tf_op jit(solution)/shard_map/nghrm,nmgd->nrghd/dot_general | solution.py:103
  53.5 0.8 maximum_maximum_fusion.1
  54.4 2.9 %fusion.6 = bf16[2,7,128,384]{2,3,1,0:T(8,128)(2,1)S(1)} fusion(bf16[384,2,128,1]{0,2,3,1:T(8,128)(2,1)S(1)} %bitcast.267, bf16[128,2,7,128]{0,3,2,1:T(8,128)(2,1)S(1)} %bitcast.263, f32[2,7,128]{2,1,0:T(8,128)S(1)} %bitcast.269, f32[2,7,128]{2,1,0:T(8,128)S(1)} %copy-done.26, f32[2,7,128]{2,1,0:T(8,128)S(1)} %get-tuple-element.36, ...), kind=kOutput, calls=%fused_computation.9 | convolution fusion | flops 181665792 | bytes 4903936 | tf_op jit(solution)/shard_map/nrghd,nmgd->nghrm/dot_general | solution.py:163
  57.3 0.6 fusion.52
  58.2 0.7 pad_maximum_fusion
  58.9 1.3 %collective-permute-start.2 = (f32[1,128,512]{2,1,0:T(8,128)}, f32[1,128,512]{2,1,0:T(8,128)}, u32[]{:S(2)}, u32[]{:S(2)}) collective-permute-start(f32[1,128,512]{2,1,0:T(8,128)} %pad_maximum_fusion), channel_id=1, source_target_pairs={{1,0},{2,1},{3,2},{4,3},{5,4},{6,5},{7,6},{9,8},{10,9},{11,10},{12... | collective-permute-start | bytes 786440 | tf_op jit(solution)/shard_map/ppermute | solution.py:40
  60.3 0.7 pad_maximum_fusion.1
  61.0 1.4 %collective-permute-start.3 = (f32[1,128,512]{2,1,0:T(8,128)}, f32[1,128,512]{2,1,0:T(8,128)}, u32[]{:S(2)}, u32[]{:S(2)}) collective-permute-start(f32[1,128,512]{2,1,0:T(8,128)} %pad_maximum_fusion.1), channel_id=1, source_target_pairs={{2,0},{3,1},{4,2},{5,3},{6,4},{7,5},{10,8},{11,9},{12,10},{13,11},... | collective-permute-start | bytes 786440 | tf_op jit(solution)/shard_map/ppermute | solution.py:40
  63.1 0.4 convolution_bitcast_fusion.6
  63.6 0.3 fusion.21
  64.0 1.0 copy.137
  65.0 1.0 copy.136
  66.6 20.1 %all-gather.7.cloned.1.call-done = f32[2176,128]{1,0:T(8,128)} async-done(((f32[272,128]{1,0:T(8,128)}), f32[2176,128]{1,0:T(8,128)}) %all-gather.7.cloned.1.call-update) | async-done | bytes 1114128 | tf_op jit(solution)/shard_map/all_gather | solution.py:135
  86.7 0.9 slice_reduce_fusion
  87.5 1.5 %collective-permute-start.4 = (f32[1792]{0:T(1024)S(1)}, f32[1792]{0:T(1024)S(1)}, u32[]{:S(2)}, u32[]{:S(2)}) collective-permute-start(f32[1792]{0:T(1024)S(1)} %bitcast.268), channel_id=1, source_target_pairs={{0,8},{8,0},{16,24},{24,16},{1,9},{9,1},{17,25},{25,17},{2,10},{10... | collective-permute-start | bytes 21512 | tf_op jit(solution)/shard_map/ppermute | solution.py:32
  89.0 1.4 %fusion.27 = bf16[256,128]{1,0:T(8,128)(2,1)S(1)} fusion(f32[8,272,128]{2,1,0:T(8,128)} %bitcast.254, pred[8]{0:T(512)(128)(4,1)S(1)} %copy-done.31), kind=kLoop, calls=%fused_computation.41 | loop fusion | flops 491520 | bytes 1114120 | tf_op jit(solution)/shard_map/reduce_sum | solution.py:22
  91.2 2.4 %collective-permute-start.5 = (f32[1792]{0:T(1024)S(1)}, f32[1792]{0:T(1024)S(1)}, u32[]{:S(2)}, u32[]{:S(2)}) collective-permute-start(f32[1792]{0:T(1024)S(1)} %bitcast_add_fusion), channel_id=1, source_target_pairs={{0,16},{8,24},{16,0},{24,8},{1,17},{9,25},{17,1},{25,9},{2,18},{10... | collective-permute-start | bytes 21512 | tf_op jit(solution)/shard_map/ppermute | solution.py:32
  93.6 1.8 %fusion.34 = (bf16[1,128,256]{2,1,0:T(8,128)(2,1)}, bf16[1,128,256]{2,1,0:T(8,128)(2,1)}) fusion(f32[1,128,512]{2,1,0:T(8,128)} %collective-permute-done.3, f32[1,128,512]{2,1,0:T(8,128)} %collective-permute-done.2, f32[1,128,256]{2,1,0:T(8,128)S(1)} %copy.135, f32[1,128,256]{2,1,0:T(8,128)S(1)} %copy-done.14, f32[1,128,256]{2,1,0:T(8,128)S(1)} %copy.125, ...), kind=kLoop, calls=%fused_computation.63 | loop fusion | flops 262144 | bytes 1179648 | tf_op jit(solution)/shard_map/convert_element_type | solution.py:205
  95.7 0.6 add_multiply_fusion
  (106 shorter events, 4.5 us)
Async XLA Ops:
  7.2 14.7 %copy-start.30 = (s32[2]{0:T(128)S(1)}, s32[2]{0:T(128)}, u32[]{:S(2)}) copy-start(s32[2]{0:T(128)} %param.11) | copy-start | bytes 28
  7.2 16.0 %copy-start.4 = (bf16[1,128,1792]{2,1,0:T(8,128)(2,1)S(1)}, bf16[1,128,1792]{2,1,0:T(8,128)(2,1)}, u32[]{:S(2)}) copy-start(bf16[1,128,1792]{2,1,0:T(8,128)(2,1)} %param.13) | copy-start | bytes 1376260
  7.2 37.6 %all-gather.5.cloned.1.call-start = ((), (), s32[]{:S(2)}) async-start(), calls=%async_computation | async-start | bytes 1179648 | tf_op jit(solution)/shard_map/all_gather | solution.py:60
  9.2 17.4 %collective-permute-start = (bf16[1,128,512]{1,2,0:T(8,128)(2,1)S(1)}, bf16[1,128,512]{1,2,0:T(8,128)(2,1)S(1)}, u32[]{:S(2)}, u32[]{:S(2)}) collective-permute-start(bf16[1,128,512]{1,2,0:T(8,128)(2,1)S(1)} %pad_maximum_fusion.2), channel_id=1, source_target_pairs={{0,2},{1,3},{2,4},{3,5},{4,6},{5,7},{8,10},{9,11},{10,12},{11,13},... | collective-permute-start | bytes 393224 | tf_op jit(solution)/shard_map/ppermute | solution.py:40
  14.1 12.5 %collective-permute-start.1 = (bf16[1,128,512]{1,2,0:T(8,128)(2,1)S(1)}, bf16[1,128,512]{1,2,0:T(8,128)(2,1)S(1)}, u32[]{:S(2)}, u32[]{:S(2)}) collective-permute-start(bf16[1,128,512]{1,2,0:T(8,128)(2,1)S(1)} %pad_maximum_fusion.2), channel_id=1, source_target_pairs={{0,1},{1,2},{2,3},{3,4},{4,5},{5,6},{6,7},{8,9},{9,10},{10,11},{11... | collective-permute-start | bytes 393224 | tf_op jit(solution)/shard_map/ppermute | solution.py:40
  18.0 1.2 %copy-start.22 = (f32[128,2]{0,1:T(2,128)}, f32[128,2]{0,1:T(2,128)S(1)}, u32[]{:S(2)}) copy-start(f32[128,2]{0,1:T(2,128)S(1)} %convert_bitcast_fusion) | copy-start | bytes 3076
  18.3 7.0 %copy-start.28 = (f32[1792]{0:T(1024)S(1)}, f32[1792]{0:T(1024)}, u32[]{:S(2)}) copy-start(f32[1792]{0:T(1024)} %param.12) | copy-start | bytes 21508
  19.1 67.5 %all-gather.7.cloned.1.call-start = ((), (), s32[]{:S(2)}) async-start(), calls=%async_computation.1 | async-start | bytes 1253376 | tf_op jit(solution)/shard_map/all_gather | solution.py:135
  19.3 7.4 %copy-start.10 = (f32[128,128]{0,1:T(8,128)}, f32[128,128]{0,1:T(8,128)S(1)}, u32[]{:S(2)}) copy-start(f32[128,128]{0,1:T(8,128)S(1)} %fusion.42) | copy-start | bytes 196612
  20.7 6.7 %copy-start.12 = (bf16[128,2,128,1]{0,2,3,1:T(8,128)(2,1)}, bf16[128,2,128,1]{0,2,3,1:T(8,128)(2,1)S(1)}, u32[]{:S(2)}) copy-start(bf16[128,2,128,1]{0,2,3,1:T(8,128)(2,1)S(1)} %copy.154) | copy-start | bytes 196612
  25.4 3.6 %copy-start.5 = (pred[2,128,384]{1,2,0:T(8,128)(4,1)S(1)}, pred[2,128,384]{1,2,0:T(8,128)(4,1)}, u32[]{:S(2)}) copy-start(pred[2,128,384]{1,2,0:T(8,128)(4,1)} %and_and_fusion) | copy-start | bytes 294916
  27.4 2.2 %copy-start.17 = (bf16[1,128,1792]{1,2,0:T(8,128)(2,1)S(1)}, bf16[1,128,1792]{1,2,0:T(8,128)(2,1)}, u32[]{:S(2)}) copy-start(bf16[1,128,1792]{1,2,0:T(8,128)(2,1)} %copy.117) | copy-start | bytes 1376260
  29.0 21.1 %copy-start = (f32[2,384,128,7]{2,1,3,0:T(8,128)}, f32[2,384,128,7]{2,1,3,0:T(8,128)S(1)}, u32[]{:S(2)}) copy-start(f32[2,384,128,7]{2,1,3,0:T(8,128)S(1)} %get-tuple-element.37) | copy-start | bytes 8257540
  29.6 0.9 copy-start.24
  47.3 2.4 %copy-start.1 = (bf16[2,7,128,128]{2,3,1,0:T(8,128)(2,1)S(1)}, bf16[2,7,128,128]{2,3,1,0:T(8,128)(2,1)}, u32[]{:S(2)}) copy-start(bf16[2,7,128,128]{2,3,1,0:T(8,128)(2,1)} %fusion.23) | copy-start | bytes 1376260
  47.3 2.8 %copy-start.3 = (f32[1,128,1792]{1,2,0:T(8,128)S(1)}, f32[1,128,1792]{1,2,0:T(8,128)}, u32[]{:S(2)}) copy-start(f32[1,128,1792]{1,2,0:T(8,128)} %copy.111) | copy-start | bytes 2752516
  47.3 2.8 %copy-start.6 = (pred[2,128,384]{1,2,0:T(8,128)(4,1)S(1)}, pred[2,128,384]{1,2,0:T(8,128)(4,1)}, u32[]{:S(2)}) copy-start(pred[2,128,384]{1,2,0:T(8,128)(4,1)} %and_and_fusion) | copy-start | bytes 294916
  47.3 2.8 %copy-start.20 = (bf16[1,384,256]{1,2,0:T(8,128)(2,1)S(1)}, bf16[1,384,256]{1,2,0:T(8,128)(2,1)}, u32[]{:S(2)}) copy-start(bf16[1,384,256]{1,2,0:T(8,128)(2,1)} %get-tuple-element.33) | copy-start | bytes 589828
  47.3 2.8 %copy-start.25 = (f32[2,7,128]{2,1,0:T(8,128)S(1)}, f32[2,7,128]{2,1,0:T(8,128)}, u32[]{:S(2)}) copy-start(f32[2,7,128]{2,1,0:T(8,128)} %copy-done.24) | copy-start | bytes 21508
  48.8 0.6 copy-start.8
  52.8 0.7 copy-start.29
  52.8 0.7 copy-start.27
  52.8 1.5 %copy-start.7 = (pred[2,128,384]{1,2,0:T(8,128)(4,1)S(1)}, pred[2,128,384]{1,2,0:T(8,128)(4,1)}, u32[]{:S(2)}) copy-start(pred[2,128,384]{1,2,0:T(8,128)(4,1)} %and_and_fusion) | copy-start | bytes 294916
  52.8 1.5 %copy-start.18 = (bf16[1,128,1792]{1,2,0:T(8,128)(2,1)S(1)}, bf16[1,128,1792]{1,2,0:T(8,128)(2,1)}, u32[]{:S(2)}) copy-start(bf16[1,128,1792]{1,2,0:T(8,128)(2,1)} %copy.117) | copy-start | bytes 1376260
  52.8 1.5 %copy-start.21 = (bf16[1,384,256]{1,2,0:T(8,128)(2,1)S(1)}, bf16[1,384,256]{1,2,0:T(8,128)(2,1)}, u32[]{:S(2)}) copy-start(bf16[1,384,256]{1,2,0:T(8,128)(2,1)} %get-tuple-element.33) | copy-start | bytes 589828
  52.8 1.5 %copy-start.26 = (f32[2,7,128]{2,1,0:T(8,128)S(1)}, f32[2,7,128]{2,1,0:T(8,128)}, u32[]{:S(2)}) copy-start(f32[2,7,128]{2,1,0:T(8,128)} %copy-done.24) | copy-start | bytes 21508
  52.8 1.5 %copy-start.32 = (f32[128,2,7]{0,2,1:T(8,128)S(1)}, f32[128,2,7]{0,2,1:T(8,128)}, u32[]{:S(2)}) copy-start(f32[128,2,7]{0,2,1:T(8,128)} %get-tuple-element.22) | copy-start | bytes 21508
  57.3 0.9 copy-start.16
  57.3 3.0 %copy-start.15 = (f32[1,128,256]{2,1,0:T(8,128)S(1)}, f32[1,128,256]{2,1,0:T(8,128)}, u32[]{:S(2)}) copy-start(f32[1,128,256]{2,1,0:T(8,128)} %copy.186) | copy-start | bytes 393220
  57.3 5.3 %copy-start.11 = (f32[128,128]{0,1:T(8,128)S(1)}, f32[128,128]{0,1:T(8,128)}, u32[]{:S(2)}) copy-start(f32[128,128]{0,1:T(8,128)} %copy-done.10) | copy-start | bytes 196612
  57.3 5.6 %copy-start.13 = (bf16[128,2,128,1]{0,2,3,1:T(8,128)(2,1)S(1)}, bf16[128,2,128,1]{0,2,3,1:T(8,128)(2,1)}, u32[]{:S(2)}) copy-start(bf16[128,2,128,1]{0,2,3,1:T(8,128)(2,1)} %copy-done.12) | copy-start | bytes 196612
  58.9 34.7 %collective-permute-start.2 = (f32[1,128,512]{2,1,0:T(8,128)}, f32[1,128,512]{2,1,0:T(8,128)}, u32[]{:S(2)}, u32[]{:S(2)}) collective-permute-start(f32[1,128,512]{2,1,0:T(8,128)} %pad_maximum_fusion), channel_id=1, source_target_pairs={{1,0},{2,1},{3,2},{4,3},{5,4},{6,5},{7,6},{9,8},{10,9},{11,10},{12... | collective-permute-start | bytes 786440 | tf_op jit(solution)/shard_map/ppermute | solution.py:40
  61.0 2.5 %copy-start.9 = (bf16[2,128,128]{1,2,0:T(8,128)(2,1)S(1)}, bf16[2,128,128]{1,2,0:T(8,128)(2,1)}, u32[]{:S(2)}) copy-start(bf16[2,128,128]{1,2,0:T(8,128)(2,1)} %copy-done.8) | copy-start | bytes 196612
  61.0 32.5 %collective-permute-start.3 = (f32[1,128,512]{2,1,0:T(8,128)}, f32[1,128,512]{2,1,0:T(8,128)}, u32[]{:S(2)}, u32[]{:S(2)}) collective-permute-start(f32[1,128,512]{2,1,0:T(8,128)} %pad_maximum_fusion.1), channel_id=1, source_target_pairs={{2,0},{3,1},{4,2},{5,3},{6,4},{7,5},{10,8},{11,9},{12,10},{13,11},... | collective-permute-start | bytes 786440 | tf_op jit(solution)/shard_map/ppermute | solution.py:40
  63.6 1.4 %copy-start.19 = (bf16[1,128,2,7,128]{1,4,3,2,0:T(8,128)(2,1)S(1)}, bf16[1,128,2,7,128]{1,4,3,2,0:T(8,128)(2,1)}, u32[]{:S(2)}) copy-start(bf16[1,128,2,7,128]{1,4,3,2,0:T(8,128)(2,1)} %get-tuple-element.23) | copy-start | bytes 1376260
  63.6 2.7 %copy-start.2 = (bf16[2,7,128,128]{2,3,1,0:T(8,128)(2,1)S(1)}, bf16[2,7,128,128]{2,3,1,0:T(8,128)(2,1)}, u32[]{:S(2)}) copy-start(bf16[2,7,128,128]{2,3,1,0:T(8,128)(2,1)} %fusion.23) | copy-start | bytes 1376260
  63.6 25.4 %copy-start.31 = (pred[8]{0:T(512)(128)(4,1)S(1)}, pred[8]{0:T(512)(128)(4,1)}, u32[]{:S(2)}) copy-start(pred[8]{0:T(512)(128)(4,1)} %iota_compare_fusion.1) | copy-start | bytes 28
  64.0 26.4 %copy-start.23 = (f32[128,2]{0,1:T(2,128)S(1)}, f32[128,2]{0,1:T(2,128)}, u32[]{:S(2)}) copy-start(f32[128,2]{0,1:T(2,128)} %copy-done.22) | copy-start | bytes 3076
  65.0 28.6 %copy-start.14 = (f32[1,128,256]{2,1,0:T(8,128)S(1)}, f32[1,128,256]{2,1,0:T(8,128)}, u32[]{:S(2)}) copy-start(f32[1,128,256]{2,1,0:T(8,128)} %copy.187) | copy-start | bytes 393220
  87.5 3.7 %collective-permute-start.4 = (f32[1792]{0:T(1024)S(1)}, f32[1792]{0:T(1024)S(1)}, u32[]{:S(2)}, u32[]{:S(2)}) collective-permute-start(f32[1792]{0:T(1024)S(1)} %bitcast.268), channel_id=1, source_target_pairs={{0,8},{8,0},{16,24},{24,16},{1,9},{9,1},{17,25},{25,17},{2,10},{10... | collective-permute-start | bytes 21512 | tf_op jit(solution)/shard_map/ppermute | solution.py:32
  91.2 4.5 %collective-permute-start.5 = (f32[1792]{0:T(1024)S(1)}, f32[1792]{0:T(1024)S(1)}, u32[]{:S(2)}, u32[]{:S(2)}) collective-permute-start(f32[1792]{0:T(1024)S(1)} %bitcast_add_fusion), channel_id=1, source_target_pairs={{0,16},{8,24},{16,0},{24,8},{1,17},{9,25},{17,1},{25,9},{2,18},{10... | collective-permute-start | bytes 21512 | tf_op jit(solution)/shard_map/ppermute | solution.py:32
Sparse Core Ops, SparseCore 0:
  19.2 25.4 all-gather.4
  54.4 32.1 all-gather.6

commit v3 on v1

v3 whole, which is shorter than its diff:
```python
import jax
import jax.numpy as jnp
from jax import lax
from jax.experimental import pallas as pl
from jax.experimental.pallas import tpu as pltpu
from jax.sharding import PartitionSpec as P

QUERY_HEADS = 14
KEY_VALUE_HEADS = 2
HEAD_SIZE = 128
WINDOW_REACH = 256


epsilon = 1e-05


def exclusive_scan(part, axis, reverse):
    count = lax.axis_size(axis)
    running = part
    total = None
    distance = 1
    while distance < count:
        if reverse:
            route = [(i + distance, i) for i in range(count - distance)]
        else:
            route = [(i, i + distance) for i in range(count - distance)]
        got = lax.ppermute(running, axis, route)
        total = got if total is None else total + got
        if distance * 2 < count:
            running = running + got
        distance *= 2
    if total is None:
        total = jnp.zeros_like(part)
    return total


def all_sum(part, axes):
    count = 1
    for axis in axes:
        count *= lax.axis_size(axis)
    step = 1
    while step < count:
        route = [(i, i ^ step) for i in range(count)]
        part = part + lax.ppermute(part, axes, route)
        step *= 2
    return part


def shifted(block, axis, distance):
    devices = range(lax.axis_size(axis))
    route = [(i - distance, i) for i in devices if i - distance in devices]
    return lax.ppermute(block, axis, route)


def window_kernel(info_ref, q_ref, c_ref, k_ref, v_ref, wout_ref, wdq_ref, dk_ref, dv_ref):
    group_size = QUERY_HEADS // KEY_VALUE_HEADS
    token_rows = q_ref.shape[0]
    window_rows = k_ref.shape[0]
    padding_rows = window_rows - token_rows
    scale = HEAD_SIZE ** (-0.5)
    row = lax.broadcasted_iota(jnp.int32, (token_rows, window_rows), 0)
    col = lax.broadcasted_iota(jnp.int32, (token_rows, window_rows), 1)
    back = row + padding_rows - col
    seen = (back >= 0) & (col + info_ref[2] >= 0)
    for g in range(KEY_VALUE_HEADS):
        visible = seen & (back < info_ref[g])
        lanes = slice(g * HEAD_SIZE, (g + 1) * HEAD_SIZE)
        kg = k_ref[:, lanes]
        vg = v_ref[:, lanes]
        dk = jnp.zeros((window_rows, HEAD_SIZE), jnp.float32)
        dv = jnp.zeros((window_rows, HEAD_SIZE), jnp.float32)
        for h in range(group_size):
            cols = slice((g * group_size + h) * HEAD_SIZE, (g * group_size + h + 1) * HEAD_SIZE)
            qh = q_ref[:, cols]
            ch = c_ref[:, cols]
            s = lax.dot_general(qh, kg, (((1,), (1,)), ((), ())), preferred_element_type=jnp.float32) * scale
            s = jnp.where(visible, s, -1e30)
            top = jnp.max(s, axis=-1, keepdims=True)
            e = jnp.exp(s - top)
            p = e / jnp.sum(e, axis=-1, keepdims=True)
            ph = p.astype(jnp.bfloat16)
            wout = jnp.dot(ph, vg, preferred_element_type=jnp.float32)
            wout_ref[:, cols] = wout
            gp = lax.dot_general(ch, vg, (((1,), (1,)), ((), ())), preferred_element_type=jnp.float32)
            delta = jnp.sum(ch.astype(jnp.float32) * wout, axis=-1, keepdims=True)
            ds = (p * (gp - delta) * scale).astype(jnp.bfloat16)
            wdq_ref[:, cols] = jnp.dot(ds, kg, preferred_element_type=jnp.float32)
            dk = dk + lax.dot_general(ds, qh, (((0,), (0,)), ((), ())), preferred_element_type=jnp.float32)
            dv = dv + lax.dot_general(ph, ch, (((0,), (0,)), ((), ())), preferred_element_type=jnp.float32)
        dk_ref[:, lanes] = dk
        dv_ref[:, lanes] = dv


def linear_kernel(q_ref, c_ref, k_ref, s_ref, prior_ref, gain_ref, wout_ref, wdq_ref,
                  mixed_ref, dq_ref, suffix_ref, gsum_ref, ldk_ref, dsp_ref):
    group_size = QUERY_HEADS // KEY_VALUE_HEADS
    token_rows = q_ref.shape[0]
    row = lax.broadcasted_iota(jnp.int32, (token_rows, token_rows), 0)
    col = lax.broadcasted_iota(jnp.int32, (token_rows, token_rows), 1)
    causal = row >= col
    for g in range(KEY_VALUE_HEADS):
        lanes = slice(g * HEAD_SIZE, (g + 1) * HEAD_SIZE)
        kg = k_ref[:, lanes]
        sg = s_ref[:, lanes]
        pg = prior_ref[g]
        suffix = jnp.zeros((HEAD_SIZE, HEAD_SIZE), jnp.float32)
        ldk = jnp.zeros((token_rows, HEAD_SIZE), jnp.float32)
        dsp = jnp.zeros((token_rows, HEAD_SIZE), jnp.float32)
        for h in range(group_size):
            cols = slice((g * group_size + h) * HEAD_SIZE, (g * group_size + h + 1) * HEAD_SIZE)
            qh = q_ref[:, cols]
            ch = c_ref[:, cols].astype(jnp.float32)
            gh = gain_ref[:, cols]
            lh = jnp.where(
                causal,
                lax.dot_general(qh, kg, (((1,), (1,)), ((), ())), preferred_element_type=jnp.float32),
                0.0,
            ).astype(jnp.bfloat16)
            lin = jnp.dot(lh, sg, preferred_element_type=jnp.float32) + jnp.dot(
                qh, pg, preferred_element_type=jnp.float32
            )
            root = jnp.sqrt(jnp.mean(lin * lin, axis=-1, keepdims=True) + epsilon)
            normed = lin / root
            mixed_ref[:, cols] = (gh * normed + wout_ref[:, cols]).astype(mixed_ref.dtype)
            gsum_ref[:, cols] = jnp.sum(ch * normed, axis=0, keepdims=True)
            scaled = ch * gh
            dl = ((scaled - normed * jnp.mean(scaled * normed, axis=-1, keepdims=True)) / root).astype(
                jnp.bfloat16
            )
            suffix = suffix + lax.dot_general(qh, dl, (((0,), (0,)), ((), ())), preferred_element_type=jnp.float32)
            bh = jnp.where(
                causal,
                lax.dot_general(dl, sg, (((1,), (1,)), ((), ())), preferred_element_type=jnp.float32),
                0.0,
            ).astype(jnp.bfloat16)
            ldq = lax.dot_general(dl, pg, (((1,), (1,)), ((), ())), preferred_element_type=jnp.float32)
            ldq = ldq + jnp.dot(bh, kg, preferred_element_type=jnp.float32)
            dq_ref[:, cols] = (ldq + wdq_ref[:, cols]).astype(dq_ref.dtype)
            ldk = ldk + lax.dot_general(bh, qh, (((0,), (0,)), ((), ())), preferred_element_type=jnp.float32)
            dsp = dsp + lax.dot_general(lh, dl, (((0,), (0,)), ((), ())), preferred_element_type=jnp.float32)
        suffix_ref[g] = suffix
        ldk_ref[:, lanes] = ldk
        dsp_ref[:, lanes] = dsp


def in_vmem(count):
    return [pl.BlockSpec(memory_space=pltpu.VMEM)] * count


def per_device(queries, keys, values, spikes, window_lengths, gain, cotangent):
    token_rows = queries.shape[1]
    width = QUERY_HEADS * HEAD_SIZE
    reach = (WINDOW_REACH + token_rows - 2) // token_rows
    padding_rows = reach * token_rows
    window_rows = (reach + 1) * token_rows
    key_value_width = KEY_VALUE_HEADS * HEAD_SIZE
    q = queries[0]
    c = cotangent[0]
    k = keys[0]
    v = values[0]
    counts = jnp.repeat(spikes[0].astype(jnp.float32), HEAD_SIZE, axis=1)
    spiked = (v.astype(jnp.float32) * counts).astype(jnp.bfloat16)
    local_state = jnp.stack(
        [
            lax.dot_general(
                k[:, g * HEAD_SIZE : (g + 1) * HEAD_SIZE],
                spiked[:, g * HEAD_SIZE : (g + 1) * HEAD_SIZE],
                (((0,), (0,)), ((), ())),
                preferred_element_type=jnp.float32,
            )
            for g in range(KEY_VALUE_HEADS)
        ]
    )
    prior_half = exclusive_scan(local_state, "ctx", False).astype(jnp.bfloat16)
    packed = jnp.concatenate([k, v], axis=1)
    earlier = []
    for distance in range(reach, 0, -1):
        earlier.append(shifted(packed, "ctx", distance))
    window_packed = jnp.concatenate(earlier + [packed], axis=0)
    info = jnp.concatenate(
        [window_lengths.astype(jnp.int32), (lax.axis_index("ctx") * token_rows - padding_rows).reshape(1)]
    ).astype(jnp.int32)
    wout, wdq, dk_win, dv_win = pl.pallas_call(
        window_kernel,
        out_shape=(
            jax.ShapeDtypeStruct((token_rows, width), jnp.float32),
            jax.ShapeDtypeStruct((token_rows, width), jnp.float32),
            jax.ShapeDtypeStruct((window_rows, key_value_width), jnp.float32),
            jax.ShapeDtypeStruct((window_rows, key_value_width), jnp.float32),
        ),
        in_specs=[pl.BlockSpec(memory_space=pltpu.SMEM)] + in_vmem(4),
        out_specs=tuple(in_vmem(4)),
    )(info, q, c, window_packed[:, :key_value_width], window_packed[:, key_value_width:])
    mixed, d_queries, suffix_local, gain_local, ldk, dsp = pl.pallas_call(
        linear_kernel,
        out_shape=(
            jax.ShapeDtypeStruct((token_rows, width), jnp.bfloat16),
            jax.ShapeDtypeStruct((token_rows, width), jnp.bfloat16),
            jax.ShapeDtypeStruct((KEY_VALUE_HEADS, HEAD_SIZE, HEAD_SIZE), jnp.float32),
            jax.ShapeDtypeStruct((1, width), jnp.float32),
            jax.ShapeDtypeStruct((token_rows, key_value_width), jnp.float32),
            jax.ShapeDtypeStruct((token_rows, key_value_width), jnp.float32),
        ),
        in_specs=in_vmem(8),
        out_specs=tuple(in_vmem(6)),
    )(q, c, k, spiked, prior_half, gain.reshape(1, width), wout, wdq)
    total_tokens = queries.shape[0] * lax.axis_size("dp") * token_rows * lax.axis_size("ctx")
    d_gain = all_sum(gain_local.reshape(width), ("dp", "ctx")) * (total_tokens ** (-0.5))
    later_half = exclusive_scan(suffix_local, "ctx", True).astype(jnp.bfloat16)
    ldk_parts = []
    dsp_parts = []
    for g in range(KEY_VALUE_HEADS):
        lanes = slice(g * HEAD_SIZE, (g + 1) * HEAD_SIZE)
        ldk_parts.append(
            ldk[:, lanes]
            + lax.dot_general(
                spiked[:, lanes], later_half[g], (((1,), (1,)), ((), ())), preferred_element_type=jnp.float32
            )
        )
        dsp_parts.append(
            dsp[:, lanes] + jnp.dot(k[:, lanes], later_half[g], preferred_element_type=jnp.float32)
        )
    linear_key_gradient = jnp.concatenate(ldk_parts, axis=1)
    linear_value_gradient = jnp.concatenate(dsp_parts, axis=1) * counts
    received = jnp.zeros((token_rows, 2 * key_value_width), jnp.float32)
    for distance in range(1, reach + 1):
        start_row = (reach - distance) * token_rows
        sent = jnp.concatenate(
            [
                dk_win[start_row : start_row + token_rows],
                dv_win[start_row : start_row + token_rows],
            ],
            axis=1,
        )
        received = received + shifted(sent, "ctx", -distance)
    keys_gradient = (
        linear_key_gradient + dk_win[padding_rows:] + received[:, :key_value_width]
    ).astype(jnp.bfloat16)
    values_gradient = (
        linear_value_gradient + dv_win[padding_rows:] + received[:, key_value_width:]
    ).astype(jnp.bfloat16)
    return (
        mixed[None],
        d_queries[None],
        keys_gradient[None],
        values_gradient[None],
        d_gain,
    )


def solution(mesh):
    placed = (
        P("dp", "ctx", None),
        P("dp", "ctx", None),
        P("dp", "ctx", None),
        P("dp", "ctx", None),
        P(),
        P(),
        P("dp", "ctx", None),
    )
    return jax.shard_map(
        per_device,
        mesh=mesh,
        in_specs=placed,
        out_specs=(
            P("dp", "ctx", None),
            P("dp", "ctx", None),
            P("dp", "ctx", None),
            P("dp", "ctx", None),
            P(),
        ),
        check_vma=False,
    )
```

time: 92.5 us -> 85.6 us (0.925)
  Pallas kernels: 0 us -> 21.7 us
  matrix products: 17.1 us -> 0.95 us
  local copies, waits for them, and re-layouts: 17.3 us -> 5.74 us
  other arithmetic: 11.4 us -> 5.42 us
  starting transfers between devices: 32 us -> 35.8 us
  waiting for transfers between devices: 12.4 us -> 14.4 us
    pallas_call x0 -> x2, Pallas kernels: none -> 21.7 us  [the longest x1 11.5 us: per_device(): pl.pallas_call(window_kernel, out_shape=(jax.ShapeDtypeStruct((token_rows...]
    dot_general x18 -> x6, matrix products: 17.1 us -> 0.95 us  [the longest x2 0.41 us: per_device(): lax.dot_general(k[:, g * HEAD_SIZE:(g + 1) * HEAD_SIZE], spiked[:, g * HE...]
    unnamed x66 -> x20, local copies, waits for them, and re-layouts: 11.5 us -> 2.94 us
    ppermute x5, starting transfers between devices: 7.11 us -> 12.6 us  [all_sum(): part = part + lax.ppermute(part, axes, route)]
    ppermute x5, waiting for transfers between devices: 3.62 us -> 8.04 us  [all_sum(): part = part + lax.ppermute(part, axes, route)]
    ppermute x6, starting transfers between devices: 16 us -> 12.7 us  [exclusive_scan(): got = lax.ppermute(running, axis, route)]
    convert_element_type x2 -> x1, local copies, waits for them, and re-layouts: 3.07 us -> 0.12 us  [per_device(): counts = jnp.repeat(spikes[0].astype(jnp.float32), HEAD_SIZE, axis=1)]
    concatenate x4 -> x5, other arithmetic: 3.35 us -> 0.67 us  [the longest x1 0.59 us: per_device(): jnp.concatenate([window_lengths.astype(jnp.int32), (lax.axis_index('ctx')...]
  transfers between devices with their start and end apart: 15 -> 15, of which waited for: 4 -> 8; matrix products, arithmetic and copies ran while one was open for 32% -> 6% of each run, Pallas kernels for 0% -> 26%
where the time goes in v3:
time: 85.6 us; the launch traced here: 84.9 us
  starting transfers between devices  35.8 us (42%)
  Pallas kernels  21.7 us (25%)
  waiting for transfers between devices  14.4 us (17%)
  local copies, waits for them, and re-layouts  5.74 us (7%)
  other arithmetic  5.42 us (6%)
  matrix products  0.95 us (1%)
  between operations  0.92 us (1%)
    ppermute x6, starting transfers between devices, exclusive_scan(): got = lax.ppermute(running, axis, route)  12.7 us
    ppermute x5, starting transfers between devices, all_sum(): part = part + lax.ppermute(part, axes, route)  12.6 us
    pallas_call x1, Pallas kernels, per_device(): pl.pallas_call(window_kernel, out_shape=(jax.ShapeDtypeStruct((token_rows...  11.5 us
    ppermute x4, starting transfers between devices, shifted(): return lax.ppermute(block, axis, route)  10.5 us
    pallas_call x1, Pallas kernels, per_device(): pl.pallas_call(linear_kernel, out_shape=(jax.ShapeDtypeStruct((token_rows...  10.2 us
    ppermute x5, waiting for transfers between devices, all_sum(): part = part + lax.ppermute(part, axes, route)  8.04 us
    ppermute x6, waiting for transfers between devices, exclusive_scan(): got = lax.ppermute(running, axis, route)  6.38 us
    unnamed x20, local copies, waits for them, and re-layouts  2.94 us
  transfers between devices with their start and end apart: 15, of which 8 were waited for; matrix products, arithmetic and copies ran while one was open for 6% of the time, Pallas kernels for 26%

profile of v3, /device:TPU:0, one launch (start us, length us, event | category | flops | bytes accessed | tf_op | source)
XLA Modules:
  0.0 84.9 jit_solution(12394058110939981144)
XLA Ops:
  0.6 0.7 convert_bitcast_fusion
  1.3 0.1 copy.12
  1.4 0.2 broadcast_in_dim.15
  1.6 0.6 copy-done.4
  2.3 0.0 copy-start.2
  2.3 0.8 copy-done
  3.1 0.2 convolution_bitcast_fusion.2
  3.3 0.2 convolution_bitcast_fusion.3
  3.6 2.4 %collective-permute-start = (f32[2,128,128]{2,1,0:T(8,128)S(1)}, f32[2,128,128]{2,1,0:T(8,128)S(1)}, u32[]{:S(2)}, u32[]{:S(2)}) collective-permute-start(f32[2,128,128]{2,1,0:T(8,128)S(1)} %pad_maximum_fusion.2), channel_id=1, source_target_pairs={{0,1},{1,2},{2,3},{3,4},{4,5},{5,6},{6,7},{8,9},{9,10},{10,11},{11... | collective-permute-start | bytes 393224 | tf_op jit(solution)/shard_map/ppermute | solution.py:27
  6.0 4.5 %collective-permute-start.4 = (bf16[128,512]{1,0:T(8,128)(2,1)S(1)}, bf16[128,512]{1,0:T(8,128)(2,1)S(1)}, u32[]{:S(2)}, u32[]{:S(2)}) collective-permute-start(bf16[128,512]{1,0:T(8,128)(2,1)S(1)} %pad_maximum_fusion.3), channel_id=1, source_target_pairs={{0,1},{1,2},{2,3},{3,4},{4,5},{5,6},{6,7},{8,9},{9,10},{10,11},{11... | collective-permute-start | bytes 393224 | tf_op jit(solution)/shard_map/ppermute | solution.py:52
  10.5 3.4 %collective-permute-start.3 = (bf16[128,512]{1,0:T(8,128)(2,1)S(1)}, bf16[128,512]{1,0:T(8,128)(2,1)S(1)}, u32[]{:S(2)}, u32[]{:S(2)}) collective-permute-start(bf16[128,512]{1,0:T(8,128)(2,1)S(1)} %pad_maximum_fusion.3), channel_id=1, source_target_pairs={{0,2},{1,3},{2,4},{3,5},{4,6},{5,7},{8,10},{9,11},{10,12},{11,13},... | collective-permute-start | bytes 393224 | tf_op jit(solution)/shard_map/ppermute | solution.py:52
  13.9 0.6 reshape.24.gain_ref
  14.5 0.7 copy-done.9
  15.2 0.6 pad_add_fusion.info_ref
  15.8 3.4 %collective-permute-start.1 = (f32[2,128,128]{2,1,0:T(8,128)S(1)}, f32[2,128,128]{2,1,0:T(8,128)S(1)}, u32[]{:S(2)}, u32[]{:S(2)}) collective-permute-start(f32[2,128,128]{2,1,0:T(8,128)S(1)} %fusion.17), channel_id=1, source_target_pairs={{0,2},{1,3},{2,4},{3,5},{4,6},{5,7},{8,10},{9,11},{10,12},{11,13},... | collective-permute-start | bytes 393224 | tf_op jit(solution)/shard_map/ppermute | solution.py:27
  19.2 0.8 fusion.20
  20.0 11.5 %shard_map.110 = (f32[128,1792]{1,0:T(8,128)}, f32[128,1792]{1,0:T(8,128)}, f32[384,256]{1,0:T(8,128)}, f32[384,256]{1,0:T(8,128)}) custom-call(s32[3]{0:T(128)} %pad_add_fusion.info_ref, bf16[128,1792]{1,0:T(8,128)(2,1)} %bitcast.60, bf16[128,1792]{1,0:T(8,128)(2,1)} %bitcast.62, bf16[384,256]{1,0:T(8,128)(2,1)} %get-tuple-element.30.k_ref, ...), custom_call_target="tpu_custom_call" | custom-call | tf_op jit(solution)/shard_map/pallas_call | solution.py:183
  31.5 1.1 %fusion.18 = (f32[128,256]{1,0:T(8,128)S(1)}, f32[128,256]{1,0:T(8,128)S(1)}, f32[128,256]{1,0:T(8,128)S(1)}, f32[128,256]{1,0:T(8,128)S(1)}) fusion(f32[384,256]{1,0:T(8,128)} %get-tuple-element.21, f32[384,256]{1,0:T(8,128)} %get-tuple-element.22), kind=kLoop, calls=%fused_computation.42 | loop fusion | bytes 1048576 | tf_op jit(solution)/shard_map/slice | solution.py:230
  32.7 2.9 %collective-permute-start.2 = (f32[2,128,128]{2,1,0:T(8,128)S(1)}, f32[2,128,128]{2,1,0:T(8,128)S(1)}, u32[]{:S(2)}, u32[]{:S(2)}) collective-permute-start(f32[2,128,128]{2,1,0:T(8,128)S(1)} %fusion.21), channel_id=1, source_target_pairs={{0,4},{1,5},{2,6},{3,7},{8,12},{9,13},{10,14},{11,15},{16,20},{17,... | collective-permute-start | bytes 393224 | tf_op jit(solution)/shard_map/ppermute | solution.py:27
  35.6 1.3 %collective-permute-start.8 = (f32[128,512]{1,0:T(8,128)S(1)}, f32[128,512]{1,0:T(8,128)S(1)}, u32[]{:S(2)}, u32[]{:S(2)}) collective-permute-start(f32[128,512]{1,0:T(8,128)S(1)} %pad_maximum_fusion), channel_id=1, source_target_pairs={{1,0},{2,1},{3,2},{4,3},{5,4},{6,5},{7,6},{9,8},{10,9},{11,10},{12... | collective-permute-start | bytes 786440 | tf_op jit(solution)/shard_map/ppermute | solution.py:52
  36.9 1.1 %collective-permute-done.2 = f32[2,128,128]{2,1,0:T(8,128)S(1)} collective-permute-done((f32[2,128,128]{2,1,0:T(8,128)S(1)}, f32[2,128,128]{2,1,0:T(8,128)S(1)}, u32[]{:S(2)}, u32[]{:S(2)}) %collective-permute-start.2) | collective-permute-done | bytes 131104 | tf_op jit(solution)/shard_map/ppermute | solution.py:27
  38.1 0.7 add_convert_fusion.1.prior_ref
  38.7 10.2 %shard_map.111 = (bf16[128,1792]{1,0:T(8,128)(2,1)}, bf16[128,1792]{1,0:T(8,128)(2,1)}, f32[2,128,128]{2,1,0:T(8,128)}, f32[1,1792]{1,0:T(1,128)}, f32[128,256]{1,0:T(8,128)}, /*index=5*/f32[128,256]{1,0:T(8,128)}) custom-call(bf16[128,1792]{1,0:T(8,128)(2,1)} %bitcast.61, bf16[128,1792]{1,0:T(8,128)(2,1)} %bitcast.63, bf16[128,256]{1,0:T(8,128)(2,1)} %bitcast.64, ...), custom_call_target="tpu_custom_call" | custom-call | tf_op jit(solution)/shard_map/pallas_call | solution.py:194
  48.9 1.4 %collective-permute-start.5 = (f32[2,128,128]{2,1,0:T(8,128)}, f32[2,128,128]{2,1,0:T(8,128)S(1)}, u32[]{:S(2)}, u32[]{:S(2)}) collective-permute-start(f32[2,128,128]{2,1,0:T(8,128)} %get-tuple-element.20), channel_id=1, source_target_pairs={{1,0},{2,1},{3,2},{4,3},{5,4},{6,5},{7,6},{9,8},{10,9},{11,10},{12... | collective-permute-start | bytes 393224 | tf_op jit(solution)/shard_map/ppermute | solution.py:27
  50.3 1.3 %collective-permute-start.9 = (f32[128,512]{1,0:T(8,128)S(1)}, f32[128,512]{1,0:T(8,128)S(1)}, u32[]{:S(2)}, u32[]{:S(2)}) collective-permute-start(f32[128,512]{1,0:T(8,128)S(1)} %pad_maximum_fusion.1), channel_id=1, source_target_pairs={{2,0},{3,1},{4,2},{5,3},{6,4},{7,5},{10,8},{11,9},{12,10},{13,11},... | collective-permute-start | bytes 786440 | tf_op jit(solution)/shard_map/ppermute | solution.py:52
  51.6 0.9 %collective-permute-done.5 = f32[2,128,128]{2,1,0:T(8,128)S(1)} collective-permute-done((f32[2,128,128]{2,1,0:T(8,128)}, f32[2,128,128]{2,1,0:T(8,128)S(1)}, u32[]{:S(2)}, u32[]{:S(2)}) %collective-permute-start.5) | collective-permute-done | bytes 131104 | tf_op jit(solution)/shard_map/ppermute | solution.py:27
  52.5 0.9 %add.71 = f32[2,128,128]{2,1,0:T(8,128)S(1)} add(f32[2,128,128]{2,1,0:T(8,128)} %get-tuple-element.20, f32[2,128,128]{2,1,0:T(8,128)S(1)} %collective-permute-done.5) | non-fusion elementwise | flops 32768 | bytes 393216 | tf_op jit(solution)/shard_map/add | solution.py:30
  53.4 1.3 %collective-permute-start.6 = (f32[2,128,128]{2,1,0:T(8,128)S(1)}, f32[2,128,128]{2,1,0:T(8,128)S(1)}, u32[]{:S(2)}, u32[]{:S(2)}) collective-permute-start(f32[2,128,128]{2,1,0:T(8,128)S(1)} %add.71), channel_id=1, source_target_pairs={{2,0},{3,1},{4,2},{5,3},{6,4},{7,5},{10,8},{11,9},{12,10},{13,11},... | collective-permute-start | bytes 393224 | tf_op jit(solution)/shard_map/ppermute | solution.py:27
  54.7 3.1 %collective-permute-start.10 = (f32[1792]{0:T(1024)S(1)}, f32[1792]{0:T(1024)S(1)}, u32[]{:S(2)}, u32[]{:S(2)}) collective-permute-start(f32[1792]{0:T(1024)S(1)} %reduce), channel_id=1, source_target_pairs={{0,1},{1,0},{2,3},{3,2},{4,5},{5,4},{6,7},{7,6},{8,9},{9,8},{10,11... | collective-permute-start | bytes 21512 | tf_op jit(solution)/shard_map/ppermute | solution.py:44
  57.9 0.8 collective-permute-done.10
  58.7 2.9 %collective-permute-start.11 = (f32[1792]{0:T(1024)S(1)}, f32[1792]{0:T(1024)S(1)}, u32[]{:S(2)}, u32[]{:S(2)}) collective-permute-start(f32[1792]{0:T(1024)S(1)} %add.84), channel_id=1, source_target_pairs={{0,2},{1,3},{2,0},{3,1},{4,6},{5,7},{6,4},{7,5},{8,10},{9,11},{10,... | collective-permute-start | bytes 21512 | tf_op jit(solution)/shard_map/ppermute | solution.py:44
  61.6 2.9 %collective-permute-done.11 = f32[1792]{0:T(1024)S(1)} collective-permute-done((f32[1792]{0:T(1024)S(1)}, f32[1792]{0:T(1024)S(1)}, u32[]{:S(2)}, u32[]{:S(2)}) %collective-permute-start.11) | collective-permute-done | bytes 7200 | tf_op jit(solution)/shard_map/ppermute | solution.py:44
  64.6 2.4 %collective-permute-start.12 = (f32[1792]{0:T(1024)S(1)}, f32[1792]{0:T(1024)S(1)}, u32[]{:S(2)}, u32[]{:S(2)}) collective-permute-start(f32[1792]{0:T(1024)S(1)} %add.85), channel_id=1, source_target_pairs={{0,4},{1,5},{2,6},{3,7},{4,0},{5,1},{6,2},{7,3},{8,12},{9,13},{10,... | collective-permute-start | bytes 21512 | tf_op jit(solution)/shard_map/ppermute | solution.py:44
  67.0 1.6 %collective-permute-done.12 = f32[1792]{0:T(1024)S(1)} collective-permute-done((f32[1792]{0:T(1024)S(1)}, f32[1792]{0:T(1024)S(1)}, u32[]{:S(2)}, u32[]{:S(2)}) %collective-permute-start.12) | collective-permute-done | bytes 7200 | tf_op jit(solution)/shard_map/ppermute | solution.py:44
  68.6 1.6 %collective-permute-start.13 = (f32[1792]{0:T(1024)S(1)}, f32[1792]{0:T(1024)S(1)}, u32[]{:S(2)}, u32[]{:S(2)}) collective-permute-start(f32[1792]{0:T(1024)S(1)} %add.86), channel_id=1, source_target_pairs={{0,8},{1,9},{2,10},{3,11},{4,12},{5,13},{6,14},{7,15},{8,0},{9,1},... | collective-permute-start | bytes 21512 | tf_op jit(solution)/shard_map/ppermute | solution.py:44
  70.2 2.1 %collective-permute-done.13 = f32[1792]{0:T(1024)S(1)} collective-permute-done((f32[1792]{0:T(1024)S(1)}, f32[1792]{0:T(1024)S(1)}, u32[]{:S(2)}, u32[]{:S(2)}) %collective-permute-start.13) | collective-permute-done | bytes 7200 | tf_op jit(solution)/shard_map/ppermute | solution.py:44
  72.3 2.6 %collective-permute-start.14 = (f32[1792]{0:T(1024)S(1)}, f32[1792]{0:T(1024)S(1)}, u32[]{:S(2)}, u32[]{:S(2)}) collective-permute-start(f32[1792]{0:T(1024)S(1)} %add.87), channel_id=1, source_target_pairs={{0,16},{1,17},{2,18},{3,19},{4,20},{5,21},{6,22},{7,23},{8,24},{9,... | collective-permute-start | bytes 21512 | tf_op jit(solution)/shard_map/ppermute | solution.py:44
  75.0 1.3 %collective-permute-start.7 = (f32[2,128,128]{2,1,0:T(8,128)S(1)}, f32[2,128,128]{2,1,0:T(8,128)S(1)}, u32[]{:S(2)}, u32[]{:S(2)}) collective-permute-start(f32[2,128,128]{2,1,0:T(8,128)S(1)} %add.73), channel_id=1, source_target_pairs={{4,0},{5,1},{6,2},{7,3},{12,8},{13,9},{14,10},{15,11},{20,16},{21,... | collective-permute-start | bytes 393224 | tf_op jit(solution)/shard_map/ppermute | solution.py:27
  76.3 0.6 collective-permute-done.14
  76.8 0.6 add_multiply_fusion
  77.4 4.4 %collective-permute-done.7 = f32[2,128,128]{2,1,0:T(8,128)S(1)} collective-permute-done((f32[2,128,128]{2,1,0:T(8,128)S(1)}, f32[2,128,128]{2,1,0:T(8,128)S(1)}, u32[]{:S(2)}, u32[]{:S(2)}) %collective-permute-start.7) | collective-permute-done | bytes 131104 | tf_op jit(solution)/shard_map/ppermute | solution.py:27
  81.9 0.1 slice_add_fusion.1
  82.0 0.1 slice_add_fusion.2
  82.1 0.7 copy-done.3
  82.8 0.1 copy-done.5
  83.0 0.1 slice_add_fusion.3
  83.1 0.1 slice_add_fusion.4
  83.2 1.7 %fusion.6 = (bf16[1,128,256]{2,1,0:T(8,128)(2,1)}, bf16[1,128,256]{2,1,0:T(8,128)(2,1)}) fusion(f32[128,512]{1,0:T(8,128)S(1)} %add.78, f32[384,256]{1,0:T(8,128)} %get-tuple-element.22, f32[16,8,2,128]{3,2,1,0:T(2,128)S(1)} %bitcast.72, f32[128,128]{1,0:T(8,128)S(1)} %slice_add_fusion.1, f32[128,128]{1,0:T(8,128)S(1)} %slice_add_fusion.2, ...), kind=kLoop, calls=%fused_computation.25 | loop fusion | flops 294912 | bytes 1048576 | tf_op jit(solution)/shard_map/broadcast_in_dim | solution.py:246
  (37 shorter events, 0.3 us)
Async XLA Ops:
  1.4 0.8 copy-start.4
  2.3 0.8 copy-start
  2.3 1.0 %copy-start.2 = (bf16[128,256]{1,0:T(8,128)(2,1)}, bf16[128,256]{1,0:T(8,128)(2,1)S(1)}, u32[]{:S(2)}) copy-start(bf16[128,256]{1,0:T(8,128)(2,1)S(1)} %fusion.s_ref) | copy-start | bytes 196612
  3.6 12.2 %collective-permute-start = (f32[2,128,128]{2,1,0:T(8,128)S(1)}, f32[2,128,128]{2,1,0:T(8,128)S(1)}, u32[]{:S(2)}, u32[]{:S(2)}) collective-permute-start(f32[2,128,128]{2,1,0:T(8,128)S(1)} %pad_maximum_fusion.2), channel_id=1, source_target_pairs={{0,1},{1,2},{2,3},{3,4},{4,5},{5,6},{6,7},{8,9},{9,10},{10,11},{11... | collective-permute-start | bytes 393224 | tf_op jit(solution)/shard_map/ppermute | solution.py:27
  5.9 8.0 %copy-start.7 = (f32[1792]{0:T(1024)S(1)}, f32[1792]{0:T(1024)}, u32[]{:S(2)}) copy-start(f32[1792]{0:T(1024)} %param.12) | copy-start | bytes 21508
  6.0 13.2 %collective-permute-start.4 = (bf16[128,512]{1,0:T(8,128)(2,1)S(1)}, bf16[128,512]{1,0:T(8,128)(2,1)S(1)}, u32[]{:S(2)}, u32[]{:S(2)}) collective-permute-start(bf16[128,512]{1,0:T(8,128)(2,1)S(1)} %pad_maximum_fusion.3), channel_id=1, source_target_pairs={{0,1},{1,2},{2,3},{3,4},{4,5},{5,6},{6,7},{8,9},{9,10},{10,11},{11... | collective-permute-start | bytes 393224 | tf_op jit(solution)/shard_map/ppermute | solution.py:52
  10.5 8.7 %collective-permute-start.3 = (bf16[128,512]{1,0:T(8,128)(2,1)S(1)}, bf16[128,512]{1,0:T(8,128)(2,1)S(1)}, u32[]{:S(2)}, u32[]{:S(2)}) collective-permute-start(bf16[128,512]{1,0:T(8,128)(2,1)S(1)} %pad_maximum_fusion.3), channel_id=1, source_target_pairs={{0,2},{1,3},{2,4},{3,5},{4,6},{5,7},{8,10},{9,11},{10,12},{11,13},... | collective-permute-start | bytes 393224 | tf_op jit(solution)/shard_map/ppermute | solution.py:52
  14.5 0.7 copy-start.9
  15.8 16.8 %collective-permute-start.1 = (f32[2,128,128]{2,1,0:T(8,128)S(1)}, f32[2,128,128]{2,1,0:T(8,128)S(1)}, u32[]{:S(2)}, u32[]{:S(2)}) collective-permute-start(f32[2,128,128]{2,1,0:T(8,128)S(1)} %fusion.17), channel_id=1, source_target_pairs={{0,2},{1,3},{2,4},{3,5},{4,6},{5,7},{8,10},{9,11},{10,12},{11,13},... | collective-permute-start | bytes 393224 | tf_op jit(solution)/shard_map/ppermute | solution.py:27
  32.7 5.4 %collective-permute-start.2 = (f32[2,128,128]{2,1,0:T(8,128)S(1)}, f32[2,128,128]{2,1,0:T(8,128)S(1)}, u32[]{:S(2)}, u32[]{:S(2)}) collective-permute-start(f32[2,128,128]{2,1,0:T(8,128)S(1)} %fusion.21), channel_id=1, source_target_pairs={{0,4},{1,5},{2,6},{3,7},{8,12},{9,13},{10,14},{11,15},{16,20},{17,... | collective-permute-start | bytes 393224 | tf_op jit(solution)/shard_map/ppermute | solution.py:27
  35.6 39.3 %collective-permute-start.8 = (f32[128,512]{1,0:T(8,128)S(1)}, f32[128,512]{1,0:T(8,128)S(1)}, u32[]{:S(2)}, u32[]{:S(2)}) collective-permute-start(f32[128,512]{1,0:T(8,128)S(1)} %pad_maximum_fusion), channel_id=1, source_target_pairs={{1,0},{2,1},{3,2},{4,3},{5,4},{6,5},{7,6},{9,8},{10,9},{11,10},{12... | collective-permute-start | bytes 786440 | tf_op jit(solution)/shard_map/ppermute | solution.py:52
  48.9 5.8 %copy-start.8 = (f32[1,1792]{1,0:T(1,128)S(1)}, f32[1,1792]{1,0:T(1,128)}, u32[]{:S(2)}) copy-start(f32[1,1792]{1,0:T(1,128)} %get-tuple-element.24) | copy-start | bytes 21508
  48.9 3.6 %collective-permute-start.5 = (f32[2,128,128]{2,1,0:T(8,128)}, f32[2,128,128]{2,1,0:T(8,128)S(1)}, u32[]{:S(2)}, u32[]{:S(2)}) collective-permute-start(f32[2,128,128]{2,1,0:T(8,128)} %get-tuple-element.20), channel_id=1, source_target_pairs={{1,0},{2,1},{3,2},{4,3},{5,4},{6,5},{7,6},{9,8},{10,9},{11,10},{12... | collective-permute-start | bytes 393224 | tf_op jit(solution)/shard_map/ppermute | solution.py:27
  50.3 24.5 %collective-permute-start.9 = (f32[128,512]{1,0:T(8,128)S(1)}, f32[128,512]{1,0:T(8,128)S(1)}, u32[]{:S(2)}, u32[]{:S(2)}) collective-permute-start(f32[128,512]{1,0:T(8,128)S(1)} %pad_maximum_fusion.1), channel_id=1, source_target_pairs={{2,0},{3,1},{4,2},{5,3},{6,4},{7,5},{10,8},{11,9},{12,10},{13,11},... | collective-permute-start | bytes 786440 | tf_op jit(solution)/shard_map/ppermute | solution.py:52
  53.4 21.5 %collective-permute-start.6 = (f32[2,128,128]{2,1,0:T(8,128)S(1)}, f32[2,128,128]{2,1,0:T(8,128)S(1)}, u32[]{:S(2)}, u32[]{:S(2)}) collective-permute-start(f32[2,128,128]{2,1,0:T(8,128)S(1)} %add.71), channel_id=1, source_target_pairs={{2,0},{3,1},{4,2},{5,3},{6,4},{7,5},{10,8},{11,9},{12,10},{13,11},... | collective-permute-start | bytes 393224 | tf_op jit(solution)/shard_map/ppermute | solution.py:27
  54.7 3.9 %collective-permute-start.10 = (f32[1792]{0:T(1024)S(1)}, f32[1792]{0:T(1024)S(1)}, u32[]{:S(2)}, u32[]{:S(2)}) collective-permute-start(f32[1792]{0:T(1024)S(1)} %reduce), channel_id=1, source_target_pairs={{0,1},{1,0},{2,3},{3,2},{4,5},{5,4},{6,7},{7,6},{8,9},{9,8},{10,11... | collective-permute-start | bytes 21512 | tf_op jit(solution)/shard_map/ppermute | solution.py:44
  58.7 5.9 %collective-permute-start.11 = (f32[1792]{0:T(1024)S(1)}, f32[1792]{0:T(1024)S(1)}, u32[]{:S(2)}, u32[]{:S(2)}) collective-permute-start(f32[1792]{0:T(1024)S(1)} %add.84), channel_id=1, source_target_pairs={{0,2},{1,3},{2,0},{3,1},{4,6},{5,7},{6,4},{7,5},{8,10},{9,11},{10,... | collective-permute-start | bytes 21512 | tf_op jit(solution)/shard_map/ppermute | solution.py:44
  64.6 4.1 %collective-permute-start.12 = (f32[1792]{0:T(1024)S(1)}, f32[1792]{0:T(1024)S(1)}, u32[]{:S(2)}, u32[]{:S(2)}) collective-permute-start(f32[1792]{0:T(1024)S(1)} %add.85), channel_id=1, source_target_pairs={{0,4},{1,5},{2,6},{3,7},{4,0},{5,1},{6,2},{7,3},{8,12},{9,13},{10,... | collective-permute-start | bytes 21512 | tf_op jit(solution)/shard_map/ppermute | solution.py:44
  68.6 3.7 %collective-permute-start.13 = (f32[1792]{0:T(1024)S(1)}, f32[1792]{0:T(1024)S(1)}, u32[]{:S(2)}, u32[]{:S(2)}) collective-permute-start(f32[1792]{0:T(1024)S(1)} %add.86), channel_id=1, source_target_pairs={{0,8},{1,9},{2,10},{3,11},{4,12},{5,13},{6,14},{7,15},{8,0},{9,1},... | collective-permute-start | bytes 21512 | tf_op jit(solution)/shard_map/ppermute | solution.py:44
  72.3 4.5 %collective-permute-start.14 = (f32[1792]{0:T(1024)S(1)}, f32[1792]{0:T(1024)S(1)}, u32[]{:S(2)}, u32[]{:S(2)}) collective-permute-start(f32[1792]{0:T(1024)S(1)} %add.87), channel_id=1, source_target_pairs={{0,16},{1,17},{2,18},{3,19},{4,20},{5,21},{6,22},{7,23},{8,24},{9,... | collective-permute-start | bytes 21512 | tf_op jit(solution)/shard_map/ppermute | solution.py:44
  75.0 6.9 %collective-permute-start.7 = (f32[2,128,128]{2,1,0:T(8,128)S(1)}, f32[2,128,128]{2,1,0:T(8,128)S(1)}, u32[]{:S(2)}, u32[]{:S(2)}) collective-permute-start(f32[2,128,128]{2,1,0:T(8,128)S(1)} %add.73), channel_id=1, source_target_pairs={{4,0},{5,1},{6,2},{7,3},{12,8},{13,9},{14,10},{15,11},{20,16},{21,... | collective-permute-start | bytes 393224 | tf_op jit(solution)/shard_map/ppermute | solution.py:27
  77.4 4.4 %copy-start.1 = (bf16[1,128,256]{2,1,0:T(8,128)(2,1)S(1)}, bf16[1,128,256]{2,1,0:T(8,128)(2,1)}, u32[]{:S(2)}) copy-start(bf16[1,128,256]{2,1,0:T(8,128)(2,1)} %param.8) | copy-start | bytes 196612
  77.4 4.4 %copy-start.6 = (f32[128,256]{1,0:T(8,128)S(1)}, f32[128,256]{1,0:T(8,128)}, u32[]{:S(2)}) copy-start(f32[128,256]{1,0:T(8,128)} %get-tuple-element.23) | copy-start | bytes 393220
  82.0 0.8 copy-start.3
  82.0 0.9 %copy-start.5 = (f32[128,256]{1,0:T(8,128)S(1)}, f32[128,256]{1,0:T(8,128)}, u32[]{:S(2)}) copy-start(f32[128,256]{1,0:T(8,128)} %get-tuple-element.19) | copy-start | bytes 393220

commit v4 on v3

--- a/solution.py
+++ b/solution.py
@@ -14,24 +14,33 @@
 epsilon = 1e-05
 
 
-def exclusive_scan(part, axis, reverse):
+def exclusive_scan(part, axis, reverse, riders):
     count = lax.axis_size(axis)
+    width = part.shape[1]
     running = part
-    total = None
+    total = jnp.zeros_like(part)
+    received = {}
     distance = 1
     while distance < count:
         if reverse:
             route = [(i + distance, i) for i in range(count - distance)]
         else:
             route = [(i, i + distance) for i in range(count - distance)]
-        got = lax.ppermute(running, axis, route)
-        total = got if total is None else total + got
+        payload = running
+        if distance in riders:
+            payload = jnp.concatenate([running, riders[distance]], axis=1)
+        got = lax.ppermute(payload, axis, route)
+        if distance in riders:
+            received[distance] = got[:, width:]
+            got = got[:, :width]
+        total = total + got
         if distance * 2 < count:
             running = running + got
         distance *= 2
-    if total is None:
-        total = jnp.zeros_like(part)
-    return total
+    for distance, rider in riders.items():
+        if distance not in received:
+            received[distance] = shifted(rider, axis, -distance if reverse else distance)
+    return total, received
 
 
 def all_sum(part, axes):
@@ -102,7 +111,7 @@
         lanes = slice(g * HEAD_SIZE, (g + 1) * HEAD_SIZE)
         kg = k_ref[:, lanes]
         sg = s_ref[:, lanes]
-        pg = prior_ref[g]
+        pg = prior_ref[:, lanes]
         suffix = jnp.zeros((HEAD_SIZE, HEAD_SIZE), jnp.float32)
         ldk = jnp.zeros((token_rows, HEAD_SIZE), jnp.float32)
         dsp = jnp.zeros((token_rows, HEAD_SIZE), jnp.float32)
@@ -138,7 +147,7 @@
             dq_ref[:, cols] = (ldq + wdq_ref[:, cols]).astype(dq_ref.dtype)
             ldk = ldk + lax.dot_general(bh, qh, (((0,), (0,)), ((), ())), preferred_element_type=jnp.float32)
             dsp = dsp + lax.dot_general(lh, dl, (((0,), (0,)), ((), ())), preferred_element_type=jnp.float32)
-        suffix_ref[g] = suffix
+        suffix_ref[:, lanes] = suffix
         ldk_ref[:, lanes] = ldk
         dsp_ref[:, lanes] = dsp
 
@@ -160,7 +169,7 @@
     v = values[0]
     counts = jnp.repeat(spikes[0].astype(jnp.float32), HEAD_SIZE, axis=1)
     spiked = (v.astype(jnp.float32) * counts).astype(jnp.bfloat16)
-    local_state = jnp.stack(
+    local_state = jnp.concatenate(
         [
             lax.dot_general(
                 k[:, g * HEAD_SIZE : (g + 1) * HEAD_SIZE],
@@ -169,14 +178,17 @@
                 preferred_element_type=jnp.float32,
             )
             for g in range(KEY_VALUE_HEADS)
-        ]
-    )
-    prior_half = exclusive_scan(local_state, "ctx", False).astype(jnp.bfloat16)
-    packed = jnp.concatenate([k, v], axis=1)
-    earlier = []
-    for distance in range(reach, 0, -1):
-        earlier.append(shifted(packed, "ctx", distance))
-    window_packed = jnp.concatenate(earlier + [packed], axis=0)
+        ],
+        axis=1,
+    )
+    packed = jnp.concatenate([k, v], axis=1).astype(jnp.float32)
+    prior, halo = exclusive_scan(
+        local_state, "ctx", False, {distance: packed for distance in range(1, reach + 1)}
+    )
+    prior_half = prior.astype(jnp.bfloat16)
+    window_packed = jnp.concatenate(
+        [halo[distance] for distance in range(reach, 0, -1)] + [packed], axis=0
+    ).astype(jnp.bfloat16)
     info = jnp.concatenate(
         [window_lengths.astype(jnp.int32), (lax.axis_index("ctx") * token_rows - padding_rows).reshape(1)]
     ).astype(jnp.int32)
@@ -196,7 +208,7 @@
         out_shape=(
             jax.ShapeDtypeStruct((token_rows, width), jnp.bfloat16),
             jax.ShapeDtypeStruct((token_rows, width), jnp.bfloat16),
-            jax.ShapeDtypeStruct((KEY_VALUE_HEADS, HEAD_SIZE, HEAD_SIZE), jnp.float32),
+            jax.ShapeDtypeStruct((HEAD_SIZE, key_value_width), jnp.float32),
             jax.ShapeDtypeStruct((1, width), jnp.float32),
             jax.ShapeDtypeStruct((token_rows, key_value_width), jnp.float32),
             jax.ShapeDtypeStruct((token_rows, key_value_width), jnp.float32),
@@ -205,8 +217,28 @@
         out_specs=tuple(in_vmem(6)),
     )(q, c, k, spiked, prior_half, gain.reshape(1, width), wout, wdq)
     total_tokens = queries.shape[0] * lax.axis_size("dp") * token_rows * lax.axis_size("ctx")
-    d_gain = all_sum(gain_local.reshape(width), ("dp", "ctx")) * (total_tokens ** (-0.5))
-    later_half = exclusive_scan(suffix_local, "ctx", True).astype(jnp.bfloat16)
+    gain_rows = width // HEAD_SIZE
+    gain_block = jnp.concatenate(
+        [
+            gain_local.reshape(gain_rows, HEAD_SIZE),
+            jnp.zeros((key_value_width - gain_rows, HEAD_SIZE), jnp.float32),
+        ],
+        axis=0,
+    )
+    gains = lax.all_gather(gain_block, "ctx")[:, :gain_rows]
+    d_gain = all_sum(jnp.sum(gains, axis=0).reshape(width), ("dp",)) * (total_tokens ** (-0.5))
+    sent = {}
+    for distance in range(1, reach + 1):
+        start_row = (reach - distance) * token_rows
+        sent[distance] = jnp.concatenate(
+            [
+                dk_win[start_row : start_row + token_rows],
+                dv_win[start_row : start_row + token_rows],
+            ],
+            axis=1,
+        )
+    later, back = exclusive_scan(suffix_local, "ctx", True, sent)
+    later_half = later.astype(jnp.bfloat16)
     ldk_parts = []
     dsp_parts = []
     for g in range(KEY_VALUE_HEADS):
@@ -214,25 +246,17 @@
         ldk_parts.append(
             ldk[:, lanes]
             + lax.dot_general(
-                spiked[:, lanes], later_half[g], (((1,), (1,)), ((), ())), preferred_element_type=jnp.float32
+                spiked[:, lanes], later_half[:, lanes], (((1,), (1,)), ((), ())), preferred_element_type=jnp.float32
             )
         )
         dsp_parts.append(
-            dsp[:, lanes] + jnp.dot(k[:, lanes], later_half[g], preferred_element_type=jnp.float32)
+            dsp[:, lanes] + jnp.dot(k[:, lanes], later_half[:, lanes], preferred_element_type=jnp.float32)
         )
     linear_key_gradient = jnp.concatenate(ldk_parts, axis=1)
     linear_value_gradient = jnp.concatenate(dsp_parts, axis=1) * counts
-    received = jnp.zeros((token_rows, 2 * key_value_width), jnp.float32)
-    for distance in range(1, reach + 1):
-        start_row = (reach - distance) * token_rows
-        sent = jnp.concatenate(
-            [
-                dk_win[start_row : start_row + token_rows],
-                dv_win[start_row : start_row + token_rows],
-            ],
-            axis=1,
-        )
-        received = received + shifted(sent, "ctx", -distance)
+    received = back[1]
+    for distance in range(2, reach + 1):
+        received = received + back[distance]
     keys_gradient = (
         linear_key_gradient + dk_win[padding_rows:] + received[:, :key_value_width]
     ).astype(jnp.bfloat16)

time: 85.6 us -> 113 us (1.32)
  waiting for transfers between devices: 14.4 us -> 37.3 us
  between operations: 0.92 us -> 14.3 us
  starting transfers between devices: 35.8 us -> 25.8 us
    ppermute x10 -> x6, waiting for transfers between devices: 6.39 us -> 28.9 us  [exclusive_scan(): got = lax.ppermute(payload, axis, route)]
    ppermute x5 -> x2, starting transfers between devices: 12.6 us -> 3.89 us  [all_sum(): part = part + lax.ppermute(part, axes, route)]
    all_gather x0 -> x1, waiting for transfers between devices: none -> 5.82 us  [per_device(): gains = lax.all_gather(gain_block, 'ctx')[:, :gain_rows]]
    ppermute x5 -> x2, waiting for transfers between devices: 8.04 us -> 2.5 us  [all_sum(): part = part + lax.ppermute(part, axes, route)]
    ppermute x10 -> x6, starting transfers between devices: 23.2 us -> 21.8 us  [exclusive_scan(): got = lax.ppermute(payload, axis, route)]
    unnamed x20 -> x22, local copies, waits for them, and re-layouts: 2.94 us -> 2.94 us
  transfers between devices with their start and end apart: 15 -> 9, of which waited for: 8 -> 8; matrix products, arithmetic and copies ran while one was open for 6% -> 5% of each run, Pallas kernels for 26% -> 10%
where the time goes in v4:
time: 113 us
  waiting for transfers between devices  37.3 us (33%)
  starting transfers between devices  25.8 us (23%)
  Pallas kernels  21.7 us (19%)
  between operations  14.3 us (13%)
  local copies, waits for them, and re-layouts  6.44 us (6%)
  other arithmetic  6.28 us (6%)
    ppermute x6, waiting for transfers between devices, exclusive_scan(): got = lax.ppermute(payload, axis, route)  28.9 us
    ppermute x6, starting transfers between devices, exclusive_scan(): got = lax.ppermute(payload, axis, route)  21.8 us
    pallas_call x1, Pallas kernels, per_device(): pl.pallas_call(window_kernel, out_shape=(jax.ShapeDtypeStruct((token_rows...  11.5 us
    pallas_call x1, Pallas kernels, per_device(): pl.pallas_call(linear_kernel, out_shape=(jax.ShapeDtypeStruct((token_rows...  10.2 us
    all_gather x1, waiting for transfers between devices, per_device(): gains = lax.all_gather(gain_block, 'ctx')[:, :gain_rows]  5.82 us
    ppermute x2, starting transfers between devices, all_sum(): part = part + lax.ppermute(part, axes, route)  3.89 us
    unnamed x22, local copies, waits for them, and re-layouts  2.94 us
    ppermute x2, waiting for transfers between devices, all_sum(): part = part + lax.ppermute(part, axes, route)  2.5 us
  transfers between devices with their start and end apart: 9, of which 8 were waited for; matrix products, arithmetic and copies ran while one was open for 5% of the time, Pallas kernels for 10%

profile of v4, /device:TPU:0, one launch (start us, length us, event | category | flops | bytes accessed | tf_op | source)
XLA Modules:
  0.0 112.7 jit_solution(13254214576331890099)
XLA Ops:
  7.2 0.0 all-gather.3.cloned.1.call-start
  7.2 0.7 convert_bitcast_fusion
  7.9 0.1 copy.12
  8.0 0.2 broadcast_in_dim.16
  8.2 0.6 copy-done.4
  8.9 0.0 copy-start.2
  8.9 0.8 copy-done
  9.7 0.2 convolution_bitcast_fusion.2
  9.9 0.2 convolution_bitcast_fusion.3
  10.2 2.4 %collective-permute-start = (f32[128,768]{1,0:T(8,128)S(1)}, f32[128,768]{1,0:T(8,128)S(1)}, u32[]{:S(2)}, u32[]{:S(2)}) collective-permute-start(f32[128,768]{1,0:T(8,128)S(1)} %pad_maximum_fusion.1), channel_id=1, source_target_pairs={{0,1},{1,2},{2,3},{3,4},{4,5},{5,6},{6,7},{8,9},{9,10},{10,11},{11... | collective-permute-start | bytes 1179656 | tf_op jit(solution)/shard_map/ppermute | solution.py:32
  12.6 1.3 %collective-permute-done = f32[128,768]{1,0:T(8,128)S(1)} collective-permute-done((f32[128,768]{1,0:T(8,128)S(1)}, f32[128,768]{1,0:T(8,128)S(1)}, u32[]{:S(2)}, u32[]{:S(2)}) %collective-permute-start) | collective-permute-done | bytes 393248 | tf_op jit(solution)/shard_map/ppermute | solution.py:32
  13.9 0.0 copy-start.8
  13.9 10.3 %collective-permute-start.1 = (f32[128,768]{1,0:T(8,128)S(1)}, f32[128,768]{1,0:T(8,128)S(1)}, u32[]{:S(2)}, u32[]{:S(2)}) collective-permute-start(f32[128,768]{1,0:T(8,128)S(1)} %pad_maximum_fusion), channel_id=1, source_target_pairs={{0,2},{1,3},{2,4},{3,5},{4,6},{5,7},{8,10},{9,11},{10,12},{11,13},... | collective-permute-start | bytes 1179656 | tf_op jit(solution)/shard_map/ppermute | solution.py:32
  24.2 0.6 reshape.27.gain_ref
  24.8 0.7 copy-done.10
  25.5 0.6 pad_add_fusion.info_ref
  26.1 5.8 %collective-permute-done.1 = f32[128,768]{1,0:T(8,128)S(1)} collective-permute-done((f32[128,768]{1,0:T(8,128)S(1)}, f32[128,768]{1,0:T(8,128)S(1)}, u32[]{:S(2)}, u32[]{:S(2)}) %collective-permute-start.1) | collective-permute-done | bytes 393248 | tf_op jit(solution)/shard_map/ppermute | solution.py:32
  31.9 0.8 fusion.31
  32.7 5.3 %collective-permute-start.2 = (f32[128,256]{1,0:T(8,128)S(1)}, f32[128,256]{1,0:T(8,128)S(1)}, u32[]{:S(2)}, u32[]{:S(2)}) collective-permute-start(f32[128,256]{1,0:T(8,128)S(1)} %slice_add_fusion.4), channel_id=1, source_target_pairs={{0,4},{1,5},{2,6},{3,7},{8,12},{9,13},{10,14},{11,15},{16,20},{17,... | collective-permute-start | bytes 393224 | tf_op jit(solution)/shard_map/ppermute | solution.py:32
  38.0 11.5 %shard_map.110 = (f32[128,1792]{1,0:T(8,128)}, f32[128,1792]{1,0:T(8,128)}, f32[384,256]{1,0:T(8,128)}, f32[384,256]{1,0:T(8,128)}) custom-call(s32[3]{0:T(128)} %pad_add_fusion.info_ref, bf16[128,1792]{1,0:T(8,128)(2,1)} %bitcast.44, bf16[128,1792]{1,0:T(8,128)(2,1)} %bitcast.46, bf16[384,256]{1,0:T(8,128)(2,1)} %get-tuple-element.30.k_ref, ...), custom_call_target="tpu_custom_call" | custom-call | tf_op jit(solution)/shard_map/pallas_call | solution.py:195
  49.5 1.1 %fusion.29 = (f32[128,256]{1,0:T(8,128)S(1)}, f32[128,256]{1,0:T(8,128)S(1)}, f32[128,256]{1,0:T(8,128)S(1)}, f32[128,256]{1,0:T(8,128)S(1)}) fusion(f32[384,256]{1,0:T(8,128)} %get-tuple-element.21, f32[384,256]{1,0:T(8,128)} %get-tuple-element.22), kind=kLoop, calls=%fused_computation.53 | loop fusion | bytes 1048576 | tf_op jit(solution)/shard_map/slice | solution.py:235
  50.6 0.7 add_convert_fusion.1.prior_ref
  51.3 10.2 %shard_map.111 = (bf16[128,1792]{1,0:T(8,128)(2,1)}, bf16[128,1792]{1,0:T(8,128)(2,1)}, f32[128,256]{1,0:T(8,128)}, f32[1,1792]{1,0:T(1,128)}, f32[128,256]{1,0:T(8,128)}, /*index=5*/f32[128,256]{1,0:T(8,128)}) custom-call(bf16[128,1792]{1,0:T(8,128)(2,1)} %bitcast.45, bf16[128,1792]{1,0:T(8,128)(2,1)} %bitcast.47, bf16[128,256]{1,0:T(8,128)(2,1)} %bitcast.48, ...), custom_call_target="tpu_custom_call" | custom-call | tf_op jit(solution)/shard_map/pallas_call | solution.py:206
  61.5 0.9 pad_maximum_fusion.2
  62.4 1.3 %collective-permute-start.3 = (f32[128,768]{1,0:T(8,128)S(1)}, f32[128,768]{1,0:T(8,128)S(1)}, u32[]{:S(2)}, u32[]{:S(2)}) collective-permute-start(f32[128,768]{1,0:T(8,128)S(1)} %pad_maximum_fusion.2), channel_id=1, source_target_pairs={{1,0},{2,1},{3,2},{4,3},{5,4},{6,5},{7,6},{9,8},{10,9},{11,10},{12... | collective-permute-start | bytes 1179656 | tf_op jit(solution)/shard_map/ppermute | solution.py:32
  63.8 0.7 concatenate.45
  64.4 0.0 all-gather.3.cloned.1.call-update
  64.5 1.6 %collective-permute-done.3 = f32[128,768]{1,0:T(8,128)S(1)} collective-permute-done((f32[128,768]{1,0:T(8,128)S(1)}, f32[128,768]{1,0:T(8,128)S(1)}, u32[]{:S(2)}, u32[]{:S(2)}) %collective-permute-start.3) | collective-permute-done | bytes 393248 | tf_op jit(solution)/shard_map/ppermute | solution.py:32
  66.1 1.3 %collective-permute-start.4 = (f32[128,768]{1,0:T(8,128)S(1)}, f32[128,768]{1,0:T(8,128)S(1)}, u32[]{:S(2)}, u32[]{:S(2)}) collective-permute-start(f32[128,768]{1,0:T(8,128)S(1)} %pad_maximum_fusion.3), channel_id=1, source_target_pairs={{2,0},{3,1},{4,2},{5,3},{6,4},{7,5},{10,8},{11,9},{12,10},{13,11},... | collective-permute-start | bytes 1179656 | tf_op jit(solution)/shard_map/ppermute | solution.py:32
  67.4 13.6 %collective-permute-done.4 = f32[128,768]{1,0:T(8,128)S(1)} collective-permute-done((f32[128,768]{1,0:T(8,128)S(1)}, f32[128,768]{1,0:T(8,128)S(1)}, u32[]{:S(2)}, u32[]{:S(2)}) %collective-permute-start.4) | collective-permute-done | bytes 393248 | tf_op jit(solution)/shard_map/ppermute | solution.py:32
  81.0 1.3 %collective-permute-start.5 = (f32[128,256]{1,0:T(8,128)S(1)}, f32[128,256]{1,0:T(8,128)S(1)}, u32[]{:S(2)}, u32[]{:S(2)}) collective-permute-start(f32[128,256]{1,0:T(8,128)S(1)} %slice_add_fusion.2), channel_id=1, source_target_pairs={{4,0},{5,1},{6,2},{7,3},{12,8},{13,9},{14,10},{15,11},{20,16},{21,... | collective-permute-start | bytes 393224 | tf_op jit(solution)/shard_map/ppermute | solution.py:32
  82.4 0.0 copy-start.1
  82.4 6.7 %collective-permute-done.5 = f32[128,256]{1,0:T(8,128)S(1)} collective-permute-done((f32[128,256]{1,0:T(8,128)S(1)}, f32[128,256]{1,0:T(8,128)S(1)}, u32[]{:S(2)}, u32[]{:S(2)}) %collective-permute-start.5) | collective-permute-done | bytes 131104 | tf_op jit(solution)/shard_map/ppermute | solution.py:32
  89.1 0.1 slice_add_fusion.6
  89.3 0.0 copy-start.6
  89.3 0.1 slice_add_fusion.5
  89.4 0.7 copy-done.3
  90.1 0.1 copy-done.6
  90.2 0.1 slice_add_fusion.7
  90.3 5.8 %all-gather.3.cloned.1.call-done = f32[2048,128]{1,0:T(8,128)} async-done(((f32[256,128]{1,0:T(8,128)}), f32[2048,128]{1,0:T(8,128)}) %all-gather.3.cloned.1.call-update) | async-done | bytes 1048592 | tf_op jit(solution)/shard_map/all_gather | solution.py:228
  96.2 0.9 slice_reduce_fusion
  97.0 1.5 %collective-permute-start.6 = (f32[1792]{0:T(1024)S(1)}, f32[1792]{0:T(1024)S(1)}, u32[]{:S(2)}, u32[]{:S(2)}) collective-permute-start(f32[1792]{0:T(1024)S(1)} %bitcast.59), channel_id=1, source_target_pairs={{0,8},{8,0},{16,24},{24,16},{1,9},{9,1},{17,25},{25,17},{2,10},{10... | collective-permute-start | bytes 21512 | tf_op jit(solution)/shard_map/ppermute | solution.py:53
  98.5 0.1 slice_add_fusion.8
  98.6 2.0 %collective-permute-done.6 = f32[1792]{0:T(1024)S(1)} collective-permute-done((f32[1792]{0:T(1024)S(1)}, f32[1792]{0:T(1024)S(1)}, u32[]{:S(2)}, u32[]{:S(2)}) %collective-permute-start.6) | collective-permute-done | bytes 7200 | tf_op jit(solution)/shard_map/ppermute | solution.py:53
  100.7 2.4 %collective-permute-start.7 = (f32[1792]{0:T(1024)S(1)}, f32[1792]{0:T(1024)S(1)}, u32[]{:S(2)}, u32[]{:S(2)}) collective-permute-start(f32[1792]{0:T(1024)S(1)} %bitcast_add_fusion), channel_id=1, source_target_pairs={{0,16},{8,24},{16,0},{24,8},{1,17},{9,25},{17,1},{25,9},{2,18},{10... | collective-permute-start | bytes 21512 | tf_op jit(solution)/shard_map/ppermute | solution.py:53
  103.1 1.7 %fusion.6 = (bf16[1,128,256]{2,1,0:T(8,128)(2,1)}, bf16[1,128,256]{2,1,0:T(8,128)(2,1)}) fusion(f32[128,512]{1,0:T(8,128)S(1)} %slice_add_fusion, f32[384,256]{1,0:T(8,128)} %get-tuple-element.22, f32[16,8,2,128]{3,2,1,0:T(2,128)S(1)} %bitcast.56, f32[128,128]{1,0:T(8,128)S(1)} %slice_add_fusion.5, f32[128,128]{1,0:T(8,128)S(1)} %slice_add_fusion.6, ...), kind=kLoop, calls=%fused_computation.34 | loop fusion | flops 294912 | bytes 1048576 | tf_op jit(solution)/shard_map/broadcast_in_dim | solution.py:270
  104.7 0.5 collective-permute-done.7
  105.2 0.6 add_multiply_fusion
  (30 shorter events, 0.4 us)
Async XLA Ops:
  7.2 89.0 %all-gather.3.cloned.1.call-start = ((), (), s32[]{:S(2)}) async-start(), calls=%async_computation | async-start | bytes 1179648 | tf_op jit(solution)/shard_map/all_gather | solution.py:228
  8.0 0.8 copy-start.4
  8.8 0.8 copy-start
  8.9 1.0 copy-start.2
  10.2 3.7 %collective-permute-start = (f32[128,768]{1,0:T(8,128)S(1)}, f32[128,768]{1,0:T(8,128)S(1)}, u32[]{:S(2)}, u32[]{:S(2)}) collective-permute-start(f32[128,768]{1,0:T(8,128)S(1)} %pad_maximum_fusion.1), channel_id=1, source_target_pairs={{0,1},{1,2},{2,3},{3,4},{4,5},{5,6},{6,7},{8,9},{9,10},{10,11},{11... | collective-permute-start | bytes 1179656 | tf_op jit(solution)/shard_map/ppermute | solution.py:32
  13.9 10.3 %copy-start.8 = (f32[1792]{0:T(1024)S(1)}, f32[1792]{0:T(1024)}, u32[]{:S(2)}) copy-start(f32[1792]{0:T(1024)} %param.12) | copy-start | bytes 21508
  13.9 17.9 %collective-permute-start.1 = (f32[128,768]{1,0:T(8,128)S(1)}, f32[128,768]{1,0:T(8,128)S(1)}, u32[]{:S(2)}, u32[]{:S(2)}) collective-permute-start(f32[128,768]{1,0:T(8,128)S(1)} %pad_maximum_fusion), channel_id=1, source_target_pairs={{0,2},{1,3},{2,4},{3,5},{4,6},{5,7},{8,10},{9,11},{10,12},{11,13},... | collective-permute-start | bytes 1179656 | tf_op jit(solution)/shard_map/ppermute | solution.py:32
  24.8 0.7 copy-start.10
  32.7 17.9 %collective-permute-start.2 = (f32[128,256]{1,0:T(8,128)S(1)}, f32[128,256]{1,0:T(8,128)S(1)}, u32[]{:S(2)}, u32[]{:S(2)}) collective-permute-start(f32[128,256]{1,0:T(8,128)S(1)} %slice_add_fusion.4), channel_id=1, source_target_pairs={{0,4},{1,5},{2,6},{3,7},{8,12},{9,13},{10,14},{11,15},{16,20},{17,... | collective-permute-start | bytes 393224 | tf_op jit(solution)/shard_map/ppermute | solution.py:32
  61.5 2.3 %copy-start.9 = (f32[1,1792]{1,0:T(1,128)S(1)}, f32[1,1792]{1,0:T(1,128)}, u32[]{:S(2)}) copy-start(f32[1,1792]{1,0:T(1,128)} %get-tuple-element.24) | copy-start | bytes 21508
  62.4 3.6 %collective-permute-start.3 = (f32[128,768]{1,0:T(8,128)S(1)}, f32[128,768]{1,0:T(8,128)S(1)}, u32[]{:S(2)}, u32[]{:S(2)}) collective-permute-start(f32[128,768]{1,0:T(8,128)S(1)} %pad_maximum_fusion.2), channel_id=1, source_target_pairs={{1,0},{2,1},{3,2},{4,3},{5,4},{6,5},{7,6},{9,8},{10,9},{11,10},{12... | collective-permute-start | bytes 1179656 | tf_op jit(solution)/shard_map/ppermute | solution.py:32
  63.8 2.3 %copy-start.5 = (f32[128,256]{1,0:T(8,128)S(1)}, f32[128,256]{1,0:T(8,128)}, u32[]{:S(2)}) copy-start(f32[128,256]{1,0:T(8,128)} %get-tuple-element.20) | copy-start | bytes 393220
  66.1 14.9 %collective-permute-start.4 = (f32[128,768]{1,0:T(8,128)S(1)}, f32[128,768]{1,0:T(8,128)S(1)}, u32[]{:S(2)}, u32[]{:S(2)}) collective-permute-start(f32[128,768]{1,0:T(8,128)S(1)} %pad_maximum_fusion.3), channel_id=1, source_target_pairs={{2,0},{3,1},{4,2},{5,3},{6,4},{7,5},{10,8},{11,9},{12,10},{13,11},... | collective-permute-start | bytes 1179656 | tf_op jit(solution)/shard_map/ppermute | solution.py:32
  81.0 8.0 %collective-permute-start.5 = (f32[128,256]{1,0:T(8,128)S(1)}, f32[128,256]{1,0:T(8,128)S(1)}, u32[]{:S(2)}, u32[]{:S(2)}) collective-permute-start(f32[128,256]{1,0:T(8,128)S(1)} %slice_add_fusion.2), channel_id=1, source_target_pairs={{4,0},{5,1},{6,2},{7,3},{12,8},{13,9},{14,10},{15,11},{20,16},{21,... | collective-permute-start | bytes 393224 | tf_op jit(solution)/shard_map/ppermute | solution.py:32
  82.4 6.7 %copy-start.1 = (bf16[1,128,256]{2,1,0:T(8,128)(2,1)S(1)}, bf16[1,128,256]{2,1,0:T(8,128)(2,1)}, u32[]{:S(2)}) copy-start(bf16[1,128,256]{2,1,0:T(8,128)(2,1)} %param.8) | copy-start | bytes 196612
  82.4 6.7 %copy-start.7 = (f32[128,256]{1,0:T(8,128)S(1)}, f32[128,256]{1,0:T(8,128)}, u32[]{:S(2)}) copy-start(f32[128,256]{1,0:T(8,128)} %get-tuple-element.23) | copy-start | bytes 393220
  89.3 0.8 copy-start.3
  89.3 0.9 copy-start.6
  97.0 3.7 %collective-permute-start.6 = (f32[1792]{0:T(1024)S(1)}, f32[1792]{0:T(1024)S(1)}, u32[]{:S(2)}, u32[]{:S(2)}) collective-permute-start(f32[1792]{0:T(1024)S(1)} %bitcast.59), channel_id=1, source_target_pairs={{0,8},{8,0},{16,24},{24,16},{1,9},{9,1},{17,25},{25,17},{2,10},{10... | collective-permute-start | bytes 21512 | tf_op jit(solution)/shard_map/ppermute | solution.py:53
  100.7 4.5 %collective-permute-start.7 = (f32[1792]{0:T(1024)S(1)}, f32[1792]{0:T(1024)S(1)}, u32[]{:S(2)}, u32[]{:S(2)}) collective-permute-start(f32[1792]{0:T(1024)S(1)} %bitcast_add_fusion), channel_id=1, source_target_pairs={{0,16},{8,24},{16,0},{24,8},{1,17},{9,25},{17,1},{25,9},{2,18},{10... | collective-permute-start | bytes 21512 | tf_op jit(solution)/shard_map/ppermute | solution.py:53
Sparse Core Ops, SparseCore 0:
  64.6 31.5 all-gather.2

commit v5 on v3

--- a/solution.py
+++ b/solution.py
@@ -32,6 +32,22 @@
     if total is None:
         total = jnp.zeros_like(part)
     return total
+
+
+def butterfly_scan(part, axis, reverse):
+    count = lax.axis_size(axis)
+    place = lax.axis_index(axis)
+    group = part
+    before = jnp.zeros_like(part)
+    step = 1
+    while step < count:
+        got = lax.ppermute(group, axis, [(i, i ^ step) for i in range(count)])
+        partner = jnp.bitwise_xor(place, step)
+        take = partner > place if reverse else partner < place
+        before = before + jnp.where(take, got, 0.0)
+        group = group + got
+        step *= 2
+    return before, group
 
 
 def all_sum(part, axes):
@@ -205,8 +221,21 @@
         out_specs=tuple(in_vmem(6)),
     )(q, c, k, spiked, prior_half, gain.reshape(1, width), wout, wdq)
     total_tokens = queries.shape[0] * lax.axis_size("dp") * token_rows * lax.axis_size("ctx")
-    d_gain = all_sum(gain_local.reshape(width), ("dp", "ctx")) * (total_tokens ** (-0.5))
-    later_half = exclusive_scan(suffix_local, "ctx", True).astype(jnp.bfloat16)
+    state_rows = KEY_VALUE_HEADS * HEAD_SIZE
+    gain_rows = width // HEAD_SIZE
+    pad_rows = (-(state_rows + gain_rows)) % 8
+    riding = jnp.concatenate(
+        [
+            suffix_local.reshape(state_rows, HEAD_SIZE),
+            gain_local.reshape(gain_rows, HEAD_SIZE),
+            jnp.zeros((pad_rows, HEAD_SIZE), jnp.float32),
+        ],
+        axis=0,
+    )
+    later_rows, total_rows = butterfly_scan(riding, "ctx", True)
+    later_half = later_rows[:state_rows].reshape(suffix_local.shape).astype(jnp.bfloat16)
+    gain_ctx = total_rows[state_rows : state_rows + gain_rows].reshape(width)
+    d_gain = all_sum(gain_ctx, ("dp",)) * (total_tokens ** (-0.5))
     ldk_parts = []
     dsp_parts = []
     for g in range(KEY_VALUE_HEADS):

time: 85.6 us -> 78.2 us (0.914)
  starting transfers between devices: 35.8 us -> 27.2 us
  waiting for transfers between devices: 14.4 us -> 18.3 us
  local copies, waits for them, and re-layouts: 5.74 us -> 3.29 us
    ppermute x0 -> x3, waiting for transfers between devices: none -> 13.4 us  [butterfly_scan(): got = lax.ppermute(group, axis, [(i, i ^ step) for i in range(count)])]
    ppermute x5 -> x2, starting transfers between devices: 12.6 us -> 4.22 us  [all_sum(): part = part + lax.ppermute(part, axes, route)]
    ppermute x5 -> x2, waiting for transfers between devices: 8.04 us -> 3.05 us  [all_sum(): part = part + lax.ppermute(part, axes, route)]
    ppermute x6 -> x3, waiting for transfers between devices: 6.38 us -> 1.88 us  [exclusive_scan(): got = lax.ppermute(running, axis, route)]
    ppermute x0 -> x3, starting transfers between devices: none -> 2.85 us  [butterfly_scan(): got = lax.ppermute(group, axis, [(i, i ^ step) for i in range(count)])]
    ppermute x6 -> x3, starting transfers between devices: 12.7 us -> 9.88 us  [exclusive_scan(): got = lax.ppermute(running, axis, route)]
    unnamed x20 -> x22, local copies, waits for them, and re-layouts: 2.94 us -> 1.5 us
    slice x1, local copies, waits for them, and re-layouts: 1.13 us -> 0.04 us  [per_device(): dk_win[start_row:start_row + token_rows]]
  transfers between devices with their start and end apart: 15 -> 12, of which waited for: 8 -> 5; matrix products, arithmetic and copies ran while one was open for 6% -> 4% of each run, Pallas kernels for 26% -> 15%
where the time goes in v5:
time: 78.2 us; the launch traced here: 77.7 us
  starting transfers between devices  27.2 us (35%)
  Pallas kernels  21.7 us (28%)
  waiting for transfers between devices  18.3 us (23%)
  other arithmetic  5.24 us (7%)
  local copies, waits for them, and re-layouts  3.29 us (4%)
  between operations  0.99 us (1%)
  matrix products  0.94 us (1%)
    ppermute x3, waiting for transfers between devices, butterfly_scan(): got = lax.ppermute(group, axis, [(i, i ^ step) for i in range(count)])  13.4 us
    pallas_call x1, Pallas kernels, per_device(): pl.pallas_call(window_kernel, out_shape=(jax.ShapeDtypeStruct((token_rows...  11.5 us
    pallas_call x1, Pallas kernels, per_device(): pl.pallas_call(linear_kernel, out_shape=(jax.ShapeDtypeStruct((token_rows...  10.3 us
    ppermute x4, starting transfers between devices, shifted(): return lax.ppermute(block, axis, route)  10.2 us
    ppermute x3, starting transfers between devices, exclusive_scan(): got = lax.ppermute(running, axis, route)  9.88 us
    ppermute x2, starting transfers between devices, all_sum(): part = part + lax.ppermute(part, axes, route)  4.22 us
    ppermute x2, waiting for transfers between devices, all_sum(): part = part + lax.ppermute(part, axes, route)  3.05 us
    ppermute x3, starting transfers between devices, butterfly_scan(): got = lax.ppermute(group, axis, [(i, i ^ step) for i in range(count)])  2.85 us
  transfers between devices with their start and end apart: 12, of which 5 were waited for; matrix products, arithmetic and copies ran while one was open for 4% of the time, Pallas kernels for 15%

profile of v5, /device:TPU:0, one launch (start us, length us, event | category | flops | bytes accessed | tf_op | source)
XLA Modules:
  0.0 77.7 jit_solution(1758627263865589079)
XLA Ops:
  0.6 0.7 convert_bitcast_fusion
  1.3 0.1 copy.12
  1.4 0.2 broadcast_in_dim.24
  1.6 0.6 copy-done.4
  2.3 0.0 copy-start.2
  2.3 0.8 %copy-done = bf16[1,128,256]{2,1,0:T(8,128)(2,1)S(1)} copy-done((bf16[1,128,256]{2,1,0:T(8,128)(2,1)S(1)}, bf16[1,128,256]{2,1,0:T(8,128)(2,1)}, u32[]{:S(2)}) %copy-start) | copy-done | bytes 65560
  3.1 0.2 convolution_bitcast_fusion.2
  3.3 0.2 convolution_bitcast_fusion.3
  3.6 2.4 %collective-permute-start = (f32[2,128,128]{2,1,0:T(8,128)S(1)}, f32[2,128,128]{2,1,0:T(8,128)S(1)}, u32[]{:S(2)}, u32[]{:S(2)}) collective-permute-start(f32[2,128,128]{2,1,0:T(8,128)S(1)} %pad_maximum_fusion.2), channel_id=1, source_target_pairs={{0,1},{1,2},{2,3},{3,4},{4,5},{5,6},{6,7},{8,9},{9,10},{10,11},{11... | collective-permute-start | bytes 393224 | tf_op jit(solution)/shard_map/ppermute | solution.py:27
  5.9 4.4 %collective-permute-start.3 = (bf16[128,512]{1,0:T(8,128)(2,1)S(1)}, bf16[128,512]{1,0:T(8,128)(2,1)S(1)}, u32[]{:S(2)}, u32[]{:S(2)}) collective-permute-start(bf16[128,512]{1,0:T(8,128)(2,1)S(1)} %pad_maximum_fusion.3), channel_id=1, source_target_pairs={{0,2},{1,3},{2,4},{3,5},{4,6},{5,7},{8,10},{9,11},{10,12},{11,13},... | collective-permute-start | bytes 393224 | tf_op jit(solution)/shard_map/ppermute | solution.py:68
  10.4 3.2 %collective-permute-start.4 = (bf16[128,512]{1,0:T(8,128)(2,1)S(1)}, bf16[128,512]{1,0:T(8,128)(2,1)S(1)}, u32[]{:S(2)}, u32[]{:S(2)}) collective-permute-start(bf16[128,512]{1,0:T(8,128)(2,1)S(1)} %pad_maximum_fusion.3), channel_id=1, source_target_pairs={{0,1},{1,2},{2,3},{3,4},{4,5},{5,6},{6,7},{8,9},{9,10},{10,11},{11... | collective-permute-start | bytes 393224 | tf_op jit(solution)/shard_map/ppermute | solution.py:68
  13.6 0.0 collective-permute-done
  13.6 0.0 copy-start.9
  13.6 0.0 copy-start.10
  13.7 3.4 %collective-permute-start.1 = (f32[2,128,128]{2,1,0:T(8,128)S(1)}, f32[2,128,128]{2,1,0:T(8,128)S(1)}, u32[]{:S(2)}, u32[]{:S(2)}) collective-permute-start(f32[2,128,128]{2,1,0:T(8,128)S(1)} %fusion.30), channel_id=1, source_target_pairs={{0,2},{1,3},{2,4},{3,5},{4,6},{5,7},{8,10},{9,11},{10,12},{11,13},... | collective-permute-start | bytes 393224 | tf_op jit(solution)/shard_map/ppermute | solution.py:27
  17.1 0.6 pad_add_fusion.info_ref
  17.7 0.6 reshape.36.gain_ref
  18.3 0.1 pad.10.clone
  18.3 0.0 collective-permute-done.3
  18.3 0.0 collective-permute-done.4
  18.4 1.9 %collective-permute-done.1 = f32[2,128,128]{2,1,0:T(8,128)S(1)} collective-permute-done((f32[2,128,128]{2,1,0:T(8,128)S(1)}, f32[2,128,128]{2,1,0:T(8,128)S(1)}, u32[]{:S(2)}, u32[]{:S(2)}) %collective-permute-start.1) | collective-permute-done | bytes 131104 | tf_op jit(solution)/shard_map/ppermute | solution.py:27
  20.3 4.1 %collective-permute-start.2 = (f32[2,128,128]{2,1,0:T(8,128)S(1)}, f32[2,128,128]{2,1,0:T(8,128)S(1)}, u32[]{:S(2)}, u32[]{:S(2)}) collective-permute-start(f32[2,128,128]{2,1,0:T(8,128)S(1)} %fusion.34), channel_id=1, source_target_pairs={{0,4},{1,5},{2,6},{3,7},{8,12},{9,13},{10,14},{11,15},{16,20},{17,... | collective-permute-start | bytes 393224 | tf_op jit(solution)/shard_map/ppermute | solution.py:27
  24.4 0.8 fusion.33
  25.2 11.5 %shard_map.110 = (f32[128,1792]{1,0:T(8,128)}, f32[128,1792]{1,0:T(8,128)}, f32[384,256]{1,0:T(8,128)}, f32[384,256]{1,0:T(8,128)}) custom-call(s32[3]{0:T(128)} %pad_add_fusion.info_ref, bf16[128,1792]{1,0:T(8,128)(2,1)} %bitcast.48, bf16[128,1792]{1,0:T(8,128)(2,1)} %bitcast.50, bf16[384,256]{1,0:T(8,128)(2,1)} %get-tuple-element.30.k_ref, ...), custom_call_target="tpu_custom_call" | custom-call | tf_op jit(solution)/shard_map/pallas_call | solution.py:199
  36.7 0.0 collective-permute-done.2
  36.7 0.7 add_convert_fusion.1.prior_ref
  37.3 10.3 %shard_map.111 = (bf16[128,1792]{1,0:T(8,128)(2,1)}, bf16[128,1792]{1,0:T(8,128)(2,1)}, f32[2,128,128]{2,1,0:T(8,128)}, f32[1,1792]{1,0:T(1,128)}, f32[128,256]{1,0:T(8,128)}, /*index=5*/f32[128,256]{1,0:T(8,128)}) custom-call(bf16[128,1792]{1,0:T(8,128)(2,1)} %bitcast.49, bf16[128,1792]{1,0:T(8,128)(2,1)} %bitcast.51, bf16[128,256]{1,0:T(8,128)(2,1)} %bitcast.52, ...), custom_call_target="tpu_custom_call" | custom-call | tf_op jit(solution)/shard_map/pallas_call | solution.py:210
  47.6 0.7 reduce
  48.3 1.0 %maximum_maximum_fusion.1 = f32[272,128]{1,0:T(8,128)S(1)} fusion(f32[14,128]{1,0:T(8,128)S(1)} %bitcast.64, f32[256,128]{1,0:T(8,128)} %bitcast.63, f32[272]{0:T(512)S(1)} %pad.10.clone), kind=kLoop, calls=%fused_computation.7 | loop fusion | flops 69632 | bytes 278592 | tf_op jit(solution)/shard_map/concatenate | solution.py:227
  49.3 0.1 collective-permute-start.5
  49.5 1.3 %collective-permute-start.9 = (f32[128,512]{1,0:T(8,128)S(1)}, f32[128,512]{1,0:T(8,128)S(1)}, u32[]{:S(2)}, u32[]{:S(2)}) collective-permute-start(f32[128,512]{1,0:T(8,128)S(1)} %pad_maximum_fusion.1), channel_id=1, source_target_pairs={{2,0},{3,1},{4,2},{5,3},{6,4},{7,5},{10,8},{11,9},{12,10},{13,11},... | collective-permute-start | bytes 786440 | tf_op jit(solution)/shard_map/ppermute | solution.py:68
  50.8 2.7 %collective-permute-start.6 = (f32[272,128]{1,0:T(8,128)S(1)}, f32[272,128]{1,0:T(8,128)S(1)}, u32[]{:S(2)}, u32[]{:S(2)}) collective-permute-start(f32[272,128]{1,0:T(8,128)S(1)} %add.65), channel_id=1, source_target_pairs={{0,2},{1,3},{2,0},{3,1},{4,6},{5,7},{6,4},{7,5},{8,10},{9,11},{10,... | collective-permute-start | bytes 417800 | tf_op jit(solution)/shard_map/ppermute | solution.py:44
  53.5 1.3 %collective-permute-start.8 = (f32[128,512]{1,0:T(8,128)S(1)}, f32[128,512]{1,0:T(8,128)S(1)}, u32[]{:S(2)}, u32[]{:S(2)}) collective-permute-start(f32[128,512]{1,0:T(8,128)S(1)} %pad_maximum_fusion), channel_id=1, source_target_pairs={{1,0},{2,1},{3,2},{4,3},{5,4},{6,5},{7,6},{9,8},{10,9},{11,10},{12... | collective-permute-start | bytes 786440 | tf_op jit(solution)/shard_map/ppermute | solution.py:68
  54.8 8.2 %collective-permute-done.6 = f32[272,128]{1,0:T(8,128)S(1)} collective-permute-done((f32[272,128]{1,0:T(8,128)S(1)}, f32[272,128]{1,0:T(8,128)S(1)}, u32[]{:S(2)}, u32[]{:S(2)}) %collective-permute-start.6) | collective-permute-done | bytes 139296 | tf_op jit(solution)/shard_map/ppermute | solution.py:44
  63.1 0.1 collective-permute-start.7
  63.2 0.0 copy-start.3
  63.2 5.2 %collective-permute-done.7 = f32[272,128]{1,0:T(8,128)S(1)} collective-permute-done((f32[272,128]{1,0:T(8,128)S(1)}, f32[272,128]{1,0:T(8,128)S(1)}, u32[]{:S(2)}, u32[]{:S(2)}) %collective-permute-start.7) | collective-permute-done | bytes 139296 | tf_op jit(solution)/shard_map/ppermute | solution.py:44
  68.5 0.1 slice_add_fusion.4
  68.6 0.0 copy-start.7
  68.6 0.1 slice_add_fusion.3
  68.8 1.6 %collective-permute-start.10 = (f32[1792]{0:T(1024)S(1)}, f32[1792]{0:T(1024)S(1)}, u32[]{:S(2)}, u32[]{:S(2)}) collective-permute-start(f32[1792]{0:T(1024)S(1)} %fusion.29), channel_id=1, source_target_pairs={{0,8},{8,0},{16,24},{24,16},{1,9},{9,1},{17,25},{25,17},{2,10},{10... | collective-permute-start | bytes 21512 | tf_op jit(solution)/shard_map/ppermute | solution.py:60
  70.4 0.1 slice_add_fusion.2
  70.6 0.1 slice_add_fusion.1
  70.7 1.8 %collective-permute-done.10 = f32[1792]{0:T(1024)S(1)} collective-permute-done((f32[1792]{0:T(1024)S(1)}, f32[1792]{0:T(1024)S(1)}, u32[]{:S(2)}, u32[]{:S(2)}) %collective-permute-start.10) | collective-permute-done | bytes 7200 | tf_op jit(solution)/shard_map/ppermute | solution.py:60
  72.5 2.6 %collective-permute-start.11 = (f32[1792]{0:T(1024)S(1)}, f32[1792]{0:T(1024)S(1)}, u32[]{:S(2)}, u32[]{:S(2)}) collective-permute-start(f32[1792]{0:T(1024)S(1)} %add.79), channel_id=1, source_target_pairs={{0,16},{8,24},{16,0},{24,8},{1,17},{9,25},{17,1},{25,9},{2,18},{10... | collective-permute-start | bytes 21512 | tf_op jit(solution)/shard_map/ppermute | solution.py:60
  75.1 0.7 fusion.6
  75.8 1.2 %collective-permute-done.11 = f32[1792]{0:T(1024)S(1)} collective-permute-done((f32[1792]{0:T(1024)S(1)}, f32[1792]{0:T(1024)S(1)}, u32[]{:S(2)}, u32[]{:S(2)}) %collective-permute-start.11) | collective-permute-done | bytes 7200 | tf_op jit(solution)/shard_map/ppermute | solution.py:60
  77.1 0.6 add_multiply_fusion
  (34 shorter events, 0.3 us)
Async XLA Ops:
  1.4 0.8 %copy-start.4 = (bf16[1,128,256]{2,1,0:T(8,128)(2,1)S(1)}, bf16[1,128,256]{2,1,0:T(8,128)(2,1)}, u32[]{:S(2)}) copy-start(bf16[1,128,256]{2,1,0:T(8,128)(2,1)} %param.9) | copy-start | bytes 196612
  2.3 0.8 %copy-start = (bf16[1,128,256]{2,1,0:T(8,128)(2,1)S(1)}, bf16[1,128,256]{2,1,0:T(8,128)(2,1)}, u32[]{:S(2)}) copy-start(bf16[1,128,256]{2,1,0:T(8,128)(2,1)} %param.8) | copy-start | bytes 196612
  2.3 1.0 %copy-start.2 = (bf16[128,256]{1,0:T(8,128)(2,1)}, bf16[128,256]{1,0:T(8,128)(2,1)S(1)}, u32[]{:S(2)}) copy-start(bf16[128,256]{1,0:T(8,128)(2,1)S(1)} %fusion.s_ref) | copy-start | bytes 196612
  3.6 10.0 %collective-permute-start = (f32[2,128,128]{2,1,0:T(8,128)S(1)}, f32[2,128,128]{2,1,0:T(8,128)S(1)}, u32[]{:S(2)}, u32[]{:S(2)}) collective-permute-start(f32[2,128,128]{2,1,0:T(8,128)S(1)} %pad_maximum_fusion.2), channel_id=1, source_target_pairs={{0,1},{1,2},{2,3},{3,4},{4,5},{5,6},{6,7},{8,9},{9,10},{10,11},{11... | collective-permute-start | bytes 393224 | tf_op jit(solution)/shard_map/ppermute | solution.py:27
  5.9 12.4 %collective-permute-start.3 = (bf16[128,512]{1,0:T(8,128)(2,1)S(1)}, bf16[128,512]{1,0:T(8,128)(2,1)S(1)}, u32[]{:S(2)}, u32[]{:S(2)}) collective-permute-start(bf16[128,512]{1,0:T(8,128)(2,1)S(1)} %pad_maximum_fusion.3), channel_id=1, source_target_pairs={{0,2},{1,3},{2,4},{3,5},{4,6},{5,7},{8,10},{9,11},{10,12},{11,13},... | collective-permute-start | bytes 393224 | tf_op jit(solution)/shard_map/ppermute | solution.py:68
  10.4 8.0 %collective-permute-start.4 = (bf16[128,512]{1,0:T(8,128)(2,1)S(1)}, bf16[128,512]{1,0:T(8,128)(2,1)S(1)}, u32[]{:S(2)}, u32[]{:S(2)}) collective-permute-start(bf16[128,512]{1,0:T(8,128)(2,1)S(1)} %pad_maximum_fusion.3), channel_id=1, source_target_pairs={{0,1},{1,2},{2,3},{3,4},{4,5},{5,6},{6,7},{8,9},{9,10},{10,11},{11... | collective-permute-start | bytes 393224 | tf_op jit(solution)/shard_map/ppermute | solution.py:68
  13.6 4.1 %copy-start.9 = (f32[1792]{0:T(1024)S(1)}, f32[1792]{0:T(1024)}, u32[]{:S(2)}) copy-start(f32[1792]{0:T(1024)} %param.12) | copy-start | bytes 21508
  13.6 3.4 %copy-start.10 = (s32[2]{0:T(128)S(1)}, s32[2]{0:T(128)}, u32[]{:S(2)}) copy-start(s32[2]{0:T(128)} %param.11) | copy-start | bytes 28
  13.7 6.6 %collective-permute-start.1 = (f32[2,128,128]{2,1,0:T(8,128)S(1)}, f32[2,128,128]{2,1,0:T(8,128)S(1)}, u32[]{:S(2)}, u32[]{:S(2)}) collective-permute-start(f32[2,128,128]{2,1,0:T(8,128)S(1)} %fusion.30), channel_id=1, source_target_pairs={{0,2},{1,3},{2,4},{3,5},{4,6},{5,7},{8,10},{9,11},{10,12},{11,13},... | collective-permute-start | bytes 393224 | tf_op jit(solution)/shard_map/ppermute | solution.py:27
  20.3 16.4 %collective-permute-start.2 = (f32[2,128,128]{2,1,0:T(8,128)S(1)}, f32[2,128,128]{2,1,0:T(8,128)S(1)}, u32[]{:S(2)}, u32[]{:S(2)}) collective-permute-start(f32[2,128,128]{2,1,0:T(8,128)S(1)} %fusion.34), channel_id=1, source_target_pairs={{0,4},{1,5},{2,6},{3,7},{8,12},{9,13},{10,14},{11,15},{16,20},{17,... | collective-permute-start | bytes 393224 | tf_op jit(solution)/shard_map/ppermute | solution.py:27
  37.3 12.1 %copy-start.5 = (f32[384,256]{1,0:T(8,128)S(1)}, f32[384,256]{1,0:T(8,128)}, u32[]{:S(2)}) copy-start(f32[384,256]{1,0:T(8,128)} %get-tuple-element.22) | copy-start | bytes 1179652
  37.3 12.1 %copy-start.6 = (f32[384,256]{1,0:T(8,128)S(1)}, f32[384,256]{1,0:T(8,128)}, u32[]{:S(2)}) copy-start(f32[384,256]{1,0:T(8,128)} %get-tuple-element.23) | copy-start | bytes 1179652
  49.3 1.5 %collective-permute-start.5 = (f32[272,128]{1,0:T(8,128)S(1)}, f32[272,128]{1,0:T(8,128)S(1)}, u32[]{:S(2)}, u32[]{:S(2)}) collective-permute-start(f32[272,128]{1,0:T(8,128)S(1)} %maximum_maximum_fusion.1), channel_id=1, source_target_pairs={{0,1},{1,0},{2,3},{3,2},{4,5},{5,4},{6,7},{7,6},{8,9},{9,8},{10,11... | collective-permute-start | bytes 417800 | tf_op jit(solution)/shard_map/ppermute | solution.py:44
  49.5 13.7 %collective-permute-start.9 = (f32[128,512]{1,0:T(8,128)S(1)}, f32[128,512]{1,0:T(8,128)S(1)}, u32[]{:S(2)}, u32[]{:S(2)}) collective-permute-start(f32[128,512]{1,0:T(8,128)S(1)} %pad_maximum_fusion.1), channel_id=1, source_target_pairs={{2,0},{3,1},{4,2},{5,3},{6,4},{7,5},{10,8},{11,9},{12,10},{13,11},... | collective-permute-start | bytes 786440 | tf_op jit(solution)/shard_map/ppermute | solution.py:68
  50.8 12.2 %collective-permute-start.6 = (f32[272,128]{1,0:T(8,128)S(1)}, f32[272,128]{1,0:T(8,128)S(1)}, u32[]{:S(2)}, u32[]{:S(2)}) collective-permute-start(f32[272,128]{1,0:T(8,128)S(1)} %add.65), channel_id=1, source_target_pairs={{0,2},{1,3},{2,0},{3,1},{4,6},{5,7},{6,4},{7,5},{8,10},{9,11},{10,... | collective-permute-start | bytes 417800 | tf_op jit(solution)/shard_map/ppermute | solution.py:44
  53.5 9.6 %collective-permute-start.8 = (f32[128,512]{1,0:T(8,128)S(1)}, f32[128,512]{1,0:T(8,128)S(1)}, u32[]{:S(2)}, u32[]{:S(2)}) collective-permute-start(f32[128,512]{1,0:T(8,128)S(1)} %pad_maximum_fusion), channel_id=1, source_target_pairs={{1,0},{2,1},{3,2},{4,3},{5,4},{6,5},{7,6},{9,8},{10,9},{11,10},{12... | collective-permute-start | bytes 786440 | tf_op jit(solution)/shard_map/ppermute | solution.py:68
  63.1 5.3 %collective-permute-start.7 = (f32[272,128]{1,0:T(8,128)S(1)}, f32[272,128]{1,0:T(8,128)S(1)}, u32[]{:S(2)}, u32[]{:S(2)}) collective-permute-start(f32[272,128]{1,0:T(8,128)S(1)} %add.67), channel_id=1, source_target_pairs={{0,4},{1,5},{2,6},{3,7},{4,0},{5,1},{6,2},{7,3},{8,12},{9,13},{10,... | collective-permute-start | bytes 417800 | tf_op jit(solution)/shard_map/ppermute | solution.py:44
  63.2 5.2 %copy-start.3 = (bf16[128,256]{1,0:T(8,128)(2,1)S(1)}, bf16[128,256]{1,0:T(8,128)(2,1)}, u32[]{:S(2)}) copy-start(bf16[128,256]{1,0:T(8,128)(2,1)} %copy-done.2) | copy-start | bytes 196612
  63.2 5.2 %copy-start.8 = (f32[128,256]{1,0:T(8,128)S(1)}, f32[128,256]{1,0:T(8,128)}, u32[]{:S(2)}) copy-start(f32[128,256]{1,0:T(8,128)} %get-tuple-element.19) | copy-start | bytes 393220
  68.6 1.8 %copy-start.1 = (bf16[1,128,256]{2,1,0:T(8,128)(2,1)S(1)}, bf16[1,128,256]{2,1,0:T(8,128)(2,1)}, u32[]{:S(2)}) copy-start(bf16[1,128,256]{2,1,0:T(8,128)(2,1)} %param.8) | copy-start | bytes 196612
  68.6 1.8 %copy-start.7 = (f32[128,256]{1,0:T(8,128)S(1)}, f32[128,256]{1,0:T(8,128)}, u32[]{:S(2)}) copy-start(f32[128,256]{1,0:T(8,128)} %get-tuple-element.24) | copy-start | bytes 393220
  68.8 3.7 %collective-permute-start.10 = (f32[1792]{0:T(1024)S(1)}, f32[1792]{0:T(1024)S(1)}, u32[]{:S(2)}, u32[]{:S(2)}) collective-permute-start(f32[1792]{0:T(1024)S(1)} %fusion.29), channel_id=1, source_target_pairs={{0,8},{8,0},{16,24},{24,16},{1,9},{9,1},{17,25},{25,17},{2,10},{10... | collective-permute-start | bytes 21512 | tf_op jit(solution)/shard_map/ppermute | solution.py:60
  72.5 4.5 %collective-permute-start.11 = (f32[1792]{0:T(1024)S(1)}, f32[1792]{0:T(1024)S(1)}, u32[]{:S(2)}, u32[]{:S(2)}) collective-permute-start(f32[1792]{0:T(1024)S(1)} %add.79), channel_id=1, source_target_pairs={{0,16},{8,24},{16,0},{24,8},{1,17},{9,25},{17,1},{25,9},{2,18},{10... | collective-permute-start | bytes 21512 | tf_op jit(solution)/shard_map/ppermute | solution.py:60

commit v6 on v5

--- a/solution.py
+++ b/solution.py
@@ -206,6 +206,11 @@
         ),
         in_specs=[pl.BlockSpec(memory_space=pltpu.SMEM)] + in_vmem(4),
         out_specs=tuple(in_vmem(4)),
+        cost_estimate=pl.CostEstimate(
+            flops=12 * QUERY_HEADS * token_rows * window_rows * HEAD_SIZE,
+            transcendentals=QUERY_HEADS * token_rows * window_rows,
+            bytes_accessed=2 * token_rows * width * (2 + 4) + 2 * window_rows * key_value_width * (2 + 4),
+        ),
     )(info, q, c, window_packed[:, :key_value_width], window_packed[:, key_value_width:])
     mixed, d_queries, suffix_local, gain_local, ldk, dsp = pl.pallas_call(
         linear_kernel,
@@ -219,6 +224,11 @@
         ),
         in_specs=in_vmem(8),
         out_specs=tuple(in_vmem(6)),
+        cost_estimate=pl.CostEstimate(
+            flops=20 * QUERY_HEADS * token_rows * token_rows * HEAD_SIZE,
+            transcendentals=QUERY_HEADS * token_rows,
+            bytes_accessed=token_rows * width * (2 + 2 + 4 + 4 + 2 + 2) + 6 * token_rows * key_value_width * 4,
+        ),
     )(q, c, k, spiked, prior_half, gain.reshape(1, width), wout, wdq)
     total_tokens = queries.shape[0] * lax.axis_size("dp") * token_rows * lax.axis_size("ctx")
     state_rows = KEY_VALUE_HEADS * HEAD_SIZE
@@ -261,7 +271,7 @@
             ],
             axis=1,
         )
-        received = received + shifted(sent, "ctx", -distance)
+        received = received + shifted(sent.astype(jnp.bfloat16), "ctx", -distance).astype(jnp.float32)
     keys_gradient = (
         linear_key_gradient + dk_win[padding_rows:] + received[:, :key_value_width]
     ).astype(jnp.bfloat16)

time: 78.2 us -> 76.4 us (0.977)
  waiting for transfers between devices: 18.3 us -> 14.5 us
  other arithmetic: 5.24 us -> 7.2 us
    ppermute x3, waiting for transfers between devices: 13.4 us -> 9.14 us  [butterfly_scan(): got = lax.ppermute(group, axis, [(i, i ^ step) for i in range(count)])]
    ppermute x4, waiting for transfers between devices: 0.01 us -> 1.3 us  [shifted(): return lax.ppermute(block, axis, route)]
    another operation x1 -> x3, other arithmetic: 0.03 us -> 1.12 us
    ppermute x2, waiting for transfers between devices: 3.05 us -> 2.15 us  [all_sum(): part = part + lax.ppermute(part, axes, route)]
    broadcast_in_dim x1, other arithmetic: 0.72 us -> 1.62 us  [per_device(): values_gradient[None]]
  transfers between devices with their start and end apart: 12 -> 12, of which waited for: 5 -> 6; matrix products, arithmetic and copies ran while one was open for 4% -> 7% of each run, Pallas kernels for 15% -> 15%
where the time goes in v6:
time: 76.4 us; the launch traced here: 75.8 us
  starting transfers between devices  27.3 us (36%)
  Pallas kernels  21.7 us (28%)
  waiting for transfers between devices  14.5 us (19%)
  other arithmetic  7.2 us (9%)
  local copies, waits for them, and re-layouts  3.31 us (4%)
  between operations  0.97 us (1%)
  matrix products  0.94 us (1%)
    pallas_call x1, Pallas kernels, per_device(): pl.pallas_call(window_kernel, out_shape=(jax.ShapeDtypeStruct((token_rows...  11.5 us
    ppermute x4, starting transfers between devices, shifted(): return lax.ppermute(block, axis, route)  10.2 us
    pallas_call x1, Pallas kernels, per_device(): pl.pallas_call(linear_kernel, out_shape=(jax.ShapeDtypeStruct((token_rows...  10.2 us
    ppermute x3, starting transfers between devices, exclusive_scan(): got = lax.ppermute(running, axis, route)  9.88 us
    ppermute x3, waiting for transfers between devices, butterfly_scan(): got = lax.ppermute(group, axis, [(i, i ^ step) for i in range(count)])  9.14 us
    ppermute x2, starting transfers between devices, all_sum(): part = part + lax.ppermute(part, axes, route)  4.23 us
    ppermute x3, starting transfers between devices, butterfly_scan(): got = lax.ppermute(group, axis, [(i, i ^ step) for i in range(count)])  2.94 us
    ppermute x2, waiting for transfers between devices, all_sum(): part = part + lax.ppermute(part, axes, route)  2.15 us
  transfers between devices with their start and end apart: 12, of which 6 were waited for; matrix products, arithmetic and copies ran while one was open for 7% of the time, Pallas kernels for 15%

profile of v6, /device:TPU:0, one launch (start us, length us, event | category | flops | bytes accessed | tf_op | source)
XLA Modules:
  0.0 75.8 jit_solution(7205921938901522167)
XLA Ops:
  0.6 0.7 convert_bitcast_fusion
  1.3 0.1 copy.12
  1.4 0.2 broadcast_in_dim.24
  1.6 0.6 copy-done.5
  2.3 0.0 copy-start.2
  2.3 0.8 %copy-done = bf16[1,128,256]{2,1,0:T(8,128)(2,1)S(1)} copy-done((bf16[1,128,256]{2,1,0:T(8,128)(2,1)S(1)}, bf16[1,128,256]{2,1,0:T(8,128)(2,1)}, u32[]{:S(2)}) %copy-start) | copy-done | bytes 65560
  3.1 0.2 convolution_bitcast_fusion.2
  3.3 0.2 convolution_bitcast_fusion.3
  3.6 2.4 %collective-permute-start = (f32[2,128,128]{2,1,0:T(8,128)S(1)}, f32[2,128,128]{2,1,0:T(8,128)S(1)}, u32[]{:S(2)}, u32[]{:S(2)}) collective-permute-start(f32[2,128,128]{2,1,0:T(8,128)S(1)} %pad_maximum_fusion), channel_id=1, source_target_pairs={{0,1},{1,2},{2,3},{3,4},{4,5},{5,6},{6,7},{8,9},{9,10},{10,11},{11... | collective-permute-start | bytes 393224 | tf_op jit(solution)/shard_map/ppermute | solution.py:27
  5.9 4.4 %collective-permute-start.3 = (bf16[128,512]{1,0:T(8,128)(2,1)S(1)}, bf16[128,512]{1,0:T(8,128)(2,1)S(1)}, u32[]{:S(2)}, u32[]{:S(2)}) collective-permute-start(bf16[128,512]{1,0:T(8,128)(2,1)S(1)} %pad_maximum_fusion.1), channel_id=1, source_target_pairs={{0,2},{1,3},{2,4},{3,5},{4,6},{5,7},{8,10},{9,11},{10,12},{11,13},... | collective-permute-start | bytes 393224 | tf_op jit(solution)/shard_map/ppermute | solution.py:68
  10.4 3.2 %collective-permute-start.4 = (bf16[128,512]{1,0:T(8,128)(2,1)S(1)}, bf16[128,512]{1,0:T(8,128)(2,1)S(1)}, u32[]{:S(2)}, u32[]{:S(2)}) collective-permute-start(bf16[128,512]{1,0:T(8,128)(2,1)S(1)} %pad_maximum_fusion.1), channel_id=1, source_target_pairs={{0,1},{1,2},{2,3},{3,4},{4,5},{5,6},{6,7},{8,9},{9,10},{10,11},{11... | collective-permute-start | bytes 393224 | tf_op jit(solution)/shard_map/ppermute | solution.py:68
  13.6 0.0 collective-permute-done
  13.6 0.0 copy-start.8
  13.6 0.0 copy-start.9
  13.7 3.4 %collective-permute-start.1 = (f32[2,128,128]{2,1,0:T(8,128)S(1)}, f32[2,128,128]{2,1,0:T(8,128)S(1)}, u32[]{:S(2)}, u32[]{:S(2)}) collective-permute-start(f32[2,128,128]{2,1,0:T(8,128)S(1)} %fusion.30), channel_id=1, source_target_pairs={{0,2},{1,3},{2,4},{3,5},{4,6},{5,7},{8,10},{9,11},{10,12},{11,13},... | collective-permute-start | bytes 393224 | tf_op jit(solution)/shard_map/ppermute | solution.py:27
  17.1 0.6 pad_add_fusion.info_ref
  17.7 0.6 reshape.36.gain_ref
  18.3 0.1 pad.10.clone
  18.4 1.9 %collective-permute-done.1 = f32[2,128,128]{2,1,0:T(8,128)S(1)} collective-permute-done((f32[2,128,128]{2,1,0:T(8,128)S(1)}, f32[2,128,128]{2,1,0:T(8,128)S(1)}, u32[]{:S(2)}, u32[]{:S(2)}) %collective-permute-start.1) | collective-permute-done | bytes 131104 | tf_op jit(solution)/shard_map/ppermute | solution.py:27
  20.3 4.1 %collective-permute-start.2 = (f32[2,128,128]{2,1,0:T(8,128)S(1)}, f32[2,128,128]{2,1,0:T(8,128)S(1)}, u32[]{:S(2)}, u32[]{:S(2)}) collective-permute-start(f32[2,128,128]{2,1,0:T(8,128)S(1)} %fusion.34), channel_id=1, source_target_pairs={{0,4},{1,5},{2,6},{3,7},{8,12},{9,13},{10,14},{11,15},{16,20},{17,... | collective-permute-start | bytes 393224 | tf_op jit(solution)/shard_map/ppermute | solution.py:27
  24.4 0.8 %fusion.31 = (bf16[384,256]{1,0:T(8,128)(2,1)}, bf16[384,256]{1,0:T(8,128)(2,1)}) fusion(bf16[384,512]{1,0:T(8,128)(2,1)S(1)} %maximum_maximum_fusion), kind=kLoop, calls=%fused_computation.48 | loop fusion | bytes 786432 | tf_op jit(solution)/shard_map/slice | solution.py:214
  25.2 11.5 %shard_map.110 = (f32[128,1792]{1,0:T(8,128)}, f32[128,1792]{1,0:T(8,128)}, f32[384,256]{1,0:T(8,128)}, f32[384,256]{1,0:T(8,128)}) custom-call(s32[3]{0:T(128)} %pad_add_fusion.info_ref, bf16[128,1792]{1,0:T(8,128)(2,1)} %bitcast.59, bf16[128,1792]{1,0:T(8,128)(2,1)} %bitcast.61, bf16[384,256]{1,0:T(8,128)(2,1)} %get-tuple-element.26.k_ref, ...), custom_call_target="tpu_custom_call" | custom-call | flops 1056964608 | bytes 3932160 | tf_op jit(solution)/shard_map/pallas_call | solution.py:199
  36.6 1.1 %convert.16 = bf16[384,256]{1,0:T(8,128)(2,1)S(1)} convert(f32[384,256]{1,0:T(8,128)} %get-tuple-element.22) | non-fusion elementwise | flops 98304 | bytes 589824 | tf_op jit(solution)/shard_map/convert.7
  37.7 0.0 copy-done.4
  37.8 0.7 add_convert_fusion.1.prior_ref
  38.4 10.2 %shard_map.111 = (bf16[128,1792]{1,0:T(8,128)(2,1)}, bf16[128,1792]{1,0:T(8,128)(2,1)}, f32[2,128,128]{2,1,0:T(8,128)}, f32[1,1792]{1,0:T(1,128)}, f32[128,256]{1,0:T(8,128)}, /*index=5*/f32[128,256]{1,0:T(8,128)}) custom-call(bf16[128,1792]{1,0:T(8,128)(2,1)} %bitcast.60, bf16[128,1792]{1,0:T(8,128)(2,1)} %bitcast.62, bf16[128,256]{1,0:T(8,128)(2,1)} %bitcast.48, ...), custom_call_target="tpu_custom_call" | custom-call | flops 587202560 | bytes 4456448 | tf_op jit(solution)/shard_map/pallas_call | solution.py:215
  48.6 0.7 reduce
  49.4 1.0 %maximum_maximum_fusion.1 = f32[272,128]{1,0:T(8,128)S(1)} fusion(f32[14,128]{1,0:T(8,128)S(1)} %bitcast.64, f32[256,128]{1,0:T(8,128)} %bitcast.63, f32[272]{0:T(512)S(1)} %pad.10.clone), kind=kLoop, calls=%fused_computation.6 | loop fusion | flops 69632 | bytes 278592 | tf_op jit(solution)/shard_map/concatenate | solution.py:237
  50.4 0.1 collective-permute-start.5
  50.5 1.3 %collective-permute-start.8 = (bf16[128,512]{1,0:T(8,128)(2,1)S(1)}, bf16[128,512]{1,0:T(8,128)(2,1)S(1)}, u32[]{:S(2)}, u32[]{:S(2)}) collective-permute-start(bf16[128,512]{1,0:T(8,128)(2,1)S(1)} %pad_maximum_fusion.2), channel_id=1, source_target_pairs={{1,0},{2,1},{3,2},{4,3},{5,4},{6,5},{7,6},{9,8},{10,9},{11,10},{12... | collective-permute-start | bytes 393224 | tf_op jit(solution)/shard_map/ppermute | solution.py:68
  51.8 2.8 %collective-permute-start.6 = (f32[272,128]{1,0:T(8,128)S(1)}, f32[272,128]{1,0:T(8,128)S(1)}, u32[]{:S(2)}, u32[]{:S(2)}) collective-permute-start(f32[272,128]{1,0:T(8,128)S(1)} %add.65), channel_id=1, source_target_pairs={{0,2},{1,3},{2,0},{3,1},{4,6},{5,7},{6,4},{7,5},{8,10},{9,11},{10,... | collective-permute-start | bytes 417800 | tf_op jit(solution)/shard_map/ppermute | solution.py:44
  54.6 1.3 %collective-permute-start.9 = (bf16[128,512]{1,0:T(8,128)(2,1)S(1)}, bf16[128,512]{1,0:T(8,128)(2,1)S(1)}, u32[]{:S(2)}, u32[]{:S(2)}) collective-permute-start(bf16[128,512]{1,0:T(8,128)(2,1)S(1)} %pad_maximum_fusion.3), channel_id=1, source_target_pairs={{2,0},{3,1},{4,2},{5,3},{6,4},{7,5},{10,8},{11,9},{12,10},{13,11},... | collective-permute-start | bytes 393224 | tf_op jit(solution)/shard_map/ppermute | solution.py:68
  56.0 5.5 %collective-permute-done.6 = f32[272,128]{1,0:T(8,128)S(1)} collective-permute-done((f32[272,128]{1,0:T(8,128)S(1)}, f32[272,128]{1,0:T(8,128)S(1)}, u32[]{:S(2)}, u32[]{:S(2)}) %collective-permute-start.6) | collective-permute-done | bytes 139296 | tf_op jit(solution)/shard_map/ppermute | solution.py:44
  61.4 0.1 collective-permute-start.7
  61.5 1.3 %collective-permute-done.9 = bf16[128,512]{1,0:T(8,128)(2,1)S(1)} collective-permute-done((bf16[128,512]{1,0:T(8,128)(2,1)S(1)}, bf16[128,512]{1,0:T(8,128)(2,1)S(1)}, u32[]{:S(2)}, u32[]{:S(2)}) %collective-permute-start.9) | collective-permute-done | bytes 131104 | tf_op jit(solution)/shard_map/ppermute | solution.py:68
  62.9 0.0 copy-start.3
  62.9 3.7 %collective-permute-done.7 = f32[272,128]{1,0:T(8,128)S(1)} collective-permute-done((f32[272,128]{1,0:T(8,128)S(1)}, f32[272,128]{1,0:T(8,128)S(1)}, u32[]{:S(2)}, u32[]{:S(2)}) %collective-permute-start.7) | collective-permute-done | bytes 139296 | tf_op jit(solution)/shard_map/ppermute | solution.py:44
  66.6 0.1 slice_add_fusion.4
  66.8 0.0 copy-start.6
  66.8 0.1 slice_add_fusion.3
  66.9 1.6 %collective-permute-start.10 = (f32[1792]{0:T(1024)S(1)}, f32[1792]{0:T(1024)S(1)}, u32[]{:S(2)}, u32[]{:S(2)}) collective-permute-start(f32[1792]{0:T(1024)S(1)} %fusion.29), channel_id=1, source_target_pairs={{0,8},{8,0},{16,24},{24,16},{1,9},{9,1},{17,25},{25,17},{2,10},{10... | collective-permute-start | bytes 21512 | tf_op jit(solution)/shard_map/ppermute | solution.py:60
  68.6 0.1 slice_add_fusion.2
  68.7 0.1 slice_add_fusion.1
  68.9 1.8 %collective-permute-done.10 = f32[1792]{0:T(1024)S(1)} collective-permute-done((f32[1792]{0:T(1024)S(1)}, f32[1792]{0:T(1024)S(1)}, u32[]{:S(2)}, u32[]{:S(2)}) %collective-permute-start.10) | collective-permute-done | bytes 7200 | tf_op jit(solution)/shard_map/ppermute | solution.py:60
  70.7 2.6 %collective-permute-start.11 = (f32[1792]{0:T(1024)S(1)}, f32[1792]{0:T(1024)S(1)}, u32[]{:S(2)}, u32[]{:S(2)}) collective-permute-start(f32[1792]{0:T(1024)S(1)} %add.79), channel_id=1, source_target_pairs={{0,16},{8,24},{16,0},{24,8},{1,17},{9,25},{17,1},{25,9},{2,18},{10... | collective-permute-start | bytes 21512 | tf_op jit(solution)/shard_map/ppermute | solution.py:60
  73.2 1.6 %fusion.6 = (bf16[1,128,256]{2,1,0:T(8,128)(2,1)}, bf16[1,128,256]{2,1,0:T(8,128)(2,1)}) fusion(f32[128,512]{1,0:T(8,128)S(1)} %convert_add_fusion, f32[384,256]{1,0:T(8,128)S(1)} %copy-done.4, f32[16,8,2,128]{3,2,1,0:T(2,128)S(1)} %bitcast.56, f32[128,128]{1,0:T(8,128)S(1)} %slice_add_fusion.1, f32[128,128]{1,0:T(8,128)S(1)} %slice_add_fusion.2, ...), kind=kLoop, calls=%fused_computation.27 | loop fusion | flops 294912 | bytes 1048576 | tf_op jit(solution)/shard_map/broadcast_in_dim | solution.py:285
  74.9 0.3 collective-permute-done.11
  75.2 0.6 add_multiply_fusion
  (34 shorter events, 0.3 us)
Async XLA Ops:
  1.4 0.8 %copy-start.5 = (bf16[1,128,256]{2,1,0:T(8,128)(2,1)S(1)}, bf16[1,128,256]{2,1,0:T(8,128)(2,1)}, u32[]{:S(2)}) copy-start(bf16[1,128,256]{2,1,0:T(8,128)(2,1)} %param.9) | copy-start | bytes 196612
  2.3 0.8 %copy-start = (bf16[1,128,256]{2,1,0:T(8,128)(2,1)S(1)}, bf16[1,128,256]{2,1,0:T(8,128)(2,1)}, u32[]{:S(2)}) copy-start(bf16[1,128,256]{2,1,0:T(8,128)(2,1)} %param.8) | copy-start | bytes 196612
  2.3 1.0 %copy-start.2 = (bf16[128,256]{1,0:T(8,128)(2,1)}, bf16[128,256]{1,0:T(8,128)(2,1)S(1)}, u32[]{:S(2)}) copy-start(bf16[128,256]{1,0:T(8,128)(2,1)S(1)} %fusion.s_ref) | copy-start | bytes 196612
  3.6 10.0 %collective-permute-start = (f32[2,128,128]{2,1,0:T(8,128)S(1)}, f32[2,128,128]{2,1,0:T(8,128)S(1)}, u32[]{:S(2)}, u32[]{:S(2)}) collective-permute-start(f32[2,128,128]{2,1,0:T(8,128)S(1)} %pad_maximum_fusion), channel_id=1, source_target_pairs={{0,1},{1,2},{2,3},{3,4},{4,5},{5,6},{6,7},{8,9},{9,10},{10,11},{11... | collective-permute-start | bytes 393224 | tf_op jit(solution)/shard_map/ppermute | solution.py:27
  5.9 12.4 %collective-permute-start.3 = (bf16[128,512]{1,0:T(8,128)(2,1)S(1)}, bf16[128,512]{1,0:T(8,128)(2,1)S(1)}, u32[]{:S(2)}, u32[]{:S(2)}) collective-permute-start(bf16[128,512]{1,0:T(8,128)(2,1)S(1)} %pad_maximum_fusion.1), channel_id=1, source_target_pairs={{0,2},{1,3},{2,4},{3,5},{4,6},{5,7},{8,10},{9,11},{10,12},{11,13},... | collective-permute-start | bytes 393224 | tf_op jit(solution)/shard_map/ppermute | solution.py:68
  10.4 8.0 %collective-permute-start.4 = (bf16[128,512]{1,0:T(8,128)(2,1)S(1)}, bf16[128,512]{1,0:T(8,128)(2,1)S(1)}, u32[]{:S(2)}, u32[]{:S(2)}) collective-permute-start(bf16[128,512]{1,0:T(8,128)(2,1)S(1)} %pad_maximum_fusion.1), channel_id=1, source_target_pairs={{0,1},{1,2},{2,3},{3,4},{4,5},{5,6},{6,7},{8,9},{9,10},{10,11},{11... | collective-permute-start | bytes 393224 | tf_op jit(solution)/shard_map/ppermute | solution.py:68
  13.6 4.1 %copy-start.8 = (f32[1792]{0:T(1024)S(1)}, f32[1792]{0:T(1024)}, u32[]{:S(2)}) copy-start(f32[1792]{0:T(1024)} %param.12) | copy-start | bytes 21508
  13.6 3.4 %copy-start.9 = (s32[2]{0:T(128)S(1)}, s32[2]{0:T(128)}, u32[]{:S(2)}) copy-start(s32[2]{0:T(128)} %param.11) | copy-start | bytes 28
  13.7 6.6 %collective-permute-start.1 = (f32[2,128,128]{2,1,0:T(8,128)S(1)}, f32[2,128,128]{2,1,0:T(8,128)S(1)}, u32[]{:S(2)}, u32[]{:S(2)}) collective-permute-start(f32[2,128,128]{2,1,0:T(8,128)S(1)} %fusion.30), channel_id=1, source_target_pairs={{0,2},{1,3},{2,4},{3,5},{4,6},{5,7},{8,10},{9,11},{10,12},{11,13},... | collective-permute-start | bytes 393224 | tf_op jit(solution)/shard_map/ppermute | solution.py:27
  20.3 17.5 %collective-permute-start.2 = (f32[2,128,128]{2,1,0:T(8,128)S(1)}, f32[2,128,128]{2,1,0:T(8,128)S(1)}, u32[]{:S(2)}, u32[]{:S(2)}) collective-permute-start(f32[2,128,128]{2,1,0:T(8,128)S(1)} %fusion.34), channel_id=1, source_target_pairs={{0,4},{1,5},{2,6},{3,7},{8,12},{9,13},{10,14},{11,15},{16,20},{17,... | collective-permute-start | bytes 393224 | tf_op jit(solution)/shard_map/ppermute | solution.py:27
  36.6 1.1 %copy-start.4 = (f32[384,256]{1,0:T(8,128)S(1)}, f32[384,256]{1,0:T(8,128)}, u32[]{:S(2)}) copy-start(f32[384,256]{1,0:T(8,128)} %get-tuple-element.23) | copy-start | bytes 1179652
  50.4 1.4 %collective-permute-start.5 = (f32[272,128]{1,0:T(8,128)S(1)}, f32[272,128]{1,0:T(8,128)S(1)}, u32[]{:S(2)}, u32[]{:S(2)}) collective-permute-start(f32[272,128]{1,0:T(8,128)S(1)} %maximum_maximum_fusion.1), channel_id=1, source_target_pairs={{0,1},{1,0},{2,3},{3,2},{4,5},{5,4},{6,7},{7,6},{8,9},{9,8},{10,11... | collective-permute-start | bytes 417800 | tf_op jit(solution)/shard_map/ppermute | solution.py:44
  50.5 11.0 %collective-permute-start.8 = (bf16[128,512]{1,0:T(8,128)(2,1)S(1)}, bf16[128,512]{1,0:T(8,128)(2,1)S(1)}, u32[]{:S(2)}, u32[]{:S(2)}) collective-permute-start(bf16[128,512]{1,0:T(8,128)(2,1)S(1)} %pad_maximum_fusion.2), channel_id=1, source_target_pairs={{1,0},{2,1},{3,2},{4,3},{5,4},{6,5},{7,6},{9,8},{10,9},{11,10},{12... | collective-permute-start | bytes 393224 | tf_op jit(solution)/shard_map/ppermute | solution.py:68
  51.8 9.6 %collective-permute-start.6 = (f32[272,128]{1,0:T(8,128)S(1)}, f32[272,128]{1,0:T(8,128)S(1)}, u32[]{:S(2)}, u32[]{:S(2)}) collective-permute-start(f32[272,128]{1,0:T(8,128)S(1)} %add.65), channel_id=1, source_target_pairs={{0,2},{1,3},{2,0},{3,1},{4,6},{5,7},{6,4},{7,5},{8,10},{9,11},{10,... | collective-permute-start | bytes 417800 | tf_op jit(solution)/shard_map/ppermute | solution.py:44
  54.6 8.2 %collective-permute-start.9 = (bf16[128,512]{1,0:T(8,128)(2,1)S(1)}, bf16[128,512]{1,0:T(8,128)(2,1)S(1)}, u32[]{:S(2)}, u32[]{:S(2)}) collective-permute-start(bf16[128,512]{1,0:T(8,128)(2,1)S(1)} %pad_maximum_fusion.3), channel_id=1, source_target_pairs={{2,0},{3,1},{4,2},{5,3},{6,4},{7,5},{10,8},{11,9},{12,10},{13,11},... | collective-permute-start | bytes 393224 | tf_op jit(solution)/shard_map/ppermute | solution.py:68
  61.4 5.1 %collective-permute-start.7 = (f32[272,128]{1,0:T(8,128)S(1)}, f32[272,128]{1,0:T(8,128)S(1)}, u32[]{:S(2)}, u32[]{:S(2)}) collective-permute-start(f32[272,128]{1,0:T(8,128)S(1)} %add.67), channel_id=1, source_target_pairs={{0,4},{1,5},{2,6},{3,7},{4,0},{5,1},{6,2},{7,3},{8,12},{9,13},{10,... | collective-permute-start | bytes 417800 | tf_op jit(solution)/shard_map/ppermute | solution.py:44
  62.9 3.7 %copy-start.3 = (bf16[128,256]{1,0:T(8,128)(2,1)S(1)}, bf16[128,256]{1,0:T(8,128)(2,1)}, u32[]{:S(2)}) copy-start(bf16[128,256]{1,0:T(8,128)(2,1)} %copy-done.2) | copy-start | bytes 196612
  62.9 3.7 %copy-start.7 = (f32[128,256]{1,0:T(8,128)S(1)}, f32[128,256]{1,0:T(8,128)}, u32[]{:S(2)}) copy-start(f32[128,256]{1,0:T(8,128)} %get-tuple-element.19) | copy-start | bytes 393220
  66.7 1.8 %copy-start.1 = (bf16[1,128,256]{2,1,0:T(8,128)(2,1)S(1)}, bf16[1,128,256]{2,1,0:T(8,128)(2,1)}, u32[]{:S(2)}) copy-start(bf16[1,128,256]{2,1,0:T(8,128)(2,1)} %param.8) | copy-start | bytes 196612
  66.8 1.8 %copy-start.6 = (f32[128,256]{1,0:T(8,128)S(1)}, f32[128,256]{1,0:T(8,128)}, u32[]{:S(2)}) copy-start(f32[128,256]{1,0:T(8,128)} %get-tuple-element.24) | copy-start | bytes 393220
  66.9 3.7 %collective-permute-start.10 = (f32[1792]{0:T(1024)S(1)}, f32[1792]{0:T(1024)S(1)}, u32[]{:S(2)}, u32[]{:S(2)}) collective-permute-start(f32[1792]{0:T(1024)S(1)} %fusion.29), channel_id=1, source_target_pairs={{0,8},{8,0},{16,24},{24,16},{1,9},{9,1},{17,25},{25,17},{2,10},{10... | collective-permute-start | bytes 21512 | tf_op jit(solution)/shard_map/ppermute | solution.py:60
  70.7 4.5 %collective-permute-start.11 = (f32[1792]{0:T(1024)S(1)}, f32[1792]{0:T(1024)S(1)}, u32[]{:S(2)}, u32[]{:S(2)}) collective-permute-start(f32[1792]{0:T(1024)S(1)} %add.79), channel_id=1, source_target_pairs={{0,16},{8,24},{16,0},{24,8},{1,17},{9,25},{17,1},{25,9},{2,18},{10... | collective-permute-start | bytes 21512 | tf_op jit(solution)/shard_map/ppermute | solution.py:60

commit v7 on v6

--- a/solution.py
+++ b/solution.py
@@ -93,7 +93,7 @@
             s = jnp.where(visible, s, -1e30)
             top = jnp.max(s, axis=-1, keepdims=True)
             e = jnp.exp(s - top)
-            p = e / jnp.sum(e, axis=-1, keepdims=True)
+            p = e * (1.0 / jnp.sum(e, axis=-1, keepdims=True))
             ph = p.astype(jnp.bfloat16)
             wout = jnp.dot(ph, vg, preferred_element_type=jnp.float32)
             wout_ref[:, cols] = wout
@@ -135,12 +135,12 @@
             lin = jnp.dot(lh, sg, preferred_element_type=jnp.float32) + jnp.dot(
                 qh, pg, preferred_element_type=jnp.float32
             )
-            root = jnp.sqrt(jnp.mean(lin * lin, axis=-1, keepdims=True) + epsilon)
-            normed = lin / root
+            inverse_root = 1.0 / jnp.sqrt(jnp.mean(lin * lin, axis=-1, keepdims=True) + epsilon)
+            normed = lin * inverse_root
             mixed_ref[:, cols] = (gh * normed + wout_ref[:, cols]).astype(mixed_ref.dtype)
             gsum_ref[:, cols] = jnp.sum(ch * normed, axis=0, keepdims=True)
             scaled = ch * gh
-            dl = ((scaled - normed * jnp.mean(scaled * normed, axis=-1, keepdims=True)) / root).astype(
+            dl = ((scaled - normed * jnp.mean(scaled * normed, axis=-1, keepdims=True)) * inverse_root).astype(
                 jnp.bfloat16
             )
             suffix = suffix + lax.dot_general(qh, dl, (((0,), (0,)), ((), ())), preferred_element_type=jnp.float32)

time: 76.4 us -> 76.4 us (level)
  no operation moved by 1% of the time
where the time goes in v7:
time: 76.4 us; the launch traced here: 75.8 us
  starting transfers between devices  27.3 us (36%)
  Pallas kernels  21.7 us (28%)
  waiting for transfers between devices  14.5 us (19%)
  other arithmetic  7.2 us (9%)
  local copies, waits for them, and re-layouts  3.31 us (4%)
  between operations  0.97 us (1%)
  matrix products  0.94 us (1%)
    pallas_call x1, Pallas kernels, per_device(): pl.pallas_call(window_kernel, out_shape=(jax.ShapeDtypeStruct((token_rows...  11.5 us
    ppermute x4, starting transfers between devices, shifted(): return lax.ppermute(block, axis, route)  10.2 us
    pallas_call x1, Pallas kernels, per_device(): pl.pallas_call(linear_kernel, out_shape=(jax.ShapeDtypeStruct((token_rows...  10.2 us
    ppermute x3, starting transfers between devices, exclusive_scan(): got = lax.ppermute(running, axis, route)  9.88 us
    ppermute x3, waiting for transfers between devices, butterfly_scan(): got = lax.ppermute(group, axis, [(i, i ^ step) for i in range(count)])  9.14 us
    ppermute x2, starting transfers between devices, all_sum(): part = part + lax.ppermute(part, axes, route)  4.23 us
    ppermute x3, starting transfers between devices, butterfly_scan(): got = lax.ppermute(group, axis, [(i, i ^ step) for i in range(count)])  2.94 us
    ppermute x2, waiting for transfers between devices, all_sum(): part = part + lax.ppermute(part, axes, route)  2.15 us
  transfers between devices with their start and end apart: 12, of which 6 were waited for; matrix products, arithmetic and copies ran while one was open for 7% of the time, Pallas kernels for 15%

profile of v7, /device:TPU:0, one launch (start us, length us, event | category | flops | bytes accessed | tf_op | source)
XLA Modules:
  0.0 75.8 jit_solution(7205921938901522167)
XLA Ops:
  0.6 0.7 convert_bitcast_fusion
  1.3 0.1 copy.12
  1.4 0.2 broadcast_in_dim.24
  1.6 0.6 copy-done.5
  2.3 0.0 copy-start.2
  2.3 0.8 %copy-done = bf16[1,128,256]{2,1,0:T(8,128)(2,1)S(1)} copy-done((bf16[1,128,256]{2,1,0:T(8,128)(2,1)S(1)}, bf16[1,128,256]{2,1,0:T(8,128)(2,1)}, u32[]{:S(2)}) %copy-start) | copy-done | bytes 65560
  3.1 0.2 convolution_bitcast_fusion.2
  3.3 0.2 convolution_bitcast_fusion.3
  3.6 2.4 %collective-permute-start = (f32[2,128,128]{2,1,0:T(8,128)S(1)}, f32[2,128,128]{2,1,0:T(8,128)S(1)}, u32[]{:S(2)}, u32[]{:S(2)}) collective-permute-start(f32[2,128,128]{2,1,0:T(8,128)S(1)} %pad_maximum_fusion), channel_id=1, source_target_pairs={{0,1},{1,2},{2,3},{3,4},{4,5},{5,6},{6,7},{8,9},{9,10},{10,11},{11... | collective-permute-start | bytes 393224 | tf_op jit(solution)/shard_map/ppermute | solution.py:27
  5.9 4.4 %collective-permute-start.3 = (bf16[128,512]{1,0:T(8,128)(2,1)S(1)}, bf16[128,512]{1,0:T(8,128)(2,1)S(1)}, u32[]{:S(2)}, u32[]{:S(2)}) collective-permute-start(bf16[128,512]{1,0:T(8,128)(2,1)S(1)} %pad_maximum_fusion.1), channel_id=1, source_target_pairs={{0,2},{1,3},{2,4},{3,5},{4,6},{5,7},{8,10},{9,11},{10,12},{11,13},... | collective-permute-start | bytes 393224 | tf_op jit(solution)/shard_map/ppermute | solution.py:68
  10.4 3.2 %collective-permute-start.4 = (bf16[128,512]{1,0:T(8,128)(2,1)S(1)}, bf16[128,512]{1,0:T(8,128)(2,1)S(1)}, u32[]{:S(2)}, u32[]{:S(2)}) collective-permute-start(bf16[128,512]{1,0:T(8,128)(2,1)S(1)} %pad_maximum_fusion.1), channel_id=1, source_target_pairs={{0,1},{1,2},{2,3},{3,4},{4,5},{5,6},{6,7},{8,9},{9,10},{10,11},{11... | collective-permute-start | bytes 393224 | tf_op jit(solution)/shard_map/ppermute | solution.py:68
  13.6 0.0 collective-permute-done
  13.6 0.0 copy-start.8
  13.6 0.0 copy-start.9
  13.7 3.4 %collective-permute-start.1 = (f32[2,128,128]{2,1,0:T(8,128)S(1)}, f32[2,128,128]{2,1,0:T(8,128)S(1)}, u32[]{:S(2)}, u32[]{:S(2)}) collective-permute-start(f32[2,128,128]{2,1,0:T(8,128)S(1)} %fusion.30), channel_id=1, source_target_pairs={{0,2},{1,3},{2,4},{3,5},{4,6},{5,7},{8,10},{9,11},{10,12},{11,13},... | collective-permute-start | bytes 393224 | tf_op jit(solution)/shard_map/ppermute | solution.py:27
  17.1 0.6 pad_add_fusion.info_ref
  17.7 0.6 reshape.36.gain_ref
  18.3 0.1 pad.10.clone
  18.4 1.9 %collective-permute-done.1 = f32[2,128,128]{2,1,0:T(8,128)S(1)} collective-permute-done((f32[2,128,128]{2,1,0:T(8,128)S(1)}, f32[2,128,128]{2,1,0:T(8,128)S(1)}, u32[]{:S(2)}, u32[]{:S(2)}) %collective-permute-start.1) | collective-permute-done | bytes 131104 | tf_op jit(solution)/shard_map/ppermute | solution.py:27
  20.3 4.1 %collective-permute-start.2 = (f32[2,128,128]{2,1,0:T(8,128)S(1)}, f32[2,128,128]{2,1,0:T(8,128)S(1)}, u32[]{:S(2)}, u32[]{:S(2)}) collective-permute-start(f32[2,128,128]{2,1,0:T(8,128)S(1)} %fusion.34), channel_id=1, source_target_pairs={{0,4},{1,5},{2,6},{3,7},{8,12},{9,13},{10,14},{11,15},{16,20},{17,... | collective-permute-start | bytes 393224 | tf_op jit(solution)/shard_map/ppermute | solution.py:27
  24.4 0.8 %fusion.31 = (bf16[384,256]{1,0:T(8,128)(2,1)}, bf16[384,256]{1,0:T(8,128)(2,1)}) fusion(bf16[384,512]{1,0:T(8,128)(2,1)S(1)} %maximum_maximum_fusion), kind=kLoop, calls=%fused_computation.48 | loop fusion | bytes 786432 | tf_op jit(solution)/shard_map/slice | solution.py:214
  25.2 11.5 %shard_map.110 = (f32[128,1792]{1,0:T(8,128)}, f32[128,1792]{1,0:T(8,128)}, f32[384,256]{1,0:T(8,128)}, f32[384,256]{1,0:T(8,128)}) custom-call(s32[3]{0:T(128)} %pad_add_fusion.info_ref, bf16[128,1792]{1,0:T(8,128)(2,1)} %bitcast.59, bf16[128,1792]{1,0:T(8,128)(2,1)} %bitcast.61, bf16[384,256]{1,0:T(8,128)(2,1)} %get-tuple-element.26.k_ref, ...), custom_call_target="tpu_custom_call" | custom-call | flops 1056964608 | bytes 3932160 | tf_op jit(solution)/shard_map/pallas_call | solution.py:199
  36.6 1.1 %convert.16 = bf16[384,256]{1,0:T(8,128)(2,1)S(1)} convert(f32[384,256]{1,0:T(8,128)} %get-tuple-element.22) | non-fusion elementwise | flops 98304 | bytes 589824 | tf_op jit(solution)/shard_map/convert.7
  37.7 0.0 copy-done.4
  37.8 0.7 add_convert_fusion.1.prior_ref
  38.4 10.2 %shard_map.111 = (bf16[128,1792]{1,0:T(8,128)(2,1)}, bf16[128,1792]{1,0:T(8,128)(2,1)}, f32[2,128,128]{2,1,0:T(8,128)}, f32[1,1792]{1,0:T(1,128)}, f32[128,256]{1,0:T(8,128)}, /*index=5*/f32[128,256]{1,0:T(8,128)}) custom-call(bf16[128,1792]{1,0:T(8,128)(2,1)} %bitcast.60, bf16[128,1792]{1,0:T(8,128)(2,1)} %bitcast.62, bf16[128,256]{1,0:T(8,128)(2,1)} %bitcast.48, ...), custom_call_target="tpu_custom_call" | custom-call | flops 587202560 | bytes 4456448 | tf_op jit(solution)/shard_map/pallas_call | solution.py:215
  48.6 0.7 reduce
  49.4 1.0 %maximum_maximum_fusion.1 = f32[272,128]{1,0:T(8,128)S(1)} fusion(f32[14,128]{1,0:T(8,128)S(1)} %bitcast.64, f32[256,128]{1,0:T(8,128)} %bitcast.63, f32[272]{0:T(512)S(1)} %pad.10.clone), kind=kLoop, calls=%fused_computation.6 | loop fusion | flops 69632 | bytes 278592 | tf_op jit(solution)/shard_map/concatenate | solution.py:237
  50.4 0.1 collective-permute-start.5
  50.5 1.3 %collective-permute-start.8 = (bf16[128,512]{1,0:T(8,128)(2,1)S(1)}, bf16[128,512]{1,0:T(8,128)(2,1)S(1)}, u32[]{:S(2)}, u32[]{:S(2)}) collective-permute-start(bf16[128,512]{1,0:T(8,128)(2,1)S(1)} %pad_maximum_fusion.2), channel_id=1, source_target_pairs={{1,0},{2,1},{3,2},{4,3},{5,4},{6,5},{7,6},{9,8},{10,9},{11,10},{12... | collective-permute-start | bytes 393224 | tf_op jit(solution)/shard_map/ppermute | solution.py:68
  51.8 2.8 %collective-permute-start.6 = (f32[272,128]{1,0:T(8,128)S(1)}, f32[272,128]{1,0:T(8,128)S(1)}, u32[]{:S(2)}, u32[]{:S(2)}) collective-permute-start(f32[272,128]{1,0:T(8,128)S(1)} %add.65), channel_id=1, source_target_pairs={{0,2},{1,3},{2,0},{3,1},{4,6},{5,7},{6,4},{7,5},{8,10},{9,11},{10,... | collective-permute-start | bytes 417800 | tf_op jit(solution)/shard_map/ppermute | solution.py:44
  54.6 1.3 %collective-permute-start.9 = (bf16[128,512]{1,0:T(8,128)(2,1)S(1)}, bf16[128,512]{1,0:T(8,128)(2,1)S(1)}, u32[]{:S(2)}, u32[]{:S(2)}) collective-permute-start(bf16[128,512]{1,0:T(8,128)(2,1)S(1)} %pad_maximum_fusion.3), channel_id=1, source_target_pairs={{2,0},{3,1},{4,2},{5,3},{6,4},{7,5},{10,8},{11,9},{12,10},{13,11},... | collective-permute-start | bytes 393224 | tf_op jit(solution)/shard_map/ppermute | solution.py:68
  56.0 5.5 %collective-permute-done.6 = f32[272,128]{1,0:T(8,128)S(1)} collective-permute-done((f32[272,128]{1,0:T(8,128)S(1)}, f32[272,128]{1,0:T(8,128)S(1)}, u32[]{:S(2)}, u32[]{:S(2)}) %collective-permute-start.6) | collective-permute-done | bytes 139296 | tf_op jit(solution)/shard_map/ppermute | solution.py:44
  61.4 0.1 collective-permute-start.7
  61.5 1.3 %collective-permute-done.9 = bf16[128,512]{1,0:T(8,128)(2,1)S(1)} collective-permute-done((bf16[128,512]{1,0:T(8,128)(2,1)S(1)}, bf16[128,512]{1,0:T(8,128)(2,1)S(1)}, u32[]{:S(2)}, u32[]{:S(2)}) %collective-permute-start.9) | collective-permute-done | bytes 131104 | tf_op jit(solution)/shard_map/ppermute | solution.py:68
  62.9 0.0 copy-start.3
  62.9 3.7 %collective-permute-done.7 = f32[272,128]{1,0:T(8,128)S(1)} collective-permute-done((f32[272,128]{1,0:T(8,128)S(1)}, f32[272,128]{1,0:T(8,128)S(1)}, u32[]{:S(2)}, u32[]{:S(2)}) %collective-permute-start.7) | collective-permute-done | bytes 139296 | tf_op jit(solution)/shard_map/ppermute | solution.py:44
  66.6 0.1 slice_add_fusion.4
  66.8 0.0 copy-start.6
  66.8 0.1 slice_add_fusion.3
  66.9 1.6 %collective-permute-start.10 = (f32[1792]{0:T(1024)S(1)}, f32[1792]{0:T(1024)S(1)}, u32[]{:S(2)}, u32[]{:S(2)}) collective-permute-start(f32[1792]{0:T(1024)S(1)} %fusion.29), channel_id=1, source_target_pairs={{0,8},{8,0},{16,24},{24,16},{1,9},{9,1},{17,25},{25,17},{2,10},{10... | collective-permute-start | bytes 21512 | tf_op jit(solution)/shard_map/ppermute | solution.py:60
  68.6 0.1 slice_add_fusion.2
  68.7 0.1 slice_add_fusion.1
  68.9 1.8 %collective-permute-done.10 = f32[1792]{0:T(1024)S(1)} collective-permute-done((f32[1792]{0:T(1024)S(1)}, f32[1792]{0:T(1024)S(1)}, u32[]{:S(2)}, u32[]{:S(2)}) %collective-permute-start.10) | collective-permute-done | bytes 7200 | tf_op jit(solution)/shard_map/ppermute | solution.py:60
  70.7 2.6 %collective-permute-start.11 = (f32[1792]{0:T(1024)S(1)}, f32[1792]{0:T(1024)S(1)}, u32[]{:S(2)}, u32[]{:S(2)}) collective-permute-start(f32[1792]{0:T(1024)S(1)} %add.79), channel_id=1, source_target_pairs={{0,16},{8,24},{16,0},{24,8},{1,17},{9,25},{17,1},{25,9},{2,18},{10... | collective-permute-start | bytes 21512 | tf_op jit(solution)/shard_map/ppermute | solution.py:60
  73.2 1.6 %fusion.6 = (bf16[1,128,256]{2,1,0:T(8,128)(2,1)}, bf16[1,128,256]{2,1,0:T(8,128)(2,1)}) fusion(f32[128,512]{1,0:T(8,128)S(1)} %convert_add_fusion, f32[384,256]{1,0:T(8,128)S(1)} %copy-done.4, f32[16,8,2,128]{3,2,1,0:T(2,128)S(1)} %bitcast.56, f32[128,128]{1,0:T(8,128)S(1)} %slice_add_fusion.1, f32[128,128]{1,0:T(8,128)S(1)} %slice_add_fusion.2, ...), kind=kLoop, calls=%fused_computation.27 | loop fusion | flops 294912 | bytes 1048576 | tf_op jit(solution)/shard_map/broadcast_in_dim | solution.py:285
  74.9 0.3 collective-permute-done.11
  75.2 0.6 add_multiply_fusion
  (34 shorter events, 0.3 us)
Async XLA Ops:
  1.4 0.8 %copy-start.5 = (bf16[1,128,256]{2,1,0:T(8,128)(2,1)S(1)}, bf16[1,128,256]{2,1,0:T(8,128)(2,1)}, u32[]{:S(2)}) copy-start(bf16[1,128,256]{2,1,0:T(8,128)(2,1)} %param.9) | copy-start | bytes 196612
  2.3 0.8 %copy-start = (bf16[1,128,256]{2,1,0:T(8,128)(2,1)S(1)}, bf16[1,128,256]{2,1,0:T(8,128)(2,1)}, u32[]{:S(2)}) copy-start(bf16[1,128,256]{2,1,0:T(8,128)(2,1)} %param.8) | copy-start | bytes 196612
  2.3 1.0 %copy-start.2 = (bf16[128,256]{1,0:T(8,128)(2,1)}, bf16[128,256]{1,0:T(8,128)(2,1)S(1)}, u32[]{:S(2)}) copy-start(bf16[128,256]{1,0:T(8,128)(2,1)S(1)} %fusion.s_ref) | copy-start | bytes 196612
  3.6 10.0 %collective-permute-start = (f32[2,128,128]{2,1,0:T(8,128)S(1)}, f32[2,128,128]{2,1,0:T(8,128)S(1)}, u32[]{:S(2)}, u32[]{:S(2)}) collective-permute-start(f32[2,128,128]{2,1,0:T(8,128)S(1)} %pad_maximum_fusion), channel_id=1, source_target_pairs={{0,1},{1,2},{2,3},{3,4},{4,5},{5,6},{6,7},{8,9},{9,10},{10,11},{11... | collective-permute-start | bytes 393224 | tf_op jit(solution)/shard_map/ppermute | solution.py:27
  5.9 12.4 %collective-permute-start.3 = (bf16[128,512]{1,0:T(8,128)(2,1)S(1)}, bf16[128,512]{1,0:T(8,128)(2,1)S(1)}, u32[]{:S(2)}, u32[]{:S(2)}) collective-permute-start(bf16[128,512]{1,0:T(8,128)(2,1)S(1)} %pad_maximum_fusion.1), channel_id=1, source_target_pairs={{0,2},{1,3},{2,4},{3,5},{4,6},{5,7},{8,10},{9,11},{10,12},{11,13},... | collective-permute-start | bytes 393224 | tf_op jit(solution)/shard_map/ppermute | solution.py:68
  10.4 8.0 %collective-permute-start.4 = (bf16[128,512]{1,0:T(8,128)(2,1)S(1)}, bf16[128,512]{1,0:T(8,128)(2,1)S(1)}, u32[]{:S(2)}, u32[]{:S(2)}) collective-permute-start(bf16[128,512]{1,0:T(8,128)(2,1)S(1)} %pad_maximum_fusion.1), channel_id=1, source_target_pairs={{0,1},{1,2},{2,3},{3,4},{4,5},{5,6},{6,7},{8,9},{9,10},{10,11},{11... | collective-permute-start | bytes 393224 | tf_op jit(solution)/shard_map/ppermute | solution.py:68
  13.6 4.1 %copy-start.8 = (f32[1792]{0:T(1024)S(1)}, f32[1792]{0:T(1024)}, u32[]{:S(2)}) copy-start(f32[1792]{0:T(1024)} %param.12) | copy-start | bytes 21508
  13.6 3.4 %copy-start.9 = (s32[2]{0:T(128)S(1)}, s32[2]{0:T(128)}, u32[]{:S(2)}) copy-start(s32[2]{0:T(128)} %param.11) | copy-start | bytes 28
  13.7 6.6 %collective-permute-start.1 = (f32[2,128,128]{2,1,0:T(8,128)S(1)}, f32[2,128,128]{2,1,0:T(8,128)S(1)}, u32[]{:S(2)}, u32[]{:S(2)}) collective-permute-start(f32[2,128,128]{2,1,0:T(8,128)S(1)} %fusion.30), channel_id=1, source_target_pairs={{0,2},{1,3},{2,4},{3,5},{4,6},{5,7},{8,10},{9,11},{10,12},{11,13},... | collective-permute-start | bytes 393224 | tf_op jit(solution)/shard_map/ppermute | solution.py:27
  20.3 17.5 %collective-permute-start.2 = (f32[2,128,128]{2,1,0:T(8,128)S(1)}, f32[2,128,128]{2,1,0:T(8,128)S(1)}, u32[]{:S(2)}, u32[]{:S(2)}) collective-permute-start(f32[2,128,128]{2,1,0:T(8,128)S(1)} %fusion.34), channel_id=1, source_target_pairs={{0,4},{1,5},{2,6},{3,7},{8,12},{9,13},{10,14},{11,15},{16,20},{17,... | collective-permute-start | bytes 393224 | tf_op jit(solution)/shard_map/ppermute | solution.py:27
  36.6 1.1 %copy-start.4 = (f32[384,256]{1,0:T(8,128)S(1)}, f32[384,256]{1,0:T(8,128)}, u32[]{:S(2)}) copy-start(f32[384,256]{1,0:T(8,128)} %get-tuple-element.23) | copy-start | bytes 1179652
  50.4 1.4 %collective-permute-start.5 = (f32[272,128]{1,0:T(8,128)S(1)}, f32[272,128]{1,0:T(8,128)S(1)}, u32[]{:S(2)}, u32[]{:S(2)}) collective-permute-start(f32[272,128]{1,0:T(8,128)S(1)} %maximum_maximum_fusion.1), channel_id=1, source_target_pairs={{0,1},{1,0},{2,3},{3,2},{4,5},{5,4},{6,7},{7,6},{8,9},{9,8},{10,11... | collective-permute-start | bytes 417800 | tf_op jit(solution)/shard_map/ppermute | solution.py:44
  50.5 11.0 %collective-permute-start.8 = (bf16[128,512]{1,0:T(8,128)(2,1)S(1)}, bf16[128,512]{1,0:T(8,128)(2,1)S(1)}, u32[]{:S(2)}, u32[]{:S(2)}) collective-permute-start(bf16[128,512]{1,0:T(8,128)(2,1)S(1)} %pad_maximum_fusion.2), channel_id=1, source_target_pairs={{1,0},{2,1},{3,2},{4,3},{5,4},{6,5},{7,6},{9,8},{10,9},{11,10},{12... | collective-permute-start | bytes 393224 | tf_op jit(solution)/shard_map/ppermute | solution.py:68
  51.8 9.6 %collective-permute-start.6 = (f32[272,128]{1,0:T(8,128)S(1)}, f32[272,128]{1,0:T(8,128)S(1)}, u32[]{:S(2)}, u32[]{:S(2)}) collective-permute-start(f32[272,128]{1,0:T(8,128)S(1)} %add.65), channel_id=1, source_target_pairs={{0,2},{1,3},{2,0},{3,1},{4,6},{5,7},{6,4},{7,5},{8,10},{9,11},{10,... | collective-permute-start | bytes 417800 | tf_op jit(solution)/shard_map/ppermute | solution.py:44
  54.6 8.2 %collective-permute-start.9 = (bf16[128,512]{1,0:T(8,128)(2,1)S(1)}, bf16[128,512]{1,0:T(8,128)(2,1)S(1)}, u32[]{:S(2)}, u32[]{:S(2)}) collective-permute-start(bf16[128,512]{1,0:T(8,128)(2,1)S(1)} %pad_maximum_fusion.3), channel_id=1, source_target_pairs={{2,0},{3,1},{4,2},{5,3},{6,4},{7,5},{10,8},{11,9},{12,10},{13,11},... | collective-permute-start | bytes 393224 | tf_op jit(solution)/shard_map/ppermute | solution.py:68
  61.4 5.1 %collective-permute-start.7 = (f32[272,128]{1,0:T(8,128)S(1)}, f32[272,128]{1,0:T(8,128)S(1)}, u32[]{:S(2)}, u32[]{:S(2)}) collective-permute-start(f32[272,128]{1,0:T(8,128)S(1)} %add.67), channel_id=1, source_target_pairs={{0,4},{1,5},{2,6},{3,7},{4,0},{5,1},{6,2},{7,3},{8,12},{9,13},{10,... | collective-permute-start | bytes 417800 | tf_op jit(solution)/shard_map/ppermute | solution.py:44
  62.9 3.7 %copy-start.3 = (bf16[128,256]{1,0:T(8,128)(2,1)S(1)}, bf16[128,256]{1,0:T(8,128)(2,1)}, u32[]{:S(2)}) copy-start(bf16[128,256]{1,0:T(8,128)(2,1)} %copy-done.2) | copy-start | bytes 196612
  62.9 3.7 %copy-start.7 = (f32[128,256]{1,0:T(8,128)S(1)}, f32[128,256]{1,0:T(8,128)}, u32[]{:S(2)}) copy-start(f32[128,256]{1,0:T(8,128)} %get-tuple-element.19) | copy-start | bytes 393220
  66.7 1.8 %copy-start.1 = (bf16[1,128,256]{2,1,0:T(8,128)(2,1)S(1)}, bf16[1,128,256]{2,1,0:T(8,128)(2,1)}, u32[]{:S(2)}) copy-start(bf16[1,128,256]{2,1,0:T(8,128)(2,1)} %param.8) | copy-start | bytes 196612
  66.8 1.8 %copy-start.6 = (f32[128,256]{1,0:T(8,128)S(1)}, f32[128,256]{1,0:T(8,128)}, u32[]{:S(2)}) copy-start(f32[128,256]{1,0:T(8,128)} %get-tuple-element.24) | copy-start | bytes 393220
  66.9 3.7 %collective-permute-start.10 = (f32[1792]{0:T(1024)S(1)}, f32[1792]{0:T(1024)S(1)}, u32[]{:S(2)}, u32[]{:S(2)}) collective-permute-start(f32[1792]{0:T(1024)S(1)} %fusion.29), channel_id=1, source_target_pairs={{0,8},{8,0},{16,24},{24,16},{1,9},{9,1},{17,25},{25,17},{2,10},{10... | collective-permute-start | bytes 21512 | tf_op jit(solution)/shard_map/ppermute | solution.py:60
  70.7 4.5 %collective-permute-start.11 = (f32[1792]{0:T(1024)S(1)}, f32[1792]{0:T(1024)S(1)}, u32[]{:S(2)}, u32[]{:S(2)}) collective-permute-start(f32[1792]{0:T(1024)S(1)} %add.79), channel_id=1, source_target_pairs={{0,16},{8,24},{16,0},{24,8},{1,17},{9,25},{17,1},{25,9},{2,18},{10... | collective-permute-start | bytes 21512 | tf_op jit(solution)/shard_map/ppermute | solution.py:60

commit v8 on v7

--- a/solution.py
+++ b/solution.py
@@ -48,6 +48,25 @@
         group = group + got
         step *= 2
     return before, group
+
+
+def spread_scan(near, own, axis):
+    count = lax.axis_size(axis)
+    total = near
+    running = own
+    stride = 3
+    while stride < count:
+        parts = []
+        for distance in (stride, 2 * stride):
+            if distance < count:
+                parts.append(shifted(running, axis, distance))
+        for got in parts:
+            total = total + got
+        if 3 * stride < count:
+            for got in parts:
+                running = running + got
+        stride *= 3
+    return total
 
 
 def all_sum(part, axes):
@@ -176,23 +195,47 @@
     v = values[0]
     counts = jnp.repeat(spikes[0].astype(jnp.float32), HEAD_SIZE, axis=1)
     spiked = (v.astype(jnp.float32) * counts).astype(jnp.bfloat16)
-    local_state = jnp.stack(
+    def state_of(block_keys, block_spiked):
+        return jnp.stack(
+            [
+                lax.dot_general(
+                    block_keys[:, g * HEAD_SIZE : (g + 1) * HEAD_SIZE],
+                    block_spiked[:, g * HEAD_SIZE : (g + 1) * HEAD_SIZE],
+                    (((0,), (0,)), ((), ())),
+                    preferred_element_type=jnp.float32,
+                )
+                for g in range(KEY_VALUE_HEADS)
+            ]
+        )
+
+    count_lanes = HEAD_SIZE
+    spike_block = jnp.concatenate(
         [
-            lax.dot_general(
-                k[:, g * HEAD_SIZE : (g + 1) * HEAD_SIZE],
-                spiked[:, g * HEAD_SIZE : (g + 1) * HEAD_SIZE],
-                (((0,), (0,)), ((), ())),
-                preferred_element_type=jnp.float32,
-            )
-            for g in range(KEY_VALUE_HEADS)
-        ]
-    )
-    prior_half = exclusive_scan(local_state, "ctx", False).astype(jnp.bfloat16)
-    packed = jnp.concatenate([k, v], axis=1)
+            spikes[0].astype(jnp.bfloat16),
+            jnp.zeros((token_rows, count_lanes - KEY_VALUE_HEADS), jnp.bfloat16),
+        ],
+        axis=1,
+    )
+    packed = jnp.concatenate([k, v, spike_block], axis=1)
     earlier = []
     for distance in range(reach, 0, -1):
         earlier.append(shifted(packed, "ctx", distance))
-    window_packed = jnp.concatenate(earlier + [packed], axis=0)
+    near = jnp.zeros((KEY_VALUE_HEADS, HEAD_SIZE, HEAD_SIZE), jnp.float32)
+    for piece in earlier:
+        piece_counts = jnp.repeat(
+            piece[:, 2 * key_value_width : 2 * key_value_width + KEY_VALUE_HEADS].astype(jnp.float32),
+            HEAD_SIZE,
+            axis=1,
+        )
+        piece_spiked = (
+            piece[:, key_value_width : 2 * key_value_width].astype(jnp.float32) * piece_counts
+        ).astype(jnp.bfloat16)
+        near = near + state_of(piece[:, :key_value_width], piece_spiked)
+    own_and_near = near + state_of(k, spiked)
+    prior_half = spread_scan(near, own_and_near, "ctx").astype(jnp.bfloat16)
+    window_packed = jnp.concatenate(
+        [piece[:, : 2 * key_value_width] for piece in earlier] + [jnp.concatenate([k, v], axis=1)], axis=0
+    )
     info = jnp.concatenate(
         [window_lengths.astype(jnp.int32), (lax.axis_index("ctx") * token_rows - padding_rows).reshape(1)]
     ).astype(jnp.int32)

time: 76.4 us -> 73.1 us (0.957)
  starting transfers between devices: 27.3 us -> 23.1 us
  local copies, waits for them, and re-layouts: 3.31 us -> 5.43 us
  waiting for transfers between devices: 14.5 us -> 13 us
    ppermute x3 -> x0, starting transfers between devices: 9.88 us -> none  [exclusive_scan(): got = lax.ppermute(running, axis, route)]
    ppermute x4 -> x6, starting transfers between devices: 10.2 us -> 15.9 us  [shifted(): return lax.ppermute(block, axis, route)]
    ppermute x3 -> x0, waiting for transfers between devices: 1.88 us -> none  [exclusive_scan(): got = lax.ppermute(running, axis, route)]
    slice x0 -> x3, local copies, waits for them, and re-layouts: none -> 0.89 us  [per_device(): piece[:, :2 * key_value_width]]
    unnamed x20 -> x25, local copies, waits for them, and re-layouts: 1.53 us -> 2.3 us
  transfers between devices with their start and end apart: 12 -> 11, of which waited for: 6 -> 5; matrix products, arithmetic and copies ran while one was open for 7% -> 9% of each run, Pallas kernels for 15% -> 16%
where the time goes in v8:
time: 73.1 us; the launch traced here: 72.5 us
  starting transfers between devices  23.1 us (32%)
  Pallas kernels  21.7 us (30%)
  waiting for transfers between devices  13 us (18%)
  other arithmetic  6.58 us (9%)
  local copies, waits for them, and re-layouts  5.43 us (7%)
  matrix products  1.67 us (2%)
  between operations  1.05 us (1%)
    ppermute x6, starting transfers between devices, shifted(): return lax.ppermute(block, axis, route)  15.9 us
    pallas_call x1, Pallas kernels, per_device(): pl.pallas_call(window_kernel, out_shape=(jax.ShapeDtypeStruct((token_rows...  11.5 us
    pallas_call x1, Pallas kernels, per_device(): pl.pallas_call(linear_kernel, out_shape=(jax.ShapeDtypeStruct((token_rows...  10.2 us
    ppermute x3, waiting for transfers between devices, butterfly_scan(): got = lax.ppermute(group, axis, [(i, i ^ step) for i in range(count)])  9.48 us
    ppermute x2, starting transfers between devices, all_sum(): part = part + lax.ppermute(part, axes, route)  4.23 us
    ppermute x3, starting transfers between devices, butterfly_scan(): got = lax.ppermute(group, axis, [(i, i ^ step) for i in range(count)])  3 us
    unnamed x25, local copies, waits for them, and re-layouts  2.3 us
    ppermute x2, waiting for transfers between devices, all_sum(): part = part + lax.ppermute(part, axes, route)  2.14 us
  transfers between devices with their start and end apart: 11, of which 5 were waited for; matrix products, arithmetic and copies ran while one was open for 9% of the time, Pallas kernels for 16%

profile of v8, /device:TPU:0, one launch (start us, length us, event | category | flops | bytes accessed | tf_op | source)
XLA Modules:
  0.0 72.5 jit_solution(265241577388459807)
XLA Ops:
  0.6 0.8 %copy.13 = s32[1,128,2]{2,1,0:T(8,128)S(1)} copy(s32[1,128,2]{1,2,0:T(2,128)} %param.10) | data formatting | bytes 2048 | tf_op args[3]
  1.5 0.1 pad.26.clone
  1.6 0.7 %copy-done = bf16[1,128,256]{2,1,0:T(8,128)(2,1)S(1)} copy-done((bf16[1,128,256]{2,1,0:T(8,128)(2,1)S(1)}, bf16[1,128,256]{2,1,0:T(8,128)(2,1)}, u32[]{:S(2)}) %copy-start) | copy-done | bytes 65560
  2.3 4.9 %collective-permute-start = (bf16[128,640]{1,0:T(8,128)(2,1)S(1)}, bf16[128,640]{1,0:T(8,128)(2,1)S(1)}, u32[]{:S(2)}, u32[]{:S(2)}) collective-permute-start(bf16[128,640]{1,0:T(8,128)(2,1)S(1)} %maximum_maximum_fusion.1), channel_id=1, source_target_pairs={{0,2},{1,3},{2,4},{3,5},{4,6},{5,7},{8,10},{9,11},{10,12},{11,13},... | collective-permute-start | bytes 491528 | tf_op jit(solution)/shard_map/ppermute | solution.py:87
  7.2 1.5 %collective-permute-start.1 = (bf16[128,640]{1,0:T(8,128)(2,1)S(1)}, bf16[128,640]{1,0:T(8,128)(2,1)S(1)}, u32[]{:S(2)}, u32[]{:S(2)}) collective-permute-start(bf16[128,640]{1,0:T(8,128)(2,1)S(1)} %maximum_maximum_fusion.1), channel_id=1, source_target_pairs={{0,1},{1,2},{2,3},{3,4},{4,5},{5,6},{6,7},{8,9},{9,10},{10,11},{11... | collective-permute-start | bytes 491528 | tf_op jit(solution)/shard_map/ppermute | solution.py:87
  8.7 0.1 copy.12
  8.8 0.2 broadcast_in_dim.33
  9.0 0.2 convolution_bitcast_fusion.2
  9.3 0.7 copy-done.11
  9.9 0.6 pad_add_fusion.info_ref
  10.5 0.6 reshape.45.gain_ref
  11.1 0.1 pad.10.clone
  11.2 0.2 convolution_bitcast_fusion.3
  11.4 0.2 broadcast_in_dim.35
  11.7 0.2 convolution_bitcast_fusion.6
  11.9 0.2 convolution_bitcast_fusion.7
  12.1 0.2 broadcast_in_dim.36
  12.3 0.2 convolution_bitcast_fusion.5
  12.5 0.2 convolution_bitcast_fusion.4
  12.7 5.0 %collective-permute-start.2 = (f32[2,128,128]{2,1,0:T(8,128)S(1)}, f32[2,128,128]{2,1,0:T(8,128)S(1)}, u32[]{:S(2)}, u32[]{:S(2)}) collective-permute-start(f32[2,128,128]{2,1,0:T(8,128)S(1)} %maximum_add_fusion.1), channel_id=1, source_target_pairs={{0,3},{1,4},{2,5},{3,6},{4,7},{8,11},{9,12},{10,13},{11,14},{12,15... | collective-permute-start | bytes 393224 | tf_op jit(solution)/shard_map/ppermute | solution.py:87
  17.7 1.9 %collective-permute-start.3 = (f32[2,128,128]{2,1,0:T(8,128)S(1)}, f32[2,128,128]{2,1,0:T(8,128)S(1)}, u32[]{:S(2)}, u32[]{:S(2)}) collective-permute-start(f32[2,128,128]{2,1,0:T(8,128)S(1)} %maximum_add_fusion.1), channel_id=1, source_target_pairs={{0,6},{1,7},{8,14},{9,15},{16,22},{17,23},{24,30},{25,31}} | collective-permute-start | bytes 393224 | tf_op jit(solution)/shard_map/ppermute | solution.py:87
  19.7 0.9 %slice-done = bf16[128,512]{1,0:T(8,128)(2,1)S(1)} async-done(((bf16[128,640]{1,0:T(8,128)(2,1)}), bf16[128,512]{1,0:T(8,128)(2,1)S(1)}, s32[]{:S(2)}) %slice-start) | async-done | bytes 131096 | tf_op jit(solution)/shard_map/slice | solution.py:237
  20.6 0.8 %fusion.40 = (bf16[384,256]{1,0:T(8,128)(2,1)}, bf16[384,256]{1,0:T(8,128)(2,1)}) fusion(bf16[384,512]{1,0:T(8,128)(2,1)S(1)} %maximum_maximum_fusion), kind=kLoop, calls=%fused_computation.67 | loop fusion | bytes 786432 | tf_op jit(solution)/shard_map/slice | solution.py:257
  21.4 11.5 %shard_map.110 = (f32[128,1792]{1,0:T(8,128)}, f32[128,1792]{1,0:T(8,128)}, f32[384,256]{1,0:T(8,128)}, f32[384,256]{1,0:T(8,128)}) custom-call(s32[3]{0:T(128)} %pad_add_fusion.info_ref, bf16[128,1792]{1,0:T(8,128)(2,1)} %bitcast.81, bf16[128,1792]{1,0:T(8,128)(2,1)} %bitcast.83, bf16[384,256]{1,0:T(8,128)(2,1)} %get-tuple-element.26.k_ref, ...), custom_call_target="tpu_custom_call" | custom-call | flops 1056964608 | bytes 3932160 | tf_op jit(solution)/shard_map/pallas_call | solution.py:242
  32.9 1.1 %convert.16 = bf16[384,256]{1,0:T(8,128)(2,1)S(1)} convert(f32[384,256]{1,0:T(8,128)} %get-tuple-element.22) | non-fusion elementwise | flops 98304 | bytes 589824 | tf_op jit(solution)/shard_map/convert.7
  33.9 0.0 copy-done.4
  34.0 0.7 add_convert_fusion.1.prior_ref
  34.7 10.2 %shard_map.111 = (bf16[128,1792]{1,0:T(8,128)(2,1)}, bf16[128,1792]{1,0:T(8,128)(2,1)}, f32[2,128,128]{2,1,0:T(8,128)}, f32[1,1792]{1,0:T(1,128)}, f32[128,256]{1,0:T(8,128)}, /*index=5*/f32[128,256]{1,0:T(8,128)}) custom-call(bf16[128,1792]{1,0:T(8,128)(2,1)} %bitcast.82, bf16[128,1792]{1,0:T(8,128)(2,1)} %bitcast.84, bf16[128,256]{1,0:T(8,128)(2,1)} %bitcast.68, ...), custom_call_target="tpu_custom_call" | custom-call | flops 587202560 | bytes 4456448 | tf_op jit(solution)/shard_map/pallas_call | solution.py:258
  44.9 0.7 reduce
  45.6 1.0 %maximum_maximum_fusion.2 = f32[272,128]{1,0:T(8,128)S(1)} fusion(f32[14,128]{1,0:T(8,128)S(1)} %bitcast.86, f32[256,128]{1,0:T(8,128)} %bitcast.85, f32[272]{0:T(512)S(1)} %pad.10.clone), kind=kLoop, calls=%fused_computation.11 | loop fusion | flops 69632 | bytes 278592 | tf_op jit(solution)/shard_map/concatenate | solution.py:280
  46.6 0.6 collective-permute-start.4
  47.3 1.3 %collective-permute-start.7 = (bf16[128,512]{1,0:T(8,128)(2,1)S(1)}, bf16[128,512]{1,0:T(8,128)(2,1)S(1)}, u32[]{:S(2)}, u32[]{:S(2)}) collective-permute-start(bf16[128,512]{1,0:T(8,128)(2,1)S(1)} %pad_maximum_fusion), channel_id=1, source_target_pairs={{1,0},{2,1},{3,2},{4,3},{5,4},{6,5},{7,6},{9,8},{10,9},{11,10},{12... | collective-permute-start | bytes 393224 | tf_op jit(solution)/shard_map/ppermute | solution.py:87
  48.6 2.3 %collective-permute-start.5 = (f32[272,128]{1,0:T(8,128)S(1)}, f32[272,128]{1,0:T(8,128)S(1)}, u32[]{:S(2)}, u32[]{:S(2)}) collective-permute-start(f32[272,128]{1,0:T(8,128)S(1)} %add.65), channel_id=1, source_target_pairs={{0,2},{1,3},{2,0},{3,1},{4,6},{5,7},{6,4},{7,5},{8,10},{9,11},{10,... | collective-permute-start | bytes 417800 | tf_op jit(solution)/shard_map/ppermute | solution.py:44
  50.9 1.3 %collective-permute-start.8 = (bf16[128,512]{1,0:T(8,128)(2,1)S(1)}, bf16[128,512]{1,0:T(8,128)(2,1)S(1)}, u32[]{:S(2)}, u32[]{:S(2)}) collective-permute-start(bf16[128,512]{1,0:T(8,128)(2,1)S(1)} %pad_maximum_fusion.1), channel_id=1, source_target_pairs={{2,0},{3,1},{4,2},{5,3},{6,4},{7,5},{10,8},{11,9},{12,10},{13,11},... | collective-permute-start | bytes 393224 | tf_op jit(solution)/shard_map/ppermute | solution.py:87
  52.3 5.8 %collective-permute-done.5 = f32[272,128]{1,0:T(8,128)S(1)} collective-permute-done((f32[272,128]{1,0:T(8,128)S(1)}, f32[272,128]{1,0:T(8,128)S(1)}, u32[]{:S(2)}, u32[]{:S(2)}) %collective-permute-start.5) | collective-permute-done | bytes 139296 | tf_op jit(solution)/shard_map/ppermute | solution.py:44
  58.1 0.1 collective-permute-start.6
  58.2 1.3 %collective-permute-done.8 = bf16[128,512]{1,0:T(8,128)(2,1)S(1)} collective-permute-done((bf16[128,512]{1,0:T(8,128)(2,1)S(1)}, bf16[128,512]{1,0:T(8,128)(2,1)S(1)}, u32[]{:S(2)}, u32[]{:S(2)}) %collective-permute-start.8) | collective-permute-done | bytes 131104 | tf_op jit(solution)/shard_map/ppermute | solution.py:87
  59.6 3.6 %collective-permute-done.6 = f32[272,128]{1,0:T(8,128)S(1)} collective-permute-done((f32[272,128]{1,0:T(8,128)S(1)}, f32[272,128]{1,0:T(8,128)S(1)}, u32[]{:S(2)}, u32[]{:S(2)}) %collective-permute-start.6) | collective-permute-done | bytes 139296 | tf_op jit(solution)/shard_map/ppermute | solution.py:44
  63.3 0.1 slice_add_fusion.4
  63.5 0.1 slice_add_fusion.3
  63.6 1.6 %collective-permute-start.9 = (f32[1792]{0:T(1024)S(1)}, f32[1792]{0:T(1024)S(1)}, u32[]{:S(2)}, u32[]{:S(2)}) collective-permute-start(f32[1792]{0:T(1024)S(1)} %fusion.39), channel_id=1, source_target_pairs={{0,8},{8,0},{16,24},{24,16},{1,9},{9,1},{17,25},{25,17},{2,10},{10... | collective-permute-start | bytes 21512 | tf_op jit(solution)/shard_map/ppermute | solution.py:79
  65.3 0.1 slice_add_fusion.2
  65.4 0.1 slice_add_fusion.1
  65.5 1.8 %collective-permute-done.9 = f32[1792]{0:T(1024)S(1)} collective-permute-done((f32[1792]{0:T(1024)S(1)}, f32[1792]{0:T(1024)S(1)}, u32[]{:S(2)}, u32[]{:S(2)}) %collective-permute-start.9) | collective-permute-done | bytes 7200 | tf_op jit(solution)/shard_map/ppermute | solution.py:79
  67.3 2.6 %collective-permute-start.10 = (f32[1792]{0:T(1024)S(1)}, f32[1792]{0:T(1024)S(1)}, u32[]{:S(2)}, u32[]{:S(2)}) collective-permute-start(f32[1792]{0:T(1024)S(1)} %add.79), channel_id=1, source_target_pairs={{0,16},{8,24},{16,0},{24,8},{1,17},{9,25},{17,1},{25,9},{2,18},{10... | collective-permute-start | bytes 21512 | tf_op jit(solution)/shard_map/ppermute | solution.py:79
  69.9 1.6 %fusion.8 = (bf16[1,128,256]{2,1,0:T(8,128)(2,1)}, bf16[1,128,256]{2,1,0:T(8,128)(2,1)}) fusion(f32[128,512]{1,0:T(8,128)S(1)} %convert_add_fusion, f32[384,256]{1,0:T(8,128)S(1)} %copy-done.4, f32[16,8,2,128]{3,2,1,0:T(2,128)S(1)} %bitcast.76, f32[128,128]{1,0:T(8,128)S(1)} %slice_add_fusion.1, f32[128,128]{1,0:T(8,128)S(1)} %slice_add_fusion.2, ...), kind=kLoop, calls=%fused_computation.36 | loop fusion | flops 294912 | bytes 1048576 | tf_op jit(solution)/shard_map/broadcast_in_dim | solution.py:328
  71.6 0.3 collective-permute-done.10
  71.9 0.6 add_multiply_fusion
  (51 shorter events, 0.4 us)
Async XLA Ops:
  0.6 0.9 %copy-start.5 = (bf16[1,128,256]{2,1,0:T(8,128)(2,1)S(1)}, bf16[1,128,256]{2,1,0:T(8,128)(2,1)}, u32[]{:S(2)}) copy-start(bf16[1,128,256]{2,1,0:T(8,128)(2,1)} %param.9) | copy-start | bytes 196612
  1.5 0.8 %copy-start = (bf16[1,128,256]{2,1,0:T(8,128)(2,1)S(1)}, bf16[1,128,256]{2,1,0:T(8,128)(2,1)}, u32[]{:S(2)}) copy-start(bf16[1,128,256]{2,1,0:T(8,128)(2,1)} %param.8) | copy-start | bytes 196612
  2.3 6.4 %copy-start.10 = (s32[1,128,2]{1,2,0:T(2,128)S(1)}, s32[1,128,2]{1,2,0:T(2,128)}, u32[]{:S(2)}) copy-start(s32[1,128,2]{1,2,0:T(2,128)} %param.10) | copy-start | bytes 3076
  2.3 9.1 %collective-permute-start = (bf16[128,640]{1,0:T(8,128)(2,1)S(1)}, bf16[128,640]{1,0:T(8,128)(2,1)S(1)}, u32[]{:S(2)}, u32[]{:S(2)}) collective-permute-start(bf16[128,640]{1,0:T(8,128)(2,1)S(1)} %maximum_maximum_fusion.1), channel_id=1, source_target_pairs={{0,2},{1,3},{2,4},{3,5},{4,6},{5,7},{8,10},{9,11},{10,12},{11,13},... | collective-permute-start | bytes 491528 | tf_op jit(solution)/shard_map/ppermute | solution.py:87
  7.2 4.8 %collective-permute-start.1 = (bf16[128,640]{1,0:T(8,128)(2,1)S(1)}, bf16[128,640]{1,0:T(8,128)(2,1)S(1)}, u32[]{:S(2)}, u32[]{:S(2)}) collective-permute-start(bf16[128,640]{1,0:T(8,128)(2,1)S(1)} %maximum_maximum_fusion.1), channel_id=1, source_target_pairs={{0,1},{1,2},{2,3},{3,4},{4,5},{5,6},{6,7},{8,9},{9,10},{10,11},{11... | collective-permute-start | bytes 491528 | tf_op jit(solution)/shard_map/ppermute | solution.py:87
  9.0 2.2 %copy-start.2 = (bf16[128,256]{1,0:T(8,128)(2,1)}, bf16[128,256]{1,0:T(8,128)(2,1)S(1)}, u32[]{:S(2)}) copy-start(bf16[128,256]{1,0:T(8,128)(2,1)S(1)} %fusion.2.s_ref) | copy-start | bytes 196612
  9.3 1.3 %copy-start.9 = (f32[1792]{0:T(1024)S(1)}, f32[1792]{0:T(1024)}, u32[]{:S(2)}) copy-start(f32[1792]{0:T(1024)} %param.12) | copy-start | bytes 21508
  9.3 0.7 copy-start.11
  11.4 8.3 %copy-start.6 = (bf16[128,640]{1,0:T(8,128)(2,1)}, bf16[128,640]{1,0:T(8,128)(2,1)S(1)}, u32[]{:S(2)}) copy-start(bf16[128,640]{1,0:T(8,128)(2,1)S(1)} %collective-permute-done) | copy-start | bytes 491524
  12.7 21.3 %collective-permute-start.2 = (f32[2,128,128]{2,1,0:T(8,128)S(1)}, f32[2,128,128]{2,1,0:T(8,128)S(1)}, u32[]{:S(2)}, u32[]{:S(2)}) collective-permute-start(f32[2,128,128]{2,1,0:T(8,128)S(1)} %maximum_add_fusion.1), channel_id=1, source_target_pairs={{0,3},{1,4},{2,5},{3,6},{4,7},{8,11},{9,12},{10,13},{11,14},{12,15... | collective-permute-start | bytes 393224 | tf_op jit(solution)/shard_map/ppermute | solution.py:87
  17.7 16.3 %collective-permute-start.3 = (f32[2,128,128]{2,1,0:T(8,128)S(1)}, f32[2,128,128]{2,1,0:T(8,128)S(1)}, u32[]{:S(2)}, u32[]{:S(2)}) collective-permute-start(f32[2,128,128]{2,1,0:T(8,128)S(1)} %maximum_add_fusion.1), channel_id=1, source_target_pairs={{0,6},{1,7},{8,14},{9,15},{16,22},{17,23},{24,30},{25,31}} | collective-permute-start | bytes 393224 | tf_op jit(solution)/shard_map/ppermute | solution.py:87
  19.7 0.9 %slice-start = ((bf16[128,640]{1,0:T(8,128)(2,1)}), bf16[128,512]{1,0:T(8,128)(2,1)S(1)}, s32[]{:S(2)}) async-start(bf16[128,640]{1,0:T(8,128)(2,1)} %copy-done.6), calls=%async_computation | async-start | bytes 262144 | tf_op jit(solution)/shard_map/slice | solution.py:237
  32.9 1.1 %copy-start.4 = (f32[384,256]{1,0:T(8,128)S(1)}, f32[384,256]{1,0:T(8,128)}, u32[]{:S(2)}) copy-start(f32[384,256]{1,0:T(8,128)} %get-tuple-element.23) | copy-start | bytes 1179652
  46.6 1.9 %collective-permute-start.4 = (f32[272,128]{1,0:T(8,128)S(1)}, f32[272,128]{1,0:T(8,128)S(1)}, u32[]{:S(2)}, u32[]{:S(2)}) collective-permute-start(f32[272,128]{1,0:T(8,128)S(1)} %maximum_maximum_fusion.2), channel_id=1, source_target_pairs={{0,1},{1,0},{2,3},{3,2},{4,5},{5,4},{6,7},{7,6},{8,9},{9,8},{10,11... | collective-permute-start | bytes 417800 | tf_op jit(solution)/shard_map/ppermute | solution.py:44
  47.3 10.9 %collective-permute-start.7 = (bf16[128,512]{1,0:T(8,128)(2,1)S(1)}, bf16[128,512]{1,0:T(8,128)(2,1)S(1)}, u32[]{:S(2)}, u32[]{:S(2)}) collective-permute-start(bf16[128,512]{1,0:T(8,128)(2,1)S(1)} %pad_maximum_fusion), channel_id=1, source_target_pairs={{1,0},{2,1},{3,2},{4,3},{5,4},{6,5},{7,6},{9,8},{10,9},{11,10},{12... | collective-permute-start | bytes 393224 | tf_op jit(solution)/shard_map/ppermute | solution.py:87
  48.6 9.5 %collective-permute-start.5 = (f32[272,128]{1,0:T(8,128)S(1)}, f32[272,128]{1,0:T(8,128)S(1)}, u32[]{:S(2)}, u32[]{:S(2)}) collective-permute-start(f32[272,128]{1,0:T(8,128)S(1)} %add.65), channel_id=1, source_target_pairs={{0,2},{1,3},{2,0},{3,1},{4,6},{5,7},{6,4},{7,5},{8,10},{9,11},{10,... | collective-permute-start | bytes 417800 | tf_op jit(solution)/shard_map/ppermute | solution.py:44
  50.9 8.6 %collective-permute-start.8 = (bf16[128,512]{1,0:T(8,128)(2,1)S(1)}, bf16[128,512]{1,0:T(8,128)(2,1)S(1)}, u32[]{:S(2)}, u32[]{:S(2)}) collective-permute-start(bf16[128,512]{1,0:T(8,128)(2,1)S(1)} %pad_maximum_fusion.1), channel_id=1, source_target_pairs={{2,0},{3,1},{4,2},{5,3},{6,4},{7,5},{10,8},{11,9},{12,10},{13,11},... | collective-permute-start | bytes 393224 | tf_op jit(solution)/shard_map/ppermute | solution.py:87
  58.1 5.1 %collective-permute-start.6 = (f32[272,128]{1,0:T(8,128)S(1)}, f32[272,128]{1,0:T(8,128)S(1)}, u32[]{:S(2)}, u32[]{:S(2)}) collective-permute-start(f32[272,128]{1,0:T(8,128)S(1)} %add.67), channel_id=1, source_target_pairs={{0,4},{1,5},{2,6},{3,7},{4,0},{5,1},{6,2},{7,3},{8,12},{9,13},{10,... | collective-permute-start | bytes 417800 | tf_op jit(solution)/shard_map/ppermute | solution.py:44
  59.6 3.7 %copy-start.3 = (bf16[128,256]{1,0:T(8,128)(2,1)S(1)}, bf16[128,256]{1,0:T(8,128)(2,1)}, u32[]{:S(2)}) copy-start(bf16[128,256]{1,0:T(8,128)(2,1)} %copy-done.2) | copy-start | bytes 196612
  59.6 3.7 %copy-start.8 = (f32[128,256]{1,0:T(8,128)S(1)}, f32[128,256]{1,0:T(8,128)}, u32[]{:S(2)}) copy-start(f32[128,256]{1,0:T(8,128)} %get-tuple-element.19) | copy-start | bytes 393220
  63.4 1.8 %copy-start.1 = (bf16[1,128,256]{2,1,0:T(8,128)(2,1)S(1)}, bf16[1,128,256]{2,1,0:T(8,128)(2,1)}, u32[]{:S(2)}) copy-start(bf16[1,128,256]{2,1,0:T(8,128)(2,1)} %param.8) | copy-start | bytes 196612
  63.4 1.8 %copy-start.7 = (f32[128,256]{1,0:T(8,128)S(1)}, f32[128,256]{1,0:T(8,128)}, u32[]{:S(2)}) copy-start(f32[128,256]{1,0:T(8,128)} %get-tuple-element.24) | copy-start | bytes 393220
  63.6 3.7 %collective-permute-start.9 = (f32[1792]{0:T(1024)S(1)}, f32[1792]{0:T(1024)S(1)}, u32[]{:S(2)}, u32[]{:S(2)}) collective-permute-start(f32[1792]{0:T(1024)S(1)} %fusion.39), channel_id=1, source_target_pairs={{0,8},{8,0},{16,24},{24,16},{1,9},{9,1},{17,25},{25,17},{2,10},{10... | collective-permute-start | bytes 21512 | tf_op jit(solution)/shard_map/ppermute | solution.py:79
  67.3 4.5 %collective-permute-start.10 = (f32[1792]{0:T(1024)S(1)}, f32[1792]{0:T(1024)S(1)}, u32[]{:S(2)}, u32[]{:S(2)}) collective-permute-start(f32[1792]{0:T(1024)S(1)} %add.79), channel_id=1, source_target_pairs={{0,16},{8,24},{16,0},{24,8},{1,17},{9,25},{17,1},{25,9},{2,18},{10... | collective-permute-start | bytes 21512 | tf_op jit(solution)/shard_map/ppermute | solution.py:79

commit v9 on v8

--- a/solution.py
+++ b/solution.py
@@ -1,3 +1,5 @@
+import functools
+
 import jax
 import jax.numpy as jnp
 from jax import lax
@@ -39,15 +41,18 @@
     place = lax.axis_index(axis)
     group = part
     before = jnp.zeros_like(part)
+    first = None
     step = 1
     while step < count:
         got = lax.ppermute(group, axis, [(i, i ^ step) for i in range(count)])
+        if first is None:
+            first = got
         partner = jnp.bitwise_xor(place, step)
         take = partner > place if reverse else partner < place
         before = before + jnp.where(take, got, 0.0)
         group = group + got
         step *= 2
-    return before, group
+    return before, group, first
 
 
 def spread_scan(near, own, axis):
@@ -87,7 +92,7 @@
     return lax.ppermute(block, axis, route)
 
 
-def window_kernel(info_ref, q_ref, c_ref, k_ref, v_ref, wout_ref, wdq_ref, dk_ref, dv_ref):
+def window_kernel(group, info_ref, q_ref, c_ref, k_ref, v_ref, wout_ref, wdq_ref, dk_ref, dv_ref):
     group_size = QUERY_HEADS // KEY_VALUE_HEADS
     token_rows = q_ref.shape[0]
     window_rows = k_ref.shape[0]
@@ -96,38 +101,60 @@
     row = lax.broadcasted_iota(jnp.int32, (token_rows, window_rows), 0)
     col = lax.broadcasted_iota(jnp.int32, (token_rows, window_rows), 1)
     back = row + padding_rows - col
-    seen = (back >= 0) & (col + info_ref[2] >= 0)
-    for g in range(KEY_VALUE_HEADS):
-        visible = seen & (back < info_ref[g])
-        lanes = slice(g * HEAD_SIZE, (g + 1) * HEAD_SIZE)
-        kg = k_ref[:, lanes]
-        vg = v_ref[:, lanes]
-        dk = jnp.zeros((window_rows, HEAD_SIZE), jnp.float32)
-        dv = jnp.zeros((window_rows, HEAD_SIZE), jnp.float32)
-        for h in range(group_size):
-            cols = slice((g * group_size + h) * HEAD_SIZE, (g * group_size + h + 1) * HEAD_SIZE)
-            qh = q_ref[:, cols]
-            ch = c_ref[:, cols]
-            s = lax.dot_general(qh, kg, (((1,), (1,)), ((), ())), preferred_element_type=jnp.float32) * scale
-            s = jnp.where(visible, s, -1e30)
-            top = jnp.max(s, axis=-1, keepdims=True)
-            e = jnp.exp(s - top)
-            p = e * (1.0 / jnp.sum(e, axis=-1, keepdims=True))
-            ph = p.astype(jnp.bfloat16)
-            wout = jnp.dot(ph, vg, preferred_element_type=jnp.float32)
-            wout_ref[:, cols] = wout
-            gp = lax.dot_general(ch, vg, (((1,), (1,)), ((), ())), preferred_element_type=jnp.float32)
-            delta = jnp.sum(ch.astype(jnp.float32) * wout, axis=-1, keepdims=True)
-            ds = (p * (gp - delta) * scale).astype(jnp.bfloat16)
-            wdq_ref[:, cols] = jnp.dot(ds, kg, preferred_element_type=jnp.float32)
-            dk = dk + lax.dot_general(ds, qh, (((0,), (0,)), ((), ())), preferred_element_type=jnp.float32)
-            dv = dv + lax.dot_general(ph, ch, (((0,), (0,)), ((), ())), preferred_element_type=jnp.float32)
-        dk_ref[:, lanes] = dk
-        dv_ref[:, lanes] = dv
-
-
-def linear_kernel(q_ref, c_ref, k_ref, s_ref, prior_ref, gain_ref, wout_ref, wdq_ref,
-                  mixed_ref, dq_ref, suffix_ref, gsum_ref, ldk_ref, dsp_ref):
+    visible = (back >= 0) & (col + info_ref[KEY_VALUE_HEADS] >= 0) & (back < info_ref[group])
+    lanes = slice(group * HEAD_SIZE, (group + 1) * HEAD_SIZE)
+    kg = k_ref[:, lanes]
+    vg = v_ref[:, lanes]
+    dk = jnp.zeros((window_rows, HEAD_SIZE), jnp.float32)
+    dv = jnp.zeros((window_rows, HEAD_SIZE), jnp.float32)
+    for h in range(group_size):
+        head = group * group_size + h
+        cols = slice(head * HEAD_SIZE, (head + 1) * HEAD_SIZE)
+        here = slice(h * HEAD_SIZE, (h + 1) * HEAD_SIZE)
+        qh = q_ref[:, cols]
+        ch = c_ref[:, cols]
+        s = lax.dot_general(qh, kg, (((1,), (1,)), ((), ())), preferred_element_type=jnp.float32) * scale
+        s = jnp.where(visible, s, -1e30)
+        top = jnp.max(s, axis=-1, keepdims=True)
+        e = jnp.exp(s - top)
+        p = e * (1.0 / jnp.sum(e, axis=-1, keepdims=True))
+        ph = p.astype(jnp.bfloat16)
+        wout = jnp.dot(ph, vg, preferred_element_type=jnp.float32)
+        wout_ref[:, here] = wout
+        gp = lax.dot_general(ch, vg, (((1,), (1,)), ((), ())), preferred_element_type=jnp.float32)
+        delta = jnp.sum(ch.astype(jnp.float32) * wout, axis=-1, keepdims=True)
+        ds = (p * (gp - delta) * scale).astype(jnp.bfloat16)
+        wdq_ref[:, here] = jnp.dot(ds, kg, preferred_element_type=jnp.float32)
+        dk = dk + lax.dot_general(ds, qh, (((0,), (0,)), ((), ())), preferred_element_type=jnp.float32)
+        dv = dv + lax.dot_general(ph, ch, (((0,), (0,)), ((), ())), preferred_element_type=jnp.float32)
+    dk_ref[...] = dk
+    dv_ref[...] = dv
+
+
+def window_call(group, info, q, c, key_window, value_window):
+    token_rows = q.shape[0]
+    window_rows = key_window.shape[0]
+    half = QUERY_HEADS * HEAD_SIZE // KEY_VALUE_HEADS
+    return pl.pallas_call(
+        functools.partial(window_kernel, group),
+        out_shape=(
+            jax.ShapeDtypeStruct((token_rows, half), jnp.float32),
+            jax.ShapeDtypeStruct((token_rows, half), jnp.float32),
+            jax.ShapeDtypeStruct((window_rows, HEAD_SIZE), jnp.float32),
+            jax.ShapeDtypeStruct((window_rows, HEAD_SIZE), jnp.float32),
+        ),
+        in_specs=[pl.BlockSpec(memory_space=pltpu.SMEM)] + in_vmem(4),
+        out_specs=tuple(in_vmem(4)),
+        cost_estimate=pl.CostEstimate(
+            flops=12 * (QUERY_HEADS // KEY_VALUE_HEADS) * token_rows * window_rows * HEAD_SIZE,
+            transcendentals=(QUERY_HEADS // KEY_VALUE_HEADS) * token_rows * window_rows,
+            bytes_accessed=token_rows * half * (2 + 2 + 4 + 4) + 2 * window_rows * HEAD_SIZE * (2 + 4),
+        ),
+    )(info, q, c, key_window, value_window)
+
+
+def linear_kernel(q_ref, c_ref, k_ref, s_ref, prior_ref, gain_ref,
+                  gn_ref, ldq_ref, suffix_ref, gsum_ref, ldk_ref, dsp_ref):
     group_size = QUERY_HEADS // KEY_VALUE_HEADS
     token_rows = q_ref.shape[0]
     row = lax.broadcasted_iota(jnp.int32, (token_rows, token_rows), 0)
@@ -156,7 +183,7 @@
             )
             inverse_root = 1.0 / jnp.sqrt(jnp.mean(lin * lin, axis=-1, keepdims=True) + epsilon)
             normed = lin * inverse_root
-            mixed_ref[:, cols] = (gh * normed + wout_ref[:, cols]).astype(mixed_ref.dtype)
+            gn_ref[:, cols] = gh * normed
             gsum_ref[:, cols] = jnp.sum(ch * normed, axis=0, keepdims=True)
             scaled = ch * gh
             dl = ((scaled - normed * jnp.mean(scaled * normed, axis=-1, keepdims=True)) * inverse_root).astype(
@@ -170,7 +197,7 @@
             ).astype(jnp.bfloat16)
             ldq = lax.dot_general(dl, pg, (((1,), (1,)), ((), ())), preferred_element_type=jnp.float32)
             ldq = ldq + jnp.dot(bh, kg, preferred_element_type=jnp.float32)
-            dq_ref[:, cols] = (ldq + wdq_ref[:, cols]).astype(dq_ref.dtype)
+            ldq_ref[:, cols] = ldq
             ldk = ldk + lax.dot_general(bh, qh, (((0,), (0,)), ((), ())), preferred_element_type=jnp.float32)
             dsp = dsp + lax.dot_general(lh, dl, (((0,), (0,)), ((), ())), preferred_element_type=jnp.float32)
         suffix_ref[g] = suffix
@@ -239,40 +266,27 @@
     info = jnp.concatenate(
         [window_lengths.astype(jnp.int32), (lax.axis_index("ctx") * token_rows - padding_rows).reshape(1)]
     ).astype(jnp.int32)
-    wout, wdq, dk_win, dv_win = pl.pallas_call(
-        window_kernel,
+    key_window = window_packed[:, :key_value_width]
+    value_window = window_packed[:, key_value_width:]
+    first_piece = window_call(0, info, q, c, key_window, value_window)
+    gn, ldq, suffix_local, gain_local, ldk, dsp = pl.pallas_call(
+        linear_kernel,
         out_shape=(
             jax.ShapeDtypeStruct((token_rows, width), jnp.float32),
             jax.ShapeDtypeStruct((token_rows, width), jnp.float32),
-            jax.ShapeDtypeStruct((window_rows, key_value_width), jnp.float32),
-            jax.ShapeDtypeStruct((window_rows, key_value_width), jnp.float32),
-        ),
-        in_specs=[pl.BlockSpec(memory_space=pltpu.SMEM)] + in_vmem(4),
-        out_specs=tuple(in_vmem(4)),
-        cost_estimate=pl.CostEstimate(
-            flops=12 * QUERY_HEADS * token_rows * window_rows * HEAD_SIZE,
-            transcendentals=QUERY_HEADS * token_rows * window_rows,
-            bytes_accessed=2 * token_rows * width * (2 + 4) + 2 * window_rows * key_value_width * (2 + 4),
-        ),
-    )(info, q, c, window_packed[:, :key_value_width], window_packed[:, key_value_width:])
-    mixed, d_queries, suffix_local, gain_local, ldk, dsp = pl.pallas_call(
-        linear_kernel,
-        out_shape=(
-            jax.ShapeDtypeStruct((token_rows, width), jnp.bfloat16),
-            jax.ShapeDtypeStruct((token_rows, width), jnp.bfloat16),
             jax.ShapeDtypeStruct((KEY_VALUE_HEADS, HEAD_SIZE, HEAD_SIZE), jnp.float32),
             jax.ShapeDtypeStruct((1, width), jnp.float32),
             jax.ShapeDtypeStruct((token_rows, key_value_width), jnp.float32),
             jax.ShapeDtypeStruct((token_rows, key_value_width), jnp.float32),
         ),
-        in_specs=in_vmem(8),
+        in_specs=in_vmem(6),
         out_specs=tuple(in_vmem(6)),
         cost_estimate=pl.CostEstimate(
             flops=20 * QUERY_HEADS * token_rows * token_rows * HEAD_SIZE,
             transcendentals=QUERY_HEADS * token_rows,
-            bytes_accessed=token_rows * width * (2 + 2 + 4 + 4 + 2 + 2) + 6 * token_rows * key_value_width * 4,
-        ),
-    )(q, c, k, spiked, prior_half, gain.reshape(1, width), wout, wdq)
+            bytes_accessed=token_rows * width * (2 + 2 + 4 + 4) + 6 * token_rows * key_value_width * 4,
+        ),
+    )(q, c, k, spiked, prior_half, gain.reshape(1, width))
     total_tokens = queries.shape[0] * lax.axis_size("dp") * token_rows * lax.axis_size("ctx")
     state_rows = KEY_VALUE_HEADS * HEAD_SIZE
     gain_rows = width // HEAD_SIZE
@@ -285,7 +299,16 @@
         ],
         axis=0,
     )
-    later_rows, total_rows = butterfly_scan(riding, "ctx", True)
+    later_rows, total_rows, first_round = butterfly_scan(riding, "ctx", True)
+    late_q, _ = lax.optimization_barrier((q, first_round))
+    second_piece = window_call(1, info, late_q, c, key_window, value_window)
+    pieces = (first_piece, second_piece)
+    window_out = jnp.concatenate([piece[0] for piece in pieces], axis=1)
+    window_dq = jnp.concatenate([piece[1] for piece in pieces], axis=1)
+    dk_win = jnp.concatenate([piece[2] for piece in pieces], axis=1)
+    dv_win = jnp.concatenate([piece[3] for piece in pieces], axis=1)
+    mixed = (gn + window_out).astype(jnp.bfloat16)
+    d_queries = (ldq + window_dq).astype(jnp.bfloat16)
     later_half = later_rows[:state_rows].reshape(suffix_local.shape).astype(jnp.bfloat16)
     gain_ctx = total_rows[state_rows : state_rows + gain_rows].reshape(width)
     d_gain = all_sum(gain_ctx, ("dp",)) * (total_tokens ** (-0.5))

time: 73.1 us -> 73.7 us (level)
  waiting for transfers between devices: 13 us -> 7.11 us
  starting transfers between devices: 23.1 us -> 25.6 us
  local copies, waits for them, and re-layouts: 5.43 us -> 7.48 us
  Pallas kernels: 21.7 us -> 23.1 us
    ppermute x3, waiting for transfers between devices: 9.48 us -> 3.8 us  [butterfly_scan(): got = lax.ppermute(group, axis, [(i, i ^ step) for i in range(count)])]
    ppermute x3, starting transfers between devices: 3 us -> 5.46 us  [butterfly_scan(): got = lax.ppermute(group, axis, [(i, i ^ step) for i in range(count)])]
    broadcast_in_dim x0 -> x1, other arithmetic: none -> 2.3 us  [per_device(): d_queries[None]]
    pallas_call x1 -> x2, Pallas kernels: 11.5 us -> 13.4 us  [window_call(): pl.pallas_call(functools.partial(window_kernel, group), out_shape=(jax.Sh...]
    concatenate x0 -> x1, local copies, waits for them, and re-layouts: none -> 1.13 us  [per_device(): dk_win = jnp.concatenate([piece[2] for piece in pieces], axis=1)]
    ppermute x6, waiting for transfers between devices: 1.35 us -> 0.26 us  [shifted(): return lax.ppermute(block, axis, route)]
    another operation x3, other arithmetic: 1.13 us -> 0.08 us
    unnamed x25 -> x37, local copies, waits for them, and re-layouts: 2.3 us -> 3.21 us
  transfers between devices with their start and end apart: 11 -> 11, of which waited for: 5 -> 4; matrix products, arithmetic and copies ran while one was open for 9% -> 11% of each run, Pallas kernels for 16% -> 18%
where the time goes in v9:
time: 73.7 us; the launch traced here: 73.1 us
  starting transfers between devices  25.6 us (35%)
  Pallas kernels  23.1 us (31%)
  local copies, waits for them, and re-layouts  7.48 us (10%)
  waiting for transfers between devices  7.11 us (10%)
  other arithmetic  7.06 us (10%)
  matrix products  1.67 us (2%)
  between operations  1.1 us (1%)
    ppermute x6, starting transfers between devices, shifted(): return lax.ppermute(block, axis, route)  15.9 us
    pallas_call x2, Pallas kernels, window_call(): pl.pallas_call(functools.partial(window_kernel, group), out_shape=(jax.Sh...  13.4 us
    pallas_call x1, Pallas kernels, per_device(): pl.pallas_call(linear_kernel, out_shape=(jax.ShapeDtypeStruct((token_rows...  9.73 us
    ppermute x3, starting transfers between devices, butterfly_scan(): got = lax.ppermute(group, axis, [(i, i ^ step) for i in range(count)])  5.46 us
    ppermute x2, starting transfers between devices, all_sum(): part = part + lax.ppermute(part, axes, route)  4.23 us
    ppermute x3, waiting for transfers between devices, butterfly_scan(): got = lax.ppermute(group, axis, [(i, i ^ step) for i in range(count)])  3.8 us
    unnamed x37, local copies, waits for them, and re-layouts  3.21 us
    ppermute x2, waiting for transfers between devices, all_sum(): part = part + lax.ppermute(part, axes, route)  3.04 us
  transfers between devices with their start and end apart: 11, of which 4 were waited for; matrix products, arithmetic and copies ran while one was open for 11% of the time, Pallas kernels for 18%

profile of v9, /device:TPU:0, one launch (start us, length us, event | category | flops | bytes accessed | tf_op | source)
XLA Modules:
  0.0 73.1 jit_solution(5682546995601793942)
XLA Ops:
  0.6 0.8 %copy.13 = s32[1,128,2]{2,1,0:T(8,128)S(1)} copy(s32[1,128,2]{1,2,0:T(2,128)} %param.10) | data formatting | bytes 2048 | tf_op args[3]
  1.5 0.1 pad.30.clone
  1.6 0.7 copy-done
  2.3 4.9 %collective-permute-start = (bf16[128,640]{1,0:T(8,128)(2,1)S(1)}, bf16[128,640]{1,0:T(8,128)(2,1)S(1)}, u32[]{:S(2)}, u32[]{:S(2)}) collective-permute-start(bf16[128,640]{1,0:T(8,128)(2,1)S(1)} %maximum_maximum_fusion.1), channel_id=1, source_target_pairs={{0,2},{1,3},{2,4},{3,5},{4,6},{5,7},{8,10},{9,11},{10,12},{11,13},... | collective-permute-start | bytes 491528 | tf_op jit(solution)/shard_map/ppermute | solution.py:92
  7.2 1.5 %collective-permute-start.1 = (bf16[128,640]{1,0:T(8,128)(2,1)S(1)}, bf16[128,640]{1,0:T(8,128)(2,1)S(1)}, u32[]{:S(2)}, u32[]{:S(2)}) collective-permute-start(bf16[128,640]{1,0:T(8,128)(2,1)S(1)} %maximum_maximum_fusion.1), channel_id=1, source_target_pairs={{0,1},{1,2},{2,3},{3,4},{4,5},{5,6},{6,7},{8,9},{9,10},{10,11},{11... | collective-permute-start | bytes 491528 | tf_op jit(solution)/shard_map/ppermute | solution.py:92
  8.7 0.1 copy.12
  8.8 0.2 broadcast_in_dim.33
  9.0 0.2 convolution_bitcast_fusion.2
  9.3 0.7 copy-done.16
  9.9 0.7 pad_add_fusion.info_ref
  10.6 0.6 reshape.45.gain_ref
  11.2 0.1 pad.14.clone
  11.3 0.2 convolution_bitcast_fusion.3
  11.5 0.2 broadcast_in_dim.35
  11.7 0.2 convolution_bitcast_fusion.6
  11.9 0.2 convolution_bitcast_fusion.7
  12.1 0.2 broadcast_in_dim.36
  12.4 0.2 convolution_bitcast_fusion.5
  12.5 0.2 convolution_bitcast_fusion.4
  12.8 5.0 %collective-permute-start.2 = (f32[2,128,128]{2,1,0:T(8,128)S(1)}, f32[2,128,128]{2,1,0:T(8,128)S(1)}, u32[]{:S(2)}, u32[]{:S(2)}) collective-permute-start(f32[2,128,128]{2,1,0:T(8,128)S(1)} %maximum_add_fusion.3), channel_id=1, source_target_pairs={{0,3},{1,4},{2,5},{3,6},{4,7},{8,11},{9,12},{10,13},{11,14},{12,15... | collective-permute-start | bytes 393224 | tf_op jit(solution)/shard_map/ppermute | solution.py:92
  17.8 1.9 %collective-permute-start.3 = (f32[2,128,128]{2,1,0:T(8,128)S(1)}, f32[2,128,128]{2,1,0:T(8,128)S(1)}, u32[]{:S(2)}, u32[]{:S(2)}) collective-permute-start(f32[2,128,128]{2,1,0:T(8,128)S(1)} %maximum_add_fusion.3), channel_id=1, source_target_pairs={{0,6},{1,7},{8,14},{9,15},{16,22},{17,23},{24,30},{25,31}} | collective-permute-start | bytes 393224 | tf_op jit(solution)/shard_map/ppermute | solution.py:92
  19.7 0.9 %slice-done = bf16[128,512]{1,0:T(8,128)(2,1)S(1)} async-done(((bf16[128,640]{1,0:T(8,128)(2,1)}), bf16[128,512]{1,0:T(8,128)(2,1)S(1)}, s32[]{:S(2)}) %slice-start) | async-done | bytes 131096 | tf_op jit(solution)/shard_map/slice | solution.py:264
  20.6 0.8 %fusion.44 = (bf16[384,256]{1,0:T(8,128)(2,1)}, bf16[384,256]{1,0:T(8,128)(2,1)}) fusion(bf16[384,512]{1,0:T(8,128)(2,1)S(1)} %maximum_maximum_fusion), kind=kLoop, calls=%fused_computation.77 | loop fusion | bytes 786432 | tf_op jit(solution)/shard_map/slice | solution.py:270
  21.4 6.7 %shard_map.111 = (f32[128,896]{1,0:T(8,128)}, f32[128,896]{1,0:T(8,128)}, f32[384,128]{1,0:T(8,128)}, f32[384,128]{1,0:T(8,128)}) custom-call(s32[3]{0:T(128)} %pad_add_fusion.info_ref, bf16[128,1792]{1,0:T(8,128)(2,1)} %bitcast.85, bf16[128,1792]{1,0:T(8,128)(2,1)} %bitcast.88, bf16[384,256]{1,0:T(8,128)(2,1)} %get-tuple-element.36.k_ref, ...), custom_call_target="tpu_custom_call" | custom-call | flops 528482304 | bytes 1966080 | tf_op jit(solution)/shard_map/pallas_call | solution.py:138
  28.1 0.7 add_convert_fusion.1.prior_ref
  28.7 9.7 %shard_map.110 = (f32[128,1792]{1,0:T(8,128)}, f32[128,1792]{1,0:T(8,128)}, f32[2,128,128]{2,1,0:T(8,128)}, f32[1,1792]{1,0:T(1,128)}, f32[128,256]{1,0:T(8,128)}, /*index=5*/f32[128,256]{1,0:T(8,128)}) custom-call(bf16[128,1792]{1,0:T(8,128)(2,1)} %bitcast.86, bf16[128,1792]{1,0:T(8,128)(2,1)} %bitcast.89, bf16[128,256]{1,0:T(8,128)(2,1)} %bitcast.72, ...), custom_call_target="tpu_custom_call" | custom-call | flops 587202560 | bytes 3538944 | tf_op jit(solution)/shard_map/pallas_call | solution.py:272
  38.5 0.8 %reduce = f32[1792]{0:T(1024)S(1)} reduce(f32[1,1792]{1,0:T(1,128)} %get-tuple-element.23, f32[]{:T(128)} %constant.27), dimensions={0}, to_apply=%get-tuple-element.23.reduce_sub_computation | reduce | bytes 14340 | tf_op jit(solution)/shard_map/pallas_call | solution.py:272
  39.2 1.0 %maximum_maximum_fusion.2 = f32[272,128]{1,0:T(8,128)S(1)} fusion(f32[14,128]{1,0:T(8,128)S(1)} %bitcast.84, f32[256,128]{1,0:T(8,128)} %bitcast.83, f32[272]{0:T(512)S(1)} %pad.14.clone), kind=kLoop, calls=%fused_computation.17 | loop fusion | flops 69632 | bytes 278592 | tf_op jit(solution)/shard_map/concatenate | solution.py:294
  40.2 0.6 collective-permute-start.4
  40.9 0.9 %copy-done.10 = f32[384,128]{1,0:T(8,128)S(1)} copy-done((f32[384,128]{1,0:T(8,128)S(1)}, f32[384,128]{1,0:T(8,128)}, u32[]{:S(2)}) %copy-start.10) | copy-done | bytes 196632
  41.9 6.7 %shard_map.112 = (f32[128,896]{1,0:T(8,128)}, f32[128,896]{1,0:T(8,128)}, f32[384,128]{1,0:T(8,128)}, f32[384,128]{1,0:T(8,128)}) custom-call(s32[3]{0:T(128)} %pad_add_fusion.info_ref, bf16[128,1792]{1,0:T(8,128)(2,1)} %bitcast.87, bf16[128,1792]{1,0:T(8,128)(2,1)} %bitcast.90, bf16[384,256]{1,0:T(8,128)(2,1)} %get-tuple-element.36.k_ref, ...), custom_call_target="tpu_custom_call" | custom-call | flops 528482304 | bytes 1966080 | tf_op jit(solution)/shard_map/pallas_call | solution.py:138
  48.6 1.1 %constant_dynamic-update-slice_fusion = (f32[384,256]{1,0:T(8,128)S(1)}, f32[384,256]{1,0:T(8,128)S(1)}) fusion(f32[384,256]{1,0:T(8,128)S(1)} %constant_dynamic-update-slice_fusion.1, f32[384,128]{1,0:T(8,128)} %get-tuple-element.31, f32[384,256]{1,0:T(8,128)S(1)} %constant_dynamic-update-slice_fusion.3, f32[384,128]{1,0:T(8,128)} %get-tuple-element.33), kind=kLoop, calls=%fused_computation.68 | loop fusion | bytes 786432 | tf_op jit(solution)/shard_map/concatenate | solution.py:308
  49.9 1.4 %collective-permute-start.7 = (bf16[128,512]{1,0:T(8,128)(2,1)S(1)}, bf16[128,512]{1,0:T(8,128)(2,1)S(1)}, u32[]{:S(2)}, u32[]{:S(2)}) collective-permute-start(bf16[128,512]{1,0:T(8,128)(2,1)S(1)} %pad_maximum_fusion), channel_id=1, source_target_pairs={{1,0},{2,1},{3,2},{4,3},{5,4},{6,5},{7,6},{9,8},{10,9},{11,10},{12... | collective-permute-start | bytes 393224 | tf_op jit(solution)/shard_map/ppermute | solution.py:92
  51.4 1.3 %collective-permute-start.8 = (bf16[128,512]{1,0:T(8,128)(2,1)S(1)}, bf16[128,512]{1,0:T(8,128)(2,1)S(1)}, u32[]{:S(2)}, u32[]{:S(2)}) collective-permute-start(bf16[128,512]{1,0:T(8,128)(2,1)S(1)} %pad_maximum_fusion.1), channel_id=1, source_target_pairs={{2,0},{3,1},{4,2},{5,3},{6,4},{7,5},{10,8},{11,9},{12,10},{13,11},... | collective-permute-start | bytes 393224 | tf_op jit(solution)/shard_map/ppermute | solution.py:92
  52.7 2.3 %fusion.2 = (bf16[1,128,1792]{2,1,0:T(8,128)(2,1)}, bf16[1,128,1792]{2,1,0:T(8,128)(2,1)}) fusion(f32[128,1792]{1,0:T(8,128)S(1)} %copy-done.3, f32[128,896]{1,0:T(8,128)} %get-tuple-element.28, f32[128,896]{1,0:T(8,128)S(1)} %copy-done.9, f32[128,1792]{1,0:T(8,128)S(1)} %copy-done.2, f32[128,896]{1,0:T(8,128)} %get-tuple-element.25, f32[128,896]{1,0:T(8,128)S(1)} %copy-done.8), kind=kLoop, calls=%fused_computation.12 | loop fusion | flops 1376256 | bytes 4587520 | tf_op jit(solution)/shard_map/broadcast_in_dim | solution.py:349
  55.0 4.8 %collective-permute-start.6 = (f32[272,128]{1,0:T(8,128)S(1)}, f32[272,128]{1,0:T(8,128)S(1)}, u32[]{:S(2)}, u32[]{:S(2)}) collective-permute-start(f32[272,128]{1,0:T(8,128)S(1)} %add.75), channel_id=1, source_target_pairs={{0,4},{1,5},{2,6},{3,7},{4,0},{5,1},{6,2},{7,3},{8,12},{9,13},{10,... | collective-permute-start | bytes 417800 | tf_op jit(solution)/shard_map/ppermute | solution.py:47
  59.8 0.2 collective-permute-done.8
  60.1 3.7 %collective-permute-done.6 = f32[272,128]{1,0:T(8,128)S(1)} collective-permute-done((f32[272,128]{1,0:T(8,128)S(1)}, f32[272,128]{1,0:T(8,128)S(1)}, u32[]{:S(2)}, u32[]{:S(2)}) %collective-permute-start.6) | collective-permute-done | bytes 139296 | tf_op jit(solution)/shard_map/ppermute | solution.py:47
  63.9 0.1 slice_add_fusion.5
  64.1 0.1 slice_add_fusion.4
  64.3 1.6 %collective-permute-start.9 = (f32[1792]{0:T(1024)S(1)}, f32[1792]{0:T(1024)S(1)}, u32[]{:S(2)}, u32[]{:S(2)}) collective-permute-start(f32[1792]{0:T(1024)S(1)} %fusion.43), channel_id=1, source_target_pairs={{0,8},{8,0},{16,24},{24,16},{1,9},{9,1},{17,25},{25,17},{2,10},{10... | collective-permute-start | bytes 21512 | tf_op jit(solution)/shard_map/ppermute | solution.py:84
  65.9 0.1 slice_add_fusion.3
  66.0 0.1 slice_add_fusion.2
  66.2 1.8 %collective-permute-done.9 = f32[1792]{0:T(1024)S(1)} collective-permute-done((f32[1792]{0:T(1024)S(1)}, f32[1792]{0:T(1024)S(1)}, u32[]{:S(2)}, u32[]{:S(2)}) %collective-permute-start.9) | collective-permute-done | bytes 7200 | tf_op jit(solution)/shard_map/ppermute | solution.py:84
  68.0 2.6 %collective-permute-start.10 = (f32[1792]{0:T(1024)S(1)}, f32[1792]{0:T(1024)S(1)}, u32[]{:S(2)}, u32[]{:S(2)}) collective-permute-start(f32[1792]{0:T(1024)S(1)} %add.87), channel_id=1, source_target_pairs={{0,16},{8,24},{16,0},{24,8},{1,17},{9,25},{17,1},{25,9},{2,18},{10... | collective-permute-start | bytes 21512 | tf_op jit(solution)/shard_map/ppermute | solution.py:84
  70.6 0.7 fusion.12
  71.3 1.2 %collective-permute-done.10 = f32[1792]{0:T(1024)S(1)} collective-permute-done((f32[1792]{0:T(1024)S(1)}, f32[1792]{0:T(1024)S(1)}, u32[]{:S(2)}, u32[]{:S(2)}) %collective-permute-start.10) | collective-permute-done | bytes 7200 | tf_op jit(solution)/shard_map/ppermute | solution.py:84
  72.5 0.6 add_multiply_fusion
  (67 shorter events, 0.6 us)
Async XLA Ops:
  0.6 0.9 %copy-start.4 = (bf16[1,128,256]{2,1,0:T(8,128)(2,1)S(1)}, bf16[1,128,256]{2,1,0:T(8,128)(2,1)}, u32[]{:S(2)}) copy-start(bf16[1,128,256]{2,1,0:T(8,128)(2,1)} %param.9) | copy-start | bytes 196612
  1.5 0.8 %copy-start = (bf16[1,128,256]{2,1,0:T(8,128)(2,1)S(1)}, bf16[1,128,256]{2,1,0:T(8,128)(2,1)}, u32[]{:S(2)}) copy-start(bf16[1,128,256]{2,1,0:T(8,128)(2,1)} %param.8) | copy-start | bytes 196612
  2.3 6.4 %copy-start.15 = (s32[1,128,2]{1,2,0:T(2,128)S(1)}, s32[1,128,2]{1,2,0:T(2,128)}, u32[]{:S(2)}) copy-start(s32[1,128,2]{1,2,0:T(2,128)} %param.10) | copy-start | bytes 3076
  2.3 9.2 %collective-permute-start = (bf16[128,640]{1,0:T(8,128)(2,1)S(1)}, bf16[128,640]{1,0:T(8,128)(2,1)S(1)}, u32[]{:S(2)}, u32[]{:S(2)}) collective-permute-start(bf16[128,640]{1,0:T(8,128)(2,1)S(1)} %maximum_maximum_fusion.1), channel_id=1, source_target_pairs={{0,2},{1,3},{2,4},{3,5},{4,6},{5,7},{8,10},{9,11},{10,12},{11,13},... | collective-permute-start | bytes 491528 | tf_op jit(solution)/shard_map/ppermute | solution.py:92
  7.2 4.9 %collective-permute-start.1 = (bf16[128,640]{1,0:T(8,128)(2,1)S(1)}, bf16[128,640]{1,0:T(8,128)(2,1)S(1)}, u32[]{:S(2)}, u32[]{:S(2)}) collective-permute-start(bf16[128,640]{1,0:T(8,128)(2,1)S(1)} %maximum_maximum_fusion.1), channel_id=1, source_target_pairs={{0,1},{1,2},{2,3},{3,4},{4,5},{5,6},{6,7},{8,9},{9,10},{10,11},{11... | collective-permute-start | bytes 491528 | tf_op jit(solution)/shard_map/ppermute | solution.py:92
  9.0 2.3 %copy-start.5 = (bf16[128,256]{1,0:T(8,128)(2,1)}, bf16[128,256]{1,0:T(8,128)(2,1)S(1)}, u32[]{:S(2)}) copy-start(bf16[128,256]{1,0:T(8,128)(2,1)S(1)} %fusion.6.s_ref) | copy-start | bytes 196612
  9.3 1.4 %copy-start.14 = (f32[1792]{0:T(1024)S(1)}, f32[1792]{0:T(1024)}, u32[]{:S(2)}) copy-start(f32[1792]{0:T(1024)} %param.12) | copy-start | bytes 21508
  9.3 0.7 copy-start.16
  11.5 8.2 %copy-start.7 = (bf16[128,640]{1,0:T(8,128)(2,1)}, bf16[128,640]{1,0:T(8,128)(2,1)S(1)}, u32[]{:S(2)}) copy-start(bf16[128,640]{1,0:T(8,128)(2,1)S(1)} %collective-permute-done) | copy-start | bytes 491524
  12.8 15.3 %collective-permute-start.2 = (f32[2,128,128]{2,1,0:T(8,128)S(1)}, f32[2,128,128]{2,1,0:T(8,128)S(1)}, u32[]{:S(2)}, u32[]{:S(2)}) collective-permute-start(f32[2,128,128]{2,1,0:T(8,128)S(1)} %maximum_add_fusion.3), channel_id=1, source_target_pairs={{0,3},{1,4},{2,5},{3,6},{4,7},{8,11},{9,12},{10,13},{11,14},{12,15... | collective-permute-start | bytes 393224 | tf_op jit(solution)/shard_map/ppermute | solution.py:92
  17.8 10.3 %collective-permute-start.3 = (f32[2,128,128]{2,1,0:T(8,128)S(1)}, f32[2,128,128]{2,1,0:T(8,128)S(1)}, u32[]{:S(2)}, u32[]{:S(2)}) collective-permute-start(f32[2,128,128]{2,1,0:T(8,128)S(1)} %maximum_add_fusion.3), channel_id=1, source_target_pairs={{0,6},{1,7},{8,14},{9,15},{16,22},{17,23},{24,30},{25,31}} | collective-permute-start | bytes 393224 | tf_op jit(solution)/shard_map/ppermute | solution.py:92
  19.7 0.9 %slice-start = ((bf16[128,640]{1,0:T(8,128)(2,1)}), bf16[128,512]{1,0:T(8,128)(2,1)S(1)}, s32[]{:S(2)}) async-start(bf16[128,640]{1,0:T(8,128)(2,1)} %copy-done.7), calls=%async_computation | async-start | bytes 262144 | tf_op jit(solution)/shard_map/slice | solution.py:264
  38.5 2.4 %copy-start.11 = (f32[384,128]{1,0:T(8,128)S(1)}, f32[384,128]{1,0:T(8,128)}, u32[]{:S(2)}) copy-start(f32[384,128]{1,0:T(8,128)} %get-tuple-element.30) | copy-start | bytes 589828
  40.2 1.6 %collective-permute-start.4 = (f32[272,128]{1,0:T(8,128)S(1)}, f32[272,128]{1,0:T(8,128)S(1)}, u32[]{:S(2)}, u32[]{:S(2)}) collective-permute-start(f32[272,128]{1,0:T(8,128)S(1)} %maximum_maximum_fusion.2), channel_id=1, source_target_pairs={{0,1},{1,0},{2,3},{3,2},{4,5},{5,4},{6,7},{7,6},{8,9},{9,8},{10,11... | collective-permute-start | bytes 417800 | tf_op jit(solution)/shard_map/ppermute | solution.py:47
  40.8 0.9 %copy-start.10 = (f32[384,128]{1,0:T(8,128)S(1)}, f32[384,128]{1,0:T(8,128)}, u32[]{:S(2)}) copy-start(f32[384,128]{1,0:T(8,128)} %get-tuple-element.32) | copy-start | bytes 589828
  41.9 13.1 %collective-permute-start.5 = (f32[272,128]{1,0:T(8,128)S(1)}, f32[272,128]{1,0:T(8,128)S(1)}, u32[]{:S(2)}, u32[]{:S(2)}) collective-permute-start(f32[272,128]{1,0:T(8,128)S(1)} %add.73), channel_id=1, source_target_pairs={{0,2},{1,3},{2,0},{3,1},{4,6},{5,7},{6,4},{7,5},{8,10},{9,11},{10,... | collective-permute-start | bytes 417800 | tf_op jit(solution)/shard_map/ppermute | solution.py:47
  48.6 4.0 %copy-start.8 = (f32[128,896]{1,0:T(8,128)S(1)}, f32[128,896]{1,0:T(8,128)}, u32[]{:S(2)}) copy-start(f32[128,896]{1,0:T(8,128)} %get-tuple-element.21) | copy-start | bytes 1376260
  48.6 4.0 %copy-start.9 = (f32[128,896]{1,0:T(8,128)S(1)}, f32[128,896]{1,0:T(8,128)}, u32[]{:S(2)}) copy-start(f32[128,896]{1,0:T(8,128)} %get-tuple-element.27) | copy-start | bytes 1376260
  49.8 2.9 %copy-start.3 = (f32[128,1792]{1,0:T(8,128)S(1)}, f32[128,1792]{1,0:T(8,128)}, u32[]{:S(2)}) copy-start(f32[128,1792]{1,0:T(8,128)} %get-tuple-element.26) | copy-start | bytes 2752516
  49.8 2.9 %copy-start.2 = (f32[128,1792]{1,0:T(8,128)S(1)}, f32[128,1792]{1,0:T(8,128)}, u32[]{:S(2)}) copy-start(f32[128,1792]{1,0:T(8,128)} %get-tuple-element.20) | copy-start | bytes 2752516
  49.9 9.9 %collective-permute-start.7 = (bf16[128,512]{1,0:T(8,128)(2,1)S(1)}, bf16[128,512]{1,0:T(8,128)(2,1)S(1)}, u32[]{:S(2)}, u32[]{:S(2)}) collective-permute-start(bf16[128,512]{1,0:T(8,128)(2,1)S(1)} %pad_maximum_fusion), channel_id=1, source_target_pairs={{1,0},{2,1},{3,2},{4,3},{5,4},{6,5},{7,6},{9,8},{10,9},{11,10},{12... | collective-permute-start | bytes 393224 | tf_op jit(solution)/shard_map/ppermute | solution.py:92
  51.4 8.7 %collective-permute-start.8 = (bf16[128,512]{1,0:T(8,128)(2,1)S(1)}, bf16[128,512]{1,0:T(8,128)(2,1)S(1)}, u32[]{:S(2)}, u32[]{:S(2)}) collective-permute-start(bf16[128,512]{1,0:T(8,128)(2,1)S(1)} %pad_maximum_fusion.1), channel_id=1, source_target_pairs={{2,0},{3,1},{4,2},{5,3},{6,4},{7,5},{10,8},{11,9},{12,10},{13,11},... | collective-permute-start | bytes 393224 | tf_op jit(solution)/shard_map/ppermute | solution.py:92
  55.0 8.8 %collective-permute-start.6 = (f32[272,128]{1,0:T(8,128)S(1)}, f32[272,128]{1,0:T(8,128)S(1)}, u32[]{:S(2)}, u32[]{:S(2)}) collective-permute-start(f32[272,128]{1,0:T(8,128)S(1)} %add.75), channel_id=1, source_target_pairs={{0,4},{1,5},{2,6},{3,7},{4,0},{5,1},{6,2},{7,3},{8,12},{9,13},{10,... | collective-permute-start | bytes 417800 | tf_op jit(solution)/shard_map/ppermute | solution.py:47
  60.1 3.8 %copy-start.6 = (bf16[128,256]{1,0:T(8,128)(2,1)S(1)}, bf16[128,256]{1,0:T(8,128)(2,1)}, u32[]{:S(2)}) copy-start(bf16[128,256]{1,0:T(8,128)(2,1)} %copy-done.5) | copy-start | bytes 196612
  60.1 3.8 %copy-start.13 = (f32[128,256]{1,0:T(8,128)S(1)}, f32[128,256]{1,0:T(8,128)}, u32[]{:S(2)}) copy-start(f32[128,256]{1,0:T(8,128)} %get-tuple-element.29) | copy-start | bytes 393220
  64.1 1.8 %copy-start.1 = (bf16[1,128,256]{2,1,0:T(8,128)(2,1)S(1)}, bf16[1,128,256]{2,1,0:T(8,128)(2,1)}, u32[]{:S(2)}) copy-start(bf16[1,128,256]{2,1,0:T(8,128)(2,1)} %param.8) | copy-start | bytes 196612
  64.1 1.8 %copy-start.12 = (f32[128,256]{1,0:T(8,128)S(1)}, f32[128,256]{1,0:T(8,128)}, u32[]{:S(2)}) copy-start(f32[128,256]{1,0:T(8,128)} %get-tuple-element.34) | copy-start | bytes 393220
  64.3 3.7 %collective-permute-start.9 = (f32[1792]{0:T(1024)S(1)}, f32[1792]{0:T(1024)S(1)}, u32[]{:S(2)}, u32[]{:S(2)}) collective-permute-start(f32[1792]{0:T(1024)S(1)} %fusion.43), channel_id=1, source_target_pairs={{0,8},{8,0},{16,24},{24,16},{1,9},{9,1},{17,25},{25,17},{2,10},{10... | collective-permute-start | bytes 21512 | tf_op jit(solution)/shard_map/ppermute | solution.py:84
  68.0 4.5 %collective-permute-start.10 = (f32[1792]{0:T(1024)S(1)}, f32[1792]{0:T(1024)S(1)}, u32[]{:S(2)}, u32[]{:S(2)}) collective-permute-start(f32[1792]{0:T(1024)S(1)} %add.87), channel_id=1, source_target_pairs={{0,16},{8,24},{16,0},{24,8},{1,17},{9,25},{17,1},{25,9},{2,18},{10... | collective-permute-start | bytes 21512 | tf_op jit(solution)/shard_map/ppermute | solution.py:84

commit v10 on v8

--- a/solution.py
+++ b/solution.py
@@ -41,11 +41,12 @@
     before = jnp.zeros_like(part)
     step = 1
     while step < count:
-        got = lax.ppermute(group, axis, [(i, i ^ step) for i in range(count)])
+        mine = group.astype(jnp.bfloat16)
+        got = lax.ppermute(mine, axis, [(i, i ^ step) for i in range(count)]).astype(jnp.float32)
         partner = jnp.bitwise_xor(place, step)
         take = partner > place if reverse else partner < place
         before = before + jnp.where(take, got, 0.0)
-        group = group + got
+        group = mine.astype(jnp.float32) + got
         step *= 2
     return before, group
 

time: 73.1 us -> 69.7 us (0.953)
  waiting for transfers between devices: 13 us -> 10.2 us
    ppermute x3, waiting for transfers between devices: 9.48 us -> 6.24 us  [butterfly_scan(): lax.ppermute(mine, axis, [(i, i ^ step) for i in range(count)])]
    another operation x3 -> x5, other arithmetic: 1.13 us -> 2.09 us
    concatenate x1, other arithmetic: 1 us -> 0.1 us  [per_device(): jnp.concatenate([suffix_local.reshape(state_rows, HEAD_SIZE), gain_local....]
    unnamed x25 -> x27, local copies, waits for them, and re-layouts: 2.3 us -> 2.3 us
  transfers between devices with their start and end apart: 11 -> 11, of which waited for: 5 -> 5; matrix products, arithmetic and copies ran while one was open for 9% -> 9% of each run, Pallas kernels for 16% -> 17%
where the time goes in v10:
time: 69.7 us; the launch traced here: 69.1 us
  starting transfers between devices  23.1 us (33%)
  Pallas kernels  21.6 us (31%)
  waiting for transfers between devices  10.2 us (15%)
  other arithmetic  5.94 us (9%)
  local copies, waits for them, and re-layouts  5.45 us (8%)
  matrix products  1.68 us (2%)
  between operations  1.06 us (2%)
    ppermute x6, starting transfers between devices, shifted(): return lax.ppermute(block, axis, route)  15.9 us
    pallas_call x1, Pallas kernels, per_device(): pl.pallas_call(window_kernel, out_shape=(jax.ShapeDtypeStruct((token_rows...  11.4 us
    pallas_call x1, Pallas kernels, per_device(): pl.pallas_call(linear_kernel, out_shape=(jax.ShapeDtypeStruct((token_rows...  10.2 us
    ppermute x3, waiting for transfers between devices, butterfly_scan(): lax.ppermute(mine, axis, [(i, i ^ step) for i in range(count)])  6.24 us
    ppermute x2, starting transfers between devices, all_sum(): part = part + lax.ppermute(part, axes, route)  4.23 us
    ppermute x3, starting transfers between devices, butterfly_scan(): lax.ppermute(mine, axis, [(i, i ^ step) for i in range(count)])  3 us
    unnamed x27, local copies, waits for them, and re-layouts  2.3 us
    ppermute x2, waiting for transfers between devices, all_sum(): part = part + lax.ppermute(part, axes, route)  2.14 us
  transfers between devices with their start and end apart: 11, of which 5 were waited for; matrix products, arithmetic and copies ran while one was open for 9% of the time, Pallas kernels for 17%

profile of v10, /device:TPU:0, one launch (start us, length us, event | category | flops | bytes accessed | tf_op | source)
XLA Modules:
  0.0 69.1 jit_solution(3331137482960558434)
XLA Ops:
  0.6 0.8 %copy.13 = s32[1,128,2]{2,1,0:T(8,128)S(1)} copy(s32[1,128,2]{1,2,0:T(2,128)} %param.10) | data formatting | bytes 2048 | tf_op args[3]
  1.5 0.1 pad.26.clone
  1.6 0.7 %copy-done = bf16[1,128,256]{2,1,0:T(8,128)(2,1)S(1)} copy-done((bf16[1,128,256]{2,1,0:T(8,128)(2,1)S(1)}, bf16[1,128,256]{2,1,0:T(8,128)(2,1)}, u32[]{:S(2)}) %copy-start) | copy-done | bytes 65560
  2.3 4.9 %collective-permute-start = (bf16[128,640]{1,0:T(8,128)(2,1)S(1)}, bf16[128,640]{1,0:T(8,128)(2,1)S(1)}, u32[]{:S(2)}, u32[]{:S(2)}) collective-permute-start(bf16[128,640]{1,0:T(8,128)(2,1)S(1)} %maximum_maximum_fusion.1), channel_id=1, source_target_pairs={{0,2},{1,3},{2,4},{3,5},{4,6},{5,7},{8,10},{9,11},{10,12},{11,13},... | collective-permute-start | bytes 491528 | tf_op jit(solution)/shard_map/ppermute | solution.py:88
  7.2 1.5 %collective-permute-start.1 = (bf16[128,640]{1,0:T(8,128)(2,1)S(1)}, bf16[128,640]{1,0:T(8,128)(2,1)S(1)}, u32[]{:S(2)}, u32[]{:S(2)}) collective-permute-start(bf16[128,640]{1,0:T(8,128)(2,1)S(1)} %maximum_maximum_fusion.1), channel_id=1, source_target_pairs={{0,1},{1,2},{2,3},{3,4},{4,5},{5,6},{6,7},{8,9},{9,10},{10,11},{11... | collective-permute-start | bytes 491528 | tf_op jit(solution)/shard_map/ppermute | solution.py:88
  8.7 0.1 copy.12
  8.8 0.2 broadcast_in_dim.33
  9.0 0.2 convolution_bitcast_fusion.2
  9.3 0.7 copy-done.12
  9.9 0.6 pad_add_fusion.info_ref
  10.5 0.6 reshape.47.gain_ref
  11.1 0.1 pad.10.clone
  11.2 0.2 convolution_bitcast_fusion.3
  11.4 0.2 broadcast_in_dim.35
  11.7 0.2 convolution_bitcast_fusion.6
  11.9 0.2 convolution_bitcast_fusion.7
  12.1 0.2 broadcast_in_dim.36
  12.3 0.2 convolution_bitcast_fusion.5
  12.5 0.2 convolution_bitcast_fusion.4
  12.7 5.0 %collective-permute-start.2 = (f32[2,128,128]{2,1,0:T(8,128)S(1)}, f32[2,128,128]{2,1,0:T(8,128)S(1)}, u32[]{:S(2)}, u32[]{:S(2)}) collective-permute-start(f32[2,128,128]{2,1,0:T(8,128)S(1)} %maximum_add_fusion.1), channel_id=1, source_target_pairs={{0,3},{1,4},{2,5},{3,6},{4,7},{8,11},{9,12},{10,13},{11,14},{12,15... | collective-permute-start | bytes 393224 | tf_op jit(solution)/shard_map/ppermute | solution.py:88
  17.7 1.9 %collective-permute-start.3 = (f32[2,128,128]{2,1,0:T(8,128)S(1)}, f32[2,128,128]{2,1,0:T(8,128)S(1)}, u32[]{:S(2)}, u32[]{:S(2)}) collective-permute-start(f32[2,128,128]{2,1,0:T(8,128)S(1)} %maximum_add_fusion.1), channel_id=1, source_target_pairs={{0,6},{1,7},{8,14},{9,15},{16,22},{17,23},{24,30},{25,31}} | collective-permute-start | bytes 393224 | tf_op jit(solution)/shard_map/ppermute | solution.py:88
  19.7 0.9 %slice-done = bf16[128,512]{1,0:T(8,128)(2,1)S(1)} async-done(((bf16[128,640]{1,0:T(8,128)(2,1)}), bf16[128,512]{1,0:T(8,128)(2,1)S(1)}, s32[]{:S(2)}) %slice-start) | async-done | bytes 131096 | tf_op jit(solution)/shard_map/slice | solution.py:238
  20.6 0.8 %fusion.45 = (bf16[384,256]{1,0:T(8,128)(2,1)}, bf16[384,256]{1,0:T(8,128)(2,1)}) fusion(bf16[384,512]{1,0:T(8,128)(2,1)S(1)} %maximum_maximum_fusion), kind=kLoop, calls=%fused_computation.76 | loop fusion | bytes 786432 | tf_op jit(solution)/shard_map/slice | solution.py:258
  21.4 11.4 %shard_map.110 = (f32[128,1792]{1,0:T(8,128)}, f32[128,1792]{1,0:T(8,128)}, f32[384,256]{1,0:T(8,128)}, f32[384,256]{1,0:T(8,128)}) custom-call(s32[3]{0:T(128)} %pad_add_fusion.info_ref, bf16[128,1792]{1,0:T(8,128)(2,1)} %bitcast.81, bf16[128,1792]{1,0:T(8,128)(2,1)} %bitcast.83, bf16[384,256]{1,0:T(8,128)(2,1)} %get-tuple-element.26.k_ref, ...), custom_call_target="tpu_custom_call" | custom-call | flops 1056964608 | bytes 3932160 | tf_op jit(solution)/shard_map/pallas_call | solution.py:243
  32.9 1.1 %convert.28 = bf16[384,256]{1,0:T(8,128)(2,1)S(1)} convert(f32[384,256]{1,0:T(8,128)} %get-tuple-element.22) | non-fusion elementwise | flops 98304 | bytes 589824 | tf_op jit(solution)/shard_map/convert.7
  33.9 0.0 copy-done.4
  34.0 0.7 add_convert_fusion.prior_ref
  34.7 10.2 %shard_map.111 = (bf16[128,1792]{1,0:T(8,128)(2,1)}, bf16[128,1792]{1,0:T(8,128)(2,1)}, f32[2,128,128]{2,1,0:T(8,128)}, f32[1,1792]{1,0:T(1,128)}, f32[128,256]{1,0:T(8,128)}, /*index=5*/f32[128,256]{1,0:T(8,128)}) custom-call(bf16[128,1792]{1,0:T(8,128)(2,1)} %bitcast.82, bf16[128,1792]{1,0:T(8,128)(2,1)} %bitcast.84, bf16[128,256]{1,0:T(8,128)(2,1)} %bitcast.68, ...), custom_call_target="tpu_custom_call" | custom-call | flops 587202560 | bytes 4456448 | tf_op jit(solution)/shard_map/pallas_call | solution.py:259
  44.9 0.9 %convert.25 = bf16[2,128,128]{2,1,0:T(8,128)(2,1)S(1)} convert(f32[2,128,128]{2,1,0:T(8,128)} %get-tuple-element.20) | non-fusion elementwise | flops 32768 | bytes 196608 | tf_op jit(solution)/shard_map/convert.13
  45.9 0.1 maximum_maximum_fusion.2
  46.0 0.6 collective-permute-start.4
  46.6 1.3 %collective-permute-start.7 = (bf16[128,512]{1,0:T(8,128)(2,1)S(1)}, bf16[128,512]{1,0:T(8,128)(2,1)S(1)}, u32[]{:S(2)}, u32[]{:S(2)}) collective-permute-start(bf16[128,512]{1,0:T(8,128)(2,1)S(1)} %pad_maximum_fusion), channel_id=1, source_target_pairs={{1,0},{2,1},{3,2},{4,3},{5,4},{6,5},{7,6},{9,8},{10,9},{11,10},{12... | collective-permute-start | bytes 393224 | tf_op jit(solution)/shard_map/ppermute | solution.py:88
  47.9 2.3 %collective-permute-start.5 = (bf16[272,128]{1,0:T(8,128)(2,1)S(1)}, bf16[272,128]{1,0:T(8,128)(2,1)S(1)}, u32[]{:S(2)}, u32[]{:S(2)}) collective-permute-start(bf16[272,128]{1,0:T(8,128)(2,1)S(1)} %fusion.3), channel_id=1, source_target_pairs={{0,2},{1,3},{2,0},{3,1},{4,6},{5,7},{6,4},{7,5},{8,10},{9,11},{10,... | collective-permute-start | bytes 208904 | tf_op jit(solution)/shard_map/ppermute | solution.py:45
  50.3 1.3 %collective-permute-start.8 = (bf16[128,512]{1,0:T(8,128)(2,1)S(1)}, bf16[128,512]{1,0:T(8,128)(2,1)S(1)}, u32[]{:S(2)}, u32[]{:S(2)}) collective-permute-start(bf16[128,512]{1,0:T(8,128)(2,1)S(1)} %pad_maximum_fusion.1), channel_id=1, source_target_pairs={{2,0},{3,1},{4,2},{5,3},{6,4},{7,5},{10,8},{11,9},{12,10},{13,11},... | collective-permute-start | bytes 393224 | tf_op jit(solution)/shard_map/ppermute | solution.py:88
  51.6 3.8 %collective-permute-done.5 = bf16[272,128]{1,0:T(8,128)(2,1)S(1)} collective-permute-done((bf16[272,128]{1,0:T(8,128)(2,1)S(1)}, bf16[272,128]{1,0:T(8,128)(2,1)S(1)}, u32[]{:S(2)}, u32[]{:S(2)}) %collective-permute-start.5) | collective-permute-done | bytes 69664 | tf_op jit(solution)/shard_map/ppermute | solution.py:45
  55.5 0.1 collective-permute-start.6
  55.6 1.8 %collective-permute-done.8 = bf16[128,512]{1,0:T(8,128)(2,1)S(1)} collective-permute-done((bf16[128,512]{1,0:T(8,128)(2,1)S(1)}, bf16[128,512]{1,0:T(8,128)(2,1)S(1)}, u32[]{:S(2)}, u32[]{:S(2)}) %collective-permute-start.8) | collective-permute-done | bytes 131104 | tf_op jit(solution)/shard_map/ppermute | solution.py:88
  57.4 2.4 %collective-permute-done.6 = bf16[272,128]{1,0:T(8,128)(2,1)S(1)} collective-permute-done((bf16[272,128]{1,0:T(8,128)(2,1)S(1)}, bf16[272,128]{1,0:T(8,128)(2,1)S(1)}, u32[]{:S(2)}, u32[]{:S(2)}) %collective-permute-start.6) | collective-permute-done | bytes 69664 | tf_op jit(solution)/shard_map/ppermute | solution.py:45
  59.9 0.1 slice_add_fusion.4
  60.0 0.2 slice_add_fusion.3
  60.3 1.6 %collective-permute-start.9 = (f32[1792]{0:T(1024)S(1)}, f32[1792]{0:T(1024)S(1)}, u32[]{:S(2)}, u32[]{:S(2)}) collective-permute-start(f32[1792]{0:T(1024)S(1)} %fusion.44), channel_id=1, source_target_pairs={{0,8},{8,0},{16,24},{24,16},{1,9},{9,1},{17,25},{25,17},{2,10},{10... | collective-permute-start | bytes 21512 | tf_op jit(solution)/shard_map/ppermute | solution.py:80
  61.9 0.1 slice_add_fusion.2
  62.0 0.1 slice_add_fusion.1
  62.2 1.8 %collective-permute-done.9 = f32[1792]{0:T(1024)S(1)} collective-permute-done((f32[1792]{0:T(1024)S(1)}, f32[1792]{0:T(1024)S(1)}, u32[]{:S(2)}, u32[]{:S(2)}) %collective-permute-start.9) | collective-permute-done | bytes 7200 | tf_op jit(solution)/shard_map/ppermute | solution.py:80
  64.0 2.6 %collective-permute-start.10 = (f32[1792]{0:T(1024)S(1)}, f32[1792]{0:T(1024)S(1)}, u32[]{:S(2)}, u32[]{:S(2)}) collective-permute-start(f32[1792]{0:T(1024)S(1)} %add.79), channel_id=1, source_target_pairs={{0,16},{8,24},{16,0},{24,8},{1,17},{9,25},{17,1},{25,9},{2,18},{10... | collective-permute-start | bytes 21512 | tf_op jit(solution)/shard_map/ppermute | solution.py:80
  66.6 1.6 %fusion.13 = (bf16[1,128,256]{2,1,0:T(8,128)(2,1)}, bf16[1,128,256]{2,1,0:T(8,128)(2,1)}) fusion(f32[128,512]{1,0:T(8,128)S(1)} %convert_add_fusion, f32[384,256]{1,0:T(8,128)S(1)} %copy-done.4, f32[16,8,2,128]{3,2,1,0:T(2,128)S(1)} %bitcast.76, f32[128,128]{1,0:T(8,128)S(1)} %slice_add_fusion.1, f32[128,128]{1,0:T(8,128)S(1)} %slice_add_fusion.2, ...), kind=kLoop, calls=%fused_computation.44 | loop fusion | flops 294912 | bytes 1048576 | tf_op jit(solution)/shard_map/broadcast_in_dim | solution.py:329
  68.2 0.3 collective-permute-done.10
  68.5 0.6 add_multiply_fusion
  (55 shorter events, 0.5 us)
Async XLA Ops:
  0.6 0.9 %copy-start.5 = (bf16[1,128,256]{2,1,0:T(8,128)(2,1)S(1)}, bf16[1,128,256]{2,1,0:T(8,128)(2,1)}, u32[]{:S(2)}) copy-start(bf16[1,128,256]{2,1,0:T(8,128)(2,1)} %param.9) | copy-start | bytes 196612
  1.5 0.8 %copy-start = (bf16[1,128,256]{2,1,0:T(8,128)(2,1)S(1)}, bf16[1,128,256]{2,1,0:T(8,128)(2,1)}, u32[]{:S(2)}) copy-start(bf16[1,128,256]{2,1,0:T(8,128)(2,1)} %param.8) | copy-start | bytes 196612
  2.3 6.4 %copy-start.11 = (s32[1,128,2]{1,2,0:T(2,128)S(1)}, s32[1,128,2]{1,2,0:T(2,128)}, u32[]{:S(2)}) copy-start(s32[1,128,2]{1,2,0:T(2,128)} %param.10) | copy-start | bytes 3076
  2.3 9.1 %collective-permute-start = (bf16[128,640]{1,0:T(8,128)(2,1)S(1)}, bf16[128,640]{1,0:T(8,128)(2,1)S(1)}, u32[]{:S(2)}, u32[]{:S(2)}) collective-permute-start(bf16[128,640]{1,0:T(8,128)(2,1)S(1)} %maximum_maximum_fusion.1), channel_id=1, source_target_pairs={{0,2},{1,3},{2,4},{3,5},{4,6},{5,7},{8,10},{9,11},{10,12},{11,13},... | collective-permute-start | bytes 491528 | tf_op jit(solution)/shard_map/ppermute | solution.py:88
  7.2 4.8 %collective-permute-start.1 = (bf16[128,640]{1,0:T(8,128)(2,1)S(1)}, bf16[128,640]{1,0:T(8,128)(2,1)S(1)}, u32[]{:S(2)}, u32[]{:S(2)}) collective-permute-start(bf16[128,640]{1,0:T(8,128)(2,1)S(1)} %maximum_maximum_fusion.1), channel_id=1, source_target_pairs={{0,1},{1,2},{2,3},{3,4},{4,5},{5,6},{6,7},{8,9},{9,10},{10,11},{11... | collective-permute-start | bytes 491528 | tf_op jit(solution)/shard_map/ppermute | solution.py:88
  9.0 2.2 %copy-start.2 = (bf16[128,256]{1,0:T(8,128)(2,1)}, bf16[128,256]{1,0:T(8,128)(2,1)S(1)}, u32[]{:S(2)}) copy-start(bf16[128,256]{1,0:T(8,128)(2,1)S(1)} %fusion.7.s_ref) | copy-start | bytes 196612
  9.3 1.3 %copy-start.9 = (f32[1792]{0:T(1024)S(1)}, f32[1792]{0:T(1024)}, u32[]{:S(2)}) copy-start(f32[1792]{0:T(1024)} %param.12) | copy-start | bytes 21508
  9.3 0.7 copy-start.12
  11.4 8.3 %copy-start.6 = (bf16[128,640]{1,0:T(8,128)(2,1)}, bf16[128,640]{1,0:T(8,128)(2,1)S(1)}, u32[]{:S(2)}) copy-start(bf16[128,640]{1,0:T(8,128)(2,1)S(1)} %collective-permute-done) | copy-start | bytes 491524
  12.7 21.3 %collective-permute-start.2 = (f32[2,128,128]{2,1,0:T(8,128)S(1)}, f32[2,128,128]{2,1,0:T(8,128)S(1)}, u32[]{:S(2)}, u32[]{:S(2)}) collective-permute-start(f32[2,128,128]{2,1,0:T(8,128)S(1)} %maximum_add_fusion.1), channel_id=1, source_target_pairs={{0,3},{1,4},{2,5},{3,6},{4,7},{8,11},{9,12},{10,13},{11,14},{12,15... | collective-permute-start | bytes 393224 | tf_op jit(solution)/shard_map/ppermute | solution.py:88
  17.7 16.3 %collective-permute-start.3 = (f32[2,128,128]{2,1,0:T(8,128)S(1)}, f32[2,128,128]{2,1,0:T(8,128)S(1)}, u32[]{:S(2)}, u32[]{:S(2)}) collective-permute-start(f32[2,128,128]{2,1,0:T(8,128)S(1)} %maximum_add_fusion.1), channel_id=1, source_target_pairs={{0,6},{1,7},{8,14},{9,15},{16,22},{17,23},{24,30},{25,31}} | collective-permute-start | bytes 393224 | tf_op jit(solution)/shard_map/ppermute | solution.py:88
  19.7 0.9 %slice-start = ((bf16[128,640]{1,0:T(8,128)(2,1)}), bf16[128,512]{1,0:T(8,128)(2,1)S(1)}, s32[]{:S(2)}) async-start(bf16[128,640]{1,0:T(8,128)(2,1)} %copy-done.6), calls=%async_computation | async-start | bytes 262144 | tf_op jit(solution)/shard_map/slice | solution.py:238
  32.9 1.1 %copy-start.4 = (f32[384,256]{1,0:T(8,128)S(1)}, f32[384,256]{1,0:T(8,128)}, u32[]{:S(2)}) copy-start(f32[384,256]{1,0:T(8,128)} %get-tuple-element.23) | copy-start | bytes 1179652
  44.9 0.9 %copy-start.10 = (f32[1,1792]{1,0:T(1,128)S(1)}, f32[1,1792]{1,0:T(1,128)}, u32[]{:S(2)}) copy-start(f32[1,1792]{1,0:T(1,128)} %get-tuple-element.21) | copy-start | bytes 21508
  46.0 1.9 %collective-permute-start.4 = (bf16[272,128]{1,0:T(8,128)(2,1)S(1)}, bf16[272,128]{1,0:T(8,128)(2,1)S(1)}, u32[]{:S(2)}, u32[]{:S(2)}) collective-permute-start(bf16[272,128]{1,0:T(8,128)(2,1)S(1)} %maximum_maximum_fusion.2), channel_id=1, source_target_pairs={{0,1},{1,0},{2,3},{3,2},{4,5},{5,4},{6,7},{7,6},{8,9},{9,8},{10,11... | collective-permute-start | bytes 208904 | tf_op jit(solution)/shard_map/ppermute | solution.py:45
  46.6 8.9 %collective-permute-start.7 = (bf16[128,512]{1,0:T(8,128)(2,1)S(1)}, bf16[128,512]{1,0:T(8,128)(2,1)S(1)}, u32[]{:S(2)}, u32[]{:S(2)}) collective-permute-start(bf16[128,512]{1,0:T(8,128)(2,1)S(1)} %pad_maximum_fusion), channel_id=1, source_target_pairs={{1,0},{2,1},{3,2},{4,3},{5,4},{6,5},{7,6},{9,8},{10,9},{11,10},{12... | collective-permute-start | bytes 393224 | tf_op jit(solution)/shard_map/ppermute | solution.py:88
  47.9 7.5 %collective-permute-start.5 = (bf16[272,128]{1,0:T(8,128)(2,1)S(1)}, bf16[272,128]{1,0:T(8,128)(2,1)S(1)}, u32[]{:S(2)}, u32[]{:S(2)}) collective-permute-start(bf16[272,128]{1,0:T(8,128)(2,1)S(1)} %fusion.3), channel_id=1, source_target_pairs={{0,2},{1,3},{2,0},{3,1},{4,6},{5,7},{6,4},{7,5},{8,10},{9,11},{10,... | collective-permute-start | bytes 208904 | tf_op jit(solution)/shard_map/ppermute | solution.py:45
  50.3 7.1 %collective-permute-start.8 = (bf16[128,512]{1,0:T(8,128)(2,1)S(1)}, bf16[128,512]{1,0:T(8,128)(2,1)S(1)}, u32[]{:S(2)}, u32[]{:S(2)}) collective-permute-start(bf16[128,512]{1,0:T(8,128)(2,1)S(1)} %pad_maximum_fusion.1), channel_id=1, source_target_pairs={{2,0},{3,1},{4,2},{5,3},{6,4},{7,5},{10,8},{11,9},{12,10},{13,11},... | collective-permute-start | bytes 393224 | tf_op jit(solution)/shard_map/ppermute | solution.py:88
  55.5 4.4 %collective-permute-start.6 = (bf16[272,128]{1,0:T(8,128)(2,1)S(1)}, bf16[272,128]{1,0:T(8,128)(2,1)S(1)}, u32[]{:S(2)}, u32[]{:S(2)}) collective-permute-start(bf16[272,128]{1,0:T(8,128)(2,1)S(1)} %fusion.4), channel_id=1, source_target_pairs={{0,4},{1,5},{2,6},{3,7},{4,0},{5,1},{6,2},{7,3},{8,12},{9,13},{10,... | collective-permute-start | bytes 208904 | tf_op jit(solution)/shard_map/ppermute | solution.py:45
  57.4 2.5 %copy-start.3 = (bf16[128,256]{1,0:T(8,128)(2,1)S(1)}, bf16[128,256]{1,0:T(8,128)(2,1)}, u32[]{:S(2)}) copy-start(bf16[128,256]{1,0:T(8,128)(2,1)} %copy-done.2) | copy-start | bytes 196612
  57.4 2.5 %copy-start.8 = (f32[128,256]{1,0:T(8,128)S(1)}, f32[128,256]{1,0:T(8,128)}, u32[]{:S(2)}) copy-start(f32[128,256]{1,0:T(8,128)} %get-tuple-element.19) | copy-start | bytes 393220
  60.2 1.7 %copy-start.1 = (bf16[1,128,256]{2,1,0:T(8,128)(2,1)S(1)}, bf16[1,128,256]{2,1,0:T(8,128)(2,1)}, u32[]{:S(2)}) copy-start(bf16[1,128,256]{2,1,0:T(8,128)(2,1)} %param.8) | copy-start | bytes 196612
  60.2 1.7 %copy-start.7 = (f32[128,256]{1,0:T(8,128)S(1)}, f32[128,256]{1,0:T(8,128)}, u32[]{:S(2)}) copy-start(f32[128,256]{1,0:T(8,128)} %get-tuple-element.24) | copy-start | bytes 393220
  60.3 3.7 %collective-permute-start.9 = (f32[1792]{0:T(1024)S(1)}, f32[1792]{0:T(1024)S(1)}, u32[]{:S(2)}, u32[]{:S(2)}) collective-permute-start(f32[1792]{0:T(1024)S(1)} %fusion.44), channel_id=1, source_target_pairs={{0,8},{8,0},{16,24},{24,16},{1,9},{9,1},{17,25},{25,17},{2,10},{10... | collective-permute-start | bytes 21512 | tf_op jit(solution)/shard_map/ppermute | solution.py:80
  64.0 4.5 %collective-permute-start.10 = (f32[1792]{0:T(1024)S(1)}, f32[1792]{0:T(1024)S(1)}, u32[]{:S(2)}, u32[]{:S(2)}) collective-permute-start(f32[1792]{0:T(1024)S(1)} %add.79), channel_id=1, source_target_pairs={{0,16},{8,24},{16,0},{24,8},{1,17},{9,25},{17,1},{25,9},{2,18},{10... | collective-permute-start | bytes 21512 | tf_op jit(solution)/shard_map/ppermute | solution.py:80

commit v11 on v10

--- a/solution.py
+++ b/solution.py
@@ -70,15 +70,23 @@
     return total
 
 
-def all_sum(part, axes):
-    count = 1
-    for axis in axes:
-        count *= lax.axis_size(axis)
-    step = 1
-    while step < count:
-        route = [(i, i ^ step) for i in range(count)]
-        part = part + lax.ppermute(part, axes, route)
-        step *= 2
+def all_sum(part, axis):
+    count = lax.axis_size(axis)
+    place = lax.axis_index(axis)
+    span = 1
+    while span < count:
+        width = min(4, count // span)
+        members = [part] + [
+            lax.ppermute(part, axis, [(i, i ^ (m * span)) for i in range(count)]) for m in range(1, width)
+        ]
+        stacked = jnp.stack(members)
+        digit = (place // span) % width
+        total = None
+        for j in range(width):
+            value = lax.dynamic_index_in_dim(stacked, jnp.bitwise_xor(digit, j), 0, False)
+            total = value if total is None else total + value
+        part = total
+        span *= width
     return part
 
 
@@ -289,7 +297,7 @@
     later_rows, total_rows = butterfly_scan(riding, "ctx", True)
     later_half = later_rows[:state_rows].reshape(suffix_local.shape).astype(jnp.bfloat16)
     gain_ctx = total_rows[state_rows : state_rows + gain_rows].reshape(width)
-    d_gain = all_sum(gain_ctx, ("dp",)) * (total_tokens ** (-0.5))
+    d_gain = all_sum(gain_ctx, "dp") * (total_tokens ** (-0.5))
     ldk_parts = []
     dsp_parts = []
     for g in range(KEY_VALUE_HEADS):

time: 69.7 us -> 70.8 us (1.016)
  local copies, waits for them, and re-layouts: 5.45 us -> 6.95 us
    unnamed x27 -> x28, local copies, waits for them, and re-layouts: 2.3 us -> 3.79 us
    ppermute x2 -> x3, starting transfers between devices: 4.23 us -> 4.45 us  [all_sum(): lax.ppermute(part, axis, [(i, i ^ m * span) for i in range(count)])]
    ppermute x2 -> x3, waiting for transfers between devices: 2.14 us -> 2.11 us  [all_sum(): lax.ppermute(part, axis, [(i, i ^ m * span) for i in range(count)])]
    another operation x5 -> x6, other arithmetic: 2.09 us -> 2.13 us
  transfers between devices with their start and end apart: 11 -> 12, of which waited for: 5 -> 4; matrix products, arithmetic and copies ran while one was open for 9% -> 10% of each run, Pallas kernels for 17% -> 16%
where the time goes in v11:
time: 70.8 us; the launch traced here: 70.3 us
  starting transfers between devices  22.7 us (32%)
  Pallas kernels  21.7 us (31%)
  waiting for transfers between devices  10.2 us (14%)
  local copies, waits for them, and re-layouts  6.95 us (10%)
  other arithmetic  6.02 us (9%)
  matrix products  1.67 us (2%)
  between operations  1.08 us (2%)
    ppermute x6, starting transfers between devices, shifted(): return lax.ppermute(block, axis, route)  15.3 us
    pallas_call x1, Pallas kernels, per_device(): pl.pallas_call(window_kernel, out_shape=(jax.ShapeDtypeStruct((token_rows...  11.5 us
    pallas_call x1, Pallas kernels, per_device(): pl.pallas_call(linear_kernel, out_shape=(jax.ShapeDtypeStruct((token_rows...  10.2 us
    ppermute x3, waiting for transfers between devices, butterfly_scan(): lax.ppermute(mine, axis, [(i, i ^ step) for i in range(count)])  6.26 us
    ppermute x3, starting transfers between devices, all_sum(): lax.ppermute(part, axis, [(i, i ^ m * span) for i in range(count)])  4.45 us
    unnamed x28, local copies, waits for them, and re-layouts  3.79 us
    ppermute x3, starting transfers between devices, butterfly_scan(): lax.ppermute(mine, axis, [(i, i ^ step) for i in range(count)])  2.96 us
    ppermute x3, waiting for transfers between devices, all_sum(): lax.ppermute(part, axis, [(i, i ^ m * span) for i in range(count)])  2.11 us
  transfers between devices with their start and end apart: 12, of which 4 were waited for; matrix products, arithmetic and copies ran while one was open for 10% of the time, Pallas kernels for 16%

profile of v11, /device:TPU:0, one launch (start us, length us, event | category | flops | bytes accessed | tf_op | source)
XLA Modules:
  0.0 70.3 jit_solution(10418842211432037065)
XLA Ops:
  0.6 0.8 %copy.13 = s32[1,128,2]{2,1,0:T(8,128)S(1)} copy(s32[1,128,2]{1,2,0:T(2,128)} %param.10) | data formatting | bytes 2048 | tf_op args[3]
  1.6 0.7 %copy-done = bf16[1,128,256]{2,1,0:T(8,128)(2,1)S(1)} copy-done((bf16[1,128,256]{2,1,0:T(8,128)(2,1)S(1)}, bf16[1,128,256]{2,1,0:T(8,128)(2,1)}, u32[]{:S(2)}) %copy-start) | copy-done | bytes 65560
  2.3 4.9 %collective-permute-start = (bf16[128,640]{1,0:T(8,128)(2,1)S(1)}, bf16[128,640]{1,0:T(8,128)(2,1)S(1)}, u32[]{:S(2)}, u32[]{:S(2)}) collective-permute-start(bf16[128,640]{1,0:T(8,128)(2,1)S(1)} %maximum_maximum_fusion.1), channel_id=1, source_target_pairs={{0,2},{1,3},{2,4},{3,5},{4,6},{5,7},{8,10},{9,11},{10,12},{11,13},... | collective-permute-start | bytes 491528 | tf_op jit(solution)/shard_map/ppermute | solution.py:96
  7.2 1.5 %collective-permute-start.1 = (bf16[128,640]{1,0:T(8,128)(2,1)S(1)}, bf16[128,640]{1,0:T(8,128)(2,1)S(1)}, u32[]{:S(2)}, u32[]{:S(2)}) collective-permute-start(bf16[128,640]{1,0:T(8,128)(2,1)S(1)} %maximum_maximum_fusion.1), channel_id=1, source_target_pairs={{0,1},{1,2},{2,3},{3,4},{4,5},{5,6},{6,7},{8,9},{9,10},{10,11},{11... | collective-permute-start | bytes 491528 | tf_op jit(solution)/shard_map/ppermute | solution.py:96
  8.7 0.1 copy.12
  8.8 0.2 broadcast_in_dim.33
  9.0 0.2 convolution_bitcast_fusion.2
  9.3 0.7 copy-done.12
  9.9 0.6 pad_add_fusion.info_ref
  10.5 0.7 copy-done.9
  11.2 0.6 reshape.52.gain_ref
  11.8 0.1 pad.14.clone
  11.9 0.2 convolution_bitcast_fusion.3
  12.1 0.2 broadcast_in_dim.35
  12.3 0.2 convolution_bitcast_fusion.6
  12.5 0.2 convolution_bitcast_fusion.7
  12.7 0.2 broadcast_in_dim.36
  13.0 0.2 convolution_bitcast_fusion.5
  13.1 0.2 convolution_bitcast_fusion.4
  13.4 5.0 %collective-permute-start.2 = (f32[2,128,128]{2,1,0:T(8,128)S(1)}, f32[2,128,128]{2,1,0:T(8,128)S(1)}, u32[]{:S(2)}, u32[]{:S(2)}) collective-permute-start(f32[2,128,128]{2,1,0:T(8,128)S(1)} %maximum_add_fusion.1), channel_id=1, source_target_pairs={{0,3},{1,4},{2,5},{3,6},{4,7},{8,11},{9,12},{10,13},{11,14},{12,15... | collective-permute-start | bytes 393224 | tf_op jit(solution)/shard_map/ppermute | solution.py:96
  18.4 1.3 %collective-permute-start.3 = (f32[2,128,128]{2,1,0:T(8,128)S(1)}, f32[2,128,128]{2,1,0:T(8,128)S(1)}, u32[]{:S(2)}, u32[]{:S(2)}) collective-permute-start(f32[2,128,128]{2,1,0:T(8,128)S(1)} %maximum_add_fusion.1), channel_id=1, source_target_pairs={{0,6},{1,7},{8,14},{9,15},{16,22},{17,23},{24,30},{25,31}} | collective-permute-start | bytes 393224 | tf_op jit(solution)/shard_map/ppermute | solution.py:96
  19.8 0.9 %slice-done = bf16[128,512]{1,0:T(8,128)(2,1)S(1)} async-done(((bf16[128,640]{1,0:T(8,128)(2,1)}), bf16[128,512]{1,0:T(8,128)(2,1)S(1)}, s32[]{:S(2)}) %slice-start) | async-done | bytes 131096 | tf_op jit(solution)/shard_map/slice | solution.py:246
  20.7 0.8 %fusion.46 = (bf16[384,256]{1,0:T(8,128)(2,1)}, bf16[384,256]{1,0:T(8,128)(2,1)}) fusion(bf16[384,512]{1,0:T(8,128)(2,1)S(1)} %maximum_maximum_fusion), kind=kLoop, calls=%fused_computation.79 | loop fusion | bytes 786432 | tf_op jit(solution)/shard_map/slice | solution.py:266
  21.4 11.5 %shard_map.110 = (f32[128,1792]{1,0:T(8,128)}, f32[128,1792]{1,0:T(8,128)}, f32[384,256]{1,0:T(8,128)}, f32[384,256]{1,0:T(8,128)}) custom-call(s32[3]{0:T(128)} %pad_add_fusion.info_ref, bf16[128,1792]{1,0:T(8,128)(2,1)} %bitcast.87, bf16[128,1792]{1,0:T(8,128)(2,1)} %bitcast.89, bf16[384,256]{1,0:T(8,128)(2,1)} %get-tuple-element.26.k_ref, ...), custom_call_target="tpu_custom_call" | custom-call | flops 1056964608 | bytes 3932160 | tf_op jit(solution)/shard_map/pallas_call | solution.py:251
  32.9 1.1 %convert.28 = bf16[384,256]{1,0:T(8,128)(2,1)S(1)} convert(f32[384,256]{1,0:T(8,128)} %get-tuple-element.22) | non-fusion elementwise | flops 98304 | bytes 589824 | tf_op jit(solution)/shard_map/convert.7
  34.1 0.7 add_convert_fusion.prior_ref
  34.8 10.2 %shard_map.111 = (bf16[128,1792]{1,0:T(8,128)(2,1)}, bf16[128,1792]{1,0:T(8,128)(2,1)}, f32[2,128,128]{2,1,0:T(8,128)}, f32[1,1792]{1,0:T(1,128)}, f32[128,256]{1,0:T(8,128)}, /*index=5*/f32[128,256]{1,0:T(8,128)}) custom-call(bf16[128,1792]{1,0:T(8,128)(2,1)} %bitcast.88, bf16[128,1792]{1,0:T(8,128)(2,1)} %bitcast.90, bf16[128,256]{1,0:T(8,128)(2,1)} %bitcast.74, ...), custom_call_target="tpu_custom_call" | custom-call | flops 587202560 | bytes 4456448 | tf_op jit(solution)/shard_map/pallas_call | solution.py:267
  45.0 0.9 %convert.25 = bf16[2,128,128]{2,1,0:T(8,128)(2,1)S(1)} convert(f32[2,128,128]{2,1,0:T(8,128)} %get-tuple-element.20) | non-fusion elementwise | flops 32768 | bytes 196608 | tf_op jit(solution)/shard_map/convert.13
  45.9 0.1 maximum_maximum_fusion.2
  46.0 0.6 collective-permute-start.4
  46.6 1.3 %collective-permute-start.7 = (bf16[128,512]{1,0:T(8,128)(2,1)S(1)}, bf16[128,512]{1,0:T(8,128)(2,1)S(1)}, u32[]{:S(2)}, u32[]{:S(2)}) collective-permute-start(bf16[128,512]{1,0:T(8,128)(2,1)S(1)} %pad_maximum_fusion), channel_id=1, source_target_pairs={{1,0},{2,1},{3,2},{4,3},{5,4},{6,5},{7,6},{9,8},{10,9},{11,10},{12... | collective-permute-start | bytes 393224 | tf_op jit(solution)/shard_map/ppermute | solution.py:96
  48.0 2.3 %collective-permute-start.5 = (bf16[272,128]{1,0:T(8,128)(2,1)S(1)}, bf16[272,128]{1,0:T(8,128)(2,1)S(1)}, u32[]{:S(2)}, u32[]{:S(2)}) collective-permute-start(bf16[272,128]{1,0:T(8,128)(2,1)S(1)} %fusion.3), channel_id=1, source_target_pairs={{0,2},{1,3},{2,0},{3,1},{4,6},{5,7},{6,4},{7,5},{8,10},{9,11},{10,... | collective-permute-start | bytes 208904 | tf_op jit(solution)/shard_map/ppermute | solution.py:45
  50.3 1.3 %collective-permute-start.8 = (bf16[128,512]{1,0:T(8,128)(2,1)S(1)}, bf16[128,512]{1,0:T(8,128)(2,1)S(1)}, u32[]{:S(2)}, u32[]{:S(2)}) collective-permute-start(bf16[128,512]{1,0:T(8,128)(2,1)S(1)} %pad_maximum_fusion.1), channel_id=1, source_target_pairs={{2,0},{3,1},{4,2},{5,3},{6,4},{7,5},{10,8},{11,9},{12,10},{13,11},... | collective-permute-start | bytes 393224 | tf_op jit(solution)/shard_map/ppermute | solution.py:96
  51.6 3.8 %collective-permute-done.5 = bf16[272,128]{1,0:T(8,128)(2,1)S(1)} collective-permute-done((bf16[272,128]{1,0:T(8,128)(2,1)S(1)}, bf16[272,128]{1,0:T(8,128)(2,1)S(1)}, u32[]{:S(2)}, u32[]{:S(2)}) %collective-permute-start.5) | collective-permute-done | bytes 69664 | tf_op jit(solution)/shard_map/ppermute | solution.py:45
  55.6 1.8 %collective-permute-done.8 = bf16[128,512]{1,0:T(8,128)(2,1)S(1)} collective-permute-done((bf16[128,512]{1,0:T(8,128)(2,1)S(1)}, bf16[128,512]{1,0:T(8,128)(2,1)S(1)}, u32[]{:S(2)}, u32[]{:S(2)}) %collective-permute-start.8) | collective-permute-done | bytes 131104 | tf_op jit(solution)/shard_map/ppermute | solution.py:96
  57.4 2.4 %collective-permute-done.6 = bf16[272,128]{1,0:T(8,128)(2,1)S(1)} collective-permute-done((bf16[272,128]{1,0:T(8,128)(2,1)S(1)}, bf16[272,128]{1,0:T(8,128)(2,1)S(1)}, u32[]{:S(2)}, u32[]{:S(2)}) %collective-permute-start.6) | collective-permute-done | bytes 69664 | tf_op jit(solution)/shard_map/ppermute | solution.py:45
  59.9 1.6 %collective-permute-start.9 = (f32[1792]{0:T(1024)S(1)}, f32[1792]{0:T(1024)S(1)}, u32[]{:S(2)}, u32[]{:S(2)}) collective-permute-start(f32[1792]{0:T(1024)S(1)} %get-tuple-element.30), channel_id=1, source_target_pairs={{0,8},{8,0},{16,24},{24,16},{1,9},{9,1},{17,25},{25,17},{2,10},{10... | collective-permute-start | bytes 21512 | tf_op jit(solution)/shard_map/ppermute | solution.py:80
  61.5 2.6 %collective-permute-start.10 = (f32[1792]{0:T(1024)S(1)}, f32[1792]{0:T(1024)S(1)}, u32[]{:S(2)}, u32[]{:S(2)}) collective-permute-start(f32[1792]{0:T(1024)S(1)} %get-tuple-element.30), channel_id=1, source_target_pairs={{0,16},{8,24},{16,0},{24,8},{1,17},{9,25},{17,1},{25,9},{2,18},{10... | collective-permute-start | bytes 21512 | tf_op jit(solution)/shard_map/ppermute | solution.py:80
  64.1 0.2 collective-permute-start.11
  64.4 0.1 slice_add_fusion.4
  64.6 0.1 slice_add_fusion.3
  64.7 0.7 copy-done.1
  65.4 0.1 copy-done.7
  65.5 0.1 slice_add_fusion.2
  65.7 0.1 slice_add_fusion.1
  65.8 1.6 %fusion.13 = (bf16[1,128,256]{2,1,0:T(8,128)(2,1)}, bf16[1,128,256]{2,1,0:T(8,128)(2,1)}) fusion(f32[128,512]{1,0:T(8,128)S(1)} %convert_add_fusion, f32[384,256]{1,0:T(8,128)S(1)} %copy-done.4, f32[16,8,2,128]{3,2,1,0:T(2,128)S(1)} %bitcast.82, f32[128,128]{1,0:T(8,128)S(1)} %slice_add_fusion.1, f32[128,128]{1,0:T(8,128)S(1)} %slice_add_fusion.2, ...), kind=kLoop, calls=%fused_computation.44 | loop fusion | flops 294912 | bytes 1048576 | tf_op jit(solution)/shard_map/broadcast_in_dim | solution.py:337
  67.5 2.1 %collective-permute-done.11 = f32[1792]{0:T(1024)S(1)} collective-permute-done((f32[1792]{0:T(1024)S(1)}, f32[1792]{0:T(1024)S(1)}, u32[]{:S(2)}, u32[]{:S(2)}) %collective-permute-start.11) | collective-permute-done | bytes 7200 | tf_op jit(solution)/shard_map/ppermute | solution.py:80
  69.6 0.6 multiply_reduce_fusion
  (61 shorter events, 0.7 us)
Async XLA Ops:
  0.6 0.9 %copy-start.5 = (bf16[1,128,256]{2,1,0:T(8,128)(2,1)S(1)}, bf16[1,128,256]{2,1,0:T(8,128)(2,1)}, u32[]{:S(2)}) copy-start(bf16[1,128,256]{2,1,0:T(8,128)(2,1)} %param.9) | copy-start | bytes 196612
  1.5 0.8 %copy-start = (bf16[1,128,256]{2,1,0:T(8,128)(2,1)S(1)}, bf16[1,128,256]{2,1,0:T(8,128)(2,1)}, u32[]{:S(2)}) copy-start(bf16[1,128,256]{2,1,0:T(8,128)(2,1)} %param.8) | copy-start | bytes 196612
  2.3 6.4 %copy-start.11 = (s32[1,128,2]{1,2,0:T(2,128)S(1)}, s32[1,128,2]{1,2,0:T(2,128)}, u32[]{:S(2)}) copy-start(s32[1,128,2]{1,2,0:T(2,128)} %param.10) | copy-start | bytes 3076
  2.3 9.7 %collective-permute-start = (bf16[128,640]{1,0:T(8,128)(2,1)S(1)}, bf16[128,640]{1,0:T(8,128)(2,1)S(1)}, u32[]{:S(2)}, u32[]{:S(2)}) collective-permute-start(bf16[128,640]{1,0:T(8,128)(2,1)S(1)} %maximum_maximum_fusion.1), channel_id=1, source_target_pairs={{0,2},{1,3},{2,4},{3,5},{4,6},{5,7},{8,10},{9,11},{10,12},{11,13},... | collective-permute-start | bytes 491528 | tf_op jit(solution)/shard_map/ppermute | solution.py:96
  7.2 5.5 %collective-permute-start.1 = (bf16[128,640]{1,0:T(8,128)(2,1)S(1)}, bf16[128,640]{1,0:T(8,128)(2,1)S(1)}, u32[]{:S(2)}, u32[]{:S(2)}) collective-permute-start(bf16[128,640]{1,0:T(8,128)(2,1)S(1)} %maximum_maximum_fusion.1), channel_id=1, source_target_pairs={{0,1},{1,2},{2,3},{3,4},{4,5},{5,6},{6,7},{8,9},{9,10},{10,11},{11... | collective-permute-start | bytes 491528 | tf_op jit(solution)/shard_map/ppermute | solution.py:96
  9.0 2.9 %copy-start.2 = (bf16[128,256]{1,0:T(8,128)(2,1)}, bf16[128,256]{1,0:T(8,128)(2,1)S(1)}, u32[]{:S(2)}) copy-start(bf16[128,256]{1,0:T(8,128)(2,1)S(1)} %fusion.7.s_ref) | copy-start | bytes 196612
  9.3 0.7 copy-start.12
  10.5 0.7 copy-start.9
  12.1 7.6 %copy-start.6 = (bf16[128,640]{1,0:T(8,128)(2,1)}, bf16[128,640]{1,0:T(8,128)(2,1)S(1)}, u32[]{:S(2)}) copy-start(bf16[128,640]{1,0:T(8,128)(2,1)S(1)} %collective-permute-done) | copy-start | bytes 491524
  13.4 20.7 %collective-permute-start.2 = (f32[2,128,128]{2,1,0:T(8,128)S(1)}, f32[2,128,128]{2,1,0:T(8,128)S(1)}, u32[]{:S(2)}, u32[]{:S(2)}) collective-permute-start(f32[2,128,128]{2,1,0:T(8,128)S(1)} %maximum_add_fusion.1), channel_id=1, source_target_pairs={{0,3},{1,4},{2,5},{3,6},{4,7},{8,11},{9,12},{10,13},{11,14},{12,15... | collective-permute-start | bytes 393224 | tf_op jit(solution)/shard_map/ppermute | solution.py:96
  18.4 15.7 %collective-permute-start.3 = (f32[2,128,128]{2,1,0:T(8,128)S(1)}, f32[2,128,128]{2,1,0:T(8,128)S(1)}, u32[]{:S(2)}, u32[]{:S(2)}) collective-permute-start(f32[2,128,128]{2,1,0:T(8,128)S(1)} %maximum_add_fusion.1), channel_id=1, source_target_pairs={{0,6},{1,7},{8,14},{9,15},{16,22},{17,23},{24,30},{25,31}} | collective-permute-start | bytes 393224 | tf_op jit(solution)/shard_map/ppermute | solution.py:96
  19.7 0.9 %slice-start = ((bf16[128,640]{1,0:T(8,128)(2,1)}), bf16[128,512]{1,0:T(8,128)(2,1)S(1)}, s32[]{:S(2)}) async-start(bf16[128,640]{1,0:T(8,128)(2,1)} %copy-done.6), calls=%async_computation | async-start | bytes 262144 | tf_op jit(solution)/shard_map/slice | solution.py:246
  32.9 1.1 %copy-start.4 = (f32[384,256]{1,0:T(8,128)S(1)}, f32[384,256]{1,0:T(8,128)}, u32[]{:S(2)}) copy-start(f32[384,256]{1,0:T(8,128)} %get-tuple-element.23) | copy-start | bytes 1179652
  45.0 0.9 %copy-start.10 = (f32[1,1792]{1,0:T(1,128)S(1)}, f32[1,1792]{1,0:T(1,128)}, u32[]{:S(2)}) copy-start(f32[1,1792]{1,0:T(1,128)} %get-tuple-element.21) | copy-start | bytes 21508
  46.0 1.9 %collective-permute-start.4 = (bf16[272,128]{1,0:T(8,128)(2,1)S(1)}, bf16[272,128]{1,0:T(8,128)(2,1)S(1)}, u32[]{:S(2)}, u32[]{:S(2)}) collective-permute-start(bf16[272,128]{1,0:T(8,128)(2,1)S(1)} %maximum_maximum_fusion.2), channel_id=1, source_target_pairs={{0,1},{1,0},{2,3},{3,2},{4,5},{5,4},{6,7},{7,6},{8,9},{9,8},{10,11... | collective-permute-start | bytes 208904 | tf_op jit(solution)/shard_map/ppermute | solution.py:45
  46.6 8.9 %collective-permute-start.7 = (bf16[128,512]{1,0:T(8,128)(2,1)S(1)}, bf16[128,512]{1,0:T(8,128)(2,1)S(1)}, u32[]{:S(2)}, u32[]{:S(2)}) collective-permute-start(bf16[128,512]{1,0:T(8,128)(2,1)S(1)} %pad_maximum_fusion), channel_id=1, source_target_pairs={{1,0},{2,1},{3,2},{4,3},{5,4},{6,5},{7,6},{9,8},{10,9},{11,10},{12... | collective-permute-start | bytes 393224 | tf_op jit(solution)/shard_map/ppermute | solution.py:96
  48.0 7.5 %collective-permute-start.5 = (bf16[272,128]{1,0:T(8,128)(2,1)S(1)}, bf16[272,128]{1,0:T(8,128)(2,1)S(1)}, u32[]{:S(2)}, u32[]{:S(2)}) collective-permute-start(bf16[272,128]{1,0:T(8,128)(2,1)S(1)} %fusion.3), channel_id=1, source_target_pairs={{0,2},{1,3},{2,0},{3,1},{4,6},{5,7},{6,4},{7,5},{8,10},{9,11},{10,... | collective-permute-start | bytes 208904 | tf_op jit(solution)/shard_map/ppermute | solution.py:45
  50.3 7.1 %collective-permute-start.8 = (bf16[128,512]{1,0:T(8,128)(2,1)S(1)}, bf16[128,512]{1,0:T(8,128)(2,1)S(1)}, u32[]{:S(2)}, u32[]{:S(2)}) collective-permute-start(bf16[128,512]{1,0:T(8,128)(2,1)S(1)} %pad_maximum_fusion.1), channel_id=1, source_target_pairs={{2,0},{3,1},{4,2},{5,3},{6,4},{7,5},{10,8},{11,9},{12,10},{13,11},... | collective-permute-start | bytes 393224 | tf_op jit(solution)/shard_map/ppermute | solution.py:96
  55.5 4.4 %collective-permute-start.6 = (bf16[272,128]{1,0:T(8,128)(2,1)S(1)}, bf16[272,128]{1,0:T(8,128)(2,1)S(1)}, u32[]{:S(2)}, u32[]{:S(2)}) collective-permute-start(bf16[272,128]{1,0:T(8,128)(2,1)S(1)} %fusion.4), channel_id=1, source_target_pairs={{0,4},{1,5},{2,6},{3,7},{4,0},{5,1},{6,2},{7,3},{8,12},{9,13},{10,... | collective-permute-start | bytes 208904 | tf_op jit(solution)/shard_map/ppermute | solution.py:45
  59.9 4.5 %copy-start.3 = (bf16[128,256]{1,0:T(8,128)(2,1)S(1)}, bf16[128,256]{1,0:T(8,128)(2,1)}, u32[]{:S(2)}) copy-start(bf16[128,256]{1,0:T(8,128)(2,1)} %copy-done.2) | copy-start | bytes 196612
  59.9 4.5 %copy-start.8 = (f32[128,256]{1,0:T(8,128)S(1)}, f32[128,256]{1,0:T(8,128)}, u32[]{:S(2)}) copy-start(f32[128,256]{1,0:T(8,128)} %get-tuple-element.19) | copy-start | bytes 393220
  59.9 7.5 %collective-permute-start.9 = (f32[1792]{0:T(1024)S(1)}, f32[1792]{0:T(1024)S(1)}, u32[]{:S(2)}, u32[]{:S(2)}) collective-permute-start(f32[1792]{0:T(1024)S(1)} %get-tuple-element.30), channel_id=1, source_target_pairs={{0,8},{8,0},{16,24},{24,16},{1,9},{9,1},{17,25},{25,17},{2,10},{10... | collective-permute-start | bytes 21512 | tf_op jit(solution)/shard_map/ppermute | solution.py:80
  61.5 5.9 %collective-permute-start.10 = (f32[1792]{0:T(1024)S(1)}, f32[1792]{0:T(1024)S(1)}, u32[]{:S(2)}, u32[]{:S(2)}) collective-permute-start(f32[1792]{0:T(1024)S(1)} %get-tuple-element.30), channel_id=1, source_target_pairs={{0,16},{8,24},{16,0},{24,8},{1,17},{9,25},{17,1},{25,9},{2,18},{10... | collective-permute-start | bytes 21512 | tf_op jit(solution)/shard_map/ppermute | solution.py:80
  64.1 5.4 %collective-permute-start.11 = (f32[1792]{0:T(1024)S(1)}, f32[1792]{0:T(1024)S(1)}, u32[]{:S(2)}, u32[]{:S(2)}) collective-permute-start(f32[1792]{0:T(1024)S(1)} %get-tuple-element.30), channel_id=1, source_target_pairs={{0,24},{8,16},{16,8},{24,0},{1,25},{9,17},{17,9},{25,1},{2,26},{10... | collective-permute-start | bytes 21512 | tf_op jit(solution)/shard_map/ppermute | solution.py:80
  64.6 0.9 %copy-start.1 = (bf16[1,128,256]{2,1,0:T(8,128)(2,1)S(1)}, bf16[1,128,256]{2,1,0:T(8,128)(2,1)}, u32[]{:S(2)}) copy-start(bf16[1,128,256]{2,1,0:T(8,128)(2,1)} %param.8) | copy-start | bytes 196612
  64.6 0.9 %copy-start.7 = (f32[128,256]{1,0:T(8,128)S(1)}, f32[128,256]{1,0:T(8,128)}, u32[]{:S(2)}) copy-start(f32[128,256]{1,0:T(8,128)} %get-tuple-element.24) | copy-start | bytes 393220

commit v12 on v10

--- a/solution.py
+++ b/solution.py
@@ -88,14 +88,22 @@
     return lax.ppermute(block, axis, route)
 
 
+def stacked_heads(ref, group, group_size):
+    return jnp.concatenate(
+        [ref[:, (group * group_size + h) * HEAD_SIZE : (group * group_size + h + 1) * HEAD_SIZE] for h in range(group_size)],
+        axis=0,
+    )
+
+
 def window_kernel(info_ref, q_ref, c_ref, k_ref, v_ref, wout_ref, wdq_ref, dk_ref, dv_ref):
     group_size = QUERY_HEADS // KEY_VALUE_HEADS
     token_rows = q_ref.shape[0]
     window_rows = k_ref.shape[0]
     padding_rows = window_rows - token_rows
     scale = HEAD_SIZE ** (-0.5)
-    row = lax.broadcasted_iota(jnp.int32, (token_rows, window_rows), 0)
-    col = lax.broadcasted_iota(jnp.int32, (token_rows, window_rows), 1)
+    stacked_rows = group_size * token_rows
+    row = lax.broadcasted_iota(jnp.int32, (stacked_rows, window_rows), 0) % token_rows
+    col = lax.broadcasted_iota(jnp.int32, (stacked_rows, window_rows), 1)
     back = row + padding_rows - col
     seen = (back >= 0) & (col + info_ref[2] >= 0)
     for g in range(KEY_VALUE_HEADS):
@@ -103,80 +111,85 @@
         lanes = slice(g * HEAD_SIZE, (g + 1) * HEAD_SIZE)
         kg = k_ref[:, lanes]
         vg = v_ref[:, lanes]
-        dk = jnp.zeros((window_rows, HEAD_SIZE), jnp.float32)
-        dv = jnp.zeros((window_rows, HEAD_SIZE), jnp.float32)
+        qs = stacked_heads(q_ref, g, group_size)
+        cs = stacked_heads(c_ref, g, group_size)
+        s = lax.dot_general(qs, kg, (((1,), (1,)), ((), ())), preferred_element_type=jnp.float32) * scale
+        s = jnp.where(visible, s, -1e30)
+        top = jnp.max(s, axis=-1, keepdims=True)
+        e = jnp.exp(s - top)
+        p = e * (1.0 / jnp.sum(e, axis=-1, keepdims=True))
+        ph = p.astype(jnp.bfloat16)
+        wout = jnp.dot(ph, vg, preferred_element_type=jnp.float32)
+        gp = lax.dot_general(cs, vg, (((1,), (1,)), ((), ())), preferred_element_type=jnp.float32)
+        delta = jnp.sum(cs.astype(jnp.float32) * wout, axis=-1, keepdims=True)
+        ds = (p * (gp - delta) * scale).astype(jnp.bfloat16)
+        wdq = jnp.dot(ds, kg, preferred_element_type=jnp.float32)
         for h in range(group_size):
             cols = slice((g * group_size + h) * HEAD_SIZE, (g * group_size + h + 1) * HEAD_SIZE)
-            qh = q_ref[:, cols]
-            ch = c_ref[:, cols]
-            s = lax.dot_general(qh, kg, (((1,), (1,)), ((), ())), preferred_element_type=jnp.float32) * scale
-            s = jnp.where(visible, s, -1e30)
-            top = jnp.max(s, axis=-1, keepdims=True)
-            e = jnp.exp(s - top)
-            p = e * (1.0 / jnp.sum(e, axis=-1, keepdims=True))
-            ph = p.astype(jnp.bfloat16)
-            wout = jnp.dot(ph, vg, preferred_element_type=jnp.float32)
-            wout_ref[:, cols] = wout
-            gp = lax.dot_general(ch, vg, (((1,), (1,)), ((), ())), preferred_element_type=jnp.float32)
-            delta = jnp.sum(ch.astype(jnp.float32) * wout, axis=-1, keepdims=True)
-            ds = (p * (gp - delta) * scale).astype(jnp.bfloat16)
-            wdq_ref[:, cols] = jnp.dot(ds, kg, preferred_element_type=jnp.float32)
-            dk = dk + lax.dot_general(ds, qh, (((0,), (0,)), ((), ())), preferred_element_type=jnp.float32)
-            dv = dv + lax.dot_general(ph, ch, (((0,), (0,)), ((), ())), preferred_element_type=jnp.float32)
-        dk_ref[:, lanes] = dk
-        dv_ref[:, lanes] = dv
+            rows = slice(h * token_rows, (h + 1) * token_rows)
+            wout_ref[:, cols] = wout[rows]
+            wdq_ref[:, cols] = wdq[rows]
+        dk_ref[:, lanes] = lax.dot_general(ds, qs, (((0,), (0,)), ((), ())), preferred_element_type=jnp.float32)
+        dv_ref[:, lanes] = lax.dot_general(ph, cs, (((0,), (0,)), ((), ())), preferred_element_type=jnp.float32)
 
 
 def linear_kernel(q_ref, c_ref, k_ref, s_ref, prior_ref, gain_ref, wout_ref, wdq_ref,
                   mixed_ref, dq_ref, suffix_ref, gsum_ref, ldk_ref, dsp_ref):
     group_size = QUERY_HEADS // KEY_VALUE_HEADS
     token_rows = q_ref.shape[0]
-    row = lax.broadcasted_iota(jnp.int32, (token_rows, token_rows), 0)
-    col = lax.broadcasted_iota(jnp.int32, (token_rows, token_rows), 1)
+    stacked_rows = group_size * token_rows
+    row = lax.broadcasted_iota(jnp.int32, (stacked_rows, token_rows), 0) % token_rows
+    col = lax.broadcasted_iota(jnp.int32, (stacked_rows, token_rows), 1)
     causal = row >= col
     for g in range(KEY_VALUE_HEADS):
         lanes = slice(g * HEAD_SIZE, (g + 1) * HEAD_SIZE)
         kg = k_ref[:, lanes]
         sg = s_ref[:, lanes]
         pg = prior_ref[g]
-        suffix = jnp.zeros((HEAD_SIZE, HEAD_SIZE), jnp.float32)
-        ldk = jnp.zeros((token_rows, HEAD_SIZE), jnp.float32)
-        dsp = jnp.zeros((token_rows, HEAD_SIZE), jnp.float32)
+        qs = stacked_heads(q_ref, g, group_size)
+        cs = stacked_heads(c_ref, g, group_size).astype(jnp.float32)
+        gs = jnp.concatenate(
+            [
+                jnp.broadcast_to(
+                    gain_ref[:, (g * group_size + h) * HEAD_SIZE : (g * group_size + h + 1) * HEAD_SIZE],
+                    (token_rows, HEAD_SIZE),
+                )
+                for h in range(group_size)
+            ],
+            axis=0,
+        )
+        lh = jnp.where(
+            causal,
+            lax.dot_general(qs, kg, (((1,), (1,)), ((), ())), preferred_element_type=jnp.float32),
+            0.0,
+        ).astype(jnp.bfloat16)
+        lin = jnp.dot(lh, sg, preferred_element_type=jnp.float32) + jnp.dot(
+            qs, pg, preferred_element_type=jnp.float32
+        )
+        inverse_root = 1.0 / jnp.sqrt(jnp.mean(lin * lin, axis=-1, keepdims=True) + epsilon)
+        normed = lin * inverse_root
+        gn = gs * normed
+        weighted = cs * normed
+        scaled = cs * gs
+        dl = ((scaled - normed * jnp.mean(scaled * normed, axis=-1, keepdims=True)) * inverse_root).astype(
+            jnp.bfloat16
+        )
+        suffix_ref[g] = lax.dot_general(qs, dl, (((0,), (0,)), ((), ())), preferred_element_type=jnp.float32)
+        bh = jnp.where(
+            causal,
+            lax.dot_general(dl, sg, (((1,), (1,)), ((), ())), preferred_element_type=jnp.float32),
+            0.0,
+        ).astype(jnp.bfloat16)
+        ldq = lax.dot_general(dl, pg, (((1,), (1,)), ((), ())), preferred_element_type=jnp.float32)
+        ldq = ldq + jnp.dot(bh, kg, preferred_element_type=jnp.float32)
         for h in range(group_size):
             cols = slice((g * group_size + h) * HEAD_SIZE, (g * group_size + h + 1) * HEAD_SIZE)
-            qh = q_ref[:, cols]
-            ch = c_ref[:, cols].astype(jnp.float32)
-            gh = gain_ref[:, cols]
-            lh = jnp.where(
-                causal,
-                lax.dot_general(qh, kg, (((1,), (1,)), ((), ())), preferred_element_type=jnp.float32),
-                0.0,
-            ).astype(jnp.bfloat16)
-            lin = jnp.dot(lh, sg, preferred_element_type=jnp.float32) + jnp.dot(
-                qh, pg, preferred_element_type=jnp.float32
-            )
-            inverse_root = 1.0 / jnp.sqrt(jnp.mean(lin * lin, axis=-1, keepdims=True) + epsilon)
-            normed = lin * inverse_root
-            mixed_ref[:, cols] = (gh * normed + wout_ref[:, cols]).astype(mixed_ref.dtype)
-            gsum_ref[:, cols] = jnp.sum(ch * normed, axis=0, keepdims=True)
-            scaled = ch * gh
-            dl = ((scaled - normed * jnp.mean(scaled * normed, axis=-1, keepdims=True)) * inverse_root).astype(
-                jnp.bfloat16
-            )
-            suffix = suffix + lax.dot_general(qh, dl, (((0,), (0,)), ((), ())), preferred_element_type=jnp.float32)
-            bh = jnp.where(
-                causal,
-                lax.dot_general(dl, sg, (((1,), (1,)), ((), ())), preferred_element_type=jnp.float32),
-                0.0,
-            ).astype(jnp.bfloat16)
-            ldq = lax.dot_general(dl, pg, (((1,), (1,)), ((), ())), preferred_element_type=jnp.float32)
-            ldq = ldq + jnp.dot(bh, kg, preferred_element_type=jnp.float32)
-            dq_ref[:, cols] = (ldq + wdq_ref[:, cols]).astype(dq_ref.dtype)
-            ldk = ldk + lax.dot_general(bh, qh, (((0,), (0,)), ((), ())), preferred_element_type=jnp.float32)
-            dsp = dsp + lax.dot_general(lh, dl, (((0,), (0,)), ((), ())), preferred_element_type=jnp.float32)
-        suffix_ref[g] = suffix
-        ldk_ref[:, lanes] = ldk
-        dsp_ref[:, lanes] = dsp
+            rows = slice(h * token_rows, (h + 1) * token_rows)
+            mixed_ref[:, cols] = (gn[rows] + wout_ref[:, cols]).astype(mixed_ref.dtype)
+            gsum_ref[:, cols] = jnp.sum(weighted[rows], axis=0, keepdims=True)
+            dq_ref[:, cols] = (ldq[rows] + wdq_ref[:, cols]).astype(dq_ref.dtype)
+        ldk_ref[:, lanes] = lax.dot_general(bh, qs, (((0,), (0,)), ((), ())), preferred_element_type=jnp.float32)
+        dsp_ref[:, lanes] = lax.dot_general(lh, dl, (((0,), (0,)), ((), ())), preferred_element_type=jnp.float32)
 
 
 def in_vmem(count):

time: 69.7 us -> 58.6 us (0.84)
  Pallas kernels: 21.6 us -> 10.6 us
    pallas_call x1, Pallas kernels: 11.4 us -> 5.59 us  [per_device(): pl.pallas_call(window_kernel, out_shape=(jax.ShapeDtypeStruct((token_rows...]
    pallas_call x1, Pallas kernels: 10.2 us -> 4.97 us  [per_device(): pl.pallas_call(linear_kernel, out_shape=(jax.ShapeDtypeStruct((token_rows...]
  transfers between devices with their start and end apart: 11 -> 11, of which waited for: 5 -> 5; matrix products, arithmetic and copies ran while one was open for 9% -> 11% of each run, Pallas kernels for 17% -> 10%
where the time goes in v12:
time: 58.6 us; the launch traced here: 58 us
  starting transfers between devices  23.1 us (39%)
  Pallas kernels  10.6 us (18%)
  waiting for transfers between devices  10.2 us (17%)
  other arithmetic  5.94 us (10%)
  local copies, waits for them, and re-layouts  5.45 us (9%)
  matrix products  1.68 us (3%)
  between operations  1.06 us (2%)
    ppermute x6, starting transfers between devices, shifted(): return lax.ppermute(block, axis, route)  15.9 us
    ppermute x3, waiting for transfers between devices, butterfly_scan(): lax.ppermute(mine, axis, [(i, i ^ step) for i in range(count)])  6.24 us
    pallas_call x1, Pallas kernels, per_device(): pl.pallas_call(window_kernel, out_shape=(jax.ShapeDtypeStruct((token_rows...  5.59 us
    pallas_call x1, Pallas kernels, per_device(): pl.pallas_call(linear_kernel, out_shape=(jax.ShapeDtypeStruct((token_rows...  4.97 us
    ppermute x2, starting transfers between devices, all_sum(): part = part + lax.ppermute(part, axes, route)  4.23 us
    ppermute x3, starting transfers between devices, butterfly_scan(): lax.ppermute(mine, axis, [(i, i ^ step) for i in range(count)])  2.99 us
    unnamed x27, local copies, waits for them, and re-layouts  2.3 us
    ppermute x2, waiting for transfers between devices, all_sum(): part = part + lax.ppermute(part, axes, route)  2.14 us
  transfers between devices with their start and end apart: 11, of which 5 were waited for; matrix products, arithmetic and copies ran while one was open for 11% of the time, Pallas kernels for 10%

profile of v12, /device:TPU:0, one launch (start us, length us, event | category | flops | bytes accessed | tf_op | source)
XLA Modules:
  0.0 58.0 jit_solution(5671928388185524150)
XLA Ops:
  0.6 0.8 %copy.13 = s32[1,128,2]{2,1,0:T(8,128)S(1)} copy(s32[1,128,2]{1,2,0:T(2,128)} %param.10) | data formatting | bytes 2048 | tf_op args[3]
  1.5 0.1 pad.26.clone
  1.6 0.7 %copy-done = bf16[1,128,256]{2,1,0:T(8,128)(2,1)S(1)} copy-done((bf16[1,128,256]{2,1,0:T(8,128)(2,1)S(1)}, bf16[1,128,256]{2,1,0:T(8,128)(2,1)}, u32[]{:S(2)}) %copy-start) | copy-done | bytes 65560
  2.3 4.9 %collective-permute-start = (bf16[128,640]{1,0:T(8,128)(2,1)S(1)}, bf16[128,640]{1,0:T(8,128)(2,1)S(1)}, u32[]{:S(2)}, u32[]{:S(2)}) collective-permute-start(bf16[128,640]{1,0:T(8,128)(2,1)S(1)} %maximum_maximum_fusion.1), channel_id=1, source_target_pairs={{0,2},{1,3},{2,4},{3,5},{4,6},{5,7},{8,10},{9,11},{10,12},{11,13},... | collective-permute-start | bytes 491528 | tf_op jit(solution)/shard_map/ppermute | solution.py:88
  7.2 1.5 %collective-permute-start.1 = (bf16[128,640]{1,0:T(8,128)(2,1)S(1)}, bf16[128,640]{1,0:T(8,128)(2,1)S(1)}, u32[]{:S(2)}, u32[]{:S(2)}) collective-permute-start(bf16[128,640]{1,0:T(8,128)(2,1)S(1)} %maximum_maximum_fusion.1), channel_id=1, source_target_pairs={{0,1},{1,2},{2,3},{3,4},{4,5},{5,6},{6,7},{8,9},{9,10},{10,11},{11... | collective-permute-start | bytes 491528 | tf_op jit(solution)/shard_map/ppermute | solution.py:88
  8.7 0.1 copy.12
  8.8 0.2 broadcast_in_dim.33
  9.0 0.2 convolution_bitcast_fusion.2
  9.3 0.7 %copy-done.12 = s32[2]{0:T(128)S(1)} copy-done((s32[2]{0:T(128)S(1)}, s32[2]{0:T(128)}, u32[]{:S(2)}) %copy-start.12) | copy-done | bytes 32
  9.9 0.6 %pad_add_fusion.info_ref = s32[3]{0:T(128)} fusion(s32[1]{0:T(128)} %bitcast.14, s32[2]{0:T(128)S(1)} %copy-done.12), kind=kLoop, calls=%fused_computation.75 | loop fusion | flops 3 | bytes 24 | tf_op jit(solution)/shard_map/concatenate | solution.py:253
  10.5 0.6 %reshape.47.gain_ref = f32[1,1792]{1,0:T(1,128)} reshape(f32[1792]{0:T(1024)S(1)} %copy-done.9) | data formatting | bytes 14336 | tf_op jit(solution)/shard_map/reshape | solution.py:289
  11.1 0.1 pad.10.clone
  11.2 0.2 convolution_bitcast_fusion.3
  11.4 0.2 broadcast_in_dim.35
  11.7 0.2 convolution_bitcast_fusion.6
  11.9 0.2 convolution_bitcast_fusion.7
  12.1 0.2 broadcast_in_dim.36
  12.3 0.2 convolution_bitcast_fusion.5
  12.5 0.2 convolution_bitcast_fusion.4
  12.7 5.0 %collective-permute-start.2 = (f32[2,128,128]{2,1,0:T(8,128)S(1)}, f32[2,128,128]{2,1,0:T(8,128)S(1)}, u32[]{:S(2)}, u32[]{:S(2)}) collective-permute-start(f32[2,128,128]{2,1,0:T(8,128)S(1)} %maximum_add_fusion.1), channel_id=1, source_target_pairs={{0,3},{1,4},{2,5},{3,6},{4,7},{8,11},{9,12},{10,13},{11,14},{12,15... | collective-permute-start | bytes 393224 | tf_op jit(solution)/shard_map/ppermute | solution.py:88
  17.7 1.9 %collective-permute-start.3 = (f32[2,128,128]{2,1,0:T(8,128)S(1)}, f32[2,128,128]{2,1,0:T(8,128)S(1)}, u32[]{:S(2)}, u32[]{:S(2)}) collective-permute-start(f32[2,128,128]{2,1,0:T(8,128)S(1)} %maximum_add_fusion.1), channel_id=1, source_target_pairs={{0,6},{1,7},{8,14},{9,15},{16,22},{17,23},{24,30},{25,31}} | collective-permute-start | bytes 393224 | tf_op jit(solution)/shard_map/ppermute | solution.py:88
  19.7 0.9 %slice-done = bf16[128,512]{1,0:T(8,128)(2,1)S(1)} async-done(((bf16[128,640]{1,0:T(8,128)(2,1)}), bf16[128,512]{1,0:T(8,128)(2,1)S(1)}, s32[]{:S(2)}) %slice-start) | async-done | bytes 131096 | tf_op jit(solution)/shard_map/slice | solution.py:251
  20.6 0.8 %fusion.45 = (bf16[384,256]{1,0:T(8,128)(2,1)}, bf16[384,256]{1,0:T(8,128)(2,1)}) fusion(bf16[384,512]{1,0:T(8,128)(2,1)S(1)} %maximum_maximum_fusion), kind=kLoop, calls=%fused_computation.76 | loop fusion | bytes 786432 | tf_op jit(solution)/shard_map/slice | solution.py:271
  21.4 5.6 %shard_map.110 = (f32[128,1792]{1,0:T(8,128)}, f32[128,1792]{1,0:T(8,128)}, f32[384,256]{1,0:T(8,128)}, f32[384,256]{1,0:T(8,128)}) custom-call(s32[3]{0:T(128)} %pad_add_fusion.info_ref, bf16[128,1792]{1,0:T(8,128)(2,1)} %bitcast.81, bf16[128,1792]{1,0:T(8,128)(2,1)} %bitcast.83, bf16[384,256]{1,0:T(8,128)(2,1)} %get-tuple-element.26.k_ref, ...), custom_call_target="tpu_custom_call" | custom-call | flops 1056964608 | bytes 3932160 | tf_op jit(solution)/shard_map/pallas_call | solution.py:256
  27.0 1.1 %convert.28 = bf16[384,256]{1,0:T(8,128)(2,1)S(1)} convert(f32[384,256]{1,0:T(8,128)} %get-tuple-element.22) | non-fusion elementwise | flops 98304 | bytes 589824 | tf_op jit(solution)/shard_map/convert.7
  28.1 0.0 copy-done.4
  28.2 0.7 %add_convert_fusion.prior_ref = bf16[2,128,128]{2,1,0:T(8,128)(2,1)} fusion(f32[2,128,128]{2,1,0:T(8,128)S(1)} %collective-permute-done.3, f32[2,128,128]{2,1,0:T(8,128)S(1)} %collective-permute-done.2, f32[1,128,128]{2,1,0:T(8,128)S(1)} %convolution_bitcast_fusion.4, f32[1,128,128]{2,1,0:T(8,128)S(1)} %convolution_bitcast_fusion.5, ...), kind=kLoop, calls=%fused_computation.37 | loop fusion | flops 196608 | bytes 589824 | tf_op jit(solution)/shard_map/convert_element_type | solution.py:249
  28.9 5.0 %shard_map.111 = (bf16[128,1792]{1,0:T(8,128)(2,1)}, bf16[128,1792]{1,0:T(8,128)(2,1)}, f32[2,128,128]{2,1,0:T(8,128)}, f32[1,1792]{1,0:T(1,128)}, f32[128,256]{1,0:T(8,128)}, /*index=5*/f32[128,256]{1,0:T(8,128)}) custom-call(bf16[128,1792]{1,0:T(8,128)(2,1)} %bitcast.82, bf16[128,1792]{1,0:T(8,128)(2,1)} %bitcast.84, bf16[128,256]{1,0:T(8,128)(2,1)} %bitcast.68, ...), custom_call_target="tpu_custom_call" | custom-call | flops 587202560 | bytes 4456448 | tf_op jit(solution)/shard_map/pallas_call | solution.py:272
  33.8 0.9 %convert.25 = bf16[2,128,128]{2,1,0:T(8,128)(2,1)S(1)} convert(f32[2,128,128]{2,1,0:T(8,128)} %get-tuple-element.20) | non-fusion elementwise | flops 32768 | bytes 196608 | tf_op jit(solution)/shard_map/convert.13
  34.8 0.1 maximum_maximum_fusion.2
  34.9 0.6 %collective-permute-start.4 = (bf16[272,128]{1,0:T(8,128)(2,1)S(1)}, bf16[272,128]{1,0:T(8,128)(2,1)S(1)}, u32[]{:S(2)}, u32[]{:S(2)}) collective-permute-start(bf16[272,128]{1,0:T(8,128)(2,1)S(1)} %maximum_maximum_fusion.2), channel_id=1, source_target_pairs={{0,1},{1,0},{2,3},{3,2},{4,5},{5,4},{6,7},{7,6},{8,9},{9,8},{10,11... | collective-permute-start | bytes 208904 | tf_op jit(solution)/shard_map/ppermute | solution.py:45
  35.5 1.3 %collective-permute-start.7 = (bf16[128,512]{1,0:T(8,128)(2,1)S(1)}, bf16[128,512]{1,0:T(8,128)(2,1)S(1)}, u32[]{:S(2)}, u32[]{:S(2)}) collective-permute-start(bf16[128,512]{1,0:T(8,128)(2,1)S(1)} %pad_maximum_fusion), channel_id=1, source_target_pairs={{1,0},{2,1},{3,2},{4,3},{5,4},{6,5},{7,6},{9,8},{10,9},{11,10},{12... | collective-permute-start | bytes 393224 | tf_op jit(solution)/shard_map/ppermute | solution.py:88
  36.8 2.3 %collective-permute-start.5 = (bf16[272,128]{1,0:T(8,128)(2,1)S(1)}, bf16[272,128]{1,0:T(8,128)(2,1)S(1)}, u32[]{:S(2)}, u32[]{:S(2)}) collective-permute-start(bf16[272,128]{1,0:T(8,128)(2,1)S(1)} %fusion.3), channel_id=1, source_target_pairs={{0,2},{1,3},{2,0},{3,1},{4,6},{5,7},{6,4},{7,5},{8,10},{9,11},{10,... | collective-permute-start | bytes 208904 | tf_op jit(solution)/shard_map/ppermute | solution.py:45
  39.2 1.3 %collective-permute-start.8 = (bf16[128,512]{1,0:T(8,128)(2,1)S(1)}, bf16[128,512]{1,0:T(8,128)(2,1)S(1)}, u32[]{:S(2)}, u32[]{:S(2)}) collective-permute-start(bf16[128,512]{1,0:T(8,128)(2,1)S(1)} %pad_maximum_fusion.1), channel_id=1, source_target_pairs={{2,0},{3,1},{4,2},{5,3},{6,4},{7,5},{10,8},{11,9},{12,10},{13,11},... | collective-permute-start | bytes 393224 | tf_op jit(solution)/shard_map/ppermute | solution.py:88
  40.5 3.8 %collective-permute-done.5 = bf16[272,128]{1,0:T(8,128)(2,1)S(1)} collective-permute-done((bf16[272,128]{1,0:T(8,128)(2,1)S(1)}, bf16[272,128]{1,0:T(8,128)(2,1)S(1)}, u32[]{:S(2)}, u32[]{:S(2)}) %collective-permute-start.5) | collective-permute-done | bytes 69664 | tf_op jit(solution)/shard_map/ppermute | solution.py:45
  44.4 0.1 collective-permute-start.6
  44.5 1.8 %collective-permute-done.8 = bf16[128,512]{1,0:T(8,128)(2,1)S(1)} collective-permute-done((bf16[128,512]{1,0:T(8,128)(2,1)S(1)}, bf16[128,512]{1,0:T(8,128)(2,1)S(1)}, u32[]{:S(2)}, u32[]{:S(2)}) %collective-permute-start.8) | collective-permute-done | bytes 131104 | tf_op jit(solution)/shard_map/ppermute | solution.py:88
  46.3 2.4 %collective-permute-done.6 = bf16[272,128]{1,0:T(8,128)(2,1)S(1)} collective-permute-done((bf16[272,128]{1,0:T(8,128)(2,1)S(1)}, bf16[272,128]{1,0:T(8,128)(2,1)S(1)}, u32[]{:S(2)}, u32[]{:S(2)}) %collective-permute-start.6) | collective-permute-done | bytes 69664 | tf_op jit(solution)/shard_map/ppermute | solution.py:45
  48.8 0.1 slice_add_fusion.4
  48.9 0.2 slice_add_fusion.3
  49.2 1.6 %collective-permute-start.9 = (f32[1792]{0:T(1024)S(1)}, f32[1792]{0:T(1024)S(1)}, u32[]{:S(2)}, u32[]{:S(2)}) collective-permute-start(f32[1792]{0:T(1024)S(1)} %fusion.44), channel_id=1, source_target_pairs={{0,8},{8,0},{16,24},{24,16},{1,9},{9,1},{17,25},{25,17},{2,10},{10... | collective-permute-start | bytes 21512 | tf_op jit(solution)/shard_map/ppermute | solution.py:80
  50.8 0.1 slice_add_fusion.2
  50.9 0.1 slice_add_fusion.1
  51.1 1.8 %collective-permute-done.9 = f32[1792]{0:T(1024)S(1)} collective-permute-done((f32[1792]{0:T(1024)S(1)}, f32[1792]{0:T(1024)S(1)}, u32[]{:S(2)}, u32[]{:S(2)}) %collective-permute-start.9) | collective-permute-done | bytes 7200 | tf_op jit(solution)/shard_map/ppermute | solution.py:80
  52.9 2.6 %collective-permute-start.10 = (f32[1792]{0:T(1024)S(1)}, f32[1792]{0:T(1024)S(1)}, u32[]{:S(2)}, u32[]{:S(2)}) collective-permute-start(f32[1792]{0:T(1024)S(1)} %add.79), channel_id=1, source_target_pairs={{0,16},{8,24},{16,0},{24,8},{1,17},{9,25},{17,1},{25,9},{2,18},{10... | collective-permute-start | bytes 21512 | tf_op jit(solution)/shard_map/ppermute | solution.py:80
  55.5 1.6 %fusion.13 = (bf16[1,128,256]{2,1,0:T(8,128)(2,1)}, bf16[1,128,256]{2,1,0:T(8,128)(2,1)}) fusion(f32[128,512]{1,0:T(8,128)S(1)} %convert_add_fusion, f32[384,256]{1,0:T(8,128)S(1)} %copy-done.4, f32[16,8,2,128]{3,2,1,0:T(2,128)S(1)} %bitcast.76, f32[128,128]{1,0:T(8,128)S(1)} %slice_add_fusion.1, f32[128,128]{1,0:T(8,128)S(1)} %slice_add_fusion.2, ...), kind=kLoop, calls=%fused_computation.44 | loop fusion | flops 294912 | bytes 1048576 | tf_op jit(solution)/shard_map/broadcast_in_dim | solution.py:342
  57.1 0.3 collective-permute-done.10
  57.4 0.6 %add_multiply_fusion = f32[1792]{0:T(1024)} fusion(f32[1792]{0:T(1024)S(1)} %add.79, f32[1792]{0:T(1024)S(1)} %collective-permute-done.10), kind=kLoop, calls=%fused_computation.72 | loop fusion | flops 3584 | bytes 21504 | tf_op jit(solution)/shard_map/mul | solution.py:305
  (55 shorter events, 0.5 us)
Async XLA Ops:
  0.6 0.9 %copy-start.5 = (bf16[1,128,256]{2,1,0:T(8,128)(2,1)S(1)}, bf16[1,128,256]{2,1,0:T(8,128)(2,1)}, u32[]{:S(2)}) copy-start(bf16[1,128,256]{2,1,0:T(8,128)(2,1)} %param.9) | copy-start | bytes 196612
  1.5 0.8 %copy-start = (bf16[1,128,256]{2,1,0:T(8,128)(2,1)S(1)}, bf16[1,128,256]{2,1,0:T(8,128)(2,1)}, u32[]{:S(2)}) copy-start(bf16[1,128,256]{2,1,0:T(8,128)(2,1)} %param.8) | copy-start | bytes 196612
  2.3 6.4 %copy-start.11 = (s32[1,128,2]{1,2,0:T(2,128)S(1)}, s32[1,128,2]{1,2,0:T(2,128)}, u32[]{:S(2)}) copy-start(s32[1,128,2]{1,2,0:T(2,128)} %param.10) | copy-start | bytes 3076
  2.3 9.1 %collective-permute-start = (bf16[128,640]{1,0:T(8,128)(2,1)S(1)}, bf16[128,640]{1,0:T(8,128)(2,1)S(1)}, u32[]{:S(2)}, u32[]{:S(2)}) collective-permute-start(bf16[128,640]{1,0:T(8,128)(2,1)S(1)} %maximum_maximum_fusion.1), channel_id=1, source_target_pairs={{0,2},{1,3},{2,4},{3,5},{4,6},{5,7},{8,10},{9,11},{10,12},{11,13},... | collective-permute-start | bytes 491528 | tf_op jit(solution)/shard_map/ppermute | solution.py:88
  7.2 4.8 %collective-permute-start.1 = (bf16[128,640]{1,0:T(8,128)(2,1)S(1)}, bf16[128,640]{1,0:T(8,128)(2,1)S(1)}, u32[]{:S(2)}, u32[]{:S(2)}) collective-permute-start(bf16[128,640]{1,0:T(8,128)(2,1)S(1)} %maximum_maximum_fusion.1), channel_id=1, source_target_pairs={{0,1},{1,2},{2,3},{3,4},{4,5},{5,6},{6,7},{8,9},{9,10},{10,11},{11... | collective-permute-start | bytes 491528 | tf_op jit(solution)/shard_map/ppermute | solution.py:88
  9.0 2.2 %copy-start.2 = (bf16[128,256]{1,0:T(8,128)(2,1)}, bf16[128,256]{1,0:T(8,128)(2,1)S(1)}, u32[]{:S(2)}) copy-start(bf16[128,256]{1,0:T(8,128)(2,1)S(1)} %fusion.7.s_ref) | copy-start | bytes 196612
  9.3 1.3 %copy-start.9 = (f32[1792]{0:T(1024)S(1)}, f32[1792]{0:T(1024)}, u32[]{:S(2)}) copy-start(f32[1792]{0:T(1024)} %param.12) | copy-start | bytes 21508
  9.3 0.7 %copy-start.12 = (s32[2]{0:T(128)S(1)}, s32[2]{0:T(128)}, u32[]{:S(2)}) copy-start(s32[2]{0:T(128)} %param.11) | copy-start | bytes 28
  11.4 8.3 %copy-start.6 = (bf16[128,640]{1,0:T(8,128)(2,1)}, bf16[128,640]{1,0:T(8,128)(2,1)S(1)}, u32[]{:S(2)}) copy-start(bf16[128,640]{1,0:T(8,128)(2,1)S(1)} %collective-permute-done) | copy-start | bytes 491524
  12.7 15.5 %collective-permute-start.2 = (f32[2,128,128]{2,1,0:T(8,128)S(1)}, f32[2,128,128]{2,1,0:T(8,128)S(1)}, u32[]{:S(2)}, u32[]{:S(2)}) collective-permute-start(f32[2,128,128]{2,1,0:T(8,128)S(1)} %maximum_add_fusion.1), channel_id=1, source_target_pairs={{0,3},{1,4},{2,5},{3,6},{4,7},{8,11},{9,12},{10,13},{11,14},{12,15... | collective-permute-start | bytes 393224 | tf_op jit(solution)/shard_map/ppermute | solution.py:88
  17.7 10.4 %collective-permute-start.3 = (f32[2,128,128]{2,1,0:T(8,128)S(1)}, f32[2,128,128]{2,1,0:T(8,128)S(1)}, u32[]{:S(2)}, u32[]{:S(2)}) collective-permute-start(f32[2,128,128]{2,1,0:T(8,128)S(1)} %maximum_add_fusion.1), channel_id=1, source_target_pairs={{0,6},{1,7},{8,14},{9,15},{16,22},{17,23},{24,30},{25,31}} | collective-permute-start | bytes 393224 | tf_op jit(solution)/shard_map/ppermute | solution.py:88
  19.7 0.9 %slice-start = ((bf16[128,640]{1,0:T(8,128)(2,1)}), bf16[128,512]{1,0:T(8,128)(2,1)S(1)}, s32[]{:S(2)}) async-start(bf16[128,640]{1,0:T(8,128)(2,1)} %copy-done.6), calls=%async_computation | async-start | bytes 262144 | tf_op jit(solution)/shard_map/slice | solution.py:251
  27.0 1.1 %copy-start.4 = (f32[384,256]{1,0:T(8,128)S(1)}, f32[384,256]{1,0:T(8,128)}, u32[]{:S(2)}) copy-start(f32[384,256]{1,0:T(8,128)} %get-tuple-element.23) | copy-start | bytes 1179652
  33.8 0.9 %copy-start.10 = (f32[1,1792]{1,0:T(1,128)S(1)}, f32[1,1792]{1,0:T(1,128)}, u32[]{:S(2)}) copy-start(f32[1,1792]{1,0:T(1,128)} %get-tuple-element.21) | copy-start | bytes 21508
  34.9 1.9 %collective-permute-start.4 = (bf16[272,128]{1,0:T(8,128)(2,1)S(1)}, bf16[272,128]{1,0:T(8,128)(2,1)S(1)}, u32[]{:S(2)}, u32[]{:S(2)}) collective-permute-start(bf16[272,128]{1,0:T(8,128)(2,1)S(1)} %maximum_maximum_fusion.2), channel_id=1, source_target_pairs={{0,1},{1,0},{2,3},{3,2},{4,5},{5,4},{6,7},{7,6},{8,9},{9,8},{10,11... | collective-permute-start | bytes 208904 | tf_op jit(solution)/shard_map/ppermute | solution.py:45
  35.5 8.9 %collective-permute-start.7 = (bf16[128,512]{1,0:T(8,128)(2,1)S(1)}, bf16[128,512]{1,0:T(8,128)(2,1)S(1)}, u32[]{:S(2)}, u32[]{:S(2)}) collective-permute-start(bf16[128,512]{1,0:T(8,128)(2,1)S(1)} %pad_maximum_fusion), channel_id=1, source_target_pairs={{1,0},{2,1},{3,2},{4,3},{5,4},{6,5},{7,6},{9,8},{10,9},{11,10},{12... | collective-permute-start | bytes 393224 | tf_op jit(solution)/shard_map/ppermute | solution.py:88
  36.8 7.5 %collective-permute-start.5 = (bf16[272,128]{1,0:T(8,128)(2,1)S(1)}, bf16[272,128]{1,0:T(8,128)(2,1)S(1)}, u32[]{:S(2)}, u32[]{:S(2)}) collective-permute-start(bf16[272,128]{1,0:T(8,128)(2,1)S(1)} %fusion.3), channel_id=1, source_target_pairs={{0,2},{1,3},{2,0},{3,1},{4,6},{5,7},{6,4},{7,5},{8,10},{9,11},{10,... | collective-permute-start | bytes 208904 | tf_op jit(solution)/shard_map/ppermute | solution.py:45
  39.2 7.1 %collective-permute-start.8 = (bf16[128,512]{1,0:T(8,128)(2,1)S(1)}, bf16[128,512]{1,0:T(8,128)(2,1)S(1)}, u32[]{:S(2)}, u32[]{:S(2)}) collective-permute-start(bf16[128,512]{1,0:T(8,128)(2,1)S(1)} %pad_maximum_fusion.1), channel_id=1, source_target_pairs={{2,0},{3,1},{4,2},{5,3},{6,4},{7,5},{10,8},{11,9},{12,10},{13,11},... | collective-permute-start | bytes 393224 | tf_op jit(solution)/shard_map/ppermute | solution.py:88
  44.4 4.4 %collective-permute-start.6 = (bf16[272,128]{1,0:T(8,128)(2,1)S(1)}, bf16[272,128]{1,0:T(8,128)(2,1)S(1)}, u32[]{:S(2)}, u32[]{:S(2)}) collective-permute-start(bf16[272,128]{1,0:T(8,128)(2,1)S(1)} %fusion.4), channel_id=1, source_target_pairs={{0,4},{1,5},{2,6},{3,7},{4,0},{5,1},{6,2},{7,3},{8,12},{9,13},{10,... | collective-permute-start | bytes 208904 | tf_op jit(solution)/shard_map/ppermute | solution.py:45
  46.3 2.5 %copy-start.3 = (bf16[128,256]{1,0:T(8,128)(2,1)S(1)}, bf16[128,256]{1,0:T(8,128)(2,1)}, u32[]{:S(2)}) copy-start(bf16[128,256]{1,0:T(8,128)(2,1)} %copy-done.2) | copy-start | bytes 196612
  46.3 2.5 %copy-start.8 = (f32[128,256]{1,0:T(8,128)S(1)}, f32[128,256]{1,0:T(8,128)}, u32[]{:S(2)}) copy-start(f32[128,256]{1,0:T(8,128)} %get-tuple-element.19) | copy-start | bytes 393220
  49.1 1.7 %copy-start.1 = (bf16[1,128,256]{2,1,0:T(8,128)(2,1)S(1)}, bf16[1,128,256]{2,1,0:T(8,128)(2,1)}, u32[]{:S(2)}) copy-start(bf16[1,128,256]{2,1,0:T(8,128)(2,1)} %param.8) | copy-start | bytes 196612
  49.1 1.7 %copy-start.7 = (f32[128,256]{1,0:T(8,128)S(1)}, f32[128,256]{1,0:T(8,128)}, u32[]{:S(2)}) copy-start(f32[128,256]{1,0:T(8,128)} %get-tuple-element.24) | copy-start | bytes 393220
  49.2 3.7 %collective-permute-start.9 = (f32[1792]{0:T(1024)S(1)}, f32[1792]{0:T(1024)S(1)}, u32[]{:S(2)}, u32[]{:S(2)}) collective-permute-start(f32[1792]{0:T(1024)S(1)} %fusion.44), channel_id=1, source_target_pairs={{0,8},{8,0},{16,24},{24,16},{1,9},{9,1},{17,25},{25,17},{2,10},{10... | collective-permute-start | bytes 21512 | tf_op jit(solution)/shard_map/ppermute | solution.py:80
  52.9 4.5 %collective-permute-start.10 = (f32[1792]{0:T(1024)S(1)}, f32[1792]{0:T(1024)S(1)}, u32[]{:S(2)}, u32[]{:S(2)}) collective-permute-start(f32[1792]{0:T(1024)S(1)} %add.79), channel_id=1, source_target_pairs={{0,16},{8,24},{16,0},{24,8},{1,17},{9,25},{17,1},{25,9},{2,18},{10... | collective-permute-start | bytes 21512 | tf_op jit(solution)/shard_map/ppermute | solution.py:80

commit v13 on v12

--- a/solution.py
+++ b/solution.py
@@ -38,7 +38,7 @@
     count = lax.axis_size(axis)
     place = lax.axis_index(axis)
     group = part
-    before = jnp.zeros_like(part)
+    before = jnp.zeros(part.shape, jnp.float32)
     step = 1
     while step < count:
         mine = group.astype(jnp.bfloat16)
@@ -95,7 +95,7 @@
     )
 
 
-def window_kernel(info_ref, q_ref, c_ref, k_ref, v_ref, wout_ref, wdq_ref, dk_ref, dv_ref):
+def window_kernel(info_ref, q_ref, c_ref, k_ref, v_ref, wout_ref, wdq_ref, halo_ref, own_ref):
     group_size = QUERY_HEADS // KEY_VALUE_HEADS
     token_rows = q_ref.shape[0]
     window_rows = k_ref.shape[0]
@@ -129,18 +129,27 @@
             rows = slice(h * token_rows, (h + 1) * token_rows)
             wout_ref[:, cols] = wout[rows]
             wdq_ref[:, cols] = wdq[rows]
-        dk_ref[:, lanes] = lax.dot_general(ds, qs, (((0,), (0,)), ((), ())), preferred_element_type=jnp.float32)
-        dv_ref[:, lanes] = lax.dot_general(ph, cs, (((0,), (0,)), ((), ())), preferred_element_type=jnp.float32)
+        dk = lax.dot_general(ds, qs, (((0,), (0,)), ((), ())), preferred_element_type=jnp.float32)
+        dv = lax.dot_general(ph, cs, (((0,), (0,)), ((), ())), preferred_element_type=jnp.float32)
+        value_lanes = slice(KEY_VALUE_HEADS * HEAD_SIZE + g * HEAD_SIZE, KEY_VALUE_HEADS * HEAD_SIZE + (g + 1) * HEAD_SIZE)
+        reach = padding_rows // token_rows
+        for distance in range(1, reach + 1):
+            start_row = (reach - distance) * token_rows
+            halo_ref[distance - 1, :, lanes] = dk[start_row : start_row + token_rows].astype(halo_ref.dtype)
+            halo_ref[distance - 1, :, value_lanes] = dv[start_row : start_row + token_rows].astype(halo_ref.dtype)
+        own_ref[:, lanes] = dk[padding_rows:]
+        own_ref[:, value_lanes] = dv[padding_rows:]
 
 
 def linear_kernel(q_ref, c_ref, k_ref, s_ref, prior_ref, gain_ref, wout_ref, wdq_ref,
-                  mixed_ref, dq_ref, suffix_ref, gsum_ref, ldk_ref, dsp_ref):
+                  mixed_ref, dq_ref, riding_ref, ldk_ref, dsp_ref):
     group_size = QUERY_HEADS // KEY_VALUE_HEADS
     token_rows = q_ref.shape[0]
     stacked_rows = group_size * token_rows
     row = lax.broadcasted_iota(jnp.int32, (stacked_rows, token_rows), 0) % token_rows
     col = lax.broadcasted_iota(jnp.int32, (stacked_rows, token_rows), 1)
     causal = row >= col
+    gain_rows = []
     for g in range(KEY_VALUE_HEADS):
         lanes = slice(g * HEAD_SIZE, (g + 1) * HEAD_SIZE)
         kg = k_ref[:, lanes]
@@ -174,7 +183,9 @@
         dl = ((scaled - normed * jnp.mean(scaled * normed, axis=-1, keepdims=True)) * inverse_root).astype(
             jnp.bfloat16
         )
-        suffix_ref[g] = lax.dot_general(qs, dl, (((0,), (0,)), ((), ())), preferred_element_type=jnp.float32)
+        riding_ref[g * HEAD_SIZE : (g + 1) * HEAD_SIZE, :] = lax.dot_general(
+            qs, dl, (((0,), (0,)), ((), ())), preferred_element_type=jnp.float32
+        ).astype(riding_ref.dtype)
         bh = jnp.where(
             causal,
             lax.dot_general(dl, sg, (((1,), (1,)), ((), ())), preferred_element_type=jnp.float32),
@@ -186,10 +197,15 @@
             cols = slice((g * group_size + h) * HEAD_SIZE, (g * group_size + h + 1) * HEAD_SIZE)
             rows = slice(h * token_rows, (h + 1) * token_rows)
             mixed_ref[:, cols] = (gn[rows] + wout_ref[:, cols]).astype(mixed_ref.dtype)
-            gsum_ref[:, cols] = jnp.sum(weighted[rows], axis=0, keepdims=True)
+            gain_rows.append(jnp.sum(weighted[rows], axis=0, keepdims=True))
             dq_ref[:, cols] = (ldq[rows] + wdq_ref[:, cols]).astype(dq_ref.dtype)
         ldk_ref[:, lanes] = lax.dot_general(bh, qs, (((0,), (0,)), ((), ())), preferred_element_type=jnp.float32)
         dsp_ref[:, lanes] = lax.dot_general(lh, dl, (((0,), (0,)), ((), ())), preferred_element_type=jnp.float32)
+    state_rows = KEY_VALUE_HEADS * HEAD_SIZE
+    spare = riding_ref.shape[0] - state_rows - len(gain_rows)
+    riding_ref[state_rows:, :] = jnp.concatenate(
+        gain_rows + [jnp.zeros((spare, HEAD_SIZE), jnp.float32)], axis=0
+    ).astype(riding_ref.dtype)
 
 
 def in_vmem(count):
@@ -253,13 +269,13 @@
     info = jnp.concatenate(
         [window_lengths.astype(jnp.int32), (lax.axis_index("ctx") * token_rows - padding_rows).reshape(1)]
     ).astype(jnp.int32)
-    wout, wdq, dk_win, dv_win = pl.pallas_call(
+    wout, wdq, halo_out, own_grad = pl.pallas_call(
         window_kernel,
         out_shape=(
             jax.ShapeDtypeStruct((token_rows, width), jnp.float32),
             jax.ShapeDtypeStruct((token_rows, width), jnp.float32),
-            jax.ShapeDtypeStruct((window_rows, key_value_width), jnp.float32),
-            jax.ShapeDtypeStruct((window_rows, key_value_width), jnp.float32),
+            jax.ShapeDtypeStruct((reach, token_rows, 2 * key_value_width), jnp.bfloat16),
+            jax.ShapeDtypeStruct((token_rows, 2 * key_value_width), jnp.float32),
         ),
         in_specs=[pl.BlockSpec(memory_space=pltpu.SMEM)] + in_vmem(4),
         out_specs=tuple(in_vmem(4)),
@@ -269,18 +285,20 @@
             bytes_accessed=2 * token_rows * width * (2 + 4) + 2 * window_rows * key_value_width * (2 + 4),
         ),
     )(info, q, c, window_packed[:, :key_value_width], window_packed[:, key_value_width:])
-    mixed, d_queries, suffix_local, gain_local, ldk, dsp = pl.pallas_call(
+    state_rows = KEY_VALUE_HEADS * HEAD_SIZE
+    gain_rows = width // HEAD_SIZE
+    riding_rows = state_rows + gain_rows + (-(state_rows + gain_rows)) % 16
+    mixed, d_queries, riding, ldk, dsp = pl.pallas_call(
         linear_kernel,
         out_shape=(
             jax.ShapeDtypeStruct((token_rows, width), jnp.bfloat16),
             jax.ShapeDtypeStruct((token_rows, width), jnp.bfloat16),
-            jax.ShapeDtypeStruct((KEY_VALUE_HEADS, HEAD_SIZE, HEAD_SIZE), jnp.float32),
-            jax.ShapeDtypeStruct((1, width), jnp.float32),
+            jax.ShapeDtypeStruct((riding_rows, HEAD_SIZE), jnp.bfloat16),
             jax.ShapeDtypeStruct((token_rows, key_value_width), jnp.float32),
             jax.ShapeDtypeStruct((token_rows, key_value_width), jnp.float32),
         ),
         in_specs=in_vmem(8),
-        out_specs=tuple(in_vmem(6)),
+        out_specs=tuple(in_vmem(5)),
         cost_estimate=pl.CostEstimate(
             flops=20 * QUERY_HEADS * token_rows * token_rows * HEAD_SIZE,
             transcendentals=QUERY_HEADS * token_rows,
@@ -288,19 +306,8 @@
         ),
     )(q, c, k, spiked, prior_half, gain.reshape(1, width), wout, wdq)
     total_tokens = queries.shape[0] * lax.axis_size("dp") * token_rows * lax.axis_size("ctx")
-    state_rows = KEY_VALUE_HEADS * HEAD_SIZE
-    gain_rows = width // HEAD_SIZE
-    pad_rows = (-(state_rows + gain_rows)) % 8
-    riding = jnp.concatenate(
-        [
-            suffix_local.reshape(state_rows, HEAD_SIZE),
-            gain_local.reshape(gain_rows, HEAD_SIZE),
-            jnp.zeros((pad_rows, HEAD_SIZE), jnp.float32),
-        ],
-        axis=0,
-    )
     later_rows, total_rows = butterfly_scan(riding, "ctx", True)
-    later_half = later_rows[:state_rows].reshape(suffix_local.shape).astype(jnp.bfloat16)
+    later_half = later_rows[:state_rows].reshape(KEY_VALUE_HEADS, HEAD_SIZE, HEAD_SIZE).astype(jnp.bfloat16)
     gain_ctx = total_rows[state_rows : state_rows + gain_rows].reshape(width)
     d_gain = all_sum(gain_ctx, ("dp",)) * (total_tokens ** (-0.5))
     ldk_parts = []
@@ -318,22 +325,14 @@
         )
     linear_key_gradient = jnp.concatenate(ldk_parts, axis=1)
     linear_value_gradient = jnp.concatenate(dsp_parts, axis=1) * counts
-    received = jnp.zeros((token_rows, 2 * key_value_width), jnp.float32)
+    received = own_grad
     for distance in range(1, reach + 1):
-        start_row = (reach - distance) * token_rows
-        sent = jnp.concatenate(
-            [
-                dk_win[start_row : start_row + token_rows],
-                dv_win[start_row : start_row + token_rows],
-            ],
-            axis=1,
-        )
-        received = received + shifted(sent.astype(jnp.bfloat16), "ctx", -distance).astype(jnp.float32)
+        received = received + shifted(halo_out[distance - 1], "ctx", -distance).astype(jnp.float32)
     keys_gradient = (
-        linear_key_gradient + dk_win[padding_rows:] + received[:, :key_value_width]
+        linear_key_gradient + received[:, :key_value_width]
     ).astype(jnp.bfloat16)
     values_gradient = (
-        linear_value_gradient + dv_win[padding_rows:] + received[:, key_value_width:]
+        linear_value_gradient + received[:, key_value_width:]
     ).astype(jnp.bfloat16)
     return (
         mixed[None],

time: 58.6 us -> 56.1 us (0.957)
  other arithmetic: 5.94 us -> 3.74 us
  waiting for transfers between devices: 10.2 us -> 8.42 us
  starting transfers between devices: 23.1 us -> 24.1 us
  local copies, waits for them, and re-layouts: 5.45 us -> 6.17 us
    ppermute x3, waiting for transfers between devices: 6.24 us -> 2.77 us  [butterfly_scan(): lax.ppermute(mine, axis, [(i, i ^ step) for i in range(count)])]
    another operation x5 -> x1, other arithmetic: 2.09 us -> 0.05 us
    broadcast_in_dim x1, other arithmetic: 1.62 us -> 0.69 us  [per_device(): values_gradient[None]]
    ppermute x2, waiting for transfers between devices: 2.14 us -> 3.07 us  [all_sum(): part = part + lax.ppermute(part, axes, route)]
    convert_element_type x2, other arithmetic: 0.05 us -> 0.93 us  [butterfly_scan(): mine = group.astype(jnp.bfloat16)]
    unnamed x27, local copies, waits for them, and re-layouts: 2.3 us -> 3.11 us
    ppermute x3, starting transfers between devices: 2.99 us -> 3.75 us  [butterfly_scan(): lax.ppermute(mine, axis, [(i, i ^ step) for i in range(count)])]
    ppermute x6, waiting for transfers between devices: 1.85 us -> 2.58 us  [shifted(): return lax.ppermute(block, axis, route)]
  transfers between devices with their start and end apart: 11 -> 11, of which waited for: 5 -> 5; matrix products, arithmetic and copies ran while one was open for 11% -> 8% of each run, Pallas kernels for 10% -> 10%
where the time goes in v13:
time: 56.1 us; the launch traced here: 55.6 us
  starting transfers between devices  24.1 us (43%)
  Pallas kernels  10.5 us (19%)
  waiting for transfers between devices  8.42 us (15%)
  local copies, waits for them, and re-layouts  6.17 us (11%)
  other arithmetic  3.74 us (7%)
  matrix products  1.69 us (3%)
  between operations  1.01 us (2%)
    ppermute x6, starting transfers between devices, shifted(): return lax.ppermute(block, axis, route)  16.1 us
    pallas_call x1, Pallas kernels, per_device(): pl.pallas_call(window_kernel, out_shape=(jax.ShapeDtypeStruct((token_rows...  5.54 us
    pallas_call x1, Pallas kernels, per_device(): pl.pallas_call(linear_kernel, out_shape=(jax.ShapeDtypeStruct((token_rows...  4.97 us
    ppermute x2, starting transfers between devices, all_sum(): part = part + lax.ppermute(part, axes, route)  4.23 us
    ppermute x3, starting transfers between devices, butterfly_scan(): lax.ppermute(mine, axis, [(i, i ^ step) for i in range(count)])  3.75 us
    unnamed x27, local copies, waits for them, and re-layouts  3.11 us
    ppermute x2, waiting for transfers between devices, all_sum(): part = part + lax.ppermute(part, axes, route)  3.07 us
    ppermute x3, waiting for transfers between devices, butterfly_scan(): lax.ppermute(mine, axis, [(i, i ^ step) for i in range(count)])  2.77 us
  transfers between devices with their start and end apart: 11, of which 5 were waited for; matrix products, arithmetic and copies ran while one was open for 8% of the time, Pallas kernels for 10%

profile of v13, /device:TPU:0, one launch (start us, length us, event | category | flops | bytes accessed | tf_op | source)
XLA Modules:
  0.0 55.6 jit_solution(14606731737104914274)
XLA Ops:
  0.6 0.8 %copy.13 = s32[1,128,2]{2,1,0:T(8,128)S(1)} copy(s32[1,128,2]{1,2,0:T(2,128)} %param.10) | data formatting | bytes 2048 | tf_op args[3]
  1.5 0.1 pad.19.clone
  1.6 0.7 %copy-done = bf16[1,128,256]{2,1,0:T(8,128)(2,1)S(1)} copy-done((bf16[1,128,256]{2,1,0:T(8,128)(2,1)S(1)}, bf16[1,128,256]{2,1,0:T(8,128)(2,1)}, u32[]{:S(2)}) %copy-start) | copy-done | bytes 65560
  2.3 4.9 %collective-permute-start = (bf16[128,640]{1,0:T(8,128)(2,1)S(1)}, bf16[128,640]{1,0:T(8,128)(2,1)S(1)}, u32[]{:S(2)}, u32[]{:S(2)}) collective-permute-start(bf16[128,640]{1,0:T(8,128)(2,1)S(1)} %maximum_maximum_fusion.1), channel_id=1, source_target_pairs={{0,2},{1,3},{2,4},{3,5},{4,6},{5,7},{8,10},{9,11},{10,12},{11,13},... | collective-permute-start | bytes 491528 | tf_op jit(solution)/shard_map/ppermute | solution.py:88
  7.2 1.5 %collective-permute-start.1 = (bf16[128,640]{1,0:T(8,128)(2,1)S(1)}, bf16[128,640]{1,0:T(8,128)(2,1)S(1)}, u32[]{:S(2)}, u32[]{:S(2)}) collective-permute-start(bf16[128,640]{1,0:T(8,128)(2,1)S(1)} %maximum_maximum_fusion.1), channel_id=1, source_target_pairs={{0,1},{1,2},{2,3},{3,4},{4,5},{5,6},{6,7},{8,9},{9,10},{10,11},{11... | collective-permute-start | bytes 491528 | tf_op jit(solution)/shard_map/ppermute | solution.py:88
  8.7 0.1 copy.12
  8.8 0.2 broadcast_in_dim.30
  9.0 0.0 copy-start.2
  9.0 0.2 convolution_bitcast_fusion.2
  9.3 0.7 %copy-done.12 = s32[2]{0:T(128)S(1)} copy-done((s32[2]{0:T(128)S(1)}, s32[2]{0:T(128)}, u32[]{:S(2)}) %copy-start.12) | copy-done | bytes 32
  9.9 0.6 %pad_add_fusion.info_ref = s32[3]{0:T(128)} fusion(s32[1]{0:T(128)} %bitcast.14, s32[2]{0:T(128)S(1)} %copy-done.12), kind=kLoop, calls=%fused_computation.71 | loop fusion | flops 3 | bytes 24 | tf_op jit(solution)/shard_map/concatenate | solution.py:269
  10.5 0.6 %reshape.39.gain_ref = f32[1,1792]{1,0:T(1,128)} reshape(f32[1792]{0:T(1024)S(1)} %copy-done.10) | data formatting | bytes 14336 | tf_op jit(solution)/shard_map/reshape | solution.py:307
  11.1 0.2 convolution_bitcast_fusion.3
  11.4 0.2 broadcast_in_dim.32
  11.6 0.2 convolution_bitcast_fusion.6
  11.8 0.2 convolution_bitcast_fusion.7
  12.0 0.2 broadcast_in_dim.33
  12.2 0.2 convolution_bitcast_fusion.5
  12.4 0.2 convolution_bitcast_fusion.4
  12.6 5.0 %collective-permute-start.2 = (f32[2,128,128]{2,1,0:T(8,128)S(1)}, f32[2,128,128]{2,1,0:T(8,128)S(1)}, u32[]{:S(2)}, u32[]{:S(2)}) collective-permute-start(f32[2,128,128]{2,1,0:T(8,128)S(1)} %maximum_add_fusion.1), channel_id=1, source_target_pairs={{0,3},{1,4},{2,5},{3,6},{4,7},{8,11},{9,12},{10,13},{11,14},{12,15... | collective-permute-start | bytes 393224 | tf_op jit(solution)/shard_map/ppermute | solution.py:88
  17.7 2.0 %collective-permute-start.3 = (f32[2,128,128]{2,1,0:T(8,128)S(1)}, f32[2,128,128]{2,1,0:T(8,128)S(1)}, u32[]{:S(2)}, u32[]{:S(2)}) collective-permute-start(f32[2,128,128]{2,1,0:T(8,128)S(1)} %maximum_add_fusion.1), channel_id=1, source_target_pairs={{0,6},{1,7},{8,14},{9,15},{16,22},{17,23},{24,30},{25,31}} | collective-permute-start | bytes 393224 | tf_op jit(solution)/shard_map/ppermute | solution.py:88
  19.7 0.9 %slice-done = bf16[128,512]{1,0:T(8,128)(2,1)S(1)} async-done(((bf16[128,640]{1,0:T(8,128)(2,1)}), bf16[128,512]{1,0:T(8,128)(2,1)S(1)}, s32[]{:S(2)}) %slice-start) | async-done | bytes 131096 | tf_op jit(solution)/shard_map/slice | solution.py:267
  20.6 0.8 %fusion.44 = (bf16[384,256]{1,0:T(8,128)(2,1)}, bf16[384,256]{1,0:T(8,128)(2,1)}) fusion(bf16[384,512]{1,0:T(8,128)(2,1)S(1)} %maximum_maximum_fusion), kind=kLoop, calls=%fused_computation.72 | loop fusion | bytes 786432 | tf_op jit(solution)/shard_map/slice | solution.py:287
  21.4 5.5 %shard_map.110 = (f32[128,1792]{1,0:T(8,128)}, f32[128,1792]{1,0:T(8,128)}, bf16[2,128,512]{2,1,0:T(8,128)(2,1)}, f32[128,512]{1,0:T(8,128)}) custom-call(s32[3]{0:T(128)} %pad_add_fusion.info_ref, bf16[128,1792]{1,0:T(8,128)(2,1)} %bitcast.81, bf16[128,1792]{1,0:T(8,128)(2,1)} %bitcast.83, bf16[384,256]{1,0:T(8,128)(2,1)} %get-tuple-element.24.k_ref, ...), custom_call_target="tpu_custom_call" | custom-call | flops 1056964608 | bytes 3932160 | tf_op jit(solution)/shard_map/pallas_call | solution.py:272
  27.0 0.7 %add_convert_fusion.prior_ref = bf16[2,128,128]{2,1,0:T(8,128)(2,1)} fusion(f32[2,128,128]{2,1,0:T(8,128)S(1)} %collective-permute-done.3, f32[2,128,128]{2,1,0:T(8,128)S(1)} %collective-permute-done.2, f32[1,128,128]{2,1,0:T(8,128)S(1)} %convolution_bitcast_fusion.4, f32[1,128,128]{2,1,0:T(8,128)S(1)} %convolution_bitcast_fusion.5, ...), kind=kLoop, calls=%fused_computation.35 | loop fusion | flops 196608 | bytes 589824 | tf_op jit(solution)/shard_map/convert_element_type | solution.py:265
  27.6 5.0 %shard_map.111 = (bf16[128,1792]{1,0:T(8,128)(2,1)}, bf16[128,1792]{1,0:T(8,128)(2,1)}, bf16[272,128]{1,0:T(8,128)(2,1)}, f32[128,256]{1,0:T(8,128)}, f32[128,256]{1,0:T(8,128)}) custom-call(bf16[128,1792]{1,0:T(8,128)(2,1)} %bitcast.82, bf16[128,1792]{1,0:T(8,128)(2,1)} %bitcast.84, bf16[128,256]{1,0:T(8,128)(2,1)} %bitcast.68, bf16[128,256]{1,0:T(8,128)(2,1)} %copy-done.2, ...), custom_call_target="tpu_custom_call" | custom-call | flops 587202560 | bytes 4456448 | tf_op jit(solution)/shard_map/pallas_call | solution.py:291
  32.6 0.5 collective-permute-start.4
  33.1 1.1 %collective-permute-done.4 = bf16[272,128]{1,0:T(8,128)(2,1)S(1)} collective-permute-done((bf16[272,128]{1,0:T(8,128)(2,1)}, bf16[272,128]{1,0:T(8,128)(2,1)S(1)}, u32[]{:S(2)}, u32[]{:S(2)}) %collective-permute-start.4) | collective-permute-done | bytes 69664 | tf_op jit(solution)/shard_map/ppermute | solution.py:45
  34.3 0.9 %fusion.3 = bf16[272,128]{1,0:T(8,128)(2,1)S(1)} fusion(bf16[272,128]{1,0:T(8,128)(2,1)S(1)} %collective-permute-done.4, bf16[272,128]{1,0:T(8,128)(2,1)} %get-tuple-element.19), kind=kLoop, calls=%fused_computation.18 | loop fusion | flops 139264 | bytes 208896 | tf_op jit(solution)/shard_map/convert_element_type | solution.py:44
  35.2 0.1 collective-permute-start.5
  35.3 1.4 %collective-permute-start.7 = (bf16[128,512]{1,0:T(8,128)(2,1)S(1)}, bf16[128,512]{1,0:T(8,128)(2,1)S(1)}, u32[]{:S(2)}, u32[]{:S(2)}) collective-permute-start(bf16[128,512]{1,0:T(8,128)(2,1)S(1)} %get-tuple-element.27), channel_id=1, source_target_pairs={{1,0},{2,1},{3,2},{4,3},{5,4},{6,5},{7,6},{9,8},{10,9},{11,10},{12... | collective-permute-start | bytes 393224 | tf_op jit(solution)/shard_map/ppermute | solution.py:88
  36.7 1.3 %collective-permute-start.8 = (bf16[128,512]{1,0:T(8,128)(2,1)S(1)}, bf16[128,512]{1,0:T(8,128)(2,1)S(1)}, u32[]{:S(2)}, u32[]{:S(2)}) collective-permute-start(bf16[128,512]{1,0:T(8,128)(2,1)S(1)} %get-tuple-element.28), channel_id=1, source_target_pairs={{2,0},{3,1},{4,2},{5,3},{6,4},{7,5},{10,8},{11,9},{12,10},{13,11},... | collective-permute-start | bytes 393224 | tf_op jit(solution)/shard_map/ppermute | solution.py:88
  38.0 1.6 %collective-permute-done.5 = bf16[272,128]{1,0:T(8,128)(2,1)S(1)} collective-permute-done((bf16[272,128]{1,0:T(8,128)(2,1)S(1)}, bf16[272,128]{1,0:T(8,128)(2,1)S(1)}, u32[]{:S(2)}, u32[]{:S(2)}) %collective-permute-start.5) | collective-permute-done | bytes 69664 | tf_op jit(solution)/shard_map/ppermute | solution.py:45
  39.7 3.1 %collective-permute-start.6 = (bf16[272,128]{1,0:T(8,128)(2,1)S(1)}, bf16[272,128]{1,0:T(8,128)(2,1)S(1)}, u32[]{:S(2)}, u32[]{:S(2)}) collective-permute-start(bf16[272,128]{1,0:T(8,128)(2,1)S(1)} %fusion.4), channel_id=1, source_target_pairs={{0,4},{1,5},{2,6},{3,7},{4,0},{5,1},{6,2},{7,3},{8,12},{9,13},{10,... | collective-permute-start | bytes 208904 | tf_op jit(solution)/shard_map/ppermute | solution.py:45
  42.8 2.6 %collective-permute-done.8 = bf16[128,512]{1,0:T(8,128)(2,1)S(1)} collective-permute-done((bf16[128,512]{1,0:T(8,128)(2,1)S(1)}, bf16[128,512]{1,0:T(8,128)(2,1)S(1)}, u32[]{:S(2)}, u32[]{:S(2)}) %collective-permute-start.8) | collective-permute-done | bytes 131104 | tf_op jit(solution)/shard_map/ppermute | solution.py:88
  45.5 0.1 fusion.2
  45.5 0.8 %copy-done.3 = bf16[128,256]{1,0:T(8,128)(2,1)S(1)} copy-done((bf16[128,256]{1,0:T(8,128)(2,1)S(1)}, bf16[128,256]{1,0:T(8,128)(2,1)}, u32[]{:S(2)}) %copy-start.3) | copy-done | bytes 65560
  46.3 0.1 copy-done.9
  46.4 0.1 slice_add_fusion.4
  46.5 0.2 slice_add_fusion.3
  46.7 1.6 %collective-permute-start.9 = (f32[1792]{0:T(1024)S(1)}, f32[1792]{0:T(1024)S(1)}, u32[]{:S(2)}, u32[]{:S(2)}) collective-permute-start(f32[1792]{0:T(1024)S(1)} %fusion.43), channel_id=1, source_target_pairs={{0,8},{8,0},{16,24},{24,16},{1,9},{9,1},{17,25},{25,17},{2,10},{10... | collective-permute-start | bytes 21512 | tf_op jit(solution)/shard_map/ppermute | solution.py:80
  48.4 0.1 slice_add_fusion.2
  48.5 0.1 slice_add_fusion.1
  48.7 1.8 %collective-permute-done.9 = f32[1792]{0:T(1024)S(1)} collective-permute-done((f32[1792]{0:T(1024)S(1)}, f32[1792]{0:T(1024)S(1)}, u32[]{:S(2)}, u32[]{:S(2)}) %collective-permute-start.9) | collective-permute-done | bytes 7200 | tf_op jit(solution)/shard_map/ppermute | solution.py:80
  50.5 2.6 %collective-permute-start.10 = (f32[1792]{0:T(1024)S(1)}, f32[1792]{0:T(1024)S(1)}, u32[]{:S(2)}, u32[]{:S(2)}) collective-permute-start(f32[1792]{0:T(1024)S(1)} %add.75), channel_id=1, source_target_pairs={{0,16},{8,24},{16,0},{24,8},{1,17},{9,25},{17,1},{25,9},{2,18},{10... | collective-permute-start | bytes 21512 | tf_op jit(solution)/shard_map/ppermute | solution.py:80
  53.1 0.7 %fusion.12 = (bf16[1,128,256]{2,1,0:T(8,128)(2,1)}, bf16[1,128,256]{2,1,0:T(8,128)(2,1)}) fusion(f32[128,512]{1,0:T(8,128)S(1)} %convert_add_fusion, f32[16,8,2,128]{3,2,1,0:T(2,128)S(1)} %bitcast.76, f32[128,128]{1,0:T(8,128)S(1)} %slice_add_fusion.1, f32[128,128]{1,0:T(8,128)S(1)} %slice_add_fusion.2, f32[128,128]{1,0:T(8,128)S(1)} %slice_add_fusion.3, ...), kind=kLoop, calls=%fused_computation.37 | loop fusion | flops 229376 | bytes 786432 | tf_op jit(solution)/shard_map/broadcast_in_dim | solution.py:341
  53.8 1.3 %collective-permute-done.10 = f32[1792]{0:T(1024)S(1)} collective-permute-done((f32[1792]{0:T(1024)S(1)}, f32[1792]{0:T(1024)S(1)}, u32[]{:S(2)}, u32[]{:S(2)}) %collective-permute-start.10) | collective-permute-done | bytes 7200 | tf_op jit(solution)/shard_map/ppermute | solution.py:80
  55.0 0.6 %add_multiply_fusion = f32[1792]{0:T(1024)} fusion(f32[1792]{0:T(1024)S(1)} %add.75, f32[1792]{0:T(1024)S(1)} %collective-permute-done.10), kind=kLoop, calls=%fused_computation.69 | loop fusion | flops 3584 | bytes 21504 | tf_op jit(solution)/shard_map/mul | solution.py:312
  (46 shorter events, 0.4 us)
Async XLA Ops:
  0.6 0.9 %copy-start.4 = (bf16[1,128,256]{2,1,0:T(8,128)(2,1)S(1)}, bf16[1,128,256]{2,1,0:T(8,128)(2,1)}, u32[]{:S(2)}) copy-start(bf16[1,128,256]{2,1,0:T(8,128)(2,1)} %param.9) | copy-start | bytes 196612
  1.5 0.8 %copy-start = (bf16[1,128,256]{2,1,0:T(8,128)(2,1)S(1)}, bf16[1,128,256]{2,1,0:T(8,128)(2,1)}, u32[]{:S(2)}) copy-start(bf16[1,128,256]{2,1,0:T(8,128)(2,1)} %param.8) | copy-start | bytes 196612
  2.3 6.4 %copy-start.11 = (s32[1,128,2]{1,2,0:T(2,128)S(1)}, s32[1,128,2]{1,2,0:T(2,128)}, u32[]{:S(2)}) copy-start(s32[1,128,2]{1,2,0:T(2,128)} %param.10) | copy-start | bytes 3076
  2.3 9.0 %collective-permute-start = (bf16[128,640]{1,0:T(8,128)(2,1)S(1)}, bf16[128,640]{1,0:T(8,128)(2,1)S(1)}, u32[]{:S(2)}, u32[]{:S(2)}) collective-permute-start(bf16[128,640]{1,0:T(8,128)(2,1)S(1)} %maximum_maximum_fusion.1), channel_id=1, source_target_pairs={{0,2},{1,3},{2,4},{3,5},{4,6},{5,7},{8,10},{9,11},{10,12},{11,13},... | collective-permute-start | bytes 491528 | tf_op jit(solution)/shard_map/ppermute | solution.py:88
  7.2 4.8 %collective-permute-start.1 = (bf16[128,640]{1,0:T(8,128)(2,1)S(1)}, bf16[128,640]{1,0:T(8,128)(2,1)S(1)}, u32[]{:S(2)}, u32[]{:S(2)}) collective-permute-start(bf16[128,640]{1,0:T(8,128)(2,1)S(1)} %maximum_maximum_fusion.1), channel_id=1, source_target_pairs={{0,1},{1,2},{2,3},{3,4},{4,5},{5,6},{6,7},{8,9},{9,10},{10,11},{11... | collective-permute-start | bytes 491528 | tf_op jit(solution)/shard_map/ppermute | solution.py:88
  9.0 2.1 %copy-start.2 = (bf16[128,256]{1,0:T(8,128)(2,1)}, bf16[128,256]{1,0:T(8,128)(2,1)S(1)}, u32[]{:S(2)}) copy-start(bf16[128,256]{1,0:T(8,128)(2,1)S(1)} %fusion.7.s_ref) | copy-start | bytes 196612
  9.3 1.3 %copy-start.10 = (f32[1792]{0:T(1024)S(1)}, f32[1792]{0:T(1024)}, u32[]{:S(2)}) copy-start(f32[1792]{0:T(1024)} %param.12) | copy-start | bytes 21508
  9.3 0.7 %copy-start.12 = (s32[2]{0:T(128)S(1)}, s32[2]{0:T(128)}, u32[]{:S(2)}) copy-start(s32[2]{0:T(128)} %param.11) | copy-start | bytes 28
  11.3 8.4 %copy-start.5 = (bf16[128,640]{1,0:T(8,128)(2,1)}, bf16[128,640]{1,0:T(8,128)(2,1)S(1)}, u32[]{:S(2)}) copy-start(bf16[128,640]{1,0:T(8,128)(2,1)S(1)} %collective-permute-done) | copy-start | bytes 491524
  12.6 14.3 %collective-permute-start.2 = (f32[2,128,128]{2,1,0:T(8,128)S(1)}, f32[2,128,128]{2,1,0:T(8,128)S(1)}, u32[]{:S(2)}, u32[]{:S(2)}) collective-permute-start(f32[2,128,128]{2,1,0:T(8,128)S(1)} %maximum_add_fusion.1), channel_id=1, source_target_pairs={{0,3},{1,4},{2,5},{3,6},{4,7},{8,11},{9,12},{10,13},{11,14},{12,15... | collective-permute-start | bytes 393224 | tf_op jit(solution)/shard_map/ppermute | solution.py:88
  17.7 9.3 %collective-permute-start.3 = (f32[2,128,128]{2,1,0:T(8,128)S(1)}, f32[2,128,128]{2,1,0:T(8,128)S(1)}, u32[]{:S(2)}, u32[]{:S(2)}) collective-permute-start(f32[2,128,128]{2,1,0:T(8,128)S(1)} %maximum_add_fusion.1), channel_id=1, source_target_pairs={{0,6},{1,7},{8,14},{9,15},{16,22},{17,23},{24,30},{25,31}} | collective-permute-start | bytes 393224 | tf_op jit(solution)/shard_map/ppermute | solution.py:88
  19.7 0.9 %slice-start = ((bf16[128,640]{1,0:T(8,128)(2,1)}), bf16[128,512]{1,0:T(8,128)(2,1)S(1)}, s32[]{:S(2)}) async-start(bf16[128,640]{1,0:T(8,128)(2,1)} %copy-done.5), calls=%async_computation | async-start | bytes 262144 | tf_op jit(solution)/shard_map/slice | solution.py:267
  27.6 7.6 %copy-start.7 = (bf16[2,128,512]{2,1,0:T(8,128)(2,1)S(1)}, bf16[2,128,512]{2,1,0:T(8,128)(2,1)}, u32[]{:S(2)}) copy-start(bf16[2,128,512]{2,1,0:T(8,128)(2,1)} %get-tuple-element.21) | copy-start | bytes 786436
  32.6 1.7 %collective-permute-start.4 = (bf16[272,128]{1,0:T(8,128)(2,1)}, bf16[272,128]{1,0:T(8,128)(2,1)S(1)}, u32[]{:S(2)}, u32[]{:S(2)}) collective-permute-start(bf16[272,128]{1,0:T(8,128)(2,1)} %get-tuple-element.19), channel_id=1, source_target_pairs={{0,1},{1,0},{2,3},{3,2},{4,5},{5,4},{6,7},{7,6},{8,9},{9,8},{10,11... | collective-permute-start | bytes 208904 | tf_op jit(solution)/shard_map/ppermute | solution.py:45
  35.2 4.5 %collective-permute-start.5 = (bf16[272,128]{1,0:T(8,128)(2,1)S(1)}, bf16[272,128]{1,0:T(8,128)(2,1)S(1)}, u32[]{:S(2)}, u32[]{:S(2)}) collective-permute-start(bf16[272,128]{1,0:T(8,128)(2,1)S(1)} %fusion.3), channel_id=1, source_target_pairs={{0,2},{1,3},{2,0},{3,1},{4,6},{5,7},{6,4},{7,5},{8,10},{9,11},{10,... | collective-permute-start | bytes 208904 | tf_op jit(solution)/shard_map/ppermute | solution.py:45
  35.3 10.2 %copy-start.6 = (f32[128,512]{1,0:T(8,128)S(1)}, f32[128,512]{1,0:T(8,128)}, u32[]{:S(2)}) copy-start(f32[128,512]{1,0:T(8,128)} %get-tuple-element.20) | copy-start | bytes 786436
  35.3 7.5 %collective-permute-start.7 = (bf16[128,512]{1,0:T(8,128)(2,1)S(1)}, bf16[128,512]{1,0:T(8,128)(2,1)S(1)}, u32[]{:S(2)}, u32[]{:S(2)}) collective-permute-start(bf16[128,512]{1,0:T(8,128)(2,1)S(1)} %get-tuple-element.27), channel_id=1, source_target_pairs={{1,0},{2,1},{3,2},{4,3},{5,4},{6,5},{7,6},{9,8},{10,9},{11,10},{12... | collective-permute-start | bytes 393224 | tf_op jit(solution)/shard_map/ppermute | solution.py:88
  36.7 8.7 %collective-permute-start.8 = (bf16[128,512]{1,0:T(8,128)(2,1)S(1)}, bf16[128,512]{1,0:T(8,128)(2,1)S(1)}, u32[]{:S(2)}, u32[]{:S(2)}) collective-permute-start(bf16[128,512]{1,0:T(8,128)(2,1)S(1)} %get-tuple-element.28), channel_id=1, source_target_pairs={{2,0},{3,1},{4,2},{5,3},{6,4},{7,5},{10,8},{11,9},{12,10},{13,11},... | collective-permute-start | bytes 393224 | tf_op jit(solution)/shard_map/ppermute | solution.py:88
  39.7 5.8 %collective-permute-start.6 = (bf16[272,128]{1,0:T(8,128)(2,1)S(1)}, bf16[272,128]{1,0:T(8,128)(2,1)S(1)}, u32[]{:S(2)}, u32[]{:S(2)}) collective-permute-start(bf16[272,128]{1,0:T(8,128)(2,1)S(1)} %fusion.4), channel_id=1, source_target_pairs={{0,4},{1,5},{2,6},{3,7},{4,0},{5,1},{6,2},{7,3},{8,12},{9,13},{10,... | collective-permute-start | bytes 208904 | tf_op jit(solution)/shard_map/ppermute | solution.py:45
  45.4 0.8 %copy-start.3 = (bf16[128,256]{1,0:T(8,128)(2,1)S(1)}, bf16[128,256]{1,0:T(8,128)(2,1)}, u32[]{:S(2)}) copy-start(bf16[128,256]{1,0:T(8,128)(2,1)} %copy-done.2) | copy-start | bytes 196612
  45.5 0.9 %copy-start.9 = (f32[128,256]{1,0:T(8,128)S(1)}, f32[128,256]{1,0:T(8,128)}, u32[]{:S(2)}) copy-start(f32[128,256]{1,0:T(8,128)} %get-tuple-element.18) | copy-start | bytes 393220
  46.7 1.7 %copy-start.1 = (bf16[1,128,256]{2,1,0:T(8,128)(2,1)S(1)}, bf16[1,128,256]{2,1,0:T(8,128)(2,1)}, u32[]{:S(2)}) copy-start(bf16[1,128,256]{2,1,0:T(8,128)(2,1)} %param.8) | copy-start | bytes 196612
  46.7 1.7 %copy-start.8 = (f32[128,256]{1,0:T(8,128)S(1)}, f32[128,256]{1,0:T(8,128)}, u32[]{:S(2)}) copy-start(f32[128,256]{1,0:T(8,128)} %get-tuple-element.22) | copy-start | bytes 393220
  46.7 3.7 %collective-permute-start.9 = (f32[1792]{0:T(1024)S(1)}, f32[1792]{0:T(1024)S(1)}, u32[]{:S(2)}, u32[]{:S(2)}) collective-permute-start(f32[1792]{0:T(1024)S(1)} %fusion.43), channel_id=1, source_target_pairs={{0,8},{8,0},{16,24},{24,16},{1,9},{9,1},{17,25},{25,17},{2,10},{10... | collective-permute-start | bytes 21512 | tf_op jit(solution)/shard_map/ppermute | solution.py:80
  50.5 4.5 %collective-permute-start.10 = (f32[1792]{0:T(1024)S(1)}, f32[1792]{0:T(1024)S(1)}, u32[]{:S(2)}, u32[]{:S(2)}) collective-permute-start(f32[1792]{0:T(1024)S(1)} %add.75), channel_id=1, source_target_pairs={{0,16},{8,24},{16,0},{24,8},{1,17},{9,25},{17,1},{25,9},{2,18},{10... | collective-permute-start | bytes 21512 | tf_op jit(solution)/shard_map/ppermute | solution.py:80

commit v14 on v13

--- a/solution.py
+++ b/solution.py
@@ -105,7 +105,8 @@
     row = lax.broadcasted_iota(jnp.int32, (stacked_rows, window_rows), 0) % token_rows
     col = lax.broadcasted_iota(jnp.int32, (stacked_rows, window_rows), 1)
     back = row + padding_rows - col
-    seen = (back >= 0) & (col + info_ref[2] >= 0)
+    base = lax.axis_index("ctx") * token_rows - padding_rows
+    seen = (back >= 0) & (col + base >= 0)
     for g in range(KEY_VALUE_HEADS):
         visible = seen & (back < info_ref[g])
         lanes = slice(g * HEAD_SIZE, (g + 1) * HEAD_SIZE)
@@ -160,7 +161,7 @@
         gs = jnp.concatenate(
             [
                 jnp.broadcast_to(
-                    gain_ref[:, (g * group_size + h) * HEAD_SIZE : (g * group_size + h + 1) * HEAD_SIZE],
+                    gain_ref[(g * group_size + h) * HEAD_SIZE : (g * group_size + h + 1) * HEAD_SIZE][None, :],
                     (token_rows, HEAD_SIZE),
                 )
                 for h in range(group_size)
@@ -266,9 +267,6 @@
     window_packed = jnp.concatenate(
         [piece[:, : 2 * key_value_width] for piece in earlier] + [jnp.concatenate([k, v], axis=1)], axis=0
     )
-    info = jnp.concatenate(
-        [window_lengths.astype(jnp.int32), (lax.axis_index("ctx") * token_rows - padding_rows).reshape(1)]
-    ).astype(jnp.int32)
     wout, wdq, halo_out, own_grad = pl.pallas_call(
         window_kernel,
         out_shape=(
@@ -284,7 +282,7 @@
             transcendentals=QUERY_HEADS * token_rows * window_rows,
             bytes_accessed=2 * token_rows * width * (2 + 4) + 2 * window_rows * key_value_width * (2 + 4),
         ),
-    )(info, q, c, window_packed[:, :key_value_width], window_packed[:, key_value_width:])
+    )(window_lengths, q, c, window_packed[:, :key_value_width], window_packed[:, key_value_width:])
     state_rows = KEY_VALUE_HEADS * HEAD_SIZE
     gain_rows = width // HEAD_SIZE
     riding_rows = state_rows + gain_rows + (-(state_rows + gain_rows)) % 16
@@ -304,7 +302,7 @@
             transcendentals=QUERY_HEADS * token_rows,
             bytes_accessed=token_rows * width * (2 + 2 + 4 + 4 + 2 + 2) + 6 * token_rows * key_value_width * 4,
         ),
-    )(q, c, k, spiked, prior_half, gain.reshape(1, width), wout, wdq)
+    )(q, c, k, spiked, prior_half, gain, wout, wdq)
     total_tokens = queries.shape[0] * lax.axis_size("dp") * token_rows * lax.axis_size("ctx")
     later_rows, total_rows = butterfly_scan(riding, "ctx", True)
     later_half = later_rows[:state_rows].reshape(KEY_VALUE_HEADS, HEAD_SIZE, HEAD_SIZE).astype(jnp.bfloat16)

time: 56.1 us -> 56.1 us (level)
  local copies, waits for them, and re-layouts: 6.17 us -> 5.32 us
  waiting for transfers between devices: 8.42 us -> 9.18 us
  starting transfers between devices: 24.1 us -> 24.8 us
  other arithmetic: 3.74 us -> 3.16 us
    ppermute x6, waiting for transfers between devices: 2.58 us -> 3.35 us  [shifted(): return lax.ppermute(block, axis, route)]
    ppermute x6, starting transfers between devices: 16.1 us -> 16.8 us  [shifted(): return lax.ppermute(block, axis, route)]
    reshape x1 -> x0, local copies, waits for them, and re-layouts: 0.6 us -> none  [per_device(): gain.reshape(1, width)]
    concatenate x1 -> x0, other arithmetic: 0.58 us -> none  [per_device(): jnp.concatenate([window_lengths.astype(jnp.int32), (lax.axis_index('ctx')...]
    unnamed x27 -> x23, local copies, waits for them, and re-layouts: 3.11 us -> 2.86 us
  transfers between devices with their start and end apart: 11 -> 11, of which waited for: 5 -> 6; matrix products, arithmetic and copies ran while one was open for 8% -> 6% of each run, Pallas kernels for 10% -> 10%
where the time goes in v14:
time: 56.1 us; the launch traced here: 55.6 us
  starting transfers between devices  24.8 us (44%)
  Pallas kernels  10.5 us (19%)
  waiting for transfers between devices  9.18 us (16%)
  local copies, waits for them, and re-layouts  5.32 us (9%)
  other arithmetic  3.16 us (6%)
  matrix products  1.69 us (3%)
  between operations  0.96 us (2%)
    ppermute x6, starting transfers between devices, shifted(): return lax.ppermute(block, axis, route)  16.8 us
    pallas_call x1, Pallas kernels, per_device(): pl.pallas_call(window_kernel, out_shape=(jax.ShapeDtypeStruct((token_rows...  5.55 us
    pallas_call x1, Pallas kernels, per_device(): pl.pallas_call(linear_kernel, out_shape=(jax.ShapeDtypeStruct((token_rows...  4.97 us
    ppermute x2, starting transfers between devices, all_sum(): part = part + lax.ppermute(part, axes, route)  4.23 us
    ppermute x3, starting transfers between devices, butterfly_scan(): lax.ppermute(mine, axis, [(i, i ^ step) for i in range(count)])  3.74 us
    ppermute x6, waiting for transfers between devices, shifted(): return lax.ppermute(block, axis, route)  3.35 us
    ppermute x2, waiting for transfers between devices, all_sum(): part = part + lax.ppermute(part, axes, route)  3.07 us
    unnamed x23, local copies, waits for them, and re-layouts  2.86 us
  transfers between devices with their start and end apart: 11, of which 6 were waited for; matrix products, arithmetic and copies ran while one was open for 6% of the time, Pallas kernels for 10%

profile of v14, /device:TPU:0, one launch (start us, length us, event | category | flops | bytes accessed | tf_op | source)
XLA Modules:
  0.0 55.6 jit_solution(18075799876885915758)
XLA Ops:
  0.6 0.8 %copy.13 = s32[1,128,2]{2,1,0:T(8,128)S(1)} copy(s32[1,128,2]{1,2,0:T(2,128)} %param.10) | data formatting | bytes 2048 | tf_op args[3]
  1.5 0.1 pad.17.clone
  1.6 0.7 %copy-done = bf16[1,128,256]{2,1,0:T(8,128)(2,1)S(1)} copy-done((bf16[1,128,256]{2,1,0:T(8,128)(2,1)S(1)}, bf16[1,128,256]{2,1,0:T(8,128)(2,1)}, u32[]{:S(2)}) %copy-start) | copy-done | bytes 65560
  2.3 4.9 %collective-permute-start = (bf16[128,640]{1,0:T(8,128)(2,1)S(1)}, bf16[128,640]{1,0:T(8,128)(2,1)S(1)}, u32[]{:S(2)}, u32[]{:S(2)}) collective-permute-start(bf16[128,640]{1,0:T(8,128)(2,1)S(1)} %maximum_maximum_fusion.1), channel_id=1, source_target_pairs={{0,2},{1,3},{2,4},{3,5},{4,6},{5,7},{8,10},{9,11},{10,12},{11,13},... | collective-permute-start | bytes 491528 | tf_op jit(solution)/shard_map/ppermute | solution.py:88
  7.2 1.5 %collective-permute-start.1 = (bf16[128,640]{1,0:T(8,128)(2,1)S(1)}, bf16[128,640]{1,0:T(8,128)(2,1)S(1)}, u32[]{:S(2)}, u32[]{:S(2)}) collective-permute-start(bf16[128,640]{1,0:T(8,128)(2,1)S(1)} %maximum_maximum_fusion.1), channel_id=1, source_target_pairs={{0,1},{1,2},{2,3},{3,4},{4,5},{5,6},{6,7},{8,9},{9,10},{10,11},{11... | collective-permute-start | bytes 491528 | tf_op jit(solution)/shard_map/ppermute | solution.py:88
  8.7 0.1 copy.12
  8.8 0.2 broadcast_in_dim.30
  9.0 0.0 copy-start.2
  9.0 0.2 convolution_bitcast_fusion.2
  9.2 0.4 copy-done.2
  9.7 0.2 convolution_bitcast_fusion.3
  9.9 0.8 %collective-permute-done = bf16[128,640]{1,0:T(8,128)(2,1)S(1)} collective-permute-done((bf16[128,640]{1,0:T(8,128)(2,1)S(1)}, bf16[128,640]{1,0:T(8,128)(2,1)S(1)}, u32[]{:S(2)}, u32[]{:S(2)}) %collective-permute-start) | collective-permute-done | bytes 163872 | tf_op jit(solution)/shard_map/ppermute | solution.py:88
  10.6 0.2 broadcast_in_dim.32
  10.9 0.2 convolution_bitcast_fusion.6
  11.0 0.2 convolution_bitcast_fusion.7
  11.3 0.2 broadcast_in_dim.33
  11.5 0.2 convolution_bitcast_fusion.5
  11.7 0.2 convolution_bitcast_fusion.4
  11.9 4.7 %collective-permute-start.2 = (f32[2,128,128]{2,1,0:T(8,128)S(1)}, f32[2,128,128]{2,1,0:T(8,128)S(1)}, u32[]{:S(2)}, u32[]{:S(2)}) collective-permute-start(f32[2,128,128]{2,1,0:T(8,128)S(1)} %maximum_add_fusion.1), channel_id=1, source_target_pairs={{0,3},{1,4},{2,5},{3,6},{4,7},{8,11},{9,12},{10,13},{11,14},{12,15... | collective-permute-start | bytes 393224 | tf_op jit(solution)/shard_map/ppermute | solution.py:88
  16.6 3.1 %collective-permute-start.3 = (f32[2,128,128]{2,1,0:T(8,128)S(1)}, f32[2,128,128]{2,1,0:T(8,128)S(1)}, u32[]{:S(2)}, u32[]{:S(2)}) collective-permute-start(f32[2,128,128]{2,1,0:T(8,128)S(1)} %maximum_add_fusion.1), channel_id=1, source_target_pairs={{0,6},{1,7},{8,14},{9,15},{16,22},{17,23},{24,30},{25,31}} | collective-permute-start | bytes 393224 | tf_op jit(solution)/shard_map/ppermute | solution.py:88
  19.7 0.9 %slice-done = bf16[128,512]{1,0:T(8,128)(2,1)S(1)} async-done(((bf16[128,640]{1,0:T(8,128)(2,1)}), bf16[128,512]{1,0:T(8,128)(2,1)S(1)}, s32[]{:S(2)}) %slice-start) | async-done | bytes 131096 | tf_op jit(solution)/shard_map/slice | solution.py:268
  20.6 0.8 %fusion.44 = (bf16[384,256]{1,0:T(8,128)(2,1)}, bf16[384,256]{1,0:T(8,128)(2,1)}) fusion(bf16[384,512]{1,0:T(8,128)(2,1)S(1)} %maximum_maximum_fusion), kind=kLoop, calls=%fused_computation.71 | loop fusion | bytes 786432 | tf_op jit(solution)/shard_map/slice | solution.py:285
  21.4 5.6 %shard_map.110 = (f32[128,1792]{1,0:T(8,128)}, f32[128,1792]{1,0:T(8,128)}, bf16[2,128,512]{2,1,0:T(8,128)(2,1)}, f32[128,512]{1,0:T(8,128)}) custom-call(s32[2]{0:T(128)} %info_ref.1, bf16[128,1792]{1,0:T(8,128)(2,1)} %bitcast.80, bf16[128,1792]{1,0:T(8,128)(2,1)} %bitcast.82, bf16[384,256]{1,0:T(8,128)(2,1)} %get-tuple-element.24.k_ref, ...), custom_call_target="tpu_custom_call" | custom-call | flops 1056964608 | bytes 3932160 | tf_op jit(solution)/shard_map/pallas_call | solution.py:270
  27.0 0.7 %add_convert_fusion.prior_ref = bf16[2,128,128]{2,1,0:T(8,128)(2,1)} fusion(f32[2,128,128]{2,1,0:T(8,128)S(1)} %collective-permute-done.3, f32[2,128,128]{2,1,0:T(8,128)S(1)} %collective-permute-done.2, f32[1,128,128]{2,1,0:T(8,128)S(1)} %convolution_bitcast_fusion.4, f32[1,128,128]{2,1,0:T(8,128)S(1)} %convolution_bitcast_fusion.5, ...), kind=kLoop, calls=%fused_computation.35 | loop fusion | flops 196608 | bytes 589824 | tf_op jit(solution)/shard_map/convert_element_type | solution.py:266
  27.6 5.0 %shard_map.111 = (bf16[128,1792]{1,0:T(8,128)(2,1)}, bf16[128,1792]{1,0:T(8,128)(2,1)}, bf16[272,128]{1,0:T(8,128)(2,1)}, f32[128,256]{1,0:T(8,128)}, f32[128,256]{1,0:T(8,128)}) custom-call(bf16[128,1792]{1,0:T(8,128)(2,1)} %bitcast.81, bf16[128,1792]{1,0:T(8,128)(2,1)} %bitcast.83, bf16[128,256]{1,0:T(8,128)(2,1)} %bitcast.67, bf16[128,256]{1,0:T(8,128)(2,1)} %copy-done.2, ...), custom_call_target="tpu_custom_call" | custom-call | flops 587202560 | bytes 4456448 | tf_op jit(solution)/shard_map/pallas_call | solution.py:289
  32.6 0.5 collective-permute-start.4
  33.1 1.1 %collective-permute-done.4 = bf16[272,128]{1,0:T(8,128)(2,1)S(1)} collective-permute-done((bf16[272,128]{1,0:T(8,128)(2,1)}, bf16[272,128]{1,0:T(8,128)(2,1)S(1)}, u32[]{:S(2)}, u32[]{:S(2)}) %collective-permute-start.4) | collective-permute-done | bytes 69664 | tf_op jit(solution)/shard_map/ppermute | solution.py:45
  34.3 0.9 %fusion.3 = bf16[272,128]{1,0:T(8,128)(2,1)S(1)} fusion(bf16[272,128]{1,0:T(8,128)(2,1)S(1)} %collective-permute-done.4, bf16[272,128]{1,0:T(8,128)(2,1)} %get-tuple-element.19), kind=kLoop, calls=%fused_computation.18 | loop fusion | flops 139264 | bytes 208896 | tf_op jit(solution)/shard_map/convert_element_type | solution.py:44
  35.2 0.1 collective-permute-start.5
  35.3 1.4 %collective-permute-start.7 = (bf16[128,512]{1,0:T(8,128)(2,1)S(1)}, bf16[128,512]{1,0:T(8,128)(2,1)S(1)}, u32[]{:S(2)}, u32[]{:S(2)}) collective-permute-start(bf16[128,512]{1,0:T(8,128)(2,1)S(1)} %get-tuple-element.27), channel_id=1, source_target_pairs={{1,0},{2,1},{3,2},{4,3},{5,4},{6,5},{7,6},{9,8},{10,9},{11,10},{12... | collective-permute-start | bytes 393224 | tf_op jit(solution)/shard_map/ppermute | solution.py:88
  36.7 1.3 %collective-permute-start.8 = (bf16[128,512]{1,0:T(8,128)(2,1)S(1)}, bf16[128,512]{1,0:T(8,128)(2,1)S(1)}, u32[]{:S(2)}, u32[]{:S(2)}) collective-permute-start(bf16[128,512]{1,0:T(8,128)(2,1)S(1)} %get-tuple-element.28), channel_id=1, source_target_pairs={{2,0},{3,1},{4,2},{5,3},{6,4},{7,5},{10,8},{11,9},{12,10},{13,11},... | collective-permute-start | bytes 393224 | tf_op jit(solution)/shard_map/ppermute | solution.py:88
  38.0 1.6 %collective-permute-done.5 = bf16[272,128]{1,0:T(8,128)(2,1)S(1)} collective-permute-done((bf16[272,128]{1,0:T(8,128)(2,1)S(1)}, bf16[272,128]{1,0:T(8,128)(2,1)S(1)}, u32[]{:S(2)}, u32[]{:S(2)}) %collective-permute-start.5) | collective-permute-done | bytes 69664 | tf_op jit(solution)/shard_map/ppermute | solution.py:45
  39.7 3.1 %collective-permute-start.6 = (bf16[272,128]{1,0:T(8,128)(2,1)S(1)}, bf16[272,128]{1,0:T(8,128)(2,1)S(1)}, u32[]{:S(2)}, u32[]{:S(2)}) collective-permute-start(bf16[272,128]{1,0:T(8,128)(2,1)S(1)} %fusion.4), channel_id=1, source_target_pairs={{0,4},{1,5},{2,6},{3,7},{4,0},{5,1},{6,2},{7,3},{8,12},{9,13},{10,... | collective-permute-start | bytes 208904 | tf_op jit(solution)/shard_map/ppermute | solution.py:45
  42.8 2.6 %collective-permute-done.8 = bf16[128,512]{1,0:T(8,128)(2,1)S(1)} collective-permute-done((bf16[128,512]{1,0:T(8,128)(2,1)S(1)}, bf16[128,512]{1,0:T(8,128)(2,1)S(1)}, u32[]{:S(2)}, u32[]{:S(2)}) %collective-permute-start.8) | collective-permute-done | bytes 131104 | tf_op jit(solution)/shard_map/ppermute | solution.py:88
  45.4 0.0 copy-start.3
  45.5 0.1 fusion.2
  45.5 0.8 %copy-done.3 = bf16[128,256]{1,0:T(8,128)(2,1)S(1)} copy-done((bf16[128,256]{1,0:T(8,128)(2,1)S(1)}, bf16[128,256]{1,0:T(8,128)(2,1)}, u32[]{:S(2)}) %copy-start.3) | copy-done | bytes 65560
  46.3 0.1 copy-done.9
  46.4 0.1 slice_add_fusion.4
  46.5 0.2 slice_add_fusion.3
  46.7 1.6 %collective-permute-start.9 = (f32[1792]{0:T(1024)S(1)}, f32[1792]{0:T(1024)S(1)}, u32[]{:S(2)}, u32[]{:S(2)}) collective-permute-start(f32[1792]{0:T(1024)S(1)} %fusion.43), channel_id=1, source_target_pairs={{0,8},{8,0},{16,24},{24,16},{1,9},{9,1},{17,25},{25,17},{2,10},{10... | collective-permute-start | bytes 21512 | tf_op jit(solution)/shard_map/ppermute | solution.py:80
  48.4 0.1 slice_add_fusion.2
  48.5 0.1 slice_add_fusion.1
  48.7 1.8 %collective-permute-done.9 = f32[1792]{0:T(1024)S(1)} collective-permute-done((f32[1792]{0:T(1024)S(1)}, f32[1792]{0:T(1024)S(1)}, u32[]{:S(2)}, u32[]{:S(2)}) %collective-permute-start.9) | collective-permute-done | bytes 7200 | tf_op jit(solution)/shard_map/ppermute | solution.py:80
  50.5 2.6 %collective-permute-start.10 = (f32[1792]{0:T(1024)S(1)}, f32[1792]{0:T(1024)S(1)}, u32[]{:S(2)}, u32[]{:S(2)}) collective-permute-start(f32[1792]{0:T(1024)S(1)} %add.74), channel_id=1, source_target_pairs={{0,16},{8,24},{16,0},{24,8},{1,17},{9,25},{17,1},{25,9},{2,18},{10... | collective-permute-start | bytes 21512 | tf_op jit(solution)/shard_map/ppermute | solution.py:80
  53.1 0.7 %fusion.12 = (bf16[1,128,256]{2,1,0:T(8,128)(2,1)}, bf16[1,128,256]{2,1,0:T(8,128)(2,1)}) fusion(f32[128,512]{1,0:T(8,128)S(1)} %convert_add_fusion, f32[16,8,2,128]{3,2,1,0:T(2,128)S(1)} %bitcast.75, f32[128,128]{1,0:T(8,128)S(1)} %slice_add_fusion.1, f32[128,128]{1,0:T(8,128)S(1)} %slice_add_fusion.2, f32[128,128]{1,0:T(8,128)S(1)} %slice_add_fusion.3, ...), kind=kLoop, calls=%fused_computation.37 | loop fusion | flops 229376 | bytes 786432 | tf_op jit(solution)/shard_map/broadcast_in_dim | solution.py:339
  53.8 1.3 %collective-permute-done.10 = f32[1792]{0:T(1024)S(1)} collective-permute-done((f32[1792]{0:T(1024)S(1)}, f32[1792]{0:T(1024)S(1)}, u32[]{:S(2)}, u32[]{:S(2)}) %collective-permute-start.10) | collective-permute-done | bytes 7200 | tf_op jit(solution)/shard_map/ppermute | solution.py:80
  55.0 0.6 %add_multiply_fusion = f32[1792]{0:T(1024)} fusion(f32[1792]{0:T(1024)S(1)} %add.74, f32[1792]{0:T(1024)S(1)} %collective-permute-done.10), kind=kLoop, calls=%fused_computation.69 | loop fusion | flops 3584 | bytes 21504 | tf_op jit(solution)/shard_map/mul | solution.py:310
  (40 shorter events, 0.3 us)
Async XLA Ops:
  0.6 0.9 %copy-start.4 = (bf16[1,128,256]{2,1,0:T(8,128)(2,1)S(1)}, bf16[1,128,256]{2,1,0:T(8,128)(2,1)}, u32[]{:S(2)}) copy-start(bf16[1,128,256]{2,1,0:T(8,128)(2,1)} %param.9) | copy-start | bytes 196612
  1.5 0.8 %copy-start = (bf16[1,128,256]{2,1,0:T(8,128)(2,1)S(1)}, bf16[1,128,256]{2,1,0:T(8,128)(2,1)}, u32[]{:S(2)}) copy-start(bf16[1,128,256]{2,1,0:T(8,128)(2,1)} %param.8) | copy-start | bytes 196612
  2.3 6.4 %copy-start.10 = (s32[1,128,2]{1,2,0:T(2,128)S(1)}, s32[1,128,2]{1,2,0:T(2,128)}, u32[]{:S(2)}) copy-start(s32[1,128,2]{1,2,0:T(2,128)} %param.10) | copy-start | bytes 3076
  2.3 8.3 %collective-permute-start = (bf16[128,640]{1,0:T(8,128)(2,1)S(1)}, bf16[128,640]{1,0:T(8,128)(2,1)S(1)}, u32[]{:S(2)}, u32[]{:S(2)}) collective-permute-start(bf16[128,640]{1,0:T(8,128)(2,1)S(1)} %maximum_maximum_fusion.1), channel_id=1, source_target_pairs={{0,2},{1,3},{2,4},{3,5},{4,6},{5,7},{8,10},{9,11},{10,12},{11,13},... | collective-permute-start | bytes 491528 | tf_op jit(solution)/shard_map/ppermute | solution.py:88
  7.2 4.0 %collective-permute-start.1 = (bf16[128,640]{1,0:T(8,128)(2,1)S(1)}, bf16[128,640]{1,0:T(8,128)(2,1)S(1)}, u32[]{:S(2)}, u32[]{:S(2)}) collective-permute-start(bf16[128,640]{1,0:T(8,128)(2,1)S(1)} %maximum_maximum_fusion.1), channel_id=1, source_target_pairs={{0,1},{1,2},{2,3},{3,4},{4,5},{5,6},{6,7},{8,9},{9,10},{10,11},{11... | collective-permute-start | bytes 491528 | tf_op jit(solution)/shard_map/ppermute | solution.py:88
  9.0 0.6 %copy-start.2 = (bf16[128,256]{1,0:T(8,128)(2,1)}, bf16[128,256]{1,0:T(8,128)(2,1)S(1)}, u32[]{:S(2)}) copy-start(bf16[128,256]{1,0:T(8,128)(2,1)S(1)} %fusion.7.s_ref) | copy-start | bytes 196612
  10.6 9.1 %copy-start.5 = (bf16[128,640]{1,0:T(8,128)(2,1)}, bf16[128,640]{1,0:T(8,128)(2,1)S(1)}, u32[]{:S(2)}) copy-start(bf16[128,640]{1,0:T(8,128)(2,1)S(1)} %collective-permute-done) | copy-start | bytes 491524
  11.9 15.1 %collective-permute-start.2 = (f32[2,128,128]{2,1,0:T(8,128)S(1)}, f32[2,128,128]{2,1,0:T(8,128)S(1)}, u32[]{:S(2)}, u32[]{:S(2)}) collective-permute-start(f32[2,128,128]{2,1,0:T(8,128)S(1)} %maximum_add_fusion.1), channel_id=1, source_target_pairs={{0,3},{1,4},{2,5},{3,6},{4,7},{8,11},{9,12},{10,13},{11,14},{12,15... | collective-permute-start | bytes 393224 | tf_op jit(solution)/shard_map/ppermute | solution.py:88
  16.6 10.4 %collective-permute-start.3 = (f32[2,128,128]{2,1,0:T(8,128)S(1)}, f32[2,128,128]{2,1,0:T(8,128)S(1)}, u32[]{:S(2)}, u32[]{:S(2)}) collective-permute-start(f32[2,128,128]{2,1,0:T(8,128)S(1)} %maximum_add_fusion.1), channel_id=1, source_target_pairs={{0,6},{1,7},{8,14},{9,15},{16,22},{17,23},{24,30},{25,31}} | collective-permute-start | bytes 393224 | tf_op jit(solution)/shard_map/ppermute | solution.py:88
  19.7 0.9 %slice-start = ((bf16[128,640]{1,0:T(8,128)(2,1)}), bf16[128,512]{1,0:T(8,128)(2,1)S(1)}, s32[]{:S(2)}) async-start(bf16[128,640]{1,0:T(8,128)(2,1)} %copy-done.5), calls=%async_computation | async-start | bytes 262144 | tf_op jit(solution)/shard_map/slice | solution.py:268
  27.6 7.6 %copy-start.7 = (bf16[2,128,512]{2,1,0:T(8,128)(2,1)S(1)}, bf16[2,128,512]{2,1,0:T(8,128)(2,1)}, u32[]{:S(2)}) copy-start(bf16[2,128,512]{2,1,0:T(8,128)(2,1)} %get-tuple-element.21) | copy-start | bytes 786436
  32.6 1.7 %collective-permute-start.4 = (bf16[272,128]{1,0:T(8,128)(2,1)}, bf16[272,128]{1,0:T(8,128)(2,1)S(1)}, u32[]{:S(2)}, u32[]{:S(2)}) collective-permute-start(bf16[272,128]{1,0:T(8,128)(2,1)} %get-tuple-element.19), channel_id=1, source_target_pairs={{0,1},{1,0},{2,3},{3,2},{4,5},{5,4},{6,7},{7,6},{8,9},{9,8},{10,11... | collective-permute-start | bytes 208904 | tf_op jit(solution)/shard_map/ppermute | solution.py:45
  35.2 4.5 %collective-permute-start.5 = (bf16[272,128]{1,0:T(8,128)(2,1)S(1)}, bf16[272,128]{1,0:T(8,128)(2,1)S(1)}, u32[]{:S(2)}, u32[]{:S(2)}) collective-permute-start(bf16[272,128]{1,0:T(8,128)(2,1)S(1)} %fusion.3), channel_id=1, source_target_pairs={{0,2},{1,3},{2,0},{3,1},{4,6},{5,7},{6,4},{7,5},{8,10},{9,11},{10,... | collective-permute-start | bytes 208904 | tf_op jit(solution)/shard_map/ppermute | solution.py:45
  35.2 10.2 %copy-start.6 = (f32[128,512]{1,0:T(8,128)S(1)}, f32[128,512]{1,0:T(8,128)}, u32[]{:S(2)}) copy-start(f32[128,512]{1,0:T(8,128)} %get-tuple-element.20) | copy-start | bytes 786436
  35.3 7.5 %collective-permute-start.7 = (bf16[128,512]{1,0:T(8,128)(2,1)S(1)}, bf16[128,512]{1,0:T(8,128)(2,1)S(1)}, u32[]{:S(2)}, u32[]{:S(2)}) collective-permute-start(bf16[128,512]{1,0:T(8,128)(2,1)S(1)} %get-tuple-element.27), channel_id=1, source_target_pairs={{1,0},{2,1},{3,2},{4,3},{5,4},{6,5},{7,6},{9,8},{10,9},{11,10},{12... | collective-permute-start | bytes 393224 | tf_op jit(solution)/shard_map/ppermute | solution.py:88
  36.7 8.7 %collective-permute-start.8 = (bf16[128,512]{1,0:T(8,128)(2,1)S(1)}, bf16[128,512]{1,0:T(8,128)(2,1)S(1)}, u32[]{:S(2)}, u32[]{:S(2)}) collective-permute-start(bf16[128,512]{1,0:T(8,128)(2,1)S(1)} %get-tuple-element.28), channel_id=1, source_target_pairs={{2,0},{3,1},{4,2},{5,3},{6,4},{7,5},{10,8},{11,9},{12,10},{13,11},... | collective-permute-start | bytes 393224 | tf_op jit(solution)/shard_map/ppermute | solution.py:88
  39.7 5.8 %collective-permute-start.6 = (bf16[272,128]{1,0:T(8,128)(2,1)S(1)}, bf16[272,128]{1,0:T(8,128)(2,1)S(1)}, u32[]{:S(2)}, u32[]{:S(2)}) collective-permute-start(bf16[272,128]{1,0:T(8,128)(2,1)S(1)} %fusion.4), channel_id=1, source_target_pairs={{0,4},{1,5},{2,6},{3,7},{4,0},{5,1},{6,2},{7,3},{8,12},{9,13},{10,... | collective-permute-start | bytes 208904 | tf_op jit(solution)/shard_map/ppermute | solution.py:45
  45.4 0.8 %copy-start.3 = (bf16[128,256]{1,0:T(8,128)(2,1)S(1)}, bf16[128,256]{1,0:T(8,128)(2,1)}, u32[]{:S(2)}) copy-start(bf16[128,256]{1,0:T(8,128)(2,1)} %copy-done.2) | copy-start | bytes 196612
  45.5 0.9 %copy-start.9 = (f32[128,256]{1,0:T(8,128)S(1)}, f32[128,256]{1,0:T(8,128)}, u32[]{:S(2)}) copy-start(f32[128,256]{1,0:T(8,128)} %get-tuple-element.18) | copy-start | bytes 393220
  46.7 1.7 %copy-start.1 = (bf16[1,128,256]{2,1,0:T(8,128)(2,1)S(1)}, bf16[1,128,256]{2,1,0:T(8,128)(2,1)}, u32[]{:S(2)}) copy-start(bf16[1,128,256]{2,1,0:T(8,128)(2,1)} %param.8) | copy-start | bytes 196612
  46.7 1.7 %copy-start.8 = (f32[128,256]{1,0:T(8,128)S(1)}, f32[128,256]{1,0:T(8,128)}, u32[]{:S(2)}) copy-start(f32[128,256]{1,0:T(8,128)} %get-tuple-element.22) | copy-start | bytes 393220
  46.7 3.7 %collective-permute-start.9 = (f32[1792]{0:T(1024)S(1)}, f32[1792]{0:T(1024)S(1)}, u32[]{:S(2)}, u32[]{:S(2)}) collective-permute-start(f32[1792]{0:T(1024)S(1)} %fusion.43), channel_id=1, source_target_pairs={{0,8},{8,0},{16,24},{24,16},{1,9},{9,1},{17,25},{25,17},{2,10},{10... | collective-permute-start | bytes 21512 | tf_op jit(solution)/shard_map/ppermute | solution.py:80
  50.5 4.5 %collective-permute-start.10 = (f32[1792]{0:T(1024)S(1)}, f32[1792]{0:T(1024)S(1)}, u32[]{:S(2)}, u32[]{:S(2)}) collective-permute-start(f32[1792]{0:T(1024)S(1)} %add.74), channel_id=1, source_target_pairs={{0,16},{8,24},{16,0},{24,8},{1,17},{9,25},{17,1},{25,9},{2,18},{10... | collective-permute-start | bytes 21512 | tf_op jit(solution)/shard_map/ppermute | solution.py:80

commit v15 on v14

--- a/solution.py
+++ b/solution.py
@@ -39,16 +39,19 @@
     place = lax.axis_index(axis)
     group = part
     before = jnp.zeros(part.shape, jnp.float32)
+    first = None
     step = 1
     while step < count:
         mine = group.astype(jnp.bfloat16)
         got = lax.ppermute(mine, axis, [(i, i ^ step) for i in range(count)]).astype(jnp.float32)
+        if first is None:
+            first = got
         partner = jnp.bitwise_xor(place, step)
         take = partner > place if reverse else partner < place
         before = before + jnp.where(take, got, 0.0)
         group = mine.astype(jnp.float32) + got
         step *= 2
-    return before, group
+    return before, group, first
 
 
 def spread_scan(near, own, axis):
@@ -142,21 +145,36 @@
         own_ref[:, value_lanes] = dv[padding_rows:]
 
 
-def linear_kernel(q_ref, c_ref, k_ref, s_ref, prior_ref, gain_ref, wout_ref, wdq_ref,
-                  mixed_ref, dq_ref, riding_ref, ldk_ref, dsp_ref):
-    group_size = QUERY_HEADS // KEY_VALUE_HEADS
-    token_rows = q_ref.shape[0]
+def linear_scores(q_ref, k_ref, group, group_size, causal):
+    lanes = slice(group * HEAD_SIZE, (group + 1) * HEAD_SIZE)
+    qs = stacked_heads(q_ref, group, group_size)
+    kg = k_ref[:, lanes]
+    lh = jnp.where(
+        causal,
+        lax.dot_general(qs, kg, (((1,), (1,)), ((), ())), preferred_element_type=jnp.float32),
+        0.0,
+    ).astype(jnp.bfloat16)
+    return qs, kg, lh
+
+
+def causal_mask(token_rows, group_size):
     stacked_rows = group_size * token_rows
     row = lax.broadcasted_iota(jnp.int32, (stacked_rows, token_rows), 0) % token_rows
     col = lax.broadcasted_iota(jnp.int32, (stacked_rows, token_rows), 1)
-    causal = row >= col
+    return row >= col
+
+
+def linear_forward_kernel(q_ref, c_ref, k_ref, s_ref, prior_ref, gain_ref, wout_ref,
+                          mixed_ref, dl_ref, riding_ref):
+    group_size = QUERY_HEADS // KEY_VALUE_HEADS
+    token_rows = q_ref.shape[0]
+    causal = causal_mask(token_rows, group_size)
     gain_rows = []
     for g in range(KEY_VALUE_HEADS):
         lanes = slice(g * HEAD_SIZE, (g + 1) * HEAD_SIZE)
-        kg = k_ref[:, lanes]
         sg = s_ref[:, lanes]
         pg = prior_ref[g]
-        qs = stacked_heads(q_ref, g, group_size)
+        qs, kg, lh = linear_scores(q_ref, k_ref, g, group_size, causal)
         cs = stacked_heads(c_ref, g, group_size).astype(jnp.float32)
         gs = jnp.concatenate(
             [
@@ -168,11 +186,6 @@
             ],
             axis=0,
         )
-        lh = jnp.where(
-            causal,
-            lax.dot_general(qs, kg, (((1,), (1,)), ((), ())), preferred_element_type=jnp.float32),
-            0.0,
-        ).astype(jnp.bfloat16)
         lin = jnp.dot(lh, sg, preferred_element_type=jnp.float32) + jnp.dot(
             qs, pg, preferred_element_type=jnp.float32
         )
@@ -184,9 +197,32 @@
         dl = ((scaled - normed * jnp.mean(scaled * normed, axis=-1, keepdims=True)) * inverse_root).astype(
             jnp.bfloat16
         )
+        dl_ref[g] = dl
         riding_ref[g * HEAD_SIZE : (g + 1) * HEAD_SIZE, :] = lax.dot_general(
             qs, dl, (((0,), (0,)), ((), ())), preferred_element_type=jnp.float32
         ).astype(riding_ref.dtype)
+        for h in range(group_size):
+            cols = slice((g * group_size + h) * HEAD_SIZE, (g * group_size + h + 1) * HEAD_SIZE)
+            rows = slice(h * token_rows, (h + 1) * token_rows)
+            mixed_ref[:, cols] = (gn[rows] + wout_ref[:, cols]).astype(mixed_ref.dtype)
+            gain_rows.append(jnp.sum(weighted[rows], axis=0, keepdims=True))
+    state_rows = KEY_VALUE_HEADS * HEAD_SIZE
+    spare = riding_ref.shape[0] - state_rows - len(gain_rows)
+    riding_ref[state_rows:, :] = jnp.concatenate(
+        gain_rows + [jnp.zeros((spare, HEAD_SIZE), jnp.float32)], axis=0
+    ).astype(riding_ref.dtype)
+
+
+def linear_backward_kernel(q_ref, k_ref, s_ref, prior_ref, dl_ref, wdq_ref, dq_ref, ldk_ref, dsp_ref):
+    group_size = QUERY_HEADS // KEY_VALUE_HEADS
+    token_rows = q_ref.shape[0]
+    causal = causal_mask(token_rows, group_size)
+    for g in range(KEY_VALUE_HEADS):
+        lanes = slice(g * HEAD_SIZE, (g + 1) * HEAD_SIZE)
+        sg = s_ref[:, lanes]
+        pg = prior_ref[g]
+        qs, kg, lh = linear_scores(q_ref, k_ref, g, group_size, causal)
+        dl = dl_ref[g]
         bh = jnp.where(
             causal,
             lax.dot_general(dl, sg, (((1,), (1,)), ((), ())), preferred_element_type=jnp.float32),
@@ -197,16 +233,9 @@
         for h in range(group_size):
             cols = slice((g * group_size + h) * HEAD_SIZE, (g * group_size + h + 1) * HEAD_SIZE)
             rows = slice(h * token_rows, (h + 1) * token_rows)
-            mixed_ref[:, cols] = (gn[rows] + wout_ref[:, cols]).astype(mixed_ref.dtype)
-            gain_rows.append(jnp.sum(weighted[rows], axis=0, keepdims=True))
             dq_ref[:, cols] = (ldq[rows] + wdq_ref[:, cols]).astype(dq_ref.dtype)
         ldk_ref[:, lanes] = lax.dot_general(bh, qs, (((0,), (0,)), ((), ())), preferred_element_type=jnp.float32)
         dsp_ref[:, lanes] = lax.dot_general(lh, dl, (((0,), (0,)), ((), ())), preferred_element_type=jnp.float32)
-    state_rows = KEY_VALUE_HEADS * HEAD_SIZE
-    spare = riding_ref.shape[0] - state_rows - len(gain_rows)
-    riding_ref[state_rows:, :] = jnp.concatenate(
-        gain_rows + [jnp.zeros((spare, HEAD_SIZE), jnp.float32)], axis=0
-    ).astype(riding_ref.dtype)
 
 
 def in_vmem(count):
@@ -286,25 +315,40 @@
     state_rows = KEY_VALUE_HEADS * HEAD_SIZE
     gain_rows = width // HEAD_SIZE
     riding_rows = state_rows + gain_rows + (-(state_rows + gain_rows)) % 16
-    mixed, d_queries, riding, ldk, dsp = pl.pallas_call(
-        linear_kernel,
+    group_size = QUERY_HEADS // KEY_VALUE_HEADS
+    mixed, d_linear, riding = pl.pallas_call(
+        linear_forward_kernel,
         out_shape=(
             jax.ShapeDtypeStruct((token_rows, width), jnp.bfloat16),
+            jax.ShapeDtypeStruct((KEY_VALUE_HEADS, group_size * token_rows, HEAD_SIZE), jnp.bfloat16),
+            jax.ShapeDtypeStruct((riding_rows, HEAD_SIZE), jnp.bfloat16),
+        ),
+        in_specs=in_vmem(7),
+        out_specs=tuple(in_vmem(3)),
+        cost_estimate=pl.CostEstimate(
+            flops=8 * QUERY_HEADS * token_rows * token_rows * HEAD_SIZE,
+            transcendentals=QUERY_HEADS * token_rows,
+            bytes_accessed=token_rows * width * (2 + 2 + 4 + 2 + 2),
+        ),
+    )(q, c, k, spiked, prior_half, gain, wout)
+    total_tokens = queries.shape[0] * lax.axis_size("dp") * token_rows * lax.axis_size("ctx")
+    later_rows, total_rows, first_round = butterfly_scan(riding, "ctx", True)
+    late_dl, _ = lax.optimization_barrier((d_linear, first_round))
+    d_queries, ldk, dsp = pl.pallas_call(
+        linear_backward_kernel,
+        out_shape=(
             jax.ShapeDtypeStruct((token_rows, width), jnp.bfloat16),
-            jax.ShapeDtypeStruct((riding_rows, HEAD_SIZE), jnp.bfloat16),
             jax.ShapeDtypeStruct((token_rows, key_value_width), jnp.float32),
             jax.ShapeDtypeStruct((token_rows, key_value_width), jnp.float32),
         ),
-        in_specs=in_vmem(8),
-        out_specs=tuple(in_vmem(5)),
+        in_specs=in_vmem(6),
+        out_specs=tuple(in_vmem(3)),
         cost_estimate=pl.CostEstimate(
-            flops=20 * QUERY_HEADS * token_rows * token_rows * HEAD_SIZE,
-            transcendentals=QUERY_HEADS * token_rows,
-            bytes_accessed=token_rows * width * (2 + 2 + 4 + 4 + 2 + 2) + 6 * token_rows * key_value_width * 4,
-        ),
-    )(q, c, k, spiked, prior_half, gain, wout, wdq)
-    total_tokens = queries.shape[0] * lax.axis_size("dp") * token_rows * lax.axis_size("ctx")
-    later_rows, total_rows = butterfly_scan(riding, "ctx", True)
+            flops=12 * QUERY_HEADS * token_rows * token_rows * HEAD_SIZE,
+            transcendentals=0,
+            bytes_accessed=token_rows * width * (2 + 2 + 4 + 2) + 2 * token_rows * key_value_width * 4,
+        ),
+    )(q, k, spiked, prior_half, late_dl, wdq)
     later_half = later_rows[:state_rows].reshape(KEY_VALUE_HEADS, HEAD_SIZE, HEAD_SIZE).astype(jnp.bfloat16)
     gain_ctx = total_rows[state_rows : state_rows + gain_rows].reshape(width)
     d_gain = all_sum(gain_ctx, ("dp",)) * (total_tokens ** (-0.5))

time: 56.1 us -> 58.5 us (1.043)
  Pallas kernels: 10.5 us -> 12.9 us
    pallas_call x1 -> x2, Pallas kernels: 4.97 us -> 7.36 us  [the longest x1 4.02 us: per_device(): pl.pallas_call(linear_forward_kernel, out_shape=(jax.ShapeDtypeStruct((to...]
  transfers between devices with their start and end apart: 11 -> 11, of which waited for: 6 -> 6; matrix products, arithmetic and copies ran while one was open for 6% -> 5% of each run, Pallas kernels for 10% -> 15%
where the time goes in v15:
time: 58.5 us; the launch traced here: 58 us
  starting transfers between devices  24.8 us (42%)
  Pallas kernels  12.9 us (22%)
  waiting for transfers between devices  9.19 us (16%)
  local copies, waits for them, and re-layouts  5.33 us (9%)
  other arithmetic  3.17 us (5%)
  matrix products  1.69 us (3%)
  between operations  0.94 us (2%)
    ppermute x6, starting transfers between devices, shifted(): return lax.ppermute(block, axis, route)  16.8 us
    pallas_call x1, Pallas kernels, per_device(): pl.pallas_call(window_kernel, out_shape=(jax.ShapeDtypeStruct((token_rows...  5.53 us
    ppermute x2, starting transfers between devices, all_sum(): part = part + lax.ppermute(part, axes, route)  4.22 us
    pallas_call x1, Pallas kernels, per_device(): pl.pallas_call(linear_forward_kernel, out_shape=(jax.ShapeDtypeStruct((to...  4.02 us
    ppermute x3, starting transfers between devices, butterfly_scan(): lax.ppermute(mine, axis, [(i, i ^ step) for i in range(count)])  3.75 us
    ppermute x6, waiting for transfers between devices, shifted(): return lax.ppermute(block, axis, route)  3.35 us
    pallas_call x1, Pallas kernels, per_device(): pl.pallas_call(linear_backward_kernel, out_shape=(jax.ShapeDtypeStruct((t...  3.33 us
    ppermute x2, waiting for transfers between devices, all_sum(): part = part + lax.ppermute(part, axes, route)  3.08 us
  transfers between devices with their start and end apart: 11, of which 6 were waited for; matrix products, arithmetic and copies ran while one was open for 5% of the time, Pallas kernels for 15%

profile of v15, /device:TPU:0, one launch (start us, length us, event | category | flops | bytes accessed | tf_op | source)
XLA Modules:
  0.0 58.0 jit_solution(5144959336148040125)
XLA Ops:
  0.6 0.8 %copy.13 = s32[1,128,2]{2,1,0:T(8,128)S(1)} copy(s32[1,128,2]{1,2,0:T(2,128)} %param.10) | data formatting | bytes 2048 | tf_op args[3]
  1.5 0.1 pad.17.clone
  1.6 0.7 %copy-done = bf16[1,128,256]{2,1,0:T(8,128)(2,1)S(1)} copy-done((bf16[1,128,256]{2,1,0:T(8,128)(2,1)S(1)}, bf16[1,128,256]{2,1,0:T(8,128)(2,1)}, u32[]{:S(2)}) %copy-start) | copy-done | bytes 65560
  2.3 4.9 %collective-permute-start = (bf16[128,640]{1,0:T(8,128)(2,1)S(1)}, bf16[128,640]{1,0:T(8,128)(2,1)S(1)}, u32[]{:S(2)}, u32[]{:S(2)}) collective-permute-start(bf16[128,640]{1,0:T(8,128)(2,1)S(1)} %maximum_maximum_fusion.1), channel_id=1, source_target_pairs={{0,2},{1,3},{2,4},{3,5},{4,6},{5,7},{8,10},{9,11},{10,12},{11,13},... | collective-permute-start | bytes 491528 | tf_op jit(solution)/shard_map/ppermute | solution.py:91
  7.2 1.5 %collective-permute-start.1 = (bf16[128,640]{1,0:T(8,128)(2,1)S(1)}, bf16[128,640]{1,0:T(8,128)(2,1)S(1)}, u32[]{:S(2)}, u32[]{:S(2)}) collective-permute-start(bf16[128,640]{1,0:T(8,128)(2,1)S(1)} %maximum_maximum_fusion.1), channel_id=1, source_target_pairs={{0,1},{1,2},{2,3},{3,4},{4,5},{5,6},{6,7},{8,9},{9,10},{10,11},{11... | collective-permute-start | bytes 491528 | tf_op jit(solution)/shard_map/ppermute | solution.py:91
  8.7 0.1 copy.12
  8.8 0.2 broadcast_in_dim.30
  9.0 0.2 convolution_bitcast_fusion.2
  9.2 0.4 copy-done.2
  9.7 0.2 convolution_bitcast_fusion.3
  9.9 0.8 %collective-permute-done = bf16[128,640]{1,0:T(8,128)(2,1)S(1)} collective-permute-done((bf16[128,640]{1,0:T(8,128)(2,1)S(1)}, bf16[128,640]{1,0:T(8,128)(2,1)S(1)}, u32[]{:S(2)}, u32[]{:S(2)}) %collective-permute-start) | collective-permute-done | bytes 163872 | tf_op jit(solution)/shard_map/ppermute | solution.py:91
  10.6 0.2 broadcast_in_dim.32
  10.9 0.2 convolution_bitcast_fusion.6
  11.0 0.2 convolution_bitcast_fusion.7
  11.3 0.2 broadcast_in_dim.33
  11.5 0.2 convolution_bitcast_fusion.5
  11.7 0.2 convolution_bitcast_fusion.4
  11.9 4.7 %collective-permute-start.2 = (f32[2,128,128]{2,1,0:T(8,128)S(1)}, f32[2,128,128]{2,1,0:T(8,128)S(1)}, u32[]{:S(2)}, u32[]{:S(2)}) collective-permute-start(f32[2,128,128]{2,1,0:T(8,128)S(1)} %maximum_add_fusion.1), channel_id=1, source_target_pairs={{0,3},{1,4},{2,5},{3,6},{4,7},{8,11},{9,12},{10,13},{11,14},{12,15... | collective-permute-start | bytes 393224 | tf_op jit(solution)/shard_map/ppermute | solution.py:91
  16.6 3.1 %collective-permute-start.3 = (f32[2,128,128]{2,1,0:T(8,128)S(1)}, f32[2,128,128]{2,1,0:T(8,128)S(1)}, u32[]{:S(2)}, u32[]{:S(2)}) collective-permute-start(f32[2,128,128]{2,1,0:T(8,128)S(1)} %maximum_add_fusion.1), channel_id=1, source_target_pairs={{0,6},{1,7},{8,14},{9,15},{16,22},{17,23},{24,30},{25,31}} | collective-permute-start | bytes 393224 | tf_op jit(solution)/shard_map/ppermute | solution.py:91
  19.7 0.0 slice-start
  19.7 0.9 %slice-done = bf16[128,512]{1,0:T(8,128)(2,1)S(1)} async-done(((bf16[128,640]{1,0:T(8,128)(2,1)}), bf16[128,512]{1,0:T(8,128)(2,1)S(1)}, s32[]{:S(2)}) %slice-start) | async-done | bytes 131096 | tf_op jit(solution)/shard_map/slice | solution.py:297
  20.6 0.8 %fusion.43 = (bf16[384,256]{1,0:T(8,128)(2,1)}, bf16[384,256]{1,0:T(8,128)(2,1)}) fusion(bf16[384,512]{1,0:T(8,128)(2,1)S(1)} %maximum_maximum_fusion), kind=kLoop, calls=%fused_computation.69 | loop fusion | bytes 786432 | tf_op jit(solution)/shard_map/slice | solution.py:314
  21.4 5.5 %shard_map.110 = (f32[128,1792]{1,0:T(8,128)}, f32[128,1792]{1,0:T(8,128)}, bf16[2,128,512]{2,1,0:T(8,128)(2,1)}, f32[128,512]{1,0:T(8,128)}) custom-call(s32[2]{0:T(128)} %info_ref.1, bf16[128,1792]{1,0:T(8,128)(2,1)} %bitcast.75, bf16[128,1792]{1,0:T(8,128)(2,1)} %bitcast.84, bf16[384,256]{1,0:T(8,128)(2,1)} %get-tuple-element.28.k_ref, ...), custom_call_target="tpu_custom_call" | custom-call | flops 1056964608 | bytes 3932160 | tf_op jit(solution)/shard_map/pallas_call | solution.py:299
  26.9 0.7 %add_convert_fusion.1.prior_ref = bf16[2,128,128]{2,1,0:T(8,128)(2,1)} fusion(f32[2,128,128]{2,1,0:T(8,128)S(1)} %collective-permute-done.3, f32[2,128,128]{2,1,0:T(8,128)S(1)} %collective-permute-done.2, f32[1,128,128]{2,1,0:T(8,128)S(1)} %convolution_bitcast_fusion.4, f32[1,128,128]{2,1,0:T(8,128)S(1)} %convolution_bitcast_fusion.5, ...), kind=kLoop, calls=%fused_computation.33 | loop fusion | flops 196608 | bytes 589824 | tf_op jit(solution)/shard_map/convert_element_type | solution.py:295
  27.6 4.0 %shard_map.111 = (bf16[128,1792]{1,0:T(8,128)(2,1)}, bf16[2,896,128]{2,1,0:T(8,128)(2,1)}, bf16[272,128]{1,0:T(8,128)(2,1)}) custom-call(bf16[128,1792]{1,0:T(8,128)(2,1)} %bitcast.76, bf16[128,1792]{1,0:T(8,128)(2,1)} %bitcast.85, bf16[128,256]{1,0:T(8,128)(2,1)} %bitcast.67, bf16[128,256]{1,0:T(8,128)(2,1)} %copy-done.2, ...), custom_call_target="tpu_custom_call" | custom-call | flops 234881024 | bytes 2752512 | tf_op jit(solution)/shard_map/pallas_call | solution.py:319
  31.6 0.5 collective-permute-start.4
  32.2 1.1 %collective-permute-done.4 = bf16[272,128]{1,0:T(8,128)(2,1)S(1)} collective-permute-done((bf16[272,128]{1,0:T(8,128)(2,1)}, bf16[272,128]{1,0:T(8,128)(2,1)S(1)}, u32[]{:S(2)}, u32[]{:S(2)}) %collective-permute-start.4) | collective-permute-done | bytes 69664 | tf_op jit(solution)/shard_map/ppermute | solution.py:46
  33.3 0.9 %add_convert_fusion = bf16[272,128]{1,0:T(8,128)(2,1)S(1)} fusion(bf16[272,128]{1,0:T(8,128)(2,1)} %get-tuple-element.19, bf16[272,128]{1,0:T(8,128)(2,1)S(1)} %collective-permute-done.4), kind=kLoop, calls=%fused_computation.17 | loop fusion | flops 139264 | bytes 208896 | tf_op jit(solution)/shard_map/convert_element_type | solution.py:45
  34.2 0.1 collective-permute-start.5
  34.3 1.4 %collective-permute-start.7 = (bf16[128,512]{1,0:T(8,128)(2,1)S(1)}, bf16[128,512]{1,0:T(8,128)(2,1)S(1)}, u32[]{:S(2)}, u32[]{:S(2)}) collective-permute-start(bf16[128,512]{1,0:T(8,128)(2,1)S(1)} %get-tuple-element.31), channel_id=1, source_target_pairs={{1,0},{2,1},{3,2},{4,3},{5,4},{6,5},{7,6},{9,8},{10,9},{11,10},{12... | collective-permute-start | bytes 393224 | tf_op jit(solution)/shard_map/ppermute | solution.py:91
  35.8 1.3 %collective-permute-start.8 = (bf16[128,512]{1,0:T(8,128)(2,1)S(1)}, bf16[128,512]{1,0:T(8,128)(2,1)S(1)}, u32[]{:S(2)}, u32[]{:S(2)}) collective-permute-start(bf16[128,512]{1,0:T(8,128)(2,1)S(1)} %get-tuple-element.32), channel_id=1, source_target_pairs={{2,0},{3,1},{4,2},{5,3},{6,4},{7,5},{10,8},{11,9},{12,10},{13,11},... | collective-permute-start | bytes 393224 | tf_op jit(solution)/shard_map/ppermute | solution.py:91
  37.1 1.6 %collective-permute-done.5 = bf16[272,128]{1,0:T(8,128)(2,1)S(1)} collective-permute-done((bf16[272,128]{1,0:T(8,128)(2,1)S(1)}, bf16[272,128]{1,0:T(8,128)(2,1)S(1)}, u32[]{:S(2)}, u32[]{:S(2)}) %collective-permute-start.5) | collective-permute-done | bytes 69664 | tf_op jit(solution)/shard_map/ppermute | solution.py:46
  38.7 3.1 %collective-permute-start.6 = (bf16[272,128]{1,0:T(8,128)(2,1)S(1)}, bf16[272,128]{1,0:T(8,128)(2,1)S(1)}, u32[]{:S(2)}, u32[]{:S(2)}) collective-permute-start(bf16[272,128]{1,0:T(8,128)(2,1)S(1)} %fusion.3), channel_id=1, source_target_pairs={{0,4},{1,5},{2,6},{3,7},{4,0},{5,1},{6,2},{7,3},{8,12},{9,13},{10,... | collective-permute-start | bytes 208904 | tf_op jit(solution)/shard_map/ppermute | solution.py:46
  41.9 2.6 %collective-permute-done.8 = bf16[128,512]{1,0:T(8,128)(2,1)S(1)} collective-permute-done((bf16[128,512]{1,0:T(8,128)(2,1)S(1)}, bf16[128,512]{1,0:T(8,128)(2,1)S(1)}, u32[]{:S(2)}, u32[]{:S(2)}) %collective-permute-start.8) | collective-permute-done | bytes 131104 | tf_op jit(solution)/shard_map/ppermute | solution.py:91
  44.5 3.3 %shard_map.112 = (bf16[128,1792]{1,0:T(8,128)(2,1)}, f32[128,256]{1,0:T(8,128)}, f32[128,256]{1,0:T(8,128)}) custom-call(bf16[128,1792]{1,0:T(8,128)(2,1)} %bitcast.77, bf16[128,256]{1,0:T(8,128)(2,1)} %bitcast.68, bf16[128,256]{1,0:T(8,128)(2,1)} %copy-done.2, bf16[2,128,128]{2,1,0:T(8,128)(2,1)} %add_convert_fusion.1.prior_ref, ...), custom_call_target="tpu_custom_call" | custom-call | flops 352321536 | bytes 2555904 | tf_op jit(solution)/shard_map/pallas_call | solution.py:337
  47.8 0.1 fusion.2
  47.9 0.8 %copy-done.3 = bf16[128,256]{1,0:T(8,128)(2,1)S(1)} copy-done((bf16[128,256]{1,0:T(8,128)(2,1)S(1)}, bf16[128,256]{1,0:T(8,128)(2,1)}, u32[]{:S(2)}) %copy-start.3) | copy-done | bytes 65560
  48.7 0.1 copy-done.9
  48.8 0.1 slice_add_fusion.4
  48.9 0.2 slice_add_fusion.3
  49.1 1.6 %collective-permute-start.9 = (f32[1792]{0:T(1024)S(1)}, f32[1792]{0:T(1024)S(1)}, u32[]{:S(2)}, u32[]{:S(2)}) collective-permute-start(f32[1792]{0:T(1024)S(1)} %fusion.42), channel_id=1, source_target_pairs={{0,8},{8,0},{16,24},{24,16},{1,9},{9,1},{17,25},{25,17},{2,10},{10... | collective-permute-start | bytes 21512 | tf_op jit(solution)/shard_map/ppermute | solution.py:83
  50.7 0.1 slice_add_fusion.2
  50.9 0.1 slice_add_fusion.1
  51.0 1.8 %collective-permute-done.9 = f32[1792]{0:T(1024)S(1)} collective-permute-done((f32[1792]{0:T(1024)S(1)}, f32[1792]{0:T(1024)S(1)}, u32[]{:S(2)}, u32[]{:S(2)}) %collective-permute-start.9) | collective-permute-done | bytes 7200 | tf_op jit(solution)/shard_map/ppermute | solution.py:83
  52.8 2.6 %collective-permute-start.10 = (f32[1792]{0:T(1024)S(1)}, f32[1792]{0:T(1024)S(1)}, u32[]{:S(2)}, u32[]{:S(2)}) collective-permute-start(f32[1792]{0:T(1024)S(1)} %add.74), channel_id=1, source_target_pairs={{0,16},{8,24},{16,0},{24,8},{1,17},{9,25},{17,1},{25,9},{2,18},{10... | collective-permute-start | bytes 21512 | tf_op jit(solution)/shard_map/ppermute | solution.py:83
  55.4 0.7 %fusion.11 = (bf16[1,128,256]{2,1,0:T(8,128)(2,1)}, bf16[1,128,256]{2,1,0:T(8,128)(2,1)}) fusion(f32[128,512]{1,0:T(8,128)S(1)} %convert_add_fusion, f32[16,8,2,128]{3,2,1,0:T(2,128)S(1)} %bitcast.79, f32[128,128]{1,0:T(8,128)S(1)} %slice_add_fusion.1, f32[128,128]{1,0:T(8,128)S(1)} %slice_add_fusion.2, f32[128,128]{1,0:T(8,128)S(1)} %slice_add_fusion.3, ...), kind=kLoop, calls=%fused_computation.35 | loop fusion | flops 229376 | bytes 786432 | tf_op jit(solution)/shard_map/broadcast_in_dim | solution.py:383
  56.1 1.3 %collective-permute-done.10 = f32[1792]{0:T(1024)S(1)} collective-permute-done((f32[1792]{0:T(1024)S(1)}, f32[1792]{0:T(1024)S(1)}, u32[]{:S(2)}, u32[]{:S(2)}) %collective-permute-start.10) | collective-permute-done | bytes 7200 | tf_op jit(solution)/shard_map/ppermute | solution.py:83
  57.4 0.6 %add_multiply_fusion = f32[1792]{0:T(1024)} fusion(f32[1792]{0:T(1024)S(1)} %add.74, f32[1792]{0:T(1024)S(1)} %collective-permute-done.10), kind=kLoop, calls=%fused_computation.67 | loop fusion | flops 3584 | bytes 21504 | tf_op jit(solution)/shard_map/mul | solution.py:354
  (41 shorter events, 0.3 us)
Async XLA Ops:
  0.6 0.9 %copy-start.4 = (bf16[1,128,256]{2,1,0:T(8,128)(2,1)S(1)}, bf16[1,128,256]{2,1,0:T(8,128)(2,1)}, u32[]{:S(2)}) copy-start(bf16[1,128,256]{2,1,0:T(8,128)(2,1)} %param.9) | copy-start | bytes 196612
  1.5 0.8 %copy-start = (bf16[1,128,256]{2,1,0:T(8,128)(2,1)S(1)}, bf16[1,128,256]{2,1,0:T(8,128)(2,1)}, u32[]{:S(2)}) copy-start(bf16[1,128,256]{2,1,0:T(8,128)(2,1)} %param.8) | copy-start | bytes 196612
  2.3 6.4 %copy-start.10 = (s32[1,128,2]{1,2,0:T(2,128)S(1)}, s32[1,128,2]{1,2,0:T(2,128)}, u32[]{:S(2)}) copy-start(s32[1,128,2]{1,2,0:T(2,128)} %param.10) | copy-start | bytes 3076
  2.3 8.3 %collective-permute-start = (bf16[128,640]{1,0:T(8,128)(2,1)S(1)}, bf16[128,640]{1,0:T(8,128)(2,1)S(1)}, u32[]{:S(2)}, u32[]{:S(2)}) collective-permute-start(bf16[128,640]{1,0:T(8,128)(2,1)S(1)} %maximum_maximum_fusion.1), channel_id=1, source_target_pairs={{0,2},{1,3},{2,4},{3,5},{4,6},{5,7},{8,10},{9,11},{10,12},{11,13},... | collective-permute-start | bytes 491528 | tf_op jit(solution)/shard_map/ppermute | solution.py:91
  7.2 4.0 %collective-permute-start.1 = (bf16[128,640]{1,0:T(8,128)(2,1)S(1)}, bf16[128,640]{1,0:T(8,128)(2,1)S(1)}, u32[]{:S(2)}, u32[]{:S(2)}) collective-permute-start(bf16[128,640]{1,0:T(8,128)(2,1)S(1)} %maximum_maximum_fusion.1), channel_id=1, source_target_pairs={{0,1},{1,2},{2,3},{3,4},{4,5},{5,6},{6,7},{8,9},{9,10},{10,11},{11... | collective-permute-start | bytes 491528 | tf_op jit(solution)/shard_map/ppermute | solution.py:91
  9.0 0.6 %copy-start.2 = (bf16[128,256]{1,0:T(8,128)(2,1)}, bf16[128,256]{1,0:T(8,128)(2,1)S(1)}, u32[]{:S(2)}) copy-start(bf16[128,256]{1,0:T(8,128)(2,1)S(1)} %fusion.6.s_ref) | copy-start | bytes 196612
  10.6 9.1 %copy-start.5 = (bf16[128,640]{1,0:T(8,128)(2,1)}, bf16[128,640]{1,0:T(8,128)(2,1)S(1)}, u32[]{:S(2)}) copy-start(bf16[128,640]{1,0:T(8,128)(2,1)S(1)} %collective-permute-done) | copy-start | bytes 491524
  11.9 15.0 %collective-permute-start.2 = (f32[2,128,128]{2,1,0:T(8,128)S(1)}, f32[2,128,128]{2,1,0:T(8,128)S(1)}, u32[]{:S(2)}, u32[]{:S(2)}) collective-permute-start(f32[2,128,128]{2,1,0:T(8,128)S(1)} %maximum_add_fusion.1), channel_id=1, source_target_pairs={{0,3},{1,4},{2,5},{3,6},{4,7},{8,11},{9,12},{10,13},{11,14},{12,15... | collective-permute-start | bytes 393224 | tf_op jit(solution)/shard_map/ppermute | solution.py:91
  16.6 10.3 %collective-permute-start.3 = (f32[2,128,128]{2,1,0:T(8,128)S(1)}, f32[2,128,128]{2,1,0:T(8,128)S(1)}, u32[]{:S(2)}, u32[]{:S(2)}) collective-permute-start(f32[2,128,128]{2,1,0:T(8,128)S(1)} %maximum_add_fusion.1), channel_id=1, source_target_pairs={{0,6},{1,7},{8,14},{9,15},{16,22},{17,23},{24,30},{25,31}} | collective-permute-start | bytes 393224 | tf_op jit(solution)/shard_map/ppermute | solution.py:91
  19.7 0.9 %slice-start = ((bf16[128,640]{1,0:T(8,128)(2,1)}), bf16[128,512]{1,0:T(8,128)(2,1)S(1)}, s32[]{:S(2)}) async-start(bf16[128,640]{1,0:T(8,128)(2,1)} %copy-done.5), calls=%async_computation | async-start | bytes 262144 | tf_op jit(solution)/shard_map/slice | solution.py:297
  27.6 6.7 %copy-start.7 = (bf16[2,128,512]{2,1,0:T(8,128)(2,1)S(1)}, bf16[2,128,512]{2,1,0:T(8,128)(2,1)}, u32[]{:S(2)}) copy-start(bf16[2,128,512]{2,1,0:T(8,128)(2,1)} %get-tuple-element.25) | copy-start | bytes 786436
  31.6 1.7 %collective-permute-start.4 = (bf16[272,128]{1,0:T(8,128)(2,1)}, bf16[272,128]{1,0:T(8,128)(2,1)S(1)}, u32[]{:S(2)}, u32[]{:S(2)}) collective-permute-start(bf16[272,128]{1,0:T(8,128)(2,1)} %get-tuple-element.19), channel_id=1, source_target_pairs={{0,1},{1,0},{2,3},{3,2},{4,5},{5,4},{6,7},{7,6},{8,9},{9,8},{10,11... | collective-permute-start | bytes 208904 | tf_op jit(solution)/shard_map/ppermute | solution.py:46
  34.2 4.5 %collective-permute-start.5 = (bf16[272,128]{1,0:T(8,128)(2,1)S(1)}, bf16[272,128]{1,0:T(8,128)(2,1)S(1)}, u32[]{:S(2)}, u32[]{:S(2)}) collective-permute-start(bf16[272,128]{1,0:T(8,128)(2,1)S(1)} %add_convert_fusion), channel_id=1, source_target_pairs={{0,2},{1,3},{2,0},{3,1},{4,6},{5,7},{6,4},{7,5},{8,10},{9,11},{10,... | collective-permute-start | bytes 208904 | tf_op jit(solution)/shard_map/ppermute | solution.py:46
  34.3 10.2 %copy-start.6 = (f32[128,512]{1,0:T(8,128)S(1)}, f32[128,512]{1,0:T(8,128)}, u32[]{:S(2)}) copy-start(f32[128,512]{1,0:T(8,128)} %get-tuple-element.24) | copy-start | bytes 786436
  34.3 7.5 %collective-permute-start.7 = (bf16[128,512]{1,0:T(8,128)(2,1)S(1)}, bf16[128,512]{1,0:T(8,128)(2,1)S(1)}, u32[]{:S(2)}, u32[]{:S(2)}) collective-permute-start(bf16[128,512]{1,0:T(8,128)(2,1)S(1)} %get-tuple-element.31), channel_id=1, source_target_pairs={{1,0},{2,1},{3,2},{4,3},{5,4},{6,5},{7,6},{9,8},{10,9},{11,10},{12... | collective-permute-start | bytes 393224 | tf_op jit(solution)/shard_map/ppermute | solution.py:91
  35.8 8.7 %collective-permute-start.8 = (bf16[128,512]{1,0:T(8,128)(2,1)S(1)}, bf16[128,512]{1,0:T(8,128)(2,1)S(1)}, u32[]{:S(2)}, u32[]{:S(2)}) collective-permute-start(bf16[128,512]{1,0:T(8,128)(2,1)S(1)} %get-tuple-element.32), channel_id=1, source_target_pairs={{2,0},{3,1},{4,2},{5,3},{6,4},{7,5},{10,8},{11,9},{12,10},{13,11},... | collective-permute-start | bytes 393224 | tf_op jit(solution)/shard_map/ppermute | solution.py:91
  38.7 9.1 %collective-permute-start.6 = (bf16[272,128]{1,0:T(8,128)(2,1)S(1)}, bf16[272,128]{1,0:T(8,128)(2,1)S(1)}, u32[]{:S(2)}, u32[]{:S(2)}) collective-permute-start(bf16[272,128]{1,0:T(8,128)(2,1)S(1)} %fusion.3), channel_id=1, source_target_pairs={{0,4},{1,5},{2,6},{3,7},{4,0},{5,1},{6,2},{7,3},{8,12},{9,13},{10,... | collective-permute-start | bytes 208904 | tf_op jit(solution)/shard_map/ppermute | solution.py:46
  47.8 0.8 %copy-start.3 = (bf16[128,256]{1,0:T(8,128)(2,1)S(1)}, bf16[128,256]{1,0:T(8,128)(2,1)}, u32[]{:S(2)}) copy-start(bf16[128,256]{1,0:T(8,128)(2,1)} %copy-done.2) | copy-start | bytes 196612
  47.8 0.9 %copy-start.9 = (f32[128,256]{1,0:T(8,128)S(1)}, f32[128,256]{1,0:T(8,128)}, u32[]{:S(2)}) copy-start(f32[128,256]{1,0:T(8,128)} %get-tuple-element.23) | copy-start | bytes 393220
  49.0 1.7 %copy-start.1 = (bf16[1,128,256]{2,1,0:T(8,128)(2,1)S(1)}, bf16[1,128,256]{2,1,0:T(8,128)(2,1)}, u32[]{:S(2)}) copy-start(bf16[1,128,256]{2,1,0:T(8,128)(2,1)} %param.8) | copy-start | bytes 196612
  49.1 1.7 %copy-start.8 = (f32[128,256]{1,0:T(8,128)S(1)}, f32[128,256]{1,0:T(8,128)}, u32[]{:S(2)}) copy-start(f32[128,256]{1,0:T(8,128)} %get-tuple-element.26) | copy-start | bytes 393220
  49.1 3.7 %collective-permute-start.9 = (f32[1792]{0:T(1024)S(1)}, f32[1792]{0:T(1024)S(1)}, u32[]{:S(2)}, u32[]{:S(2)}) collective-permute-start(f32[1792]{0:T(1024)S(1)} %fusion.42), channel_id=1, source_target_pairs={{0,8},{8,0},{16,24},{24,16},{1,9},{9,1},{17,25},{25,17},{2,10},{10... | collective-permute-start | bytes 21512 | tf_op jit(solution)/shard_map/ppermute | solution.py:83
  52.8 4.5 %collective-permute-start.10 = (f32[1792]{0:T(1024)S(1)}, f32[1792]{0:T(1024)S(1)}, u32[]{:S(2)}, u32[]{:S(2)}) collective-permute-start(f32[1792]{0:T(1024)S(1)} %add.74), channel_id=1, source_target_pairs={{0,16},{8,24},{16,0},{24,8},{1,17},{9,25},{17,1},{25,9},{2,18},{10... | collective-permute-start | bytes 21512 | tf_op jit(solution)/shard_map/ppermute | solution.py:83

commit v16 on v14

--- a/solution.py
+++ b/solution.py
@@ -60,7 +60,7 @@
         parts = []
         for distance in (stride, 2 * stride):
             if distance < count:
-                parts.append(shifted(running, axis, distance))
+                parts.append(shifted(running.astype(jnp.bfloat16), axis, distance).astype(jnp.float32))
         for got in parts:
             total = total + got
         if 3 * stride < count:

time: 56.1 us -> 56.1 us (level)
  no operation moved by 1% of the time
where the time goes in v16:
time: 56.1 us; the launch traced here: 55.6 us
  starting transfers between devices  24.8 us (44%)
  Pallas kernels  10.5 us (19%)
  waiting for transfers between devices  9.2 us (16%)
  local copies, waits for them, and re-layouts  5.32 us (9%)
  other arithmetic  3.16 us (6%)
  matrix products  1.69 us (3%)
  between operations  0.96 us (2%)
    ppermute x6, starting transfers between devices, shifted(): return lax.ppermute(block, axis, route)  16.8 us
    pallas_call x1, Pallas kernels, per_device(): pl.pallas_call(window_kernel, out_shape=(jax.ShapeDtypeStruct((token_rows...  5.57 us
    pallas_call x1, Pallas kernels, per_device(): pl.pallas_call(linear_kernel, out_shape=(jax.ShapeDtypeStruct((token_rows...  4.97 us
    ppermute x2, starting transfers between devices, all_sum(): part = part + lax.ppermute(part, axes, route)  4.22 us
    ppermute x3, starting transfers between devices, butterfly_scan(): lax.ppermute(mine, axis, [(i, i ^ step) for i in range(count)])  3.72 us
    ppermute x6, waiting for transfers between devices, shifted(): return lax.ppermute(block, axis, route)  3.35 us
    ppermute x2, waiting for transfers between devices, all_sum(): part = part + lax.ppermute(part, axes, route)  3.08 us
    unnamed x23, local copies, waits for them, and re-layouts  2.86 us
  transfers between devices with their start and end apart: 11, of which 6 were waited for; matrix products, arithmetic and copies ran while one was open for 6% of the time, Pallas kernels for 10%

profile of v16, /device:TPU:0, one launch (start us, length us, event | category | flops | bytes accessed | tf_op | source)
XLA Modules:
  0.0 55.6 jit_solution(2102363609554824130)
XLA Ops:
  0.6 0.8 %copy.13 = s32[1,128,2]{2,1,0:T(8,128)S(1)} copy(s32[1,128,2]{1,2,0:T(2,128)} %param.10) | data formatting | bytes 2048 | tf_op args[3]
  1.5 0.1 pad.17.clone
  1.6 0.7 %copy-done = bf16[1,128,256]{2,1,0:T(8,128)(2,1)S(1)} copy-done((bf16[1,128,256]{2,1,0:T(8,128)(2,1)S(1)}, bf16[1,128,256]{2,1,0:T(8,128)(2,1)}, u32[]{:S(2)}) %copy-start) | copy-done | bytes 65560
  2.3 4.9 %collective-permute-start = (bf16[128,640]{1,0:T(8,128)(2,1)S(1)}, bf16[128,640]{1,0:T(8,128)(2,1)S(1)}, u32[]{:S(2)}, u32[]{:S(2)}) collective-permute-start(bf16[128,640]{1,0:T(8,128)(2,1)S(1)} %maximum_maximum_fusion.1), channel_id=1, source_target_pairs={{0,2},{1,3},{2,4},{3,5},{4,6},{5,7},{8,10},{9,11},{10,12},{11,13},... | collective-permute-start | bytes 491528 | tf_op jit(solution)/shard_map/ppermute | solution.py:88
  7.2 1.5 %collective-permute-start.1 = (bf16[128,640]{1,0:T(8,128)(2,1)S(1)}, bf16[128,640]{1,0:T(8,128)(2,1)S(1)}, u32[]{:S(2)}, u32[]{:S(2)}) collective-permute-start(bf16[128,640]{1,0:T(8,128)(2,1)S(1)} %maximum_maximum_fusion.1), channel_id=1, source_target_pairs={{0,1},{1,2},{2,3},{3,4},{4,5},{5,6},{6,7},{8,9},{9,10},{10,11},{11... | collective-permute-start | bytes 491528 | tf_op jit(solution)/shard_map/ppermute | solution.py:88
  8.7 0.1 copy.12
  8.8 0.2 broadcast_in_dim.30
  9.0 0.0 copy-start.2
  9.0 0.2 convolution_bitcast_fusion.2
  9.2 0.4 copy-done.2
  9.7 0.2 convolution_bitcast_fusion.3
  9.9 0.8 %collective-permute-done = bf16[128,640]{1,0:T(8,128)(2,1)S(1)} collective-permute-done((bf16[128,640]{1,0:T(8,128)(2,1)S(1)}, bf16[128,640]{1,0:T(8,128)(2,1)S(1)}, u32[]{:S(2)}, u32[]{:S(2)}) %collective-permute-start) | collective-permute-done | bytes 163872 | tf_op jit(solution)/shard_map/ppermute | solution.py:88
  10.6 0.2 broadcast_in_dim.32
  10.9 0.2 convolution_bitcast_fusion.6
  11.0 0.2 convolution_bitcast_fusion.7
  11.3 0.2 broadcast_in_dim.33
  11.5 0.2 convolution_bitcast_fusion.5
  11.7 0.2 convolution_bitcast_fusion.4
  11.9 4.7 %collective-permute-start.2 = (bf16[2,128,128]{2,1,0:T(8,128)(2,1)S(1)}, bf16[2,128,128]{2,1,0:T(8,128)(2,1)S(1)}, u32[]{:S(2)}, u32[]{:S(2)}) collective-permute-start(bf16[2,128,128]{2,1,0:T(8,128)(2,1)S(1)} %fusion.13), channel_id=1, source_target_pairs={{0,3},{1,4},{2,5},{3,6},{4,7},{8,11},{9,12},{10,13},{11,14},{12,15... | collective-permute-start | bytes 196616 | tf_op jit(solution)/shard_map/ppermute | solution.py:88
  16.6 3.1 %collective-permute-start.3 = (bf16[2,128,128]{2,1,0:T(8,128)(2,1)S(1)}, bf16[2,128,128]{2,1,0:T(8,128)(2,1)S(1)}, u32[]{:S(2)}, u32[]{:S(2)}) collective-permute-start(bf16[2,128,128]{2,1,0:T(8,128)(2,1)S(1)} %fusion.13), channel_id=1, source_target_pairs={{0,6},{1,7},{8,14},{9,15},{16,22},{17,23},{24,30},{25,31}} | collective-permute-start | bytes 196616 | tf_op jit(solution)/shard_map/ppermute | solution.py:88
  19.7 0.0 slice-start
  19.7 0.9 %slice-done = bf16[128,512]{1,0:T(8,128)(2,1)S(1)} async-done(((bf16[128,640]{1,0:T(8,128)(2,1)}), bf16[128,512]{1,0:T(8,128)(2,1)S(1)}, s32[]{:S(2)}) %slice-start) | async-done | bytes 131096 | tf_op jit(solution)/shard_map/slice | solution.py:268
  20.6 0.8 %fusion.37 = (bf16[384,256]{1,0:T(8,128)(2,1)}, bf16[384,256]{1,0:T(8,128)(2,1)}) fusion(bf16[384,512]{1,0:T(8,128)(2,1)S(1)} %maximum_maximum_fusion), kind=kLoop, calls=%fused_computation.70 | loop fusion | bytes 786432 | tf_op jit(solution)/shard_map/slice | solution.py:285
  21.4 5.6 %shard_map.110 = (f32[128,1792]{1,0:T(8,128)}, f32[128,1792]{1,0:T(8,128)}, bf16[2,128,512]{2,1,0:T(8,128)(2,1)}, f32[128,512]{1,0:T(8,128)}) custom-call(s32[2]{0:T(128)} %info_ref.1, bf16[128,1792]{1,0:T(8,128)(2,1)} %bitcast.80, bf16[128,1792]{1,0:T(8,128)(2,1)} %bitcast.82, bf16[384,256]{1,0:T(8,128)(2,1)} %get-tuple-element.24.k_ref, ...), custom_call_target="tpu_custom_call" | custom-call | flops 1056964608 | bytes 3932160 | tf_op jit(solution)/shard_map/pallas_call | solution.py:270
  27.0 0.7 %add_convert_fusion.prior_ref = bf16[2,128,128]{2,1,0:T(8,128)(2,1)} fusion(bf16[2,128,128]{2,1,0:T(8,128)(2,1)S(1)} %collective-permute-done.3, bf16[2,128,128]{2,1,0:T(8,128)(2,1)S(1)} %collective-permute-done.2, f32[1,128,128]{2,1,0:T(8,128)S(1)} %convolution_bitcast_fusion.4, f32[1,128,128]{2,1,0:T(8,128)S(1)} %convolution_bitcast_fusion.5, ...), kind=kLoop, calls=%fused_computation.40 | loop fusion | flops 262144 | bytes 458752 | tf_op jit(solution)/shard_map/convert_element_type | solution.py:266
  27.6 5.0 %shard_map.111 = (bf16[128,1792]{1,0:T(8,128)(2,1)}, bf16[128,1792]{1,0:T(8,128)(2,1)}, bf16[272,128]{1,0:T(8,128)(2,1)}, f32[128,256]{1,0:T(8,128)}, f32[128,256]{1,0:T(8,128)}) custom-call(bf16[128,1792]{1,0:T(8,128)(2,1)} %bitcast.81, bf16[128,1792]{1,0:T(8,128)(2,1)} %bitcast.83, bf16[128,256]{1,0:T(8,128)(2,1)} %bitcast.67, bf16[128,256]{1,0:T(8,128)(2,1)} %copy-done.2, ...), custom_call_target="tpu_custom_call" | custom-call | flops 587202560 | bytes 4456448 | tf_op jit(solution)/shard_map/pallas_call | solution.py:289
  32.6 0.5 collective-permute-start.4
  33.1 1.1 %collective-permute-done.4 = bf16[272,128]{1,0:T(8,128)(2,1)S(1)} collective-permute-done((bf16[272,128]{1,0:T(8,128)(2,1)}, bf16[272,128]{1,0:T(8,128)(2,1)S(1)}, u32[]{:S(2)}, u32[]{:S(2)}) %collective-permute-start.4) | collective-permute-done | bytes 69664 | tf_op jit(solution)/shard_map/ppermute | solution.py:45
  34.2 0.9 %fusion.5 = bf16[272,128]{1,0:T(8,128)(2,1)S(1)} fusion(bf16[272,128]{1,0:T(8,128)(2,1)S(1)} %collective-permute-done.4, bf16[272,128]{1,0:T(8,128)(2,1)} %get-tuple-element.19), kind=kLoop, calls=%fused_computation.22 | loop fusion | flops 139264 | bytes 208896 | tf_op jit(solution)/shard_map/convert_element_type | solution.py:44
  35.2 0.1 collective-permute-start.5
  35.3 1.4 %collective-permute-start.7 = (bf16[128,512]{1,0:T(8,128)(2,1)S(1)}, bf16[128,512]{1,0:T(8,128)(2,1)S(1)}, u32[]{:S(2)}, u32[]{:S(2)}) collective-permute-start(bf16[128,512]{1,0:T(8,128)(2,1)S(1)} %get-tuple-element.27), channel_id=1, source_target_pairs={{1,0},{2,1},{3,2},{4,3},{5,4},{6,5},{7,6},{9,8},{10,9},{11,10},{12... | collective-permute-start | bytes 393224 | tf_op jit(solution)/shard_map/ppermute | solution.py:88
  36.7 1.3 %collective-permute-start.8 = (bf16[128,512]{1,0:T(8,128)(2,1)S(1)}, bf16[128,512]{1,0:T(8,128)(2,1)S(1)}, u32[]{:S(2)}, u32[]{:S(2)}) collective-permute-start(bf16[128,512]{1,0:T(8,128)(2,1)S(1)} %get-tuple-element.28), channel_id=1, source_target_pairs={{2,0},{3,1},{4,2},{5,3},{6,4},{7,5},{10,8},{11,9},{12,10},{13,11},... | collective-permute-start | bytes 393224 | tf_op jit(solution)/shard_map/ppermute | solution.py:88
  38.0 1.6 %collective-permute-done.5 = bf16[272,128]{1,0:T(8,128)(2,1)S(1)} collective-permute-done((bf16[272,128]{1,0:T(8,128)(2,1)S(1)}, bf16[272,128]{1,0:T(8,128)(2,1)S(1)}, u32[]{:S(2)}, u32[]{:S(2)}) %collective-permute-start.5) | collective-permute-done | bytes 69664 | tf_op jit(solution)/shard_map/ppermute | solution.py:45
  39.7 3.1 %collective-permute-start.6 = (bf16[272,128]{1,0:T(8,128)(2,1)S(1)}, bf16[272,128]{1,0:T(8,128)(2,1)S(1)}, u32[]{:S(2)}, u32[]{:S(2)}) collective-permute-start(bf16[272,128]{1,0:T(8,128)(2,1)S(1)} %fusion.6), channel_id=1, source_target_pairs={{0,4},{1,5},{2,6},{3,7},{4,0},{5,1},{6,2},{7,3},{8,12},{9,13},{10,... | collective-permute-start | bytes 208904 | tf_op jit(solution)/shard_map/ppermute | solution.py:45
  42.8 2.6 %collective-permute-done.8 = bf16[128,512]{1,0:T(8,128)(2,1)S(1)} collective-permute-done((bf16[128,512]{1,0:T(8,128)(2,1)S(1)}, bf16[128,512]{1,0:T(8,128)(2,1)S(1)}, u32[]{:S(2)}, u32[]{:S(2)}) %collective-permute-start.8) | collective-permute-done | bytes 131104 | tf_op jit(solution)/shard_map/ppermute | solution.py:88
  45.5 0.1 fusion.4
  45.5 0.8 %copy-done.3 = bf16[128,256]{1,0:T(8,128)(2,1)S(1)} copy-done((bf16[128,256]{1,0:T(8,128)(2,1)S(1)}, bf16[128,256]{1,0:T(8,128)(2,1)}, u32[]{:S(2)}) %copy-start.3) | copy-done | bytes 65560
  46.3 0.1 copy-done.9
  46.4 0.1 convolution_add_fusion.1
  46.5 0.2 convolution_add_fusion
  46.7 1.6 %collective-permute-start.9 = (f32[1792]{0:T(1024)S(1)}, f32[1792]{0:T(1024)S(1)}, u32[]{:S(2)}, u32[]{:S(2)}) collective-permute-start(f32[1792]{0:T(1024)S(1)} %fusion.36), channel_id=1, source_target_pairs={{0,8},{8,0},{16,24},{24,16},{1,9},{9,1},{17,25},{25,17},{2,10},{10... | collective-permute-start | bytes 21512 | tf_op jit(solution)/shard_map/ppermute | solution.py:80
  48.4 0.1 fusion.1
  48.5 0.1 fusion
  48.6 1.8 %collective-permute-done.9 = f32[1792]{0:T(1024)S(1)} collective-permute-done((f32[1792]{0:T(1024)S(1)}, f32[1792]{0:T(1024)S(1)}, u32[]{:S(2)}, u32[]{:S(2)}) %collective-permute-start.9) | collective-permute-done | bytes 7200 | tf_op jit(solution)/shard_map/ppermute | solution.py:80
  50.5 2.6 %collective-permute-start.10 = (f32[1792]{0:T(1024)S(1)}, f32[1792]{0:T(1024)S(1)}, u32[]{:S(2)}, u32[]{:S(2)}) collective-permute-start(f32[1792]{0:T(1024)S(1)} %add.74), channel_id=1, source_target_pairs={{0,16},{8,24},{16,0},{24,8},{1,17},{9,25},{17,1},{25,9},{2,18},{10... | collective-permute-start | bytes 21512 | tf_op jit(solution)/shard_map/ppermute | solution.py:80
  53.0 0.7 %fusion.15 = (bf16[1,128,256]{2,1,0:T(8,128)(2,1)}, bf16[1,128,256]{2,1,0:T(8,128)(2,1)}) fusion(f32[128,512]{1,0:T(8,128)S(1)} %convert_add_fusion, f32[16,8,2,128]{3,2,1,0:T(2,128)S(1)} %bitcast.75, f32[128,128]{1,0:T(8,128)S(1)} %fusion, f32[128,128]{1,0:T(8,128)S(1)} %fusion.1, f32[128,128]{1,0:T(8,128)S(1)} %convolution_add_fusion, ...), kind=kLoop, calls=%fused_computation.42 | loop fusion | flops 229376 | bytes 786432 | tf_op jit(solution)/shard_map/broadcast_in_dim | solution.py:339
  53.7 1.3 %collective-permute-done.10 = f32[1792]{0:T(1024)S(1)} collective-permute-done((f32[1792]{0:T(1024)S(1)}, f32[1792]{0:T(1024)S(1)}, u32[]{:S(2)}, u32[]{:S(2)}) %collective-permute-start.10) | collective-permute-done | bytes 7200 | tf_op jit(solution)/shard_map/ppermute | solution.py:80
  55.0 0.6 %add_multiply_fusion = f32[1792]{0:T(1024)} fusion(f32[1792]{0:T(1024)S(1)} %add.74, f32[1792]{0:T(1024)S(1)} %collective-permute-done.10), kind=kLoop, calls=%fused_computation.68 | loop fusion | flops 3584 | bytes 21504 | tf_op jit(solution)/shard_map/mul | solution.py:310
  (40 shorter events, 0.3 us)
Async XLA Ops:
  0.6 0.9 %copy-start.4 = (bf16[1,128,256]{2,1,0:T(8,128)(2,1)S(1)}, bf16[1,128,256]{2,1,0:T(8,128)(2,1)}, u32[]{:S(2)}) copy-start(bf16[1,128,256]{2,1,0:T(8,128)(2,1)} %param.9) | copy-start | bytes 196612
  1.5 0.8 %copy-start = (bf16[1,128,256]{2,1,0:T(8,128)(2,1)S(1)}, bf16[1,128,256]{2,1,0:T(8,128)(2,1)}, u32[]{:S(2)}) copy-start(bf16[1,128,256]{2,1,0:T(8,128)(2,1)} %param.8) | copy-start | bytes 196612
  2.3 6.4 %copy-start.10 = (s32[1,128,2]{1,2,0:T(2,128)S(1)}, s32[1,128,2]{1,2,0:T(2,128)}, u32[]{:S(2)}) copy-start(s32[1,128,2]{1,2,0:T(2,128)} %param.10) | copy-start | bytes 3076
  2.3 8.3 %collective-permute-start = (bf16[128,640]{1,0:T(8,128)(2,1)S(1)}, bf16[128,640]{1,0:T(8,128)(2,1)S(1)}, u32[]{:S(2)}, u32[]{:S(2)}) collective-permute-start(bf16[128,640]{1,0:T(8,128)(2,1)S(1)} %maximum_maximum_fusion.1), channel_id=1, source_target_pairs={{0,2},{1,3},{2,4},{3,5},{4,6},{5,7},{8,10},{9,11},{10,12},{11,13},... | collective-permute-start | bytes 491528 | tf_op jit(solution)/shard_map/ppermute | solution.py:88
  7.2 4.0 %collective-permute-start.1 = (bf16[128,640]{1,0:T(8,128)(2,1)S(1)}, bf16[128,640]{1,0:T(8,128)(2,1)S(1)}, u32[]{:S(2)}, u32[]{:S(2)}) collective-permute-start(bf16[128,640]{1,0:T(8,128)(2,1)S(1)} %maximum_maximum_fusion.1), channel_id=1, source_target_pairs={{0,1},{1,2},{2,3},{3,4},{4,5},{5,6},{6,7},{8,9},{9,10},{10,11},{11... | collective-permute-start | bytes 491528 | tf_op jit(solution)/shard_map/ppermute | solution.py:88
  9.0 0.6 %copy-start.2 = (bf16[128,256]{1,0:T(8,128)(2,1)}, bf16[128,256]{1,0:T(8,128)(2,1)S(1)}, u32[]{:S(2)}) copy-start(bf16[128,256]{1,0:T(8,128)(2,1)S(1)} %fusion.9.s_ref) | copy-start | bytes 196612
  10.6 9.1 %copy-start.5 = (bf16[128,640]{1,0:T(8,128)(2,1)}, bf16[128,640]{1,0:T(8,128)(2,1)S(1)}, u32[]{:S(2)}) copy-start(bf16[128,640]{1,0:T(8,128)(2,1)S(1)} %collective-permute-done) | copy-start | bytes 491524
  11.9 15.1 %collective-permute-start.2 = (bf16[2,128,128]{2,1,0:T(8,128)(2,1)S(1)}, bf16[2,128,128]{2,1,0:T(8,128)(2,1)S(1)}, u32[]{:S(2)}, u32[]{:S(2)}) collective-permute-start(bf16[2,128,128]{2,1,0:T(8,128)(2,1)S(1)} %fusion.13), channel_id=1, source_target_pairs={{0,3},{1,4},{2,5},{3,6},{4,7},{8,11},{9,12},{10,13},{11,14},{12,15... | collective-permute-start | bytes 196616 | tf_op jit(solution)/shard_map/ppermute | solution.py:88
  16.6 10.4 %collective-permute-start.3 = (bf16[2,128,128]{2,1,0:T(8,128)(2,1)S(1)}, bf16[2,128,128]{2,1,0:T(8,128)(2,1)S(1)}, u32[]{:S(2)}, u32[]{:S(2)}) collective-permute-start(bf16[2,128,128]{2,1,0:T(8,128)(2,1)S(1)} %fusion.13), channel_id=1, source_target_pairs={{0,6},{1,7},{8,14},{9,15},{16,22},{17,23},{24,30},{25,31}} | collective-permute-start | bytes 196616 | tf_op jit(solution)/shard_map/ppermute | solution.py:88
  19.7 0.9 %slice-start = ((bf16[128,640]{1,0:T(8,128)(2,1)}), bf16[128,512]{1,0:T(8,128)(2,1)S(1)}, s32[]{:S(2)}) async-start(bf16[128,640]{1,0:T(8,128)(2,1)} %copy-done.5), calls=%async_computation | async-start | bytes 262144 | tf_op jit(solution)/shard_map/slice | solution.py:268
  27.6 7.6 %copy-start.7 = (bf16[2,128,512]{2,1,0:T(8,128)(2,1)S(1)}, bf16[2,128,512]{2,1,0:T(8,128)(2,1)}, u32[]{:S(2)}) copy-start(bf16[2,128,512]{2,1,0:T(8,128)(2,1)} %get-tuple-element.21) | copy-start | bytes 786436
  32.6 1.6 %collective-permute-start.4 = (bf16[272,128]{1,0:T(8,128)(2,1)}, bf16[272,128]{1,0:T(8,128)(2,1)S(1)}, u32[]{:S(2)}, u32[]{:S(2)}) collective-permute-start(bf16[272,128]{1,0:T(8,128)(2,1)} %get-tuple-element.19), channel_id=1, source_target_pairs={{0,1},{1,0},{2,3},{3,2},{4,5},{5,4},{6,7},{7,6},{8,9},{9,8},{10,11... | collective-permute-start | bytes 208904 | tf_op jit(solution)/shard_map/ppermute | solution.py:45
  35.2 4.5 %collective-permute-start.5 = (bf16[272,128]{1,0:T(8,128)(2,1)S(1)}, bf16[272,128]{1,0:T(8,128)(2,1)S(1)}, u32[]{:S(2)}, u32[]{:S(2)}) collective-permute-start(bf16[272,128]{1,0:T(8,128)(2,1)S(1)} %fusion.5), channel_id=1, source_target_pairs={{0,2},{1,3},{2,0},{3,1},{4,6},{5,7},{6,4},{7,5},{8,10},{9,11},{10,... | collective-permute-start | bytes 208904 | tf_op jit(solution)/shard_map/ppermute | solution.py:45
  35.2 10.2 %copy-start.6 = (f32[128,512]{1,0:T(8,128)S(1)}, f32[128,512]{1,0:T(8,128)}, u32[]{:S(2)}) copy-start(f32[128,512]{1,0:T(8,128)} %get-tuple-element.20) | copy-start | bytes 786436
  35.3 7.5 %collective-permute-start.7 = (bf16[128,512]{1,0:T(8,128)(2,1)S(1)}, bf16[128,512]{1,0:T(8,128)(2,1)S(1)}, u32[]{:S(2)}, u32[]{:S(2)}) collective-permute-start(bf16[128,512]{1,0:T(8,128)(2,1)S(1)} %get-tuple-element.27), channel_id=1, source_target_pairs={{1,0},{2,1},{3,2},{4,3},{5,4},{6,5},{7,6},{9,8},{10,9},{11,10},{12... | collective-permute-start | bytes 393224 | tf_op jit(solution)/shard_map/ppermute | solution.py:88
  36.7 8.7 %collective-permute-start.8 = (bf16[128,512]{1,0:T(8,128)(2,1)S(1)}, bf16[128,512]{1,0:T(8,128)(2,1)S(1)}, u32[]{:S(2)}, u32[]{:S(2)}) collective-permute-start(bf16[128,512]{1,0:T(8,128)(2,1)S(1)} %get-tuple-element.28), channel_id=1, source_target_pairs={{2,0},{3,1},{4,2},{5,3},{6,4},{7,5},{10,8},{11,9},{12,10},{13,11},... | collective-permute-start | bytes 393224 | tf_op jit(solution)/shard_map/ppermute | solution.py:88
  39.7 5.8 %collective-permute-start.6 = (bf16[272,128]{1,0:T(8,128)(2,1)S(1)}, bf16[272,128]{1,0:T(8,128)(2,1)S(1)}, u32[]{:S(2)}, u32[]{:S(2)}) collective-permute-start(bf16[272,128]{1,0:T(8,128)(2,1)S(1)} %fusion.6), channel_id=1, source_target_pairs={{0,4},{1,5},{2,6},{3,7},{4,0},{5,1},{6,2},{7,3},{8,12},{9,13},{10,... | collective-permute-start | bytes 208904 | tf_op jit(solution)/shard_map/ppermute | solution.py:45
  45.4 0.8 %copy-start.3 = (bf16[128,256]{1,0:T(8,128)(2,1)S(1)}, bf16[128,256]{1,0:T(8,128)(2,1)}, u32[]{:S(2)}) copy-start(bf16[128,256]{1,0:T(8,128)(2,1)} %copy-done.2) | copy-start | bytes 196612
  45.5 0.9 %copy-start.9 = (f32[128,256]{1,0:T(8,128)S(1)}, f32[128,256]{1,0:T(8,128)}, u32[]{:S(2)}) copy-start(f32[128,256]{1,0:T(8,128)} %get-tuple-element.18) | copy-start | bytes 393220
  46.7 1.7 %copy-start.1 = (bf16[1,128,256]{2,1,0:T(8,128)(2,1)S(1)}, bf16[1,128,256]{2,1,0:T(8,128)(2,1)}, u32[]{:S(2)}) copy-start(bf16[1,128,256]{2,1,0:T(8,128)(2,1)} %param.8) | copy-start | bytes 196612
  46.7 1.7 %copy-start.8 = (f32[128,256]{1,0:T(8,128)S(1)}, f32[128,256]{1,0:T(8,128)}, u32[]{:S(2)}) copy-start(f32[128,256]{1,0:T(8,128)} %get-tuple-element.22) | copy-start | bytes 393220
  46.7 3.7 %collective-permute-start.9 = (f32[1792]{0:T(1024)S(1)}, f32[1792]{0:T(1024)S(1)}, u32[]{:S(2)}, u32[]{:S(2)}) collective-permute-start(f32[1792]{0:T(1024)S(1)} %fusion.36), channel_id=1, source_target_pairs={{0,8},{8,0},{16,24},{24,16},{1,9},{9,1},{17,25},{25,17},{2,10},{10... | collective-permute-start | bytes 21512 | tf_op jit(solution)/shard_map/ppermute | solution.py:80
  50.5 4.5 %collective-permute-start.10 = (f32[1792]{0:T(1024)S(1)}, f32[1792]{0:T(1024)S(1)}, u32[]{:S(2)}, u32[]{:S(2)}) collective-permute-start(f32[1792]{0:T(1024)S(1)} %add.74), channel_id=1, source_target_pairs={{0,16},{8,24},{16,0},{24,8},{1,17},{9,25},{17,1},{25,9},{2,18},{10... | collective-permute-start | bytes 21512 | tf_op jit(solution)/shard_map/ppermute | solution.py:80

commit v17 on v14

--- a/solution.py
+++ b/solution.py
@@ -304,6 +304,10 @@
         ),
     )(q, c, k, spiked, prior_half, gain, wout, wdq)
     total_tokens = queries.shape[0] * lax.axis_size("dp") * token_rows * lax.axis_size("ctx")
+    received = own_grad
+    for distance in range(1, reach + 1):
+        received = received + shifted(halo_out[distance - 1], "ctx", -distance).astype(jnp.float32)
+    riding, received = lax.optimization_barrier((riding, received))
     later_rows, total_rows = butterfly_scan(riding, "ctx", True)
     later_half = later_rows[:state_rows].reshape(KEY_VALUE_HEADS, HEAD_SIZE, HEAD_SIZE).astype(jnp.bfloat16)
     gain_ctx = total_rows[state_rows : state_rows + gain_rows].reshape(width)
@@ -323,9 +327,6 @@
         )
     linear_key_gradient = jnp.concatenate(ldk_parts, axis=1)
     linear_value_gradient = jnp.concatenate(dsp_parts, axis=1) * counts
-    received = own_grad
-    for distance in range(1, reach + 1):
-        received = received + shifted(halo_out[distance - 1], "ctx", -distance).astype(jnp.float32)
     keys_gradient = (
         linear_key_gradient + received[:, :key_value_width]
     ).astype(jnp.bfloat16)

time: 56.1 us -> 59.7 us (1.064)
  waiting for transfers between devices: 9.18 us -> 11.5 us
  starting transfers between devices: 24.8 us -> 26.2 us
  local copies, waits for them, and re-layouts: 5.32 us -> 6.25 us
  other arithmetic: 3.16 us -> 2.28 us
    ppermute x3, waiting for transfers between devices: 2.77 us -> 6.04 us  [butterfly_scan(): lax.ppermute(mine, axis, [(i, i ^ step) for i in range(count)])]
    ppermute x3, starting transfers between devices: 3.74 us -> 5.27 us  [butterfly_scan(): lax.ppermute(mine, axis, [(i, i ^ step) for i in range(count)])]
    ppermute x6, waiting for transfers between devices: 3.35 us -> 2.32 us  [shifted(): return lax.ppermute(block, axis, route)]
    squeeze x1, local copies, waits for them, and re-layouts: 0.02 us -> 0.98 us  [per_device(): halo_out[distance - 1]]
    convert_element_type x2, other arithmetic: 0.93 us -> 0.04 us  [butterfly_scan(): mine = group.astype(jnp.bfloat16)]
  transfers between devices with their start and end apart: 11 -> 11, of which waited for: 6 -> 7; matrix products, arithmetic and copies ran while one was open for 6% -> 8% of each run, Pallas kernels for 10% -> 18%
where the time goes in v17:
time: 59.7 us; the launch traced here: 59.3 us
  starting transfers between devices  26.2 us (44%)
  waiting for transfers between devices  11.5 us (19%)
  Pallas kernels  10.5 us (18%)
  local copies, waits for them, and re-layouts  6.25 us (10%)
  other arithmetic  2.28 us (4%)
  matrix products  1.69 us (3%)
  between operations  0.93 us (2%)
    ppermute x6, starting transfers between devices, shifted(): return lax.ppermute(block, axis, route)  16.7 us
    ppermute x3, waiting for transfers between devices, butterfly_scan(): lax.ppermute(mine, axis, [(i, i ^ step) for i in range(count)])  6.04 us
    pallas_call x1, Pallas kernels, per_device(): pl.pallas_call(window_kernel, out_shape=(jax.ShapeDtypeStruct((token_rows...  5.53 us
    ppermute x3, starting transfers between devices, butterfly_scan(): lax.ppermute(mine, axis, [(i, i ^ step) for i in range(count)])  5.27 us
    pallas_call x1, Pallas kernels, per_device(): pl.pallas_call(linear_kernel, out_shape=(jax.ShapeDtypeStruct((token_rows...  4.98 us
    ppermute x2, starting transfers between devices, all_sum(): part = part + lax.ppermute(part, axes, route)  4.21 us
    ppermute x2, waiting for transfers between devices, all_sum(): part = part + lax.ppermute(part, axes, route)  3.09 us
    unnamed x23, local copies, waits for them, and re-layouts  2.84 us
  transfers between devices with their start and end apart: 11, of which 7 were waited for; matrix products, arithmetic and copies ran while one was open for 8% of the time, Pallas kernels for 18%

profile of v17, /device:TPU:0, one launch (start us, length us, event | category | flops | bytes accessed | tf_op | source)
XLA Modules:
  0.0 59.3 jit_solution(9574586663422069198)
XLA Ops:
  0.6 0.8 %copy.13 = s32[1,128,2]{2,1,0:T(8,128)S(1)} copy(s32[1,128,2]{1,2,0:T(2,128)} %param.10) | data formatting | bytes 2048 | tf_op args[3]
  1.5 0.1 pad.17.clone
  1.6 0.7 %copy-done = bf16[1,128,256]{2,1,0:T(8,128)(2,1)S(1)} copy-done((bf16[1,128,256]{2,1,0:T(8,128)(2,1)S(1)}, bf16[1,128,256]{2,1,0:T(8,128)(2,1)}, u32[]{:S(2)}) %copy-start) | copy-done | bytes 65560
  2.3 4.9 %collective-permute-start = (bf16[128,640]{1,0:T(8,128)(2,1)S(1)}, bf16[128,640]{1,0:T(8,128)(2,1)S(1)}, u32[]{:S(2)}, u32[]{:S(2)}) collective-permute-start(bf16[128,640]{1,0:T(8,128)(2,1)S(1)} %maximum_maximum_fusion.1), channel_id=1, source_target_pairs={{0,2},{1,3},{2,4},{3,5},{4,6},{5,7},{8,10},{9,11},{10,12},{11,13},... | collective-permute-start | bytes 491528 | tf_op jit(solution)/shard_map/ppermute | solution.py:88
  7.2 1.5 %collective-permute-start.1 = (bf16[128,640]{1,0:T(8,128)(2,1)S(1)}, bf16[128,640]{1,0:T(8,128)(2,1)S(1)}, u32[]{:S(2)}, u32[]{:S(2)}) collective-permute-start(bf16[128,640]{1,0:T(8,128)(2,1)S(1)} %maximum_maximum_fusion.1), channel_id=1, source_target_pairs={{0,1},{1,2},{2,3},{3,4},{4,5},{5,6},{6,7},{8,9},{9,10},{10,11},{11... | collective-permute-start | bytes 491528 | tf_op jit(solution)/shard_map/ppermute | solution.py:88
  8.7 0.1 copy.12
  8.8 0.2 broadcast_in_dim.30
  9.0 0.0 copy-start.2
  9.0 0.2 convolution_bitcast_fusion.2
  9.2 0.4 copy-done.2
  9.7 0.2 convolution_bitcast_fusion.3
  9.9 0.8 %collective-permute-done = bf16[128,640]{1,0:T(8,128)(2,1)S(1)} collective-permute-done((bf16[128,640]{1,0:T(8,128)(2,1)S(1)}, bf16[128,640]{1,0:T(8,128)(2,1)S(1)}, u32[]{:S(2)}, u32[]{:S(2)}) %collective-permute-start) | collective-permute-done | bytes 163872 | tf_op jit(solution)/shard_map/ppermute | solution.py:88
  10.6 0.2 broadcast_in_dim.32
  10.9 0.2 convolution_bitcast_fusion.6
  11.0 0.2 convolution_bitcast_fusion.7
  11.3 0.2 broadcast_in_dim.33
  11.5 0.2 convolution_bitcast_fusion.5
  11.7 0.2 convolution_bitcast_fusion.4
  11.9 4.7 %collective-permute-start.2 = (f32[2,128,128]{2,1,0:T(8,128)S(1)}, f32[2,128,128]{2,1,0:T(8,128)S(1)}, u32[]{:S(2)}, u32[]{:S(2)}) collective-permute-start(f32[2,128,128]{2,1,0:T(8,128)S(1)} %maximum_add_fusion.1), channel_id=1, source_target_pairs={{0,3},{1,4},{2,5},{3,6},{4,7},{8,11},{9,12},{10,13},{11,14},{12,15... | collective-permute-start | bytes 393224 | tf_op jit(solution)/shard_map/ppermute | solution.py:88
  16.6 3.1 %collective-permute-start.3 = (f32[2,128,128]{2,1,0:T(8,128)S(1)}, f32[2,128,128]{2,1,0:T(8,128)S(1)}, u32[]{:S(2)}, u32[]{:S(2)}) collective-permute-start(f32[2,128,128]{2,1,0:T(8,128)S(1)} %maximum_add_fusion.1), channel_id=1, source_target_pairs={{0,6},{1,7},{8,14},{9,15},{16,22},{17,23},{24,30},{25,31}} | collective-permute-start | bytes 393224 | tf_op jit(solution)/shard_map/ppermute | solution.py:88
  19.7 0.0 slice-start
  19.7 0.9 %slice-done = bf16[128,512]{1,0:T(8,128)(2,1)S(1)} async-done(((bf16[128,640]{1,0:T(8,128)(2,1)}), bf16[128,512]{1,0:T(8,128)(2,1)S(1)}, s32[]{:S(2)}) %slice-start) | async-done | bytes 131096 | tf_op jit(solution)/shard_map/slice | solution.py:268
  20.6 0.8 %fusion.44 = (bf16[384,256]{1,0:T(8,128)(2,1)}, bf16[384,256]{1,0:T(8,128)(2,1)}) fusion(bf16[384,512]{1,0:T(8,128)(2,1)S(1)} %maximum_maximum_fusion), kind=kLoop, calls=%fused_computation.71 | loop fusion | bytes 786432 | tf_op jit(solution)/shard_map/slice | solution.py:285
  21.4 5.5 %shard_map.110 = (f32[128,1792]{1,0:T(8,128)}, f32[128,1792]{1,0:T(8,128)}, bf16[2,128,512]{2,1,0:T(8,128)(2,1)}, f32[128,512]{1,0:T(8,128)}) custom-call(s32[2]{0:T(128)} %info_ref.1, bf16[128,1792]{1,0:T(8,128)(2,1)} %bitcast.80, bf16[128,1792]{1,0:T(8,128)(2,1)} %bitcast.82, bf16[384,256]{1,0:T(8,128)(2,1)} %get-tuple-element.28.k_ref, ...), custom_call_target="tpu_custom_call" | custom-call | flops 1056964608 | bytes 3932160 | tf_op jit(solution)/shard_map/pallas_call | solution.py:270
  26.9 1.0 %slice_bitcast_fusion.1 = (bf16[128,512]{1,0:T(8,128)(2,1)S(1)}, bf16[128,512]{1,0:T(8,128)(2,1)S(1)}) fusion(bf16[2,128,512]{2,1,0:T(8,128)(2,1)} %get-tuple-element.23), kind=kLoop, calls=%fused_computation.34 | loop fusion | bytes 524288 | tf_op jit(solution)/shard_map/squeeze | solution.py:309
  27.9 1.3 %collective-permute-start.4 = (bf16[128,512]{1,0:T(8,128)(2,1)S(1)}, bf16[128,512]{1,0:T(8,128)(2,1)S(1)}, u32[]{:S(2)}, u32[]{:S(2)}) collective-permute-start(bf16[128,512]{1,0:T(8,128)(2,1)S(1)} %get-tuple-element.31), channel_id=1, source_target_pairs={{1,0},{2,1},{3,2},{4,3},{5,4},{6,5},{7,6},{9,8},{10,9},{11,10},{12... | collective-permute-start | bytes 393224 | tf_op jit(solution)/shard_map/ppermute | solution.py:88
  29.2 1.3 %collective-permute-start.5 = (bf16[128,512]{1,0:T(8,128)(2,1)S(1)}, bf16[128,512]{1,0:T(8,128)(2,1)S(1)}, u32[]{:S(2)}, u32[]{:S(2)}) collective-permute-start(bf16[128,512]{1,0:T(8,128)(2,1)S(1)} %get-tuple-element.32), channel_id=1, source_target_pairs={{2,0},{3,1},{4,2},{5,3},{6,4},{7,5},{10,8},{11,9},{12,10},{13,11},... | collective-permute-start | bytes 393224 | tf_op jit(solution)/shard_map/ppermute | solution.py:88
  30.5 0.7 %add_convert_fusion.prior_ref = bf16[2,128,128]{2,1,0:T(8,128)(2,1)} fusion(f32[2,128,128]{2,1,0:T(8,128)S(1)} %collective-permute-done.3, f32[2,128,128]{2,1,0:T(8,128)S(1)} %collective-permute-done.2, f32[1,128,128]{2,1,0:T(8,128)S(1)} %convolution_bitcast_fusion.4, f32[1,128,128]{2,1,0:T(8,128)S(1)} %convolution_bitcast_fusion.5, ...), kind=kLoop, calls=%fused_computation.35 | loop fusion | flops 196608 | bytes 589824 | tf_op jit(solution)/shard_map/convert_element_type | solution.py:266
  31.2 5.0 %shard_map.111 = (bf16[128,1792]{1,0:T(8,128)(2,1)}, bf16[128,1792]{1,0:T(8,128)(2,1)}, bf16[272,128]{1,0:T(8,128)(2,1)}, f32[128,256]{1,0:T(8,128)}, f32[128,256]{1,0:T(8,128)}) custom-call(bf16[128,1792]{1,0:T(8,128)(2,1)} %bitcast.81, bf16[128,1792]{1,0:T(8,128)(2,1)} %bitcast.83, bf16[128,256]{1,0:T(8,128)(2,1)} %bitcast.67, bf16[128,256]{1,0:T(8,128)(2,1)} %copy-done.2, ...), custom_call_target="tpu_custom_call" | custom-call | flops 587202560 | bytes 4456448 | tf_op jit(solution)/shard_map/pallas_call | solution.py:289
  36.2 1.5 %collective-permute-done.5 = bf16[128,512]{1,0:T(8,128)(2,1)S(1)} collective-permute-done((bf16[128,512]{1,0:T(8,128)(2,1)S(1)}, bf16[128,512]{1,0:T(8,128)(2,1)S(1)}, u32[]{:S(2)}, u32[]{:S(2)}) %collective-permute-start.5) | collective-permute-done | bytes 131104 | tf_op jit(solution)/shard_map/ppermute | solution.py:88
  37.8 0.8 %copy-done.9 = bf16[272,128]{1,0:T(8,128)(2,1)S(1)} copy-done((bf16[272,128]{1,0:T(8,128)(2,1)S(1)}, bf16[272,128]{1,0:T(8,128)(2,1)}, u32[]{:S(2)}) %copy-start.9) | copy-done | bytes 69656
  38.6 0.0 collective-permute-start.6
  38.6 1.3 %collective-permute-done.6 = bf16[272,128]{1,0:T(8,128)(2,1)S(1)} collective-permute-done((bf16[272,128]{1,0:T(8,128)(2,1)S(1)}, bf16[272,128]{1,0:T(8,128)(2,1)S(1)}, u32[]{:S(2)}, u32[]{:S(2)}) %collective-permute-start.6) | collective-permute-done | bytes 69664 | tf_op jit(solution)/shard_map/ppermute | solution.py:45
  39.9 2.1 %collective-permute-start.7 = (bf16[272,128]{1,0:T(8,128)(2,1)S(1)}, bf16[272,128]{1,0:T(8,128)(2,1)S(1)}, u32[]{:S(2)}, u32[]{:S(2)}) collective-permute-start(bf16[272,128]{1,0:T(8,128)(2,1)S(1)} %fusion.3), channel_id=1, source_target_pairs={{0,2},{1,3},{2,0},{3,1},{4,6},{5,7},{6,4},{7,5},{8,10},{9,11},{10,... | collective-permute-start | bytes 208904 | tf_op jit(solution)/shard_map/ppermute | solution.py:45
  42.0 2.5 %collective-permute-done.7 = bf16[272,128]{1,0:T(8,128)(2,1)S(1)} collective-permute-done((bf16[272,128]{1,0:T(8,128)(2,1)S(1)}, bf16[272,128]{1,0:T(8,128)(2,1)S(1)}, u32[]{:S(2)}, u32[]{:S(2)}) %collective-permute-start.7) | collective-permute-done | bytes 69664 | tf_op jit(solution)/shard_map/ppermute | solution.py:45
  44.5 3.2 %collective-permute-start.8 = (bf16[272,128]{1,0:T(8,128)(2,1)S(1)}, bf16[272,128]{1,0:T(8,128)(2,1)S(1)}, u32[]{:S(2)}, u32[]{:S(2)}) collective-permute-start(bf16[272,128]{1,0:T(8,128)(2,1)S(1)} %fusion.4), channel_id=1, source_target_pairs={{0,4},{1,5},{2,6},{3,7},{4,0},{5,1},{6,2},{7,3},{8,12},{9,13},{10,... | collective-permute-start | bytes 208904 | tf_op jit(solution)/shard_map/ppermute | solution.py:45
  47.7 2.3 %collective-permute-done.8 = bf16[272,128]{1,0:T(8,128)(2,1)S(1)} collective-permute-done((bf16[272,128]{1,0:T(8,128)(2,1)S(1)}, bf16[272,128]{1,0:T(8,128)(2,1)S(1)}, u32[]{:S(2)}, u32[]{:S(2)}) %collective-permute-start.8) | collective-permute-done | bytes 69664 | tf_op jit(solution)/shard_map/ppermute | solution.py:45
  50.0 0.1 slice_add_fusion.3
  50.2 0.2 slice_add_fusion.2
  50.4 0.0 copy-start.7
  50.4 1.6 %collective-permute-start.9 = (f32[1792]{0:T(1024)S(1)}, f32[1792]{0:T(1024)S(1)}, u32[]{:S(2)}, u32[]{:S(2)}) collective-permute-start(f32[1792]{0:T(1024)S(1)} %fusion.43), channel_id=1, source_target_pairs={{0,8},{8,0},{16,24},{24,16},{1,9},{9,1},{17,25},{25,17},{2,10},{10... | collective-permute-start | bytes 21512 | tf_op jit(solution)/shard_map/ppermute | solution.py:80
  52.0 0.1 slice_add_fusion.1
  52.2 0.1 slice_add_fusion
  52.3 1.8 %collective-permute-done.9 = f32[1792]{0:T(1024)S(1)} collective-permute-done((f32[1792]{0:T(1024)S(1)}, f32[1792]{0:T(1024)S(1)}, u32[]{:S(2)}, u32[]{:S(2)}) %collective-permute-start.9) | collective-permute-done | bytes 7200 | tf_op jit(solution)/shard_map/ppermute | solution.py:80
  54.1 2.6 %collective-permute-start.10 = (f32[1792]{0:T(1024)S(1)}, f32[1792]{0:T(1024)S(1)}, u32[]{:S(2)}, u32[]{:S(2)}) collective-permute-start(f32[1792]{0:T(1024)S(1)} %add.74), channel_id=1, source_target_pairs={{0,16},{8,24},{16,0},{24,8},{1,17},{9,25},{17,1},{25,9},{2,18},{10... | collective-permute-start | bytes 21512 | tf_op jit(solution)/shard_map/ppermute | solution.py:80
  56.7 0.7 %fusion.12 = (bf16[1,128,256]{2,1,0:T(8,128)(2,1)}, bf16[1,128,256]{2,1,0:T(8,128)(2,1)}) fusion(f32[128,512]{1,0:T(8,128)S(1)} %convert_add_fusion, f32[16,8,2,128]{3,2,1,0:T(2,128)S(1)} %bitcast.75, f32[128,128]{1,0:T(8,128)S(1)} %slice_add_fusion, f32[128,128]{1,0:T(8,128)S(1)} %slice_add_fusion.1, f32[128,128]{1,0:T(8,128)S(1)} %slice_add_fusion.2, ...), kind=kLoop, calls=%fused_computation.37 | loop fusion | flops 229376 | bytes 786432 | tf_op jit(solution)/shard_map/broadcast_in_dim | solution.py:340
  57.4 1.3 %collective-permute-done.10 = f32[1792]{0:T(1024)S(1)} collective-permute-done((f32[1792]{0:T(1024)S(1)}, f32[1792]{0:T(1024)S(1)}, u32[]{:S(2)}, u32[]{:S(2)}) %collective-permute-start.10) | collective-permute-done | bytes 7200 | tf_op jit(solution)/shard_map/ppermute | solution.py:80
  58.7 0.6 %add_multiply_fusion = f32[1792]{0:T(1024)} fusion(f32[1792]{0:T(1024)S(1)} %add.74, f32[1792]{0:T(1024)S(1)} %collective-permute-done.10), kind=kLoop, calls=%fused_computation.69 | loop fusion | flops 3584 | bytes 21504 | tf_op jit(solution)/shard_map/mul | solution.py:314
  (40 shorter events, 0.4 us)
Async XLA Ops:
  0.6 0.9 %copy-start.4 = (bf16[1,128,256]{2,1,0:T(8,128)(2,1)S(1)}, bf16[1,128,256]{2,1,0:T(8,128)(2,1)}, u32[]{:S(2)}) copy-start(bf16[1,128,256]{2,1,0:T(8,128)(2,1)} %param.9) | copy-start | bytes 196612
  1.5 0.8 %copy-start = (bf16[1,128,256]{2,1,0:T(8,128)(2,1)S(1)}, bf16[1,128,256]{2,1,0:T(8,128)(2,1)}, u32[]{:S(2)}) copy-start(bf16[1,128,256]{2,1,0:T(8,128)(2,1)} %param.8) | copy-start | bytes 196612
  2.3 6.4 %copy-start.10 = (s32[1,128,2]{1,2,0:T(2,128)S(1)}, s32[1,128,2]{1,2,0:T(2,128)}, u32[]{:S(2)}) copy-start(s32[1,128,2]{1,2,0:T(2,128)} %param.10) | copy-start | bytes 3076
  2.3 8.3 %collective-permute-start = (bf16[128,640]{1,0:T(8,128)(2,1)S(1)}, bf16[128,640]{1,0:T(8,128)(2,1)S(1)}, u32[]{:S(2)}, u32[]{:S(2)}) collective-permute-start(bf16[128,640]{1,0:T(8,128)(2,1)S(1)} %maximum_maximum_fusion.1), channel_id=1, source_target_pairs={{0,2},{1,3},{2,4},{3,5},{4,6},{5,7},{8,10},{9,11},{10,12},{11,13},... | collective-permute-start | bytes 491528 | tf_op jit(solution)/shard_map/ppermute | solution.py:88
  7.2 4.0 %collective-permute-start.1 = (bf16[128,640]{1,0:T(8,128)(2,1)S(1)}, bf16[128,640]{1,0:T(8,128)(2,1)S(1)}, u32[]{:S(2)}, u32[]{:S(2)}) collective-permute-start(bf16[128,640]{1,0:T(8,128)(2,1)S(1)} %maximum_maximum_fusion.1), channel_id=1, source_target_pairs={{0,1},{1,2},{2,3},{3,4},{4,5},{5,6},{6,7},{8,9},{9,10},{10,11},{11... | collective-permute-start | bytes 491528 | tf_op jit(solution)/shard_map/ppermute | solution.py:88
  9.0 0.6 %copy-start.2 = (bf16[128,256]{1,0:T(8,128)(2,1)}, bf16[128,256]{1,0:T(8,128)(2,1)S(1)}, u32[]{:S(2)}) copy-start(bf16[128,256]{1,0:T(8,128)(2,1)S(1)} %fusion.7.s_ref) | copy-start | bytes 196612
  10.6 9.1 %copy-start.5 = (bf16[128,640]{1,0:T(8,128)(2,1)}, bf16[128,640]{1,0:T(8,128)(2,1)S(1)}, u32[]{:S(2)}) copy-start(bf16[128,640]{1,0:T(8,128)(2,1)S(1)} %collective-permute-done) | copy-start | bytes 491524
  11.9 18.6 %collective-permute-start.2 = (f32[2,128,128]{2,1,0:T(8,128)S(1)}, f32[2,128,128]{2,1,0:T(8,128)S(1)}, u32[]{:S(2)}, u32[]{:S(2)}) collective-permute-start(f32[2,128,128]{2,1,0:T(8,128)S(1)} %maximum_add_fusion.1), channel_id=1, source_target_pairs={{0,3},{1,4},{2,5},{3,6},{4,7},{8,11},{9,12},{10,13},{11,14},{12,15... | collective-permute-start | bytes 393224 | tf_op jit(solution)/shard_map/ppermute | solution.py:88
  16.6 13.9 %collective-permute-start.3 = (f32[2,128,128]{2,1,0:T(8,128)S(1)}, f32[2,128,128]{2,1,0:T(8,128)S(1)}, u32[]{:S(2)}, u32[]{:S(2)}) collective-permute-start(f32[2,128,128]{2,1,0:T(8,128)S(1)} %maximum_add_fusion.1), channel_id=1, source_target_pairs={{0,6},{1,7},{8,14},{9,15},{16,22},{17,23},{24,30},{25,31}} | collective-permute-start | bytes 393224 | tf_op jit(solution)/shard_map/ppermute | solution.py:88
  19.7 0.9 %slice-start = ((bf16[128,640]{1,0:T(8,128)(2,1)}), bf16[128,512]{1,0:T(8,128)(2,1)S(1)}, s32[]{:S(2)}) async-start(bf16[128,640]{1,0:T(8,128)(2,1)} %copy-done.5), calls=%async_computation | async-start | bytes 262144 | tf_op jit(solution)/shard_map/slice | solution.py:268
  27.9 8.3 %collective-permute-start.4 = (bf16[128,512]{1,0:T(8,128)(2,1)S(1)}, bf16[128,512]{1,0:T(8,128)(2,1)S(1)}, u32[]{:S(2)}, u32[]{:S(2)}) collective-permute-start(bf16[128,512]{1,0:T(8,128)(2,1)S(1)} %get-tuple-element.31), channel_id=1, source_target_pairs={{1,0},{2,1},{3,2},{4,3},{5,4},{6,5},{7,6},{9,8},{10,9},{11,10},{12... | collective-permute-start | bytes 393224 | tf_op jit(solution)/shard_map/ppermute | solution.py:88
  29.2 8.5 %collective-permute-start.5 = (bf16[128,512]{1,0:T(8,128)(2,1)S(1)}, bf16[128,512]{1,0:T(8,128)(2,1)S(1)}, u32[]{:S(2)}, u32[]{:S(2)}) collective-permute-start(bf16[128,512]{1,0:T(8,128)(2,1)S(1)} %get-tuple-element.32), channel_id=1, source_target_pairs={{2,0},{3,1},{4,2},{5,3},{6,4},{7,5},{10,8},{11,9},{12,10},{13,11},... | collective-permute-start | bytes 393224 | tf_op jit(solution)/shard_map/ppermute | solution.py:88
  31.2 6.5 %copy-start.6 = (f32[128,512]{1,0:T(8,128)S(1)}, f32[128,512]{1,0:T(8,128)}, u32[]{:S(2)}) copy-start(f32[128,512]{1,0:T(8,128)} %get-tuple-element.22) | copy-start | bytes 786436
  37.7 0.9 %copy-start.9 = (bf16[272,128]{1,0:T(8,128)(2,1)S(1)}, bf16[272,128]{1,0:T(8,128)(2,1)}, u32[]{:S(2)}) copy-start(bf16[272,128]{1,0:T(8,128)(2,1)} %get-tuple-element.24) | copy-start | bytes 208900
  38.6 1.3 %collective-permute-start.6 = (bf16[272,128]{1,0:T(8,128)(2,1)S(1)}, bf16[272,128]{1,0:T(8,128)(2,1)S(1)}, u32[]{:S(2)}, u32[]{:S(2)}) collective-permute-start(bf16[272,128]{1,0:T(8,128)(2,1)S(1)} %copy-done.9), channel_id=1, source_target_pairs={{0,1},{1,0},{2,3},{3,2},{4,5},{5,4},{6,7},{7,6},{8,9},{9,8},{10,11... | collective-permute-start | bytes 208904 | tf_op jit(solution)/shard_map/ppermute | solution.py:45
  39.9 4.6 %collective-permute-start.7 = (bf16[272,128]{1,0:T(8,128)(2,1)S(1)}, bf16[272,128]{1,0:T(8,128)(2,1)S(1)}, u32[]{:S(2)}, u32[]{:S(2)}) collective-permute-start(bf16[272,128]{1,0:T(8,128)(2,1)S(1)} %fusion.3), channel_id=1, source_target_pairs={{0,2},{1,3},{2,0},{3,1},{4,6},{5,7},{6,4},{7,5},{8,10},{9,11},{10,... | collective-permute-start | bytes 208904 | tf_op jit(solution)/shard_map/ppermute | solution.py:45
  44.5 5.5 %collective-permute-start.8 = (bf16[272,128]{1,0:T(8,128)(2,1)S(1)}, bf16[272,128]{1,0:T(8,128)(2,1)S(1)}, u32[]{:S(2)}, u32[]{:S(2)}) collective-permute-start(bf16[272,128]{1,0:T(8,128)(2,1)S(1)} %fusion.4), channel_id=1, source_target_pairs={{0,4},{1,5},{2,6},{3,7},{4,0},{5,1},{6,2},{7,3},{8,12},{9,13},{10,... | collective-permute-start | bytes 208904 | tf_op jit(solution)/shard_map/ppermute | solution.py:45
  47.7 2.3 %copy-start.3 = (bf16[128,256]{1,0:T(8,128)(2,1)S(1)}, bf16[128,256]{1,0:T(8,128)(2,1)}, u32[]{:S(2)}) copy-start(bf16[128,256]{1,0:T(8,128)(2,1)} %copy-done.2) | copy-start | bytes 196612
  47.7 2.3 %copy-start.8 = (f32[128,256]{1,0:T(8,128)S(1)}, f32[128,256]{1,0:T(8,128)}, u32[]{:S(2)}) copy-start(f32[128,256]{1,0:T(8,128)} %get-tuple-element.20) | copy-start | bytes 393220
  50.3 1.7 %copy-start.1 = (bf16[1,128,256]{2,1,0:T(8,128)(2,1)S(1)}, bf16[1,128,256]{2,1,0:T(8,128)(2,1)}, u32[]{:S(2)}) copy-start(bf16[1,128,256]{2,1,0:T(8,128)(2,1)} %param.8) | copy-start | bytes 196612
  50.4 1.7 %copy-start.7 = (f32[128,256]{1,0:T(8,128)S(1)}, f32[128,256]{1,0:T(8,128)}, u32[]{:S(2)}) copy-start(f32[128,256]{1,0:T(8,128)} %get-tuple-element.26) | copy-start | bytes 393220
  50.4 3.7 %collective-permute-start.9 = (f32[1792]{0:T(1024)S(1)}, f32[1792]{0:T(1024)S(1)}, u32[]{:S(2)}, u32[]{:S(2)}) collective-permute-start(f32[1792]{0:T(1024)S(1)} %fusion.43), channel_id=1, source_target_pairs={{0,8},{8,0},{16,24},{24,16},{1,9},{9,1},{17,25},{25,17},{2,10},{10... | collective-permute-start | bytes 21512 | tf_op jit(solution)/shard_map/ppermute | solution.py:80
  54.1 4.5 %collective-permute-start.10 = (f32[1792]{0:T(1024)S(1)}, f32[1792]{0:T(1024)S(1)}, u32[]{:S(2)}, u32[]{:S(2)}) collective-permute-start(f32[1792]{0:T(1024)S(1)} %add.74), channel_id=1, source_target_pairs={{0,16},{8,24},{16,0},{24,8},{1,17},{9,25},{17,1},{25,9},{2,18},{10... | collective-permute-start | bytes 21512 | tf_op jit(solution)/shard_map/ppermute | solution.py:80

commit v18 on v14

--- a/solution.py
+++ b/solution.py
@@ -1,3 +1,5 @@
+import functools
+
 import jax
 import jax.numpy as jnp
 from jax import lax
@@ -53,7 +55,7 @@
 
 def spread_scan(near, own, axis):
     count = lax.axis_size(axis)
-    total = near
+    terms = [near]
     running = own
     stride = 3
     while stride < count:
@@ -61,13 +63,12 @@
         for distance in (stride, 2 * stride):
             if distance < count:
                 parts.append(shifted(running, axis, distance))
-        for got in parts:
-            total = total + got
+        terms.extend(parts)
         if 3 * stride < count:
             for got in parts:
                 running = running + got
         stride *= 3
-    return total
+    return terms
 
 
 def all_sum(part, axes):
@@ -142,8 +143,9 @@
         own_ref[:, value_lanes] = dv[padding_rows:]
 
 
-def linear_kernel(q_ref, c_ref, k_ref, s_ref, prior_ref, gain_ref, wout_ref, wdq_ref,
-                  mixed_ref, dq_ref, riding_ref, ldk_ref, dsp_ref):
+def linear_kernel(prior_count, q_ref, c_ref, k_ref, s_ref, *refs):
+    prior_refs = refs[:prior_count]
+    gain_ref, wout_ref, wdq_ref, mixed_ref, dq_ref, riding_ref, ldk_ref, dsp_ref = refs[prior_count:]
     group_size = QUERY_HEADS // KEY_VALUE_HEADS
     token_rows = q_ref.shape[0]
     stacked_rows = group_size * token_rows
@@ -155,7 +157,10 @@
         lanes = slice(g * HEAD_SIZE, (g + 1) * HEAD_SIZE)
         kg = k_ref[:, lanes]
         sg = s_ref[:, lanes]
-        pg = prior_ref[g]
+        pg = prior_refs[0][g]
+        for extra in prior_refs[1:]:
+            pg = pg + extra[g]
+        pg = pg.astype(jnp.bfloat16)
         qs = stacked_heads(q_ref, g, group_size)
         cs = stacked_heads(c_ref, g, group_size).astype(jnp.float32)
         gs = jnp.concatenate(
@@ -263,7 +268,7 @@
         ).astype(jnp.bfloat16)
         near = near + state_of(piece[:, :key_value_width], piece_spiked)
     own_and_near = near + state_of(k, spiked)
-    prior_half = spread_scan(near, own_and_near, "ctx").astype(jnp.bfloat16)
+    prior_terms = spread_scan(near, own_and_near, "ctx")
     window_packed = jnp.concatenate(
         [piece[:, : 2 * key_value_width] for piece in earlier] + [jnp.concatenate([k, v], axis=1)], axis=0
     )
@@ -287,7 +292,7 @@
     gain_rows = width // HEAD_SIZE
     riding_rows = state_rows + gain_rows + (-(state_rows + gain_rows)) % 16
     mixed, d_queries, riding, ldk, dsp = pl.pallas_call(
-        linear_kernel,
+        functools.partial(linear_kernel, len(prior_terms)),
         out_shape=(
             jax.ShapeDtypeStruct((token_rows, width), jnp.bfloat16),
             jax.ShapeDtypeStruct((token_rows, width), jnp.bfloat16),
@@ -295,14 +300,14 @@
             jax.ShapeDtypeStruct((token_rows, key_value_width), jnp.float32),
             jax.ShapeDtypeStruct((token_rows, key_value_width), jnp.float32),
         ),
-        in_specs=in_vmem(8),
+        in_specs=in_vmem(7 + len(prior_terms)),
         out_specs=tuple(in_vmem(5)),
         cost_estimate=pl.CostEstimate(
             flops=20 * QUERY_HEADS * token_rows * token_rows * HEAD_SIZE,
             transcendentals=QUERY_HEADS * token_rows,
             bytes_accessed=token_rows * width * (2 + 2 + 4 + 4 + 2 + 2) + 6 * token_rows * key_value_width * 4,
         ),
-    )(q, c, k, spiked, prior_half, gain, wout, wdq)
+    )(q, c, k, spiked, *prior_terms, gain, wout, wdq)
     total_tokens = queries.shape[0] * lax.axis_size("dp") * token_rows * lax.axis_size("ctx")
     later_rows, total_rows = butterfly_scan(riding, "ctx", True)
     later_half = later_rows[:state_rows].reshape(KEY_VALUE_HEADS, HEAD_SIZE, HEAD_SIZE).astype(jnp.bfloat16)

time: 56.1 us -> 56.8 us (1.012)
  local copies, waits for them, and re-layouts: 5.32 us -> 5.99 us
    unnamed x23 -> x27, local copies, waits for them, and re-layouts: 2.86 us -> 3.54 us
    convert_element_type x1 -> x0, other arithmetic: 0.66 us -> none  [per_device(): prior_half = spread_scan(near, own_and_near, 'ctx').astype(jnp.bfloat16)]
    add x1, other arithmetic: 0.03 us -> 0.68 us  [per_device(): own_and_near = near + state_of(k, spiked)]
where the time goes in v18:
time: 56.8 us; the launch traced here: 56.4 us
  starting transfers between devices  24.8 us (44%)
  Pallas kernels  10.6 us (19%)
  waiting for transfers between devices  9.2 us (16%)
  local copies, waits for them, and re-layouts  5.99 us (11%)
  other arithmetic  3.14 us (6%)
  matrix products  1.69 us (3%)
  between operations  0.97 us (2%)
    ppermute x6, starting transfers between devices, shifted(): return lax.ppermute(block, axis, route)  16.8 us
    pallas_call x1, Pallas kernels, per_device(): pl.pallas_call(window_kernel, out_shape=(jax.ShapeDtypeStruct((token_rows...  5.55 us
    pallas_call x1, Pallas kernels, per_device(): pl.pallas_call(functools.partial(linear_kernel, len(prior_terms)), out_sh...  5.07 us
    ppermute x2, starting transfers between devices, all_sum(): part = part + lax.ppermute(part, axes, route)  4.22 us
    ppermute x3, starting transfers between devices, butterfly_scan(): lax.ppermute(mine, axis, [(i, i ^ step) for i in range(count)])  3.74 us
    unnamed x27, local copies, waits for them, and re-layouts  3.54 us
    ppermute x6, waiting for transfers between devices, shifted(): return lax.ppermute(block, axis, route)  3.35 us
    ppermute x2, waiting for transfers between devices, all_sum(): part = part + lax.ppermute(part, axes, route)  3.08 us
  transfers between devices with their start and end apart: 11, of which 6 were waited for; matrix products, arithmetic and copies ran while one was open for 6% of the time, Pallas kernels for 10%

profile of v18, /device:TPU:0, one launch (start us, length us, event | category | flops | bytes accessed | tf_op | source)
XLA Modules:
  0.0 56.4 jit_solution(7267745451950872431)
XLA Ops:
  0.6 0.8 %copy.13 = s32[1,128,2]{2,1,0:T(8,128)S(1)} copy(s32[1,128,2]{1,2,0:T(2,128)} %param.10) | data formatting | bytes 2048 | tf_op args[3]
  1.5 0.1 pad.17.clone
  1.6 0.7 %copy-done = bf16[1,128,256]{2,1,0:T(8,128)(2,1)S(1)} copy-done((bf16[1,128,256]{2,1,0:T(8,128)(2,1)S(1)}, bf16[1,128,256]{2,1,0:T(8,128)(2,1)}, u32[]{:S(2)}) %copy-start) | copy-done | bytes 65560
  2.3 4.9 %collective-permute-start = (bf16[128,640]{1,0:T(8,128)(2,1)S(1)}, bf16[128,640]{1,0:T(8,128)(2,1)S(1)}, u32[]{:S(2)}, u32[]{:S(2)}) collective-permute-start(bf16[128,640]{1,0:T(8,128)(2,1)S(1)} %maximum_maximum_fusion.1), channel_id=1, source_target_pairs={{0,2},{1,3},{2,4},{3,5},{4,6},{5,7},{8,10},{9,11},{10,12},{11,13},... | collective-permute-start | bytes 491528 | tf_op jit(solution)/shard_map/ppermute | solution.py:89
  7.2 1.5 %collective-permute-start.1 = (bf16[128,640]{1,0:T(8,128)(2,1)S(1)}, bf16[128,640]{1,0:T(8,128)(2,1)S(1)}, u32[]{:S(2)}, u32[]{:S(2)}) collective-permute-start(bf16[128,640]{1,0:T(8,128)(2,1)S(1)} %maximum_maximum_fusion.1), channel_id=1, source_target_pairs={{0,1},{1,2},{2,3},{3,4},{4,5},{5,6},{6,7},{8,9},{9,10},{10,11},{11... | collective-permute-start | bytes 491528 | tf_op jit(solution)/shard_map/ppermute | solution.py:89
  8.7 0.1 copy.12
  8.8 0.2 broadcast_in_dim.30
  9.0 0.2 convolution_bitcast_fusion.2
  9.2 0.4 copy-done.2
  9.7 0.2 convolution_bitcast_fusion.3
  9.9 0.8 %collective-permute-done = bf16[128,640]{1,0:T(8,128)(2,1)S(1)} collective-permute-done((bf16[128,640]{1,0:T(8,128)(2,1)S(1)}, bf16[128,640]{1,0:T(8,128)(2,1)S(1)}, u32[]{:S(2)}, u32[]{:S(2)}) %collective-permute-start) | collective-permute-done | bytes 163872 | tf_op jit(solution)/shard_map/ppermute | solution.py:89
  10.6 0.2 broadcast_in_dim.32
  10.9 0.2 convolution_bitcast_fusion.6
  11.1 0.2 convolution_bitcast_fusion.7
  11.3 0.2 broadcast_in_dim.33
  11.5 0.2 convolution_bitcast_fusion.5
  11.7 0.2 convolution_bitcast_fusion.4
  11.9 0.7 %maximum_add_fusion.1 = (f32[2,128,128]{2,1,0:T(8,128)S(1)}, f32[2,128,128]{2,1,0:T(8,128)}) fusion(f32[1,128,128]{2,1,0:T(8,128)S(1)} %convolution_bitcast_fusion.2, f32[1,128,128]{2,1,0:T(8,128)S(1)} %convolution_bitcast_fusion.3, f32[1,128,128]{2,1,0:T(8,128)S(1)} %convolution_bitcast_fusion.4, f32[1,128,128]{2,1,0:T(8,128)S(1)} %convolution_bitcast_fusion.5, ...), kind=kLoop, calls=%fused_computation.32 | loop fusion | flops 163840 | bytes 655360 | tf_op jit(solution)/shard_map/add | solution.py:270
  12.5 4.7 %collective-permute-start.2 = (f32[2,128,128]{2,1,0:T(8,128)S(1)}, f32[2,128,128]{2,1,0:T(8,128)S(1)}, u32[]{:S(2)}, u32[]{:S(2)}) collective-permute-start(f32[2,128,128]{2,1,0:T(8,128)S(1)} %get-tuple-element.23), channel_id=1, source_target_pairs={{0,3},{1,4},{2,5},{3,6},{4,7},{8,11},{9,12},{10,13},{11,14},{12,15... | collective-permute-start | bytes 393224 | tf_op jit(solution)/shard_map/ppermute | solution.py:89
  17.2 3.1 %collective-permute-start.3 = (f32[2,128,128]{2,1,0:T(8,128)S(1)}, f32[2,128,128]{2,1,0:T(8,128)S(1)}, u32[]{:S(2)}, u32[]{:S(2)}) collective-permute-start(f32[2,128,128]{2,1,0:T(8,128)S(1)} %get-tuple-element.23), channel_id=1, source_target_pairs={{0,6},{1,7},{8,14},{9,15},{16,22},{17,23},{24,30},{25,31}} | collective-permute-start | bytes 393224 | tf_op jit(solution)/shard_map/ppermute | solution.py:89
  20.4 0.9 %slice-done = bf16[128,512]{1,0:T(8,128)(2,1)S(1)} async-done(((bf16[128,640]{1,0:T(8,128)(2,1)}), bf16[128,512]{1,0:T(8,128)(2,1)S(1)}, s32[]{:S(2)}) %slice-start) | async-done | bytes 131096 | tf_op jit(solution)/shard_map/slice | solution.py:273
  21.3 0.8 %fusion.44 = (bf16[384,256]{1,0:T(8,128)(2,1)}, bf16[384,256]{1,0:T(8,128)(2,1)}) fusion(bf16[384,512]{1,0:T(8,128)(2,1)S(1)} %maximum_maximum_fusion), kind=kLoop, calls=%fused_computation.70 | loop fusion | bytes 786432 | tf_op jit(solution)/shard_map/slice | solution.py:290
  22.0 5.5 %shard_map.110 = (f32[128,1792]{1,0:T(8,128)}, f32[128,1792]{1,0:T(8,128)}, bf16[2,128,512]{2,1,0:T(8,128)(2,1)}, f32[128,512]{1,0:T(8,128)}) custom-call(s32[2]{0:T(128)} %info_ref.1, bf16[128,1792]{1,0:T(8,128)(2,1)} %bitcast.80, bf16[128,1792]{1,0:T(8,128)(2,1)} %bitcast.82, bf16[384,256]{1,0:T(8,128)(2,1)} %get-tuple-element.26.k_ref, ...), custom_call_target="tpu_custom_call" | custom-call | flops 1056964608 | bytes 3932160 | tf_op jit(solution)/shard_map/pallas_call | solution.py:275
  27.6 0.6 %copy-done.10 = f32[2,128,128]{2,1,0:T(8,128)} copy-done((f32[2,128,128]{2,1,0:T(8,128)}, f32[2,128,128]{2,1,0:T(8,128)S(1)}, u32[]{:S(2)}) %copy-start.10) | copy-done | bytes 131096
  28.2 0.1 copy-done.11
  28.3 5.1 %shard_map.111 = (bf16[128,1792]{1,0:T(8,128)(2,1)}, bf16[128,1792]{1,0:T(8,128)(2,1)}, bf16[272,128]{1,0:T(8,128)(2,1)}, f32[128,256]{1,0:T(8,128)}, f32[128,256]{1,0:T(8,128)}) custom-call(bf16[128,1792]{1,0:T(8,128)(2,1)} %bitcast.81, bf16[128,1792]{1,0:T(8,128)(2,1)} %bitcast.83, bf16[128,256]{1,0:T(8,128)(2,1)} %bitcast.67, bf16[128,256]{1,0:T(8,128)(2,1)} %copy-done.2, ...), custom_call_target="tpu_custom_call" | custom-call | flops 587202560 | bytes 4456448 | tf_op jit(solution)/shard_map/pallas_call | solution.py:294
  33.4 0.5 collective-permute-start.4
  33.9 1.1 %collective-permute-done.4 = bf16[272,128]{1,0:T(8,128)(2,1)S(1)} collective-permute-done((bf16[272,128]{1,0:T(8,128)(2,1)}, bf16[272,128]{1,0:T(8,128)(2,1)S(1)}, u32[]{:S(2)}, u32[]{:S(2)}) %collective-permute-start.4) | collective-permute-done | bytes 69664 | tf_op jit(solution)/shard_map/ppermute | solution.py:47
  35.0 0.9 %fusion.3 = bf16[272,128]{1,0:T(8,128)(2,1)S(1)} fusion(bf16[272,128]{1,0:T(8,128)(2,1)S(1)} %collective-permute-done.4, bf16[272,128]{1,0:T(8,128)(2,1)} %get-tuple-element.19), kind=kLoop, calls=%fused_computation.18 | loop fusion | flops 139264 | bytes 208896 | tf_op jit(solution)/shard_map/convert_element_type | solution.py:46
  35.9 0.1 collective-permute-start.5
  36.1 1.4 %collective-permute-start.7 = (bf16[128,512]{1,0:T(8,128)(2,1)S(1)}, bf16[128,512]{1,0:T(8,128)(2,1)S(1)}, u32[]{:S(2)}, u32[]{:S(2)}) collective-permute-start(bf16[128,512]{1,0:T(8,128)(2,1)S(1)} %get-tuple-element.29), channel_id=1, source_target_pairs={{1,0},{2,1},{3,2},{4,3},{5,4},{6,5},{7,6},{9,8},{10,9},{11,10},{12... | collective-permute-start | bytes 393224 | tf_op jit(solution)/shard_map/ppermute | solution.py:89
  37.5 1.3 %collective-permute-start.8 = (bf16[128,512]{1,0:T(8,128)(2,1)S(1)}, bf16[128,512]{1,0:T(8,128)(2,1)S(1)}, u32[]{:S(2)}, u32[]{:S(2)}) collective-permute-start(bf16[128,512]{1,0:T(8,128)(2,1)S(1)} %get-tuple-element.30), channel_id=1, source_target_pairs={{2,0},{3,1},{4,2},{5,3},{6,4},{7,5},{10,8},{11,9},{12,10},{13,11},... | collective-permute-start | bytes 393224 | tf_op jit(solution)/shard_map/ppermute | solution.py:89
  38.8 1.6 %collective-permute-done.5 = bf16[272,128]{1,0:T(8,128)(2,1)S(1)} collective-permute-done((bf16[272,128]{1,0:T(8,128)(2,1)S(1)}, bf16[272,128]{1,0:T(8,128)(2,1)S(1)}, u32[]{:S(2)}, u32[]{:S(2)}) %collective-permute-start.5) | collective-permute-done | bytes 69664 | tf_op jit(solution)/shard_map/ppermute | solution.py:47
  40.5 3.1 %collective-permute-start.6 = (bf16[272,128]{1,0:T(8,128)(2,1)S(1)}, bf16[272,128]{1,0:T(8,128)(2,1)S(1)}, u32[]{:S(2)}, u32[]{:S(2)}) collective-permute-start(bf16[272,128]{1,0:T(8,128)(2,1)S(1)} %fusion.4), channel_id=1, source_target_pairs={{0,4},{1,5},{2,6},{3,7},{4,0},{5,1},{6,2},{7,3},{8,12},{9,13},{10,... | collective-permute-start | bytes 208904 | tf_op jit(solution)/shard_map/ppermute | solution.py:47
  43.6 2.6 %collective-permute-done.8 = bf16[128,512]{1,0:T(8,128)(2,1)S(1)} collective-permute-done((bf16[128,512]{1,0:T(8,128)(2,1)S(1)}, bf16[128,512]{1,0:T(8,128)(2,1)S(1)}, u32[]{:S(2)}, u32[]{:S(2)}) %collective-permute-start.8) | collective-permute-done | bytes 131104 | tf_op jit(solution)/shard_map/ppermute | solution.py:89
  46.2 0.1 fusion.2
  46.3 0.8 %copy-done.3 = bf16[128,256]{1,0:T(8,128)(2,1)S(1)} copy-done((bf16[128,256]{1,0:T(8,128)(2,1)S(1)}, bf16[128,256]{1,0:T(8,128)(2,1)}, u32[]{:S(2)}) %copy-start.3) | copy-done | bytes 65560
  47.1 0.1 copy-done.9
  47.2 0.1 slice_add_fusion.4
  47.3 0.2 slice_add_fusion.3
  47.5 1.6 %collective-permute-start.9 = (f32[1792]{0:T(1024)S(1)}, f32[1792]{0:T(1024)S(1)}, u32[]{:S(2)}, u32[]{:S(2)}) collective-permute-start(f32[1792]{0:T(1024)S(1)} %fusion.43), channel_id=1, source_target_pairs={{0,8},{8,0},{16,24},{24,16},{1,9},{9,1},{17,25},{25,17},{2,10},{10... | collective-permute-start | bytes 21512 | tf_op jit(solution)/shard_map/ppermute | solution.py:81
  49.2 0.1 slice_add_fusion.2
  49.3 0.1 slice_add_fusion.1
  49.4 1.8 %collective-permute-done.9 = f32[1792]{0:T(1024)S(1)} collective-permute-done((f32[1792]{0:T(1024)S(1)}, f32[1792]{0:T(1024)S(1)}, u32[]{:S(2)}, u32[]{:S(2)}) %collective-permute-start.9) | collective-permute-done | bytes 7200 | tf_op jit(solution)/shard_map/ppermute | solution.py:81
  51.2 2.6 %collective-permute-start.10 = (f32[1792]{0:T(1024)S(1)}, f32[1792]{0:T(1024)S(1)}, u32[]{:S(2)}, u32[]{:S(2)}) collective-permute-start(f32[1792]{0:T(1024)S(1)} %add.66), channel_id=1, source_target_pairs={{0,16},{8,24},{16,0},{24,8},{1,17},{9,25},{17,1},{25,9},{2,18},{10... | collective-permute-start | bytes 21512 | tf_op jit(solution)/shard_map/ppermute | solution.py:81
  53.8 0.7 %fusion.12 = (bf16[1,128,256]{2,1,0:T(8,128)(2,1)}, bf16[1,128,256]{2,1,0:T(8,128)(2,1)}) fusion(f32[128,512]{1,0:T(8,128)S(1)} %convert_add_fusion, f32[16,8,2,128]{3,2,1,0:T(2,128)S(1)} %bitcast.75, f32[128,128]{1,0:T(8,128)S(1)} %slice_add_fusion.1, f32[128,128]{1,0:T(8,128)S(1)} %slice_add_fusion.2, f32[128,128]{1,0:T(8,128)S(1)} %slice_add_fusion.3, ...), kind=kLoop, calls=%fused_computation.36 | loop fusion | flops 229376 | bytes 786432 | tf_op jit(solution)/shard_map/broadcast_in_dim | solution.py:344
  54.5 1.3 %collective-permute-done.10 = f32[1792]{0:T(1024)S(1)} collective-permute-done((f32[1792]{0:T(1024)S(1)}, f32[1792]{0:T(1024)S(1)}, u32[]{:S(2)}, u32[]{:S(2)}) %collective-permute-start.10) | collective-permute-done | bytes 7200 | tf_op jit(solution)/shard_map/ppermute | solution.py:81
  55.8 0.6 %add_multiply_fusion = f32[1792]{0:T(1024)} fusion(f32[1792]{0:T(1024)S(1)} %add.66, f32[1792]{0:T(1024)S(1)} %collective-permute-done.10), kind=kLoop, calls=%fused_computation.68 | loop fusion | flops 3584 | bytes 21504 | tf_op jit(solution)/shard_map/mul | solution.py:315
  (43 shorter events, 0.3 us)
Async XLA Ops:
  0.6 0.9 %copy-start.4 = (bf16[1,128,256]{2,1,0:T(8,128)(2,1)S(1)}, bf16[1,128,256]{2,1,0:T(8,128)(2,1)}, u32[]{:S(2)}) copy-start(bf16[1,128,256]{2,1,0:T(8,128)(2,1)} %param.9) | copy-start | bytes 196612
  1.5 0.8 %copy-start = (bf16[1,128,256]{2,1,0:T(8,128)(2,1)S(1)}, bf16[1,128,256]{2,1,0:T(8,128)(2,1)}, u32[]{:S(2)}) copy-start(bf16[1,128,256]{2,1,0:T(8,128)(2,1)} %param.8) | copy-start | bytes 196612
  2.3 6.4 %copy-start.12 = (s32[1,128,2]{1,2,0:T(2,128)S(1)}, s32[1,128,2]{1,2,0:T(2,128)}, u32[]{:S(2)}) copy-start(s32[1,128,2]{1,2,0:T(2,128)} %param.10) | copy-start | bytes 3076
  2.3 8.3 %collective-permute-start = (bf16[128,640]{1,0:T(8,128)(2,1)S(1)}, bf16[128,640]{1,0:T(8,128)(2,1)S(1)}, u32[]{:S(2)}, u32[]{:S(2)}) collective-permute-start(bf16[128,640]{1,0:T(8,128)(2,1)S(1)} %maximum_maximum_fusion.1), channel_id=1, source_target_pairs={{0,2},{1,3},{2,4},{3,5},{4,6},{5,7},{8,10},{9,11},{10,12},{11,13},... | collective-permute-start | bytes 491528 | tf_op jit(solution)/shard_map/ppermute | solution.py:89
  7.2 4.0 %collective-permute-start.1 = (bf16[128,640]{1,0:T(8,128)(2,1)S(1)}, bf16[128,640]{1,0:T(8,128)(2,1)S(1)}, u32[]{:S(2)}, u32[]{:S(2)}) collective-permute-start(bf16[128,640]{1,0:T(8,128)(2,1)S(1)} %maximum_maximum_fusion.1), channel_id=1, source_target_pairs={{0,1},{1,2},{2,3},{3,4},{4,5},{5,6},{6,7},{8,9},{9,10},{10,11},{11... | collective-permute-start | bytes 491528 | tf_op jit(solution)/shard_map/ppermute | solution.py:89
  9.0 0.6 %copy-start.2 = (bf16[128,256]{1,0:T(8,128)(2,1)}, bf16[128,256]{1,0:T(8,128)(2,1)S(1)}, u32[]{:S(2)}) copy-start(bf16[128,256]{1,0:T(8,128)(2,1)S(1)} %fusion.7.s_ref) | copy-start | bytes 196612
  10.6 9.7 %copy-start.5 = (bf16[128,640]{1,0:T(8,128)(2,1)}, bf16[128,640]{1,0:T(8,128)(2,1)S(1)}, u32[]{:S(2)}) copy-start(bf16[128,640]{1,0:T(8,128)(2,1)S(1)} %collective-permute-done) | copy-start | bytes 491524
  12.5 15.1 %collective-permute-start.2 = (f32[2,128,128]{2,1,0:T(8,128)S(1)}, f32[2,128,128]{2,1,0:T(8,128)S(1)}, u32[]{:S(2)}, u32[]{:S(2)}) collective-permute-start(f32[2,128,128]{2,1,0:T(8,128)S(1)} %get-tuple-element.23), channel_id=1, source_target_pairs={{0,3},{1,4},{2,5},{3,6},{4,7},{8,11},{9,12},{10,13},{11,14},{12,15... | collective-permute-start | bytes 393224 | tf_op jit(solution)/shard_map/ppermute | solution.py:89
  17.2 10.4 %collective-permute-start.3 = (f32[2,128,128]{2,1,0:T(8,128)S(1)}, f32[2,128,128]{2,1,0:T(8,128)S(1)}, u32[]{:S(2)}, u32[]{:S(2)}) collective-permute-start(f32[2,128,128]{2,1,0:T(8,128)S(1)} %get-tuple-element.23), channel_id=1, source_target_pairs={{0,6},{1,7},{8,14},{9,15},{16,22},{17,23},{24,30},{25,31}} | collective-permute-start | bytes 393224 | tf_op jit(solution)/shard_map/ppermute | solution.py:89
  20.3 0.9 %slice-start = ((bf16[128,640]{1,0:T(8,128)(2,1)}), bf16[128,512]{1,0:T(8,128)(2,1)S(1)}, s32[]{:S(2)}) async-start(bf16[128,640]{1,0:T(8,128)(2,1)} %copy-done.5), calls=%async_computation | async-start | bytes 262144 | tf_op jit(solution)/shard_map/slice | solution.py:273
  27.6 0.6 %copy-start.10 = (f32[2,128,128]{2,1,0:T(8,128)}, f32[2,128,128]{2,1,0:T(8,128)S(1)}, u32[]{:S(2)}) copy-start(f32[2,128,128]{2,1,0:T(8,128)S(1)} %collective-permute-done.2.refs_1_) | copy-start | bytes 393220
  27.6 0.7 %copy-start.11 = (f32[2,128,128]{2,1,0:T(8,128)}, f32[2,128,128]{2,1,0:T(8,128)S(1)}, u32[]{:S(2)}) copy-start(f32[2,128,128]{2,1,0:T(8,128)S(1)} %collective-permute-done.3.refs_2_) | copy-start | bytes 393220
  28.3 7.7 %copy-start.7 = (bf16[2,128,512]{2,1,0:T(8,128)(2,1)S(1)}, bf16[2,128,512]{2,1,0:T(8,128)(2,1)}, u32[]{:S(2)}) copy-start(bf16[2,128,512]{2,1,0:T(8,128)(2,1)} %get-tuple-element.21) | copy-start | bytes 786436
  33.4 1.7 %collective-permute-start.4 = (bf16[272,128]{1,0:T(8,128)(2,1)}, bf16[272,128]{1,0:T(8,128)(2,1)S(1)}, u32[]{:S(2)}, u32[]{:S(2)}) collective-permute-start(bf16[272,128]{1,0:T(8,128)(2,1)} %get-tuple-element.19), channel_id=1, source_target_pairs={{0,1},{1,0},{2,3},{3,2},{4,5},{5,4},{6,7},{7,6},{8,9},{9,8},{10,11... | collective-permute-start | bytes 208904 | tf_op jit(solution)/shard_map/ppermute | solution.py:47
  35.9 4.5 %collective-permute-start.5 = (bf16[272,128]{1,0:T(8,128)(2,1)S(1)}, bf16[272,128]{1,0:T(8,128)(2,1)S(1)}, u32[]{:S(2)}, u32[]{:S(2)}) collective-permute-start(bf16[272,128]{1,0:T(8,128)(2,1)S(1)} %fusion.3), channel_id=1, source_target_pairs={{0,2},{1,3},{2,0},{3,1},{4,6},{5,7},{6,4},{7,5},{8,10},{9,11},{10,... | collective-permute-start | bytes 208904 | tf_op jit(solution)/shard_map/ppermute | solution.py:47
  36.0 10.2 %copy-start.6 = (f32[128,512]{1,0:T(8,128)S(1)}, f32[128,512]{1,0:T(8,128)}, u32[]{:S(2)}) copy-start(f32[128,512]{1,0:T(8,128)} %get-tuple-element.20) | copy-start | bytes 786436
  36.1 7.5 %collective-permute-start.7 = (bf16[128,512]{1,0:T(8,128)(2,1)S(1)}, bf16[128,512]{1,0:T(8,128)(2,1)S(1)}, u32[]{:S(2)}, u32[]{:S(2)}) collective-permute-start(bf16[128,512]{1,0:T(8,128)(2,1)S(1)} %get-tuple-element.29), channel_id=1, source_target_pairs={{1,0},{2,1},{3,2},{4,3},{5,4},{6,5},{7,6},{9,8},{10,9},{11,10},{12... | collective-permute-start | bytes 393224 | tf_op jit(solution)/shard_map/ppermute | solution.py:89
  37.5 8.7 %collective-permute-start.8 = (bf16[128,512]{1,0:T(8,128)(2,1)S(1)}, bf16[128,512]{1,0:T(8,128)(2,1)S(1)}, u32[]{:S(2)}, u32[]{:S(2)}) collective-permute-start(bf16[128,512]{1,0:T(8,128)(2,1)S(1)} %get-tuple-element.30), channel_id=1, source_target_pairs={{2,0},{3,1},{4,2},{5,3},{6,4},{7,5},{10,8},{11,9},{12,10},{13,11},... | collective-permute-start | bytes 393224 | tf_op jit(solution)/shard_map/ppermute | solution.py:89
  40.5 5.8 %collective-permute-start.6 = (bf16[272,128]{1,0:T(8,128)(2,1)S(1)}, bf16[272,128]{1,0:T(8,128)(2,1)S(1)}, u32[]{:S(2)}, u32[]{:S(2)}) collective-permute-start(bf16[272,128]{1,0:T(8,128)(2,1)S(1)} %fusion.4), channel_id=1, source_target_pairs={{0,4},{1,5},{2,6},{3,7},{4,0},{5,1},{6,2},{7,3},{8,12},{9,13},{10,... | collective-permute-start | bytes 208904 | tf_op jit(solution)/shard_map/ppermute | solution.py:47
  46.2 0.8 %copy-start.3 = (bf16[128,256]{1,0:T(8,128)(2,1)S(1)}, bf16[128,256]{1,0:T(8,128)(2,1)}, u32[]{:S(2)}) copy-start(bf16[128,256]{1,0:T(8,128)(2,1)} %copy-done.2) | copy-start | bytes 196612
  46.2 0.9 %copy-start.9 = (f32[128,256]{1,0:T(8,128)S(1)}, f32[128,256]{1,0:T(8,128)}, u32[]{:S(2)}) copy-start(f32[128,256]{1,0:T(8,128)} %get-tuple-element.18) | copy-start | bytes 393220
  47.4 1.7 %copy-start.1 = (bf16[1,128,256]{2,1,0:T(8,128)(2,1)S(1)}, bf16[1,128,256]{2,1,0:T(8,128)(2,1)}, u32[]{:S(2)}) copy-start(bf16[1,128,256]{2,1,0:T(8,128)(2,1)} %param.8) | copy-start | bytes 196612
  47.5 1.7 %copy-start.8 = (f32[128,256]{1,0:T(8,128)S(1)}, f32[128,256]{1,0:T(8,128)}, u32[]{:S(2)}) copy-start(f32[128,256]{1,0:T(8,128)} %get-tuple-element.22) | copy-start | bytes 393220
  47.5 3.7 %collective-permute-start.9 = (f32[1792]{0:T(1024)S(1)}, f32[1792]{0:T(1024)S(1)}, u32[]{:S(2)}, u32[]{:S(2)}) collective-permute-start(f32[1792]{0:T(1024)S(1)} %fusion.43), channel_id=1, source_target_pairs={{0,8},{8,0},{16,24},{24,16},{1,9},{9,1},{17,25},{25,17},{2,10},{10... | collective-permute-start | bytes 21512 | tf_op jit(solution)/shard_map/ppermute | solution.py:81
  51.2 4.5 %collective-permute-start.10 = (f32[1792]{0:T(1024)S(1)}, f32[1792]{0:T(1024)S(1)}, u32[]{:S(2)}, u32[]{:S(2)}) collective-permute-start(f32[1792]{0:T(1024)S(1)} %add.66), channel_id=1, source_target_pairs={{0,16},{8,24},{16,0},{24,8},{1,17},{9,25},{17,1},{25,9},{2,18},{10... | collective-permute-start | bytes 21512 | tf_op jit(solution)/shard_map/ppermute | solution.py:81

commit v19 on v14

--- a/solution.py
+++ b/solution.py
@@ -263,7 +263,6 @@
         ).astype(jnp.bfloat16)
         near = near + state_of(piece[:, :key_value_width], piece_spiked)
     own_and_near = near + state_of(k, spiked)
-    prior_half = spread_scan(near, own_and_near, "ctx").astype(jnp.bfloat16)
     window_packed = jnp.concatenate(
         [piece[:, : 2 * key_value_width] for piece in earlier] + [jnp.concatenate([k, v], axis=1)], axis=0
     )
@@ -283,6 +282,8 @@
             bytes_accessed=2 * token_rows * width * (2 + 4) + 2 * window_rows * key_value_width * (2 + 4),
         ),
     )(window_lengths, q, c, window_packed[:, :key_value_width], window_packed[:, key_value_width:])
+    near, own_and_near, _ = lax.optimization_barrier((near, own_and_near, wdq))
+    prior_half = spread_scan(near, own_and_near, "ctx").astype(jnp.bfloat16)
     state_rows = KEY_VALUE_HEADS * HEAD_SIZE
     gain_rows = width // HEAD_SIZE
     riding_rows = state_rows + gain_rows + (-(state_rows + gain_rows)) % 16

time: 56.1 us -> 60.3 us (1.075)
  the two profiles are of different devices: /device:TPU:0 before, /device:TPU:26 now
where the time goes in v19:
time: 60.3 us; the launch traced here: 59.9 us
  starting transfers between devices  22.2 us (37%)
  waiting for transfers between devices  17.4 us (29%)
  Pallas kernels  10.5 us (17%)
  local copies, waits for them, and re-layouts  3.99 us (7%)
  other arithmetic  3.15 us (5%)
  matrix products  1.69 us (3%)
  between operations  0.93 us (2%)
    ppermute x6, starting transfers between devices, shifted(): return lax.ppermute(block, axis, route)  11.6 us
    ppermute x3, starting transfers between devices, butterfly_scan(): lax.ppermute(mine, axis, [(i, i ^ step) for i in range(count)])  9.7 us
    ppermute x6, waiting for transfers between devices, shifted(): return lax.ppermute(block, axis, route)  8.9 us
    ppermute x2, waiting for transfers between devices, all_sum(): part = part + lax.ppermute(part, axes, route)  6.09 us
    pallas_call x1, Pallas kernels, per_device(): pl.pallas_call(window_kernel, out_shape=(jax.ShapeDtypeStruct((token_rows...  5.55 us
    pallas_call x1, Pallas kernels, per_device(): pl.pallas_call(linear_kernel, out_shape=(jax.ShapeDtypeStruct((token_rows...  4.97 us
    ppermute x3, waiting for transfers between devices, butterfly_scan(): lax.ppermute(mine, axis, [(i, i ^ step) for i in range(count)])  2.44 us
    unnamed x21, local copies, waits for them, and re-layouts  2.41 us
  transfers between devices with their start and end apart: 11, of which 8 were waited for; matrix products, arithmetic and copies ran while one was open for 3% of the time, Pallas kernels for 0%

profile of v19, /device:TPU:26, one launch (start us, length us, event | category | flops | bytes accessed | tf_op | source)
XLA Modules:
  0.0 59.9 jit_solution(16694928704743731726)
XLA Ops:
  0.6 0.8 %copy.13 = s32[1,128,2]{2,1,0:T(8,128)S(1)} copy(s32[1,128,2]{1,2,0:T(2,128)} %param.10) | data formatting | bytes 2048 | tf_op args[3]
  1.5 0.1 pad.17.clone
  1.6 0.7 %copy-done = bf16[1,128,256]{2,1,0:T(8,128)(2,1)S(1)} copy-done((bf16[1,128,256]{2,1,0:T(8,128)(2,1)S(1)}, bf16[1,128,256]{2,1,0:T(8,128)(2,1)}, u32[]{:S(2)}) %copy-start) | copy-done | bytes 65560
  2.3 3.4 %collective-permute-start = (bf16[128,640]{1,0:T(8,128)(2,1)S(1)}, bf16[128,640]{1,0:T(8,128)(2,1)S(1)}, u32[]{:S(2)}, u32[]{:S(2)}) collective-permute-start(bf16[128,640]{1,0:T(8,128)(2,1)S(1)} %maximum_maximum_fusion.1), channel_id=1, source_target_pairs={{0,2},{1,3},{2,4},{3,5},{4,6},{5,7},{8,10},{9,11},{10,12},{11,13},... | collective-permute-start | bytes 491528 | tf_op jit(solution)/shard_map/ppermute | solution.py:88
  5.7 1.9 %collective-permute-start.1 = (bf16[128,640]{1,0:T(8,128)(2,1)S(1)}, bf16[128,640]{1,0:T(8,128)(2,1)S(1)}, u32[]{:S(2)}, u32[]{:S(2)}) collective-permute-start(bf16[128,640]{1,0:T(8,128)(2,1)S(1)} %maximum_maximum_fusion.1), channel_id=1, source_target_pairs={{0,1},{1,2},{2,3},{3,4},{4,5},{5,6},{6,7},{8,9},{9,10},{10,11},{11... | collective-permute-start | bytes 491528 | tf_op jit(solution)/shard_map/ppermute | solution.py:88
  7.7 0.1 copy.12
  7.8 0.2 broadcast_in_dim.30
  8.0 0.0 copy-start.2
  8.0 0.2 convolution_bitcast_fusion.2
  8.2 0.4 copy-done.2
  8.7 0.2 convolution_bitcast_fusion.3
  8.9 1.3 %collective-permute-done = bf16[128,640]{1,0:T(8,128)(2,1)S(1)} collective-permute-done((bf16[128,640]{1,0:T(8,128)(2,1)S(1)}, bf16[128,640]{1,0:T(8,128)(2,1)S(1)}, u32[]{:S(2)}, u32[]{:S(2)}) %collective-permute-start) | collective-permute-done | bytes 163872 | tf_op jit(solution)/shard_map/ppermute | solution.py:88
  10.2 2.2 %collective-permute-done.1 = bf16[128,640]{1,0:T(8,128)(2,1)S(1)} collective-permute-done((bf16[128,640]{1,0:T(8,128)(2,1)S(1)}, bf16[128,640]{1,0:T(8,128)(2,1)S(1)}, u32[]{:S(2)}, u32[]{:S(2)}) %collective-permute-start.1) | collective-permute-done | bytes 163872 | tf_op jit(solution)/shard_map/ppermute | solution.py:88
  12.4 0.8 %fusion.44 = (bf16[384,256]{1,0:T(8,128)(2,1)}, bf16[384,256]{1,0:T(8,128)(2,1)}) fusion(bf16[384,512]{1,0:T(8,128)(2,1)S(1)} %maximum_maximum_fusion), kind=kLoop, calls=%fused_computation.71 | loop fusion | bytes 786432 | tf_op jit(solution)/shard_map/slice | solution.py:284
  13.2 5.5 %shard_map.110 = (f32[128,1792]{1,0:T(8,128)}, f32[128,1792]{1,0:T(8,128)}, bf16[2,128,512]{2,1,0:T(8,128)(2,1)}, f32[128,512]{1,0:T(8,128)}) custom-call(s32[2]{0:T(128)} %info_ref.1, bf16[128,1792]{1,0:T(8,128)(2,1)} %bitcast.80, bf16[128,1792]{1,0:T(8,128)(2,1)} %bitcast.82, bf16[384,256]{1,0:T(8,128)(2,1)} %get-tuple-element.30.k_ref, ...), custom_call_target="tpu_custom_call" | custom-call | flops 1056964608 | bytes 3932160 | tf_op jit(solution)/shard_map/pallas_call | solution.py:269
  18.8 0.2 broadcast_in_dim.32
  19.0 0.2 convolution_bitcast_fusion.6
  19.2 0.2 convolution_bitcast_fusion.7
  19.4 0.2 broadcast_in_dim.33
  19.6 0.2 convolution_bitcast_fusion.5
  19.8 0.2 convolution_bitcast_fusion.4
  20.0 1.7 %collective-permute-start.2 = (f32[2,128,128]{2,1,0:T(8,128)S(1)}, f32[2,128,128]{2,1,0:T(8,128)S(1)}, u32[]{:S(2)}, u32[]{:S(2)}) collective-permute-start(f32[2,128,128]{2,1,0:T(8,128)S(1)} %get-tuple-element.18), channel_id=1, source_target_pairs={{0,3},{1,4},{2,5},{3,6},{4,7},{8,11},{9,12},{10,13},{11,14},{12,15... | collective-permute-start | bytes 393224 | tf_op jit(solution)/shard_map/ppermute | solution.py:88
  21.7 0.7 %collective-permute-start.3 = (f32[2,128,128]{2,1,0:T(8,128)S(1)}, f32[2,128,128]{2,1,0:T(8,128)S(1)}, u32[]{:S(2)}, u32[]{:S(2)}) collective-permute-start(f32[2,128,128]{2,1,0:T(8,128)S(1)} %get-tuple-element.18), channel_id=1, source_target_pairs={{0,6},{1,7},{8,14},{9,15},{16,22},{17,23},{24,30},{25,31}} | collective-permute-start | bytes 393224 | tf_op jit(solution)/shard_map/ppermute | solution.py:88
  22.4 1.8 %collective-permute-done.2 = f32[2,128,128]{2,1,0:T(8,128)S(1)} collective-permute-done((f32[2,128,128]{2,1,0:T(8,128)S(1)}, f32[2,128,128]{2,1,0:T(8,128)S(1)}, u32[]{:S(2)}, u32[]{:S(2)}) %collective-permute-start.2) | collective-permute-done | bytes 131104 | tf_op jit(solution)/shard_map/ppermute | solution.py:88
  24.2 0.7 %add_convert_fusion.prior_ref = bf16[2,128,128]{2,1,0:T(8,128)(2,1)} fusion(f32[2,128,128]{2,1,0:T(8,128)S(1)} %collective-permute-done.3, f32[2,128,128]{2,1,0:T(8,128)S(1)} %get-tuple-element.17, f32[2,128,128]{2,1,0:T(8,128)S(1)} %collective-permute-done.2), kind=kLoop, calls=%fused_computation.35 | loop fusion | flops 98304 | bytes 458752 | tf_op jit(solution)/shard_map/convert_element_type | solution.py:286
  24.9 5.0 %shard_map.111 = (bf16[128,1792]{1,0:T(8,128)(2,1)}, bf16[128,1792]{1,0:T(8,128)(2,1)}, bf16[272,128]{1,0:T(8,128)(2,1)}, f32[128,256]{1,0:T(8,128)}, f32[128,256]{1,0:T(8,128)}) custom-call(bf16[128,1792]{1,0:T(8,128)(2,1)} %bitcast.81, bf16[128,1792]{1,0:T(8,128)(2,1)} %bitcast.83, bf16[128,256]{1,0:T(8,128)(2,1)} %bitcast.67, bf16[128,256]{1,0:T(8,128)(2,1)} %copy-done.2, ...), custom_call_target="tpu_custom_call" | custom-call | flops 587202560 | bytes 4456448 | tf_op jit(solution)/shard_map/pallas_call | solution.py:290
  29.8 1.2 %collective-permute-start.4 = (bf16[272,128]{1,0:T(8,128)(2,1)}, bf16[272,128]{1,0:T(8,128)(2,1)S(1)}, u32[]{:S(2)}, u32[]{:S(2)}) collective-permute-start(bf16[272,128]{1,0:T(8,128)(2,1)} %get-tuple-element.23), channel_id=1, source_target_pairs={{0,1},{1,0},{2,3},{3,2},{4,5},{5,4},{6,7},{7,6},{8,9},{9,8},{10,11... | collective-permute-start | bytes 208904 | tf_op jit(solution)/shard_map/ppermute | solution.py:45
  31.1 1.1 %collective-permute-done.4 = bf16[272,128]{1,0:T(8,128)(2,1)S(1)} collective-permute-done((bf16[272,128]{1,0:T(8,128)(2,1)}, bf16[272,128]{1,0:T(8,128)(2,1)S(1)}, u32[]{:S(2)}, u32[]{:S(2)}) %collective-permute-start.4) | collective-permute-done | bytes 69664 | tf_op jit(solution)/shard_map/ppermute | solution.py:45
  32.2 0.9 %fusion.3 = bf16[272,128]{1,0:T(8,128)(2,1)S(1)} fusion(bf16[272,128]{1,0:T(8,128)(2,1)S(1)} %collective-permute-done.4, bf16[272,128]{1,0:T(8,128)(2,1)} %get-tuple-element.23), kind=kLoop, calls=%fused_computation.18 | loop fusion | flops 139264 | bytes 208896 | tf_op jit(solution)/shard_map/convert_element_type | solution.py:44
  33.1 4.5 %collective-permute-start.5 = (bf16[272,128]{1,0:T(8,128)(2,1)S(1)}, bf16[272,128]{1,0:T(8,128)(2,1)S(1)}, u32[]{:S(2)}, u32[]{:S(2)}) collective-permute-start(bf16[272,128]{1,0:T(8,128)(2,1)S(1)} %fusion.3), channel_id=1, source_target_pairs={{0,2},{1,3},{2,0},{3,1},{4,6},{5,7},{6,4},{7,5},{8,10},{9,11},{10,... | collective-permute-start | bytes 208904 | tf_op jit(solution)/shard_map/ppermute | solution.py:45
  37.6 2.1 %collective-permute-start.7 = (bf16[128,512]{1,0:T(8,128)(2,1)S(1)}, bf16[128,512]{1,0:T(8,128)(2,1)S(1)}, u32[]{:S(2)}, u32[]{:S(2)}) collective-permute-start(bf16[128,512]{1,0:T(8,128)(2,1)S(1)} %get-tuple-element.33), channel_id=1, source_target_pairs={{1,0},{2,1},{3,2},{4,3},{5,4},{6,5},{7,6},{9,8},{10,9},{11,10},{12... | collective-permute-start | bytes 393224 | tf_op jit(solution)/shard_map/ppermute | solution.py:88
  39.6 1.9 %collective-permute-start.8 = (bf16[128,512]{1,0:T(8,128)(2,1)S(1)}, bf16[128,512]{1,0:T(8,128)(2,1)S(1)}, u32[]{:S(2)}, u32[]{:S(2)}) collective-permute-start(bf16[128,512]{1,0:T(8,128)(2,1)S(1)} %get-tuple-element.34), channel_id=1, source_target_pairs={{2,0},{3,1},{4,2},{5,3},{6,4},{7,5},{10,8},{11,9},{12,10},{13,11},... | collective-permute-start | bytes 393224 | tf_op jit(solution)/shard_map/ppermute | solution.py:88
  41.6 4.0 %collective-permute-start.6 = (bf16[272,128]{1,0:T(8,128)(2,1)S(1)}, bf16[272,128]{1,0:T(8,128)(2,1)S(1)}, u32[]{:S(2)}, u32[]{:S(2)}) collective-permute-start(bf16[272,128]{1,0:T(8,128)(2,1)S(1)} %fusion.4), channel_id=1, source_target_pairs={{0,4},{1,5},{2,6},{3,7},{4,0},{5,1},{6,2},{7,3},{8,12},{9,13},{10,... | collective-permute-start | bytes 208904 | tf_op jit(solution)/shard_map/ppermute | solution.py:45
  45.6 3.6 %collective-permute-done.8 = bf16[128,512]{1,0:T(8,128)(2,1)S(1)} collective-permute-done((bf16[128,512]{1,0:T(8,128)(2,1)S(1)}, bf16[128,512]{1,0:T(8,128)(2,1)S(1)}, u32[]{:S(2)}, u32[]{:S(2)}) %collective-permute-start.8) | collective-permute-done | bytes 131104 | tf_op jit(solution)/shard_map/ppermute | solution.py:88
  49.2 0.0 copy-start.3
  49.3 1.3 %collective-permute-done.6 = bf16[272,128]{1,0:T(8,128)(2,1)S(1)} collective-permute-done((bf16[272,128]{1,0:T(8,128)(2,1)S(1)}, bf16[272,128]{1,0:T(8,128)(2,1)S(1)}, u32[]{:S(2)}, u32[]{:S(2)}) %collective-permute-start.6) | collective-permute-done | bytes 69664 | tf_op jit(solution)/shard_map/ppermute | solution.py:45
  50.6 0.1 slice_add_fusion.4
  50.8 0.2 slice_add_fusion.3
  51.0 0.5 collective-permute-start.9
  51.5 0.3 copy-done.1
  51.8 0.1 copy-done.7
  51.9 0.1 slice_add_fusion.2
  52.0 0.1 slice_add_fusion.1
  52.2 2.5 %collective-permute-done.9 = f32[1792]{0:T(1024)S(1)} collective-permute-done((f32[1792]{0:T(1024)S(1)}, f32[1792]{0:T(1024)S(1)}, u32[]{:S(2)}, u32[]{:S(2)}) %collective-permute-start.9) | collective-permute-done | bytes 7200 | tf_op jit(solution)/shard_map/ppermute | solution.py:80
  54.7 0.3 collective-permute-start.10
  55.0 0.7 %fusion.12 = (bf16[1,128,256]{2,1,0:T(8,128)(2,1)}, bf16[1,128,256]{2,1,0:T(8,128)(2,1)}) fusion(f32[128,512]{1,0:T(8,128)S(1)} %convert_add_fusion, f32[16,8,2,128]{3,2,1,0:T(2,128)S(1)} %bitcast.75, f32[128,128]{1,0:T(8,128)S(1)} %slice_add_fusion.1, f32[128,128]{1,0:T(8,128)S(1)} %slice_add_fusion.2, f32[128,128]{1,0:T(8,128)S(1)} %slice_add_fusion.3, ...), kind=kLoop, calls=%fused_computation.37 | loop fusion | flops 229376 | bytes 786432 | tf_op jit(solution)/shard_map/broadcast_in_dim | solution.py:340
  55.7 3.5 %collective-permute-done.10 = f32[1792]{0:T(1024)S(1)} collective-permute-done((f32[1792]{0:T(1024)S(1)}, f32[1792]{0:T(1024)S(1)}, u32[]{:S(2)}, u32[]{:S(2)}) %collective-permute-start.10) | collective-permute-done | bytes 7200 | tf_op jit(solution)/shard_map/ppermute | solution.py:80
  59.3 0.6 %add_multiply_fusion = f32[1792]{0:T(1024)} fusion(f32[1792]{0:T(1024)S(1)} %add.74, f32[1792]{0:T(1024)S(1)} %collective-permute-done.10), kind=kLoop, calls=%fused_computation.69 | loop fusion | flops 3584 | bytes 21504 | tf_op jit(solution)/shard_map/mul | solution.py:311
  (37 shorter events, 0.4 us)
Async XLA Ops:
  0.6 0.9 %copy-start.4 = (bf16[1,128,256]{2,1,0:T(8,128)(2,1)S(1)}, bf16[1,128,256]{2,1,0:T(8,128)(2,1)}, u32[]{:S(2)}) copy-start(bf16[1,128,256]{2,1,0:T(8,128)(2,1)} %param.9) | copy-start | bytes 196612
  1.5 0.8 %copy-start = (bf16[1,128,256]{2,1,0:T(8,128)(2,1)S(1)}, bf16[1,128,256]{2,1,0:T(8,128)(2,1)}, u32[]{:S(2)}) copy-start(bf16[1,128,256]{2,1,0:T(8,128)(2,1)} %param.8) | copy-start | bytes 196612
  2.3 5.4 %copy-start.9 = (s32[1,128,2]{1,2,0:T(2,128)S(1)}, s32[1,128,2]{1,2,0:T(2,128)}, u32[]{:S(2)}) copy-start(s32[1,128,2]{1,2,0:T(2,128)} %param.10) | copy-start | bytes 3076
  2.3 7.8 %collective-permute-start = (bf16[128,640]{1,0:T(8,128)(2,1)S(1)}, bf16[128,640]{1,0:T(8,128)(2,1)S(1)}, u32[]{:S(2)}, u32[]{:S(2)}) collective-permute-start(bf16[128,640]{1,0:T(8,128)(2,1)S(1)} %maximum_maximum_fusion.1), channel_id=1, source_target_pairs={{0,2},{1,3},{2,4},{3,5},{4,6},{5,7},{8,10},{9,11},{10,12},{11,13},... | collective-permute-start | bytes 491528 | tf_op jit(solution)/shard_map/ppermute | solution.py:88
  5.7 6.6 %collective-permute-start.1 = (bf16[128,640]{1,0:T(8,128)(2,1)S(1)}, bf16[128,640]{1,0:T(8,128)(2,1)S(1)}, u32[]{:S(2)}, u32[]{:S(2)}) collective-permute-start(bf16[128,640]{1,0:T(8,128)(2,1)S(1)} %maximum_maximum_fusion.1), channel_id=1, source_target_pairs={{0,1},{1,2},{2,3},{3,4},{4,5},{5,6},{6,7},{8,9},{9,10},{10,11},{11... | collective-permute-start | bytes 491528 | tf_op jit(solution)/shard_map/ppermute | solution.py:88
  8.0 0.6 %copy-start.2 = (bf16[128,256]{1,0:T(8,128)(2,1)}, bf16[128,256]{1,0:T(8,128)(2,1)S(1)}, u32[]{:S(2)}) copy-start(bf16[128,256]{1,0:T(8,128)(2,1)S(1)} %fusion.7.s_ref) | copy-start | bytes 196612
  20.0 4.2 %collective-permute-start.2 = (f32[2,128,128]{2,1,0:T(8,128)S(1)}, f32[2,128,128]{2,1,0:T(8,128)S(1)}, u32[]{:S(2)}, u32[]{:S(2)}) collective-permute-start(f32[2,128,128]{2,1,0:T(8,128)S(1)} %get-tuple-element.18), channel_id=1, source_target_pairs={{0,3},{1,4},{2,5},{3,6},{4,7},{8,11},{9,12},{10,13},{11,14},{12,15... | collective-permute-start | bytes 393224 | tf_op jit(solution)/shard_map/ppermute | solution.py:88
  21.7 2.5 %collective-permute-start.3 = (f32[2,128,128]{2,1,0:T(8,128)S(1)}, f32[2,128,128]{2,1,0:T(8,128)S(1)}, u32[]{:S(2)}, u32[]{:S(2)}) collective-permute-start(f32[2,128,128]{2,1,0:T(8,128)S(1)} %get-tuple-element.18), channel_id=1, source_target_pairs={{0,6},{1,7},{8,14},{9,15},{16,22},{17,23},{24,30},{25,31}} | collective-permute-start | bytes 393224 | tf_op jit(solution)/shard_map/ppermute | solution.py:88
  24.8 12.7 %copy-start.6 = (bf16[2,128,512]{2,1,0:T(8,128)(2,1)S(1)}, bf16[2,128,512]{2,1,0:T(8,128)(2,1)}, u32[]{:S(2)}) copy-start(bf16[2,128,512]{2,1,0:T(8,128)(2,1)} %get-tuple-element.25) | copy-start | bytes 786436
  29.8 2.4 %collective-permute-start.4 = (bf16[272,128]{1,0:T(8,128)(2,1)}, bf16[272,128]{1,0:T(8,128)(2,1)S(1)}, u32[]{:S(2)}, u32[]{:S(2)}) collective-permute-start(bf16[272,128]{1,0:T(8,128)(2,1)} %get-tuple-element.23), channel_id=1, source_target_pairs={{0,1},{1,0},{2,3},{3,2},{4,5},{5,4},{6,7},{7,6},{8,9},{9,8},{10,11... | collective-permute-start | bytes 208904 | tf_op jit(solution)/shard_map/ppermute | solution.py:45
  33.1 8.5 %collective-permute-start.5 = (bf16[272,128]{1,0:T(8,128)(2,1)S(1)}, bf16[272,128]{1,0:T(8,128)(2,1)S(1)}, u32[]{:S(2)}, u32[]{:S(2)}) collective-permute-start(bf16[272,128]{1,0:T(8,128)(2,1)S(1)} %fusion.3), channel_id=1, source_target_pairs={{0,2},{1,3},{2,0},{3,1},{4,6},{5,7},{6,4},{7,5},{8,10},{9,11},{10,... | collective-permute-start | bytes 208904 | tf_op jit(solution)/shard_map/ppermute | solution.py:45
  37.6 11.6 %copy-start.5 = (f32[128,512]{1,0:T(8,128)S(1)}, f32[128,512]{1,0:T(8,128)}, u32[]{:S(2)}) copy-start(f32[128,512]{1,0:T(8,128)} %get-tuple-element.24) | copy-start | bytes 786436
  37.6 8.0 %collective-permute-start.7 = (bf16[128,512]{1,0:T(8,128)(2,1)S(1)}, bf16[128,512]{1,0:T(8,128)(2,1)S(1)}, u32[]{:S(2)}, u32[]{:S(2)}) collective-permute-start(bf16[128,512]{1,0:T(8,128)(2,1)S(1)} %get-tuple-element.33), channel_id=1, source_target_pairs={{1,0},{2,1},{3,2},{4,3},{5,4},{6,5},{7,6},{9,8},{10,9},{11,10},{12... | collective-permute-start | bytes 393224 | tf_op jit(solution)/shard_map/ppermute | solution.py:88
  39.6 9.5 %collective-permute-start.8 = (bf16[128,512]{1,0:T(8,128)(2,1)S(1)}, bf16[128,512]{1,0:T(8,128)(2,1)S(1)}, u32[]{:S(2)}, u32[]{:S(2)}) collective-permute-start(bf16[128,512]{1,0:T(8,128)(2,1)S(1)} %get-tuple-element.34), channel_id=1, source_target_pairs={{2,0},{3,1},{4,2},{5,3},{6,4},{7,5},{10,8},{11,9},{12,10},{13,11},... | collective-permute-start | bytes 393224 | tf_op jit(solution)/shard_map/ppermute | solution.py:88
  41.6 9.0 %collective-permute-start.6 = (bf16[272,128]{1,0:T(8,128)(2,1)S(1)}, bf16[272,128]{1,0:T(8,128)(2,1)S(1)}, u32[]{:S(2)}, u32[]{:S(2)}) collective-permute-start(bf16[272,128]{1,0:T(8,128)(2,1)S(1)} %fusion.4), channel_id=1, source_target_pairs={{0,4},{1,5},{2,6},{3,7},{4,0},{5,1},{6,2},{7,3},{8,12},{9,13},{10,... | collective-permute-start | bytes 208904 | tf_op jit(solution)/shard_map/ppermute | solution.py:45
  49.2 1.4 %copy-start.3 = (bf16[128,256]{1,0:T(8,128)(2,1)S(1)}, bf16[128,256]{1,0:T(8,128)(2,1)}, u32[]{:S(2)}) copy-start(bf16[128,256]{1,0:T(8,128)(2,1)} %copy-done.2) | copy-start | bytes 196612
  49.2 1.4 %copy-start.8 = (f32[128,256]{1,0:T(8,128)S(1)}, f32[128,256]{1,0:T(8,128)}, u32[]{:S(2)}) copy-start(f32[128,256]{1,0:T(8,128)} %get-tuple-element.22) | copy-start | bytes 393220
  50.9 0.9 %copy-start.1 = (bf16[1,128,256]{2,1,0:T(8,128)(2,1)S(1)}, bf16[1,128,256]{2,1,0:T(8,128)(2,1)}, u32[]{:S(2)}) copy-start(bf16[1,128,256]{2,1,0:T(8,128)(2,1)} %param.8) | copy-start | bytes 196612
  51.0 0.9 %copy-start.7 = (f32[128,256]{1,0:T(8,128)S(1)}, f32[128,256]{1,0:T(8,128)}, u32[]{:S(2)}) copy-start(f32[128,256]{1,0:T(8,128)} %get-tuple-element.26) | copy-start | bytes 393220
  51.0 3.7 %collective-permute-start.9 = (f32[1792]{0:T(1024)S(1)}, f32[1792]{0:T(1024)S(1)}, u32[]{:S(2)}, u32[]{:S(2)}) collective-permute-start(f32[1792]{0:T(1024)S(1)} %fusion.43), channel_id=1, source_target_pairs={{0,8},{8,0},{16,24},{24,16},{1,9},{9,1},{17,25},{25,17},{2,10},{10... | collective-permute-start | bytes 21512 | tf_op jit(solution)/shard_map/ppermute | solution.py:80
  54.7 4.5 %collective-permute-start.10 = (f32[1792]{0:T(1024)S(1)}, f32[1792]{0:T(1024)S(1)}, u32[]{:S(2)}, u32[]{:S(2)}) collective-permute-start(f32[1792]{0:T(1024)S(1)} %add.74), channel_id=1, source_target_pairs={{0,16},{8,24},{16,0},{24,8},{1,17},{9,25},{17,1},{25,9},{2,18},{10... | collective-permute-start | bytes 21512 | tf_op jit(solution)/shard_map/ppermute | solution.py:80
